TPU v7x, 32 devices: a whole 2x2x4 slice. The times are simulated.
32 devices in a mesh: tile: 8 (over z, x), inf: 4 (over y, core).
Axes of the slice: x: 2, y: 2, z: 4, core: 2. Of those that a mesh axis runs over, the one named last changes fastest.
Arguments:
- u_field: float32 [64, 512, 512], P(None, 'tile', 'inf'), may hold values from -6 to 6
- v_field: float32 [64, 512, 512], P(None, 'tile', 'inf'), may hold values from -6 to 6
- diffusivity: float32 [512, 512], P('tile', 'inf'), may hold values from 0.03 to 0.24
- active_columns: int32 [65536], P(('tile', 'inf')), may hold values from 0 to 8191, as said below
- regimes: int32 [65536, 1], P(('tile', 'inf')), may hold values from 0 to 31; in each aligned block of 2048 rows (0 to 2047, 2048 to 4095, ...) at most 128 rows name the same one
- first_layer: float32 [32, 128, 256], P(('tile', 'inf')), may hold values from -0.5 to 0.5
- second_layer: float32 [32, 256, 256], P(('tile', 'inf')), may hold values from -0.375 to 0.375
- third_layer: float32 [32, 256, 256], P(('tile', 'inf')), may hold values from -0.375 to 0.375
- last_layer: float32 [32, 256, 128], P(('tile', 'inf')), may hold values from -0.375 to 0.375
Outputs:
- u_next: float32 [64, 512, 512], P(None, 'tile', 'inf')
- v_next: float32 [64, 512, 512], P(None, 'tile', 'inf')
Inputs may be any that keep to these rules, and one draw needn't show every extreme that they name: `active_columns`: the 2048 entries of one device are distinct flat indices x * 128 + y of columns of its own tile. `regimes`: among the rows of one device no network is named more than 128 times.
All inputs are finite; a program needn't handle non-finite values.
Results may differ from a plain program's by a relative error of at most 0.0003.
Values sent between devices are 32-bit elements; how exact they have to be, the bound alone decides.
No kernel may reach another device: no remote copies, remote signals or barrier semaphores. Data moves between devices by JAX's collectives and lax.ppermute only.
A program may use at most 128 MiB of HBM per device.

v0:
```python
import jax
import jax.numpy as jnp
from jax import lax
from jax.experimental import pallas as pl
from jax.experimental.pallas import tpu as pltpu
from jax.sharding import PartitionSpec as P

PASSES = 4
LEVEL_BLOCK = 8


def halos(x, axis, dim, width):
    count, length = (lax.axis_size(axis), x.shape[dim])
    up = [(i, i + 1) for i in range(count - 1)]
    down = [(j, i) for i, j in up]
    last = lax.slice_in_dim(x, length - width, length, axis=dim)
    first = lax.slice_in_dim(x, 0, width, axis=dim)
    before = lax.ppermute(last, axis, up)
    after = lax.ppermute(first, axis, down)
    return before, after


def extend(x, width, lanes):
    before, after = halos(x, "tile", x.ndim - 2, width)
    x = jnp.concatenate([x, after, before], axis=x.ndim - 2)
    before, after = halos(x, "inf", x.ndim - 1, width)
    gap = lanes - x.shape[-1] - 2 * width
    filler = jnp.zeros(x.shape[:-1] + (gap,), x.dtype)
    return jnp.concatenate([x, after, filler, before], axis=x.ndim - 1)


def standardize(rows):
    center = jnp.mean(rows, axis=-1, keepdims=True)
    spread = jnp.mean(jnp.square(rows - center), axis=-1, keepdims=True)
    return (rows - center) * lax.rsqrt(spread + 1e-05)


def network_rows(rows, first_layer, second_layer, third_layer, last_layer):
    highest = lax.Precision.HIGHEST
    hidden = jax.nn.silu(jnp.dot(rows, first_layer, precision=highest))
    hidden = jax.nn.silu(jnp.dot(hidden, second_layer, precision=highest))
    hidden = jax.nn.silu(jnp.dot(hidden, third_layer, precision=highest))
    return jnp.dot(hidden, last_layer, precision=highest)


def gather_kernel(cell_ref, u_ref, v_ref, o_ref, t_ref):
    levels_x, width_y = u_ref.shape
    features = o_ref.shape[1]
    levels = features // 2
    width_x = levels_x // levels
    cells = width_x * width_y

    def transpose_tile(x, carry):
        a = u_ref[pl.ds(x, levels, stride=width_x), :]
        b = v_ref[pl.ds(x, levels, stride=width_x), :]
        tile = jnp.concatenate([a, b], axis=0)
        t_ref[pl.ds(pl.multiple_of(x * width_y, width_y), width_y), :] = tile.T
        return carry

    lax.fori_loop(0, width_x, transpose_tile, 0)
    t_ref[pl.ds(cells, 8), :] = jnp.zeros((8, features), jnp.float32)

    def pick(s, carry):
        o_ref[pl.ds(s, 1), :] = t_ref[pl.ds(cell_ref[s], 1), :]
        return carry

    lax.fori_loop(0, o_ref.shape[0], pick, 0, unroll=8)


def drag_kernel(slot_ref, act_ref, r_ref, du_ref, dv_ref, d_ref):
    levels_x, width_y = du_ref.shape
    features = r_ref.shape[1]
    levels = features // 2
    width_x = levels_x // levels

    def clear(x, carry):
        d_ref[pl.ds(pl.multiple_of(x * width_y, width_y), width_y), :] = jnp.zeros(
            (width_y, features), jnp.float32
        )
        return carry

    lax.fori_loop(0, width_x, clear, 0)

    def place(r, carry):
        d_ref[pl.ds(act_ref[r], 1), :] = r_ref[pl.ds(slot_ref[r], 1), :]
        return carry

    lax.fori_loop(0, act_ref.shape[0], place, 0, unroll=8)

    def transpose_tile(x, carry):
        tile = d_ref[pl.ds(pl.multiple_of(x * width_y, width_y), width_y), :].T
        du_ref[pl.ds(x, levels, stride=width_x), :] = tile[:levels]
        dv_ref[pl.ds(x, levels, stride=width_x), :] = tile[levels:]
        return carry

    lax.fori_loop(0, width_x, transpose_tile, 0)


def diffuse_kernel(eu_ref, ev_ref, c_ref, du_ref, dv_ref, ou_ref, ov_ref):
    rows, lanes = c_ref.shape
    width_x, width_y = ou_ref.shape[1:]

    def one(e_ref, d_ref, o_ref, l):
        coeff = c_ref[...]
        q = e_ref[l]
        for _ in range(PASSES):
            n = pltpu.roll(q, rows - 1, 0) + pltpu.roll(q, 1, 0)
            n = n + pltpu.roll(q, lanes - 1, 1) + pltpu.roll(q, 1, 1)
            q = q + coeff * (n - 4.0 * q)
        o_ref[l] = q[:width_x, :width_y] + d_ref[l]

    def step(l, carry):
        one(eu_ref, du_ref, ou_ref, l)
        one(ev_ref, dv_ref, ov_ref, l)
        return carry

    lax.fori_loop(0, eu_ref.shape[0], step, 0)


def body(
    u_field,
    v_field,
    diffusivity,
    active_columns,
    regimes,
    first_layer,
    second_layer,
    third_layer,
    last_layer,
):
    levels, width_x, width_y = u_field.shape
    features = 2 * levels
    cells = width_x * width_y
    active_count = active_columns.shape[0]
    devices_all = lax.axis_size(("tile", "inf"))
    capacity = 2 * active_count // devices_all
    slot_total = devices_all * capacity
    block_rows = min(512, active_count)
    block_count = active_count // block_rows
    target = regimes[:, 0]
    labels = jnp.arange(devices_all, dtype=jnp.int32)
    one_hot = (
        (target[:, None] == labels[None, :])
        .astype(jnp.bfloat16)
        .reshape(block_count, block_rows, devices_all)
    )
    row_ids = jnp.arange(block_rows, dtype=jnp.int32)
    lower = (row_ids[:, None] > row_ids[None, :]).astype(jnp.bfloat16)

    def rank_step(counts, piece):
        earlier = jnp.dot(lower, piece, preferred_element_type=jnp.float32) + counts[None, :]
        wide_piece = piece.astype(jnp.float32)
        rank = jnp.sum(earlier * wide_piece, axis=1)
        return (counts + jnp.sum(wide_piece, axis=0), rank)

    _, ranks = lax.scan(rank_step, jnp.zeros((devices_all,), jnp.float32), one_hot)
    slot_index = target * capacity + ranks.reshape(-1).astype(jnp.int32)
    cell_of_slot = jnp.full((slot_total,), cells, jnp.int32).at[slot_index].set(
        active_columns, unique_indices=True
    )
    vmem = pl.BlockSpec(memory_space=pltpu.VMEM)
    smem = pl.BlockSpec(memory_space=pltpu.SMEM)
    u_rows = u_field.reshape(levels * width_x, width_y)
    v_rows = v_field.reshape(levels * width_x, width_y)
    outgoing = pl.pallas_call(
        gather_kernel,
        out_shape=jax.ShapeDtypeStruct((slot_total, features), jnp.float32),
        in_specs=[smem, vmem, vmem],
        out_specs=vmem,
        scratch_shapes=[pltpu.VMEM((cells + 8, features), jnp.float32)],
    )(cell_of_slot, u_rows, v_rows)
    block = lax.all_to_all(
        outgoing.reshape(devices_all, capacity, features),
        ("tile", "inf"),
        split_axis=0,
        concat_axis=0,
        tiled=True,
    )
    block_shape = block.shape
    rows = standardize(block.reshape(-1, features))
    result = network_rows(rows, first_layer[0], second_layer[0], third_layer[0], last_layer[0])
    answered = result.reshape(block_shape)
    returned = lax.all_to_all(answered, ("tile", "inf"), split_axis=0, concat_axis=0, tiled=True)
    returned_rows = returned.reshape(slot_total, features)
    drag_u, drag_v = pl.pallas_call(
        drag_kernel,
        out_shape=(
            jax.ShapeDtypeStruct((levels * width_x, width_y), jnp.float32),
            jax.ShapeDtypeStruct((levels * width_x, width_y), jnp.float32),
        ),
        in_specs=[smem, smem, vmem],
        out_specs=(vmem, vmem),
        scratch_shapes=[pltpu.VMEM((cells, features), jnp.float32)],
    )(slot_index, active_columns, returned_rows)
    drag_u = drag_u.reshape(levels, width_x, width_y)
    drag_v = drag_v.reshape(levels, width_x, width_y)

    depth = PASSES
    lanes = 2 * width_y
    ext_u = extend(u_field, depth, lanes)
    ext_v = extend(v_field, depth, lanes)
    coeff = extend(diffusivity, depth, lanes)
    rows_ext = width_x + 2 * depth
    lb = LEVEL_BLOCK
    ext_spec = pl.BlockSpec((lb, rows_ext, lanes), lambda i: (i, 0, 0))
    field_spec = pl.BlockSpec((lb, width_x, width_y), lambda i: (i, 0, 0))
    u_next, v_next = pl.pallas_call(
        diffuse_kernel,
        out_shape=(
            jax.ShapeDtypeStruct(u_field.shape, jnp.float32),
            jax.ShapeDtypeStruct(v_field.shape, jnp.float32),
        ),
        grid=(levels // lb,),
        in_specs=[
            ext_spec,
            ext_spec,
            pl.BlockSpec((rows_ext, lanes), lambda i: (0, 0)),
            field_spec,
            field_spec,
        ],
        out_specs=(field_spec, field_spec),
    )(ext_u, ext_v, coeff, drag_u, drag_v)
    return (u_next, v_next)


def solution(mesh):
    in_specs = (
        P(None, "tile", "inf"),
        P(None, "tile", "inf"),
        P("tile", "inf"),
        P(("tile", "inf")),
        P(("tile", "inf"), None),
        P(("tile", "inf"), None, None),
        P(("tile", "inf"), None, None),
        P(("tile", "inf"), None, None),
        P(("tile", "inf"), None, None),
    )
    out_specs = (P(None, "tile", "inf"), P(None, "tile", "inf"))
    return jax.shard_map(body, mesh=mesh, in_specs=in_specs, out_specs=out_specs, check_vma=False)
```

profile of v0, /device:TPU:9, one launch (start us, length us, event | category | flops | bytes accessed | tf_op | source)
XLA Modules:
  0.0 275.7 jit_solution(12919973760576497277)
XLA Ops:
  2.6 1.9 while.13
  4.6 8.8 %scatter_custom_fusion.cell_ref = s32[4096]{0:T(1024)} fusion(s32[2048]{0:T(1024)S(1)} %bitcast.64, s32[2048]{0:T(1024)} %act_ref.1, s32[]{:T(128)} %constant.13.clone.1), kind=kCustom, calls=%fused_computation.47 | custom fusion | bytes 16896 | tf_op jit(solution)/shard_map/scatter | solution.py:158
  13.4 18.0 %shard_map.104 = f32[4096,128]{1,0:T(8,128)} custom-call(s32[4096]{0:T(1024)} %scatter_custom_fusion.cell_ref, f32[4096,128]{1,0:T(8,128)} %bitcast.54, f32[4096,128]{1,0:T(8,128)} %bitcast.53), custom_call_target="tpu_custom_call" | custom-call | tf_op jit(solution)/shard_map/pallas_call | solution.py:165
  31.4 54.1 %all_to_all.10 = f32[32,128,128]{2,1,0:T(8,128)S(1)} all-to-all(f32[32,128,128]{2,1,0:T(8,128)} %bitcast.56), channel_id=1, replica_groups=mesh['tile'=8,'inf'=4] {'tile','inf'}, dimensions={0} | all-to-all | bytes 4194304 | tf_op jit(solution)/shard_map/all_to_all | solution.py:172
  88.9 3.5 %fusion.31 = f32[4096,256]{1,0:T(8,128)S(1)} fusion(f32[4096,128]{1,0:T(8,128)S(1)} %bitcast.55, f32[1,128,256]{2,1,0:T(8,128)S(1)} %copy-done.4), kind=kOutput, calls=%fused_computation.40 | convolution fusion | flops 1610612736 | bytes 6422528 | tf_op jit(solution)/shard_map/dot_general | solution.py:40
  92.4 4.1 %fusion.16 = f32[4096,256]{1,0:T(8,128)S(1)} fusion(f32[4096,256]{1,0:T(8,128)S(1)} %fusion.31, f32[1,256,256]{2,1,0:T(8,128)S(1)} %copy-done), kind=kOutput, calls=%fused_computation.22 | convolution fusion | flops 3225419776 | bytes 8650752 | tf_op jit(solution)/shard_map/dot_general | solution.py:41
  96.6 4.6 %divide_multiply_fusion = f32[4096,256]{1,0:T(8,128)S(1)} fusion(f32[4096,256]{1,0:T(8,128)S(1)} %fusion.16, f32[1,256,256]{2,1,0:T(8,128)S(1)} %copy-done.9), kind=kOutput, calls=%fused_computation.15 | convolution fusion | flops 3229614080 | bytes 8650752 | tf_op jit(solution)/shard_map/dot_general | solution.py:42
  101.2 4.7 %fusion.29 = f32[32,128,128]{2,1,0:T(8,128)} fusion(f32[32,128,256]{2,1,0:T(8,128)S(1)} %bitcast.57, f32[1,256,128]{2,1,0:T(8,128)S(1)} %copy-done.5), kind=kOutput, calls=%fused_computation.38 | convolution fusion | flops 1610612736 | bytes 6422528 | tf_op jit(solution)/shard_map/dot_general | solution.py:43
  106.0 4.6 %all-to-all-start.1 = ((f32[32,128,128]{2,1,0:T(8,128)}), f32[32,128,128]{2,1,0:T(8,128)}, u32[]{:S(2)}, u32[]{:S(2)}) async-start(f32[32,128,128]{2,1,0:T(8,128)} %fusion.29), calls=%async_computation.1 | async-start | bytes 4194304 | tf_op jit(solution)/shard_map/all_to_all | solution.py:183
  111.7 3.1 %collective-permute-start = (f32[64,4,128]{2,1,0:T(4,128)S(1)}, f32[64,4,128]{2,1,0:T(4,128)S(1)}, u32[]{:S(2)}, u32[]{:S(2)}) collective-permute-start(f32[64,4,128]{2,1,0:T(4,128)S(1)} %get-tuple-element.67), channel_id=1, source_target_pairs={{4,0},{8,4},{12,8},{16,12},{20,16},{24,20},{28,24},{5,1},{9,5},{13... | collective-permute-start | bytes 393224 | tf_op jit(solution)/shard_map/ppermute | solution.py:19
  114.8 2.2 collective-permute-start.1
  117.0 4.0 %collective-permute-start.8 = (f32[4,128]{1,0:T(4,128)S(1)}, f32[4,128]{1,0:T(4,128)S(1)}, u32[]{:S(2)}, u32[]{:S(2)}) collective-permute-start(f32[4,128]{1,0:T(4,128)S(1)} %get-tuple-element.71), channel_id=1, source_target_pairs={{4,0},{8,4},{12,8},{16,12},{20,16},{24,20},{28,24},{5,1},{9,5},{13... | collective-permute-start | bytes 6152 | tf_op jit(solution)/shard_map/ppermute | solution.py:19
  123.0 4.3 %collective-permute-start.4 = (f32[64,4,128]{2,1,0:T(4,128)S(1)}, f32[64,4,128]{2,1,0:T(4,128)S(1)}, u32[]{:S(2)}, u32[]{:S(2)}) collective-permute-start(f32[64,4,128]{2,1,0:T(4,128)S(1)} %get-tuple-element.65), channel_id=1, source_target_pairs={{4,0},{8,4},{12,8},{16,12},{20,16},{24,20},{28,24},{5,1},{9,5},{13... | collective-permute-start | bytes 393224 | tf_op jit(solution)/shard_map/ppermute | solution.py:19
  128.0 9.3 %collective-permute-done.8 = f32[4,128]{1,0:T(4,128)S(1)} collective-permute-done((f32[4,128]{1,0:T(4,128)S(1)}, f32[4,128]{1,0:T(4,128)S(1)}, u32[]{:S(2)}, u32[]{:S(2)}) %collective-permute-start.8) | collective-permute-done | bytes 2080 | tf_op jit(solution)/shard_map/ppermute | solution.py:19
  137.3 26.1 %collective-permute-start.5 = (f32[64,4,128]{2,1,0:T(4,128)S(1)}, f32[64,4,128]{2,1,0:T(4,128)S(1)}, u32[]{:S(2)}, u32[]{:S(2)}) collective-permute-start(f32[64,4,128]{2,1,0:T(4,128)S(1)} %get-tuple-element.66), channel_id=1, source_target_pairs={{0,4},{4,8},{8,12},{12,16},{16,20},{20,24},{24,28},{1,5},{5,9},{9,... | collective-permute-start | bytes 393224 | tf_op jit(solution)/shard_map/ppermute | solution.py:18
  164.1 3.7 %collective-permute-start.10 = (f32[72,4]{1,0:T(8,128)}, f32[72,4]{1,0:T(8,128)S(1)}, u32[]{:S(2)}, u32[]{:S(2)}) collective-permute-start(f32[72,4]{1,0:T(8,128)} %get-tuple-element.69), channel_id=1, source_target_pairs={{1,0},{2,1},{3,2},{5,4},{6,5},{7,6},{9,8},{10,9},{11,10},{13,12},{... | collective-permute-start | bytes 3464 | tf_op jit(solution)/shard_map/ppermute | solution.py:19
  167.8 3.0 %collective-permute-start.11 = (f32[72,4]{1,0:T(8,128)S(1)}, f32[72,4]{1,0:T(8,128)S(1)}, u32[]{:S(2)}, u32[]{:S(2)}) collective-permute-start(f32[72,4]{1,0:T(8,128)S(1)} %get-tuple-element.70), channel_id=1, source_target_pairs={{0,1},{1,2},{2,3},{4,5},{5,6},{6,7},{8,9},{9,10},{10,11},{12,13},{... | collective-permute-start | bytes 3464 | tf_op jit(solution)/shard_map/ppermute | solution.py:18
  172.7 2.9 %fusion.39 = (f32[64,72,4]{2,1,0:T(8,128)}, f32[64,72,4]{2,1,0:T(8,128)}) fusion(f32[64,72,128]{2,1,0:T(8,128)S(1)} %pad_maximum_fusion.2), kind=kLoop, calls=%fused_computation.56 | loop fusion | bytes 294912 | tf_op jit(solution)/shard_map/slice | solution.py:17
  175.5 2.4 copy.11
  179.9 2.4 copy.12
  182.3 3.6 %collective-permute-start.3 = (f32[64,72,4]{1,0,2:T(8,128)S(1)}, f32[64,72,4]{1,0,2:T(8,128)S(1)}, u32[]{:S(2)}, u32[]{:S(2)}) collective-permute-start(f32[64,72,4]{1,0,2:T(8,128)S(1)} %copy.12), channel_id=1, source_target_pairs={{0,1},{1,2},{2,3},{4,5},{5,6},{6,7},{8,9},{9,10},{10,11},{12,13},{... | collective-permute-start | bytes 221192 | tf_op jit(solution)/shard_map/ppermute | solution.py:18
  186.2 2.9 %fusion.38 = (f32[64,72,4]{2,1,0:T(8,128)}, f32[64,72,4]{2,1,0:T(8,128)}) fusion(f32[64,72,128]{2,1,0:T(8,128)S(1)} %pad_maximum_fusion.3), kind=kLoop, calls=%fused_computation.55 | loop fusion | bytes 294912 | tf_op jit(solution)/shard_map/slice | solution.py:17
  189.0 2.4 copy.15
  193.4 3.1 %copy.16 = f32[64,72,4]{1,0,2:T(8,128)} copy(f32[64,72,4]{2,1,0:T(8,128)} %get-tuple-element.62) | data formatting | bytes 147456 | tf_op jit(solution)/shard_map/slice | solution.py:16
  196.5 3.6 %collective-permute-start.7 = (f32[64,72,4]{1,0,2:T(8,128)}, f32[64,72,4]{1,0,2:T(8,128)}, u32[]{:S(2)}, u32[]{:S(2)}) collective-permute-start(f32[64,72,4]{1,0,2:T(8,128)} %copy.16), channel_id=1, source_target_pairs={{0,1},{1,2},{2,3},{4,5},{5,6},{6,7},{8,9},{9,10},{10,11},{12,13},{... | collective-permute-start | bytes 221192 | tf_op jit(solution)/shard_map/ppermute | solution.py:18
  201.5 2.2 copy.13
  203.7 2.1 copy.14
  205.9 2.2 copy.17
  208.1 3.0 %copy.18 = f32[64,72,4]{2,1,0:T(8,128)} copy(f32[64,72,4]{1,0,2:T(8,128)} %collective-permute-done.7) | data formatting | bytes 147456 | tf_op jit(solution)/shard_map/ppermute | solution.py:18
  211.1 7.6 %pad_maximum_fusion.1 = (f32[64,72,256]{2,1,0:T(8,128)}, f32[64,72,256]{2,1,0:T(8,128)}) fusion(f32[64,72,4]{2,1,0:T(8,128)} %copy.18, f32[64,72,4]{2,1,0:T(8,128)} %copy.17, f32[64,4,128]{2,1,0:T(4,128)S(1)} %collective-permute-done.5, f32[64,4,128]{2,1,0:T(4,128)S(1)} %collective-permute-done.4, f32[64,64,128]{2,1,0:T(8,128)S(1)} %copy-done.2, ...), kind=kLoop, calls=%fused_computation.14 | loop fusion | flops 11796480 | bytes 14451712 | tf_op jit(solution)/shard_map/concatenate | solution.py:29
  218.8 16.4 %shard_map.105 = (f32[4096,128]{1,0:T(8,128)}, f32[4096,128]{1,0:T(8,128)}) custom-call(s32[2048]{0:T(1024)} %add.50.slot_ref, s32[2048]{0:T(1024)} %act_ref.1, f32[4096,128]{1,0:T(8,128)} %bitcast.12.r_ref), custom_call_target="tpu_custom_call" | custom-call | tf_op jit(solution)/shard_map/pallas_call | solution.py:185
  235.1 40.4 %shard_map.106 = (f32[64,64,128]{2,1,0:T(8,128)}, f32[64,64,128]{2,1,0:T(8,128)}) custom-call(f32[64,72,256]{2,1,0:T(8,128)} %get-tuple-element.78.eu_ref, f32[64,72,256]{2,1,0:T(8,128)} %get-tuple-element.77.ev_ref, f32[72,256]{1,0:T(8,128)} %pad_maximum_fusion.4.c_ref, f32[64,64,128]{2,1,0:T(8,128)} %bitcast.58, f32[64,64,128]{2,1,0:T(8,128)} %bitcast.59), custom_call_target="tpu_custom_call" | custom-call | tf_op jit(solution)/shard_map/pallas_call | solution.py:207
  (77 shorter events, 18.8 us)
Async XLA Ops:
  0.6 91.8 %copy-start = (f32[1,256,256]{2,1,0:T(8,128)S(1)}, f32[1,256,256]{2,1,0:T(8,128)}, u32[]{:S(2)}) copy-start(f32[1,256,256]{2,1,0:T(8,128)} %param.17) | copy-start | bytes 786436
  0.6 3.9 %copy-start.6 = (s32[2048,1]{0,1:T(1,128)S(1)}, s32[2048,1]{0,1:T(1,128)}, u32[]{:S(2)}) copy-start(s32[2048,1]{0,1:T(1,128)} %param.15) | copy-start | bytes 24580
  87.4 1.5 copy-start.4
  92.4 4.2 %copy-start.9 = (f32[1,256,256]{2,1,0:T(8,128)S(1)}, f32[1,256,256]{2,1,0:T(8,128)}, u32[]{:S(2)}) copy-start(f32[1,256,256]{2,1,0:T(8,128)} %param.18) | copy-start | bytes 786436
  96.6 4.6 %copy-start.5 = (f32[1,256,128]{2,1,0:T(8,128)S(1)}, f32[1,256,128]{2,1,0:T(8,128)}, u32[]{:S(2)}) copy-start(f32[1,256,128]{2,1,0:T(8,128)} %param.19) | copy-start | bytes 393220
  106.0 11.0 %copy-start.3 = (f32[64,128]{1,0:T(8,128)S(1)}, f32[64,128]{1,0:T(8,128)}, u32[]{:S(2)}) copy-start(f32[64,128]{1,0:T(8,128)} %param.13) | copy-start | bytes 98308
  106.0 17.0 %copy-start.2 = (f32[64,64,128]{2,1,0:T(8,128)S(1)}, f32[64,64,128]{2,1,0:T(8,128)}, u32[]{:S(2)}) copy-start(f32[64,64,128]{2,1,0:T(8,128)} %param.12) | copy-start | bytes 6291460
  106.0 112.8 %all-to-all-start.1 = ((f32[32,128,128]{2,1,0:T(8,128)}), f32[32,128,128]{2,1,0:T(8,128)}, u32[]{:S(2)}, u32[]{:S(2)}) async-start(f32[32,128,128]{2,1,0:T(8,128)} %fusion.29), calls=%async_computation.1 | async-start | bytes 4194304 | tf_op jit(solution)/shard_map/all_to_all | solution.py:183
  111.7 56.1 %collective-permute-start = (f32[64,4,128]{2,1,0:T(4,128)S(1)}, f32[64,4,128]{2,1,0:T(4,128)S(1)}, u32[]{:S(2)}, u32[]{:S(2)}) collective-permute-start(f32[64,4,128]{2,1,0:T(4,128)S(1)} %get-tuple-element.67), channel_id=1, source_target_pairs={{4,0},{8,4},{12,8},{16,12},{20,16},{24,20},{28,24},{5,1},{9,5},{13... | collective-permute-start | bytes 393224 | tf_op jit(solution)/shard_map/ppermute | solution.py:19
  114.8 56.0 %collective-permute-start.1 = (f32[64,4,128]{2,1,0:T(4,128)S(1)}, f32[64,4,128]{2,1,0:T(4,128)S(1)}, u32[]{:S(2)}, u32[]{:S(2)}) collective-permute-start(f32[64,4,128]{2,1,0:T(4,128)S(1)} %get-tuple-element.68), channel_id=1, source_target_pairs={{0,4},{4,8},{8,12},{12,16},{16,20},{20,24},{24,28},{1,5},{5,9},{9,... | collective-permute-start | bytes 393224 | tf_op jit(solution)/shard_map/ppermute | solution.py:18
  117.0 20.3 %collective-permute-start.8 = (f32[4,128]{1,0:T(4,128)S(1)}, f32[4,128]{1,0:T(4,128)S(1)}, u32[]{:S(2)}, u32[]{:S(2)}) collective-permute-start(f32[4,128]{1,0:T(4,128)S(1)} %get-tuple-element.71), channel_id=1, source_target_pairs={{4,0},{8,4},{12,8},{16,12},{20,16},{24,20},{28,24},{5,1},{9,5},{13... | collective-permute-start | bytes 6152 | tf_op jit(solution)/shard_map/ppermute | solution.py:19
  121.0 42.4 %collective-permute-start.9 = (f32[4,128]{1,0:T(4,128)S(1)}, f32[4,128]{1,0:T(4,128)S(1)}, u32[]{:S(2)}, u32[]{:S(2)}) collective-permute-start(f32[4,128]{1,0:T(4,128)S(1)} %get-tuple-element.72), channel_id=1, source_target_pairs={{0,4},{4,8},{8,12},{12,16},{16,20},{20,24},{24,28},{1,5},{5,9},{9,... | collective-permute-start | bytes 6152 | tf_op jit(solution)/shard_map/ppermute | solution.py:18
  123.0 59.3 %collective-permute-start.4 = (f32[64,4,128]{2,1,0:T(4,128)S(1)}, f32[64,4,128]{2,1,0:T(4,128)S(1)}, u32[]{:S(2)}, u32[]{:S(2)}) collective-permute-start(f32[64,4,128]{2,1,0:T(4,128)S(1)} %get-tuple-element.65), channel_id=1, source_target_pairs={{4,0},{8,4},{12,8},{16,12},{20,16},{24,20},{28,24},{5,1},{9,5},{13... | collective-permute-start | bytes 393224 | tf_op jit(solution)/shard_map/ppermute | solution.py:19
  137.3 35.3 %copy-start.7 = (f32[4,128]{1,0:T(4,128)}, f32[4,128]{1,0:T(4,128)S(1)}, u32[]{:S(2)}) copy-start(f32[4,128]{1,0:T(4,128)S(1)} %collective-permute-done.8) | copy-start | bytes 6148
  137.3 48.7 %collective-permute-start.5 = (f32[64,4,128]{2,1,0:T(4,128)S(1)}, f32[64,4,128]{2,1,0:T(4,128)S(1)}, u32[]{:S(2)}, u32[]{:S(2)}) collective-permute-start(f32[64,4,128]{2,1,0:T(4,128)S(1)} %get-tuple-element.66), channel_id=1, source_target_pairs={{0,4},{4,8},{8,12},{12,16},{16,20},{20,24},{24,28},{1,5},{5,9},{9,... | collective-permute-start | bytes 393224 | tf_op jit(solution)/shard_map/ppermute | solution.py:18
  163.4 9.2 %copy-start.8 = (f32[4,128]{1,0:T(4,128)}, f32[4,128]{1,0:T(4,128)S(1)}, u32[]{:S(2)}) copy-start(f32[4,128]{1,0:T(4,128)S(1)} %collective-permute-done.9) | copy-start | bytes 6148
  164.1 32.4 %collective-permute-start.10 = (f32[72,4]{1,0:T(8,128)}, f32[72,4]{1,0:T(8,128)S(1)}, u32[]{:S(2)}, u32[]{:S(2)}) collective-permute-start(f32[72,4]{1,0:T(8,128)} %get-tuple-element.69), channel_id=1, source_target_pairs={{1,0},{2,1},{3,2},{5,4},{6,5},{7,6},{9,8},{10,9},{11,10},{13,12},{... | collective-permute-start | bytes 3464 | tf_op jit(solution)/shard_map/ppermute | solution.py:19
  167.8 32.3 %collective-permute-start.11 = (f32[72,4]{1,0:T(8,128)S(1)}, f32[72,4]{1,0:T(8,128)S(1)}, u32[]{:S(2)}, u32[]{:S(2)}) collective-permute-start(f32[72,4]{1,0:T(8,128)S(1)} %get-tuple-element.70), channel_id=1, source_target_pairs={{0,1},{1,2},{2,3},{4,5},{5,6},{6,7},{8,9},{9,10},{10,11},{12,13},{... | collective-permute-start | bytes 3464 | tf_op jit(solution)/shard_map/ppermute | solution.py:18
  177.9 23.6 %collective-permute-start.2 = (f32[64,72,4]{1,0,2:T(8,128)S(1)}, f32[64,72,4]{1,0,2:T(8,128)S(1)}, u32[]{:S(2)}, u32[]{:S(2)}) collective-permute-start(f32[64,72,4]{1,0,2:T(8,128)S(1)} %copy.11), channel_id=1, source_target_pairs={{1,0},{2,1},{3,2},{5,4},{6,5},{7,6},{9,8},{10,9},{11,10},{13,12},{... | collective-permute-start | bytes 221192 | tf_op jit(solution)/shard_map/ppermute | solution.py:19
  182.3 21.4 %collective-permute-start.3 = (f32[64,72,4]{1,0,2:T(8,128)S(1)}, f32[64,72,4]{1,0,2:T(8,128)S(1)}, u32[]{:S(2)}, u32[]{:S(2)}) collective-permute-start(f32[64,72,4]{1,0,2:T(8,128)S(1)} %copy.12), channel_id=1, source_target_pairs={{0,1},{1,2},{2,3},{4,5},{5,6},{6,7},{8,9},{9,10},{10,11},{12,13},{... | collective-permute-start | bytes 221192 | tf_op jit(solution)/shard_map/ppermute | solution.py:18
  191.5 14.4 %collective-permute-start.6 = (f32[64,72,4]{1,0,2:T(8,128)S(1)}, f32[64,72,4]{1,0,2:T(8,128)S(1)}, u32[]{:S(2)}, u32[]{:S(2)}) collective-permute-start(f32[64,72,4]{1,0,2:T(8,128)S(1)} %copy.15), channel_id=1, source_target_pairs={{1,0},{2,1},{3,2},{5,4},{6,5},{7,6},{9,8},{10,9},{11,10},{13,12},{... | collective-permute-start | bytes 221192 | tf_op jit(solution)/shard_map/ppermute | solution.py:19
  196.5 11.6 %collective-permute-start.7 = (f32[64,72,4]{1,0,2:T(8,128)}, f32[64,72,4]{1,0,2:T(8,128)}, u32[]{:S(2)}, u32[]{:S(2)}) collective-permute-start(f32[64,72,4]{1,0,2:T(8,128)} %copy.16), channel_id=1, source_target_pairs={{0,1},{1,2},{2,3},{4,5},{5,6},{6,7},{8,9},{9,10},{10,11},{12,13},{... | collective-permute-start | bytes 221192 | tf_op jit(solution)/shard_map/ppermute | solution.py:18
  235.1 40.4 %copy-start.1 = (f32[1,256,256]{2,1,0:T(8,128)S(1)}, f32[1,256,256]{2,1,0:T(8,128)}, u32[]{:S(2)}) copy-start(f32[1,256,256]{2,1,0:T(8,128)} %param.17) | copy-start | bytes 786436
where the time goes:
time: 277 us; the launch traced here: 276 us
  Pallas kernels  74.8 us (27%)
  starting transfers between devices  64 us (23%)
  blocking collectives  54.1 us (20%)
  local copies, waits for them, and re-layouts  37.1 us (13%)
  matrix products  18.1 us (7%)
  other arithmetic  16.9 us (6%)
  waiting for transfers between devices  9.38 us (3%)
    all_to_all x1, blocking collectives, body(): lax.all_to_all(outgoing.reshape(devices_all, capacity, features), ('tile'...  54.1 us
    ppermute x6, starting transfers between devices, halos(): before = lax.ppermute(last, axis, up)  40.5 us
    pallas_call x1, Pallas kernels, body(): pl.pallas_call(diffuse_kernel, out_shape=(jax.ShapeDtypeStruct(u_field.sh...  40.4 us
    ppermute x6, starting transfers between devices, halos(): after = lax.ppermute(first, axis, down)  18.9 us
    pallas_call x1, Pallas kernels, body(): pl.pallas_call(gather_kernel, out_shape=jax.ShapeDtypeStruct((slot_total,...  18 us
    pallas_call x1, Pallas kernels, body(): pl.pallas_call(drag_kernel, out_shape=(jax.ShapeDtypeStruct((levels * wid...  16.4 us
    slice x8, local copies, waits for them, and re-layouts, halos(): first = lax.slice_in_dim(x, 0, width, axis=dim)  12.3 us
    ppermute x6, waiting for transfers between devices, halos(): after = lax.ppermute(first, axis, down)  9.36 us
  transfers between devices with their start and end apart: 13, of which 1 were waited for; matrix products, arithmetic and copies ran while one was open for 14% of the time, Pallas kernels for 0%

commit v1 on v0

v1 whole, which is shorter than its diff:
```python
import jax
import jax.numpy as jnp
from jax import lax
from jax.experimental import pallas as pl
from jax.experimental.pallas import tpu as pltpu
from jax.sharding import PartitionSpec as P

PASSES = 4


def halos(x, axis, dim, width):
    count, length = (lax.axis_size(axis), x.shape[dim])
    up = [(i, i + 1) for i in range(count - 1)]
    down = [(j, i) for i, j in up]
    last = lax.slice_in_dim(x, length - width, length, axis=dim)
    first = lax.slice_in_dim(x, 0, width, axis=dim)
    before = lax.ppermute(last, axis, up)
    after = lax.ppermute(first, axis, down)
    return before, after


def standardize(rows):
    center = jnp.mean(rows, axis=-1, keepdims=True)
    spread = jnp.mean(jnp.square(rows - center), axis=-1, keepdims=True)
    return (rows - center) * lax.rsqrt(spread + 1e-05)


def network_rows(rows, first_layer, second_layer, third_layer, last_layer):
    highest = lax.Precision.HIGHEST
    hidden = jax.nn.silu(jnp.dot(rows, first_layer, precision=highest))
    hidden = jax.nn.silu(jnp.dot(hidden, second_layer, precision=highest))
    hidden = jax.nn.silu(jnp.dot(hidden, third_layer, precision=highest))
    return jnp.dot(hidden, last_layer, precision=highest)


def gather_kernel(cell_ref, u_ref, v_ref, st_ref, o_ref):
    levels_x, width_y = u_ref.shape
    cells, features = st_ref.shape
    levels = features // 2
    width_x = levels_x // levels

    def transpose_tile(x, carry):
        a = u_ref[pl.ds(x, levels, stride=width_x), :]
        b = v_ref[pl.ds(x, levels, stride=width_x), :]
        tile = jnp.concatenate([a, b], axis=0)
        st_ref[pl.ds(pl.multiple_of(x * width_y, width_y), width_y), :] = tile.T
        return carry

    lax.fori_loop(0, width_x, transpose_tile, 0)

    def pick(s, carry):
        cell = cell_ref[s]
        keep = (cell < cells).astype(jnp.float32)
        row = st_ref[pl.ds(jnp.minimum(cell, cells - 1), 1), :]
        o_ref[pl.ds(s, 1), :] = row * keep
        return carry

    lax.fori_loop(0, o_ref.shape[0], pick, 0, unroll=8)


def diffuse_kernel(st_ref, xb_ref, xa_ref, yh_ref, c_ref, f_ref, e_ref, a_ref):
    width_x, width_y, _ = st_ref.shape
    depth = xb_ref.shape[0]
    rows_ext, ylen, _ = c_ref.shape
    e_ref[0:depth, 0:width_y, :] = xb_ref[...]
    e_ref[depth + width_x :, 0:width_y, :] = xa_ref[...]

    def fill(x, carry):
        e_ref[x + depth, 0:width_y, :] = st_ref[x]
        return carry

    lax.fori_loop(0, width_x, fill, 0)
    e_ref[:, width_y:, :] = yh_ref[...]

    def sweep(src, dst, p, last):
        def one(x, carry):
            q = src[x]
            n = src[x + 1] + src[x - 1]
            n = n + pltpu.roll(q, ylen - 1, 0) + pltpu.roll(q, 1, 0)
            new = q + c_ref[x] * (n - 4.0 * q)
            if last:
                f_ref[x - depth] = new[:width_y]
            else:
                dst[x] = new
            return carry

        lax.fori_loop(p + 1, rows_ext - 1 - p, one, 0)

    for p in range(PASSES):
        src, dst = (e_ref, a_ref) if p % 2 == 0 else (a_ref, e_ref)
        sweep(src, dst, p, p == PASSES - 1)


def finish_kernel(slot_ref, act_ref, r_ref, f_ref, uo_ref, vo_ref, d_ref):
    levels_x, width_y = uo_ref.shape
    cells, features = f_ref.shape
    levels = features // 2
    width_x = levels_x // levels

    def copy_tile(x, carry):
        at = pl.ds(pl.multiple_of(x * width_y, width_y), width_y)
        d_ref[at, :] = f_ref[at, :]
        return carry

    lax.fori_loop(0, width_x, copy_tile, 0)

    def place(r, carry):
        at = pl.ds(act_ref[r], 1)
        d_ref[at, :] = d_ref[at, :] + r_ref[pl.ds(slot_ref[r], 1), :]
        return carry

    lax.fori_loop(0, act_ref.shape[0], place, 0, unroll=8)

    def transpose_tile(x, carry):
        tile = d_ref[pl.ds(pl.multiple_of(x * width_y, width_y), width_y), :].T
        uo_ref[pl.ds(x, levels, stride=width_x), :] = tile[:levels]
        vo_ref[pl.ds(x, levels, stride=width_x), :] = tile[levels:]
        return carry

    lax.fori_loop(0, width_x, transpose_tile, 0)


def body(
    u_field,
    v_field,
    diffusivity,
    active_columns,
    regimes,
    first_layer,
    second_layer,
    third_layer,
    last_layer,
):
    levels, width_x, width_y = u_field.shape
    features = 2 * levels
    cells = width_x * width_y
    active_count = active_columns.shape[0]
    devices_all = lax.axis_size(("tile", "inf"))
    capacity = 2 * active_count // devices_all
    slot_total = devices_all * capacity
    block_rows = min(512, active_count)
    block_count = active_count // block_rows
    target = regimes[:, 0]
    labels = jnp.arange(devices_all, dtype=jnp.int32)
    one_hot = (
        (target[:, None] == labels[None, :])
        .astype(jnp.bfloat16)
        .reshape(block_count, block_rows, devices_all)
    )
    row_ids = jnp.arange(block_rows, dtype=jnp.int32)
    lower = (row_ids[:, None] > row_ids[None, :]).astype(jnp.bfloat16)

    def rank_step(counts, piece):
        earlier = jnp.dot(lower, piece, preferred_element_type=jnp.float32) + counts[None, :]
        wide_piece = piece.astype(jnp.float32)
        rank = jnp.sum(earlier * wide_piece, axis=1)
        return (counts + jnp.sum(wide_piece, axis=0), rank)

    _, ranks = lax.scan(rank_step, jnp.zeros((devices_all,), jnp.float32), one_hot)
    slot_index = target * capacity + ranks.reshape(-1).astype(jnp.int32)
    cell_of_slot = jnp.full((slot_total,), cells, jnp.int32).at[slot_index].set(
        active_columns, unique_indices=True
    )
    vmem = pl.BlockSpec(memory_space=pltpu.VMEM)
    smem = pl.BlockSpec(memory_space=pltpu.SMEM)
    u_rows = u_field.reshape(levels * width_x, width_y)
    v_rows = v_field.reshape(levels * width_x, width_y)
    state_t, outgoing = pl.pallas_call(
        gather_kernel,
        out_shape=(
            jax.ShapeDtypeStruct((cells, features), jnp.float32),
            jax.ShapeDtypeStruct((slot_total, features), jnp.float32),
        ),
        in_specs=[smem, vmem, vmem],
        out_specs=(vmem, vmem),
    )(cell_of_slot, u_rows, v_rows)
    block = lax.all_to_all(
        outgoing.reshape(devices_all, capacity, features),
        ("tile", "inf"),
        split_axis=0,
        concat_axis=0,
        tiled=True,
    )
    block_shape = block.shape
    rows = standardize(block.reshape(-1, features))
    result = network_rows(rows, first_layer[0], second_layer[0], third_layer[0], last_layer[0])
    answered = result.reshape(block_shape)
    returned = lax.all_to_all(answered, ("tile", "inf"), split_axis=0, concat_axis=0, tiled=True)
    returned_rows = returned.reshape(slot_total, features)

    depth = PASSES
    state_t = state_t.reshape(width_x, width_y, features)
    x_before, x_after = halos(state_t, "tile", 0, depth)
    extended = jnp.concatenate([x_before, state_t, x_after], axis=0)
    y_before, y_after = halos(extended, "inf", 1, depth)
    y_halo = jnp.concatenate([y_after, y_before], axis=1)
    c_before, c_after = halos(diffusivity, "tile", 0, depth)
    c_ext = jnp.concatenate([c_before, diffusivity, c_after], axis=0)
    c_before, c_after = halos(c_ext, "inf", 1, depth)
    c_ext = jnp.concatenate([c_ext, c_after, c_before], axis=1)
    rows_ext, ylen = c_ext.shape
    coeff = jnp.broadcast_to(c_ext[:, :, None], (rows_ext, ylen, features))
    diffused = pl.pallas_call(
        diffuse_kernel,
        out_shape=jax.ShapeDtypeStruct((width_x, width_y, features), jnp.float32),
        in_specs=[vmem] * 5,
        out_specs=vmem,
        scratch_shapes=[
            pltpu.VMEM((rows_ext, ylen, features), jnp.float32),
            pltpu.VMEM((rows_ext, ylen, features), jnp.float32),
        ],
        compiler_params=pltpu.CompilerParams(vmem_limit_bytes=100 * 1024 * 1024),
    )(state_t, x_before, x_after, y_halo, coeff)
    u_next, v_next = pl.pallas_call(
        finish_kernel,
        out_shape=(
            jax.ShapeDtypeStruct((levels * width_x, width_y), jnp.float32),
            jax.ShapeDtypeStruct((levels * width_x, width_y), jnp.float32),
        ),
        in_specs=[smem, smem, vmem, vmem],
        out_specs=(vmem, vmem),
        scratch_shapes=[pltpu.VMEM((cells, features), jnp.float32)],
    )(slot_index, active_columns, returned_rows, diffused.reshape(cells, features))
    return (u_next.reshape(u_field.shape), v_next.reshape(v_field.shape))


def solution(mesh):
    in_specs = (
        P(None, "tile", "inf"),
        P(None, "tile", "inf"),
        P("tile", "inf"),
        P(("tile", "inf")),
        P(("tile", "inf"), None),
        P(("tile", "inf"), None, None),
        P(("tile", "inf"), None, None),
        P(("tile", "inf"), None, None),
        P(("tile", "inf"), None, None),
    )
    out_specs = (P(None, "tile", "inf"), P(None, "tile", "inf"))
    return jax.shard_map(body, mesh=mesh, in_specs=in_specs, out_specs=out_specs, check_vma=False)
```

time: 277 us -> 228 us (0.82)
  the two profiles are of different devices: /device:TPU:9 before, /device:TPU:20 now
where the time goes in v1:
time: 228 us; the launch traced here: 227 us
  Pallas kernels  62 us (27%)
  blocking collectives  52.6 us (23%)
  waiting for transfers between devices  41.8 us (18%)
  starting transfers between devices  28.5 us (12%)
  matrix products  18.1 us (8%)
  local copies, waits for them, and re-layouts  14.8 us (6%)
  other arithmetic  8.52 us (4%)
    all_to_all x1, blocking collectives, body(): lax.all_to_all(outgoing.reshape(devices_all, capacity, features), ('tile'...  52.6 us
    ppermute x4, waiting for transfers between devices, halos(): before = lax.ppermute(last, axis, up)  41.7 us
    pallas_call x1, Pallas kernels, body(): pl.pallas_call(gather_kernel, out_shape=(jax.ShapeDtypeStruct((cells, fea...  26.6 us
    pallas_call x1, Pallas kernels, body(): pl.pallas_call(finish_kernel, out_shape=(jax.ShapeDtypeStruct((levels * w...  20.1 us
    pallas_call x1, Pallas kernels, body(): pl.pallas_call(diffuse_kernel, out_shape=jax.ShapeDtypeStruct((width_x, w...  15.3 us
    ppermute x4, starting transfers between devices, halos(): after = lax.ppermute(first, axis, down)  12.7 us
    ppermute x4, starting transfers between devices, halos(): before = lax.ppermute(last, axis, up)  10.2 us
    scatter x1, local copies, waits for them, and re-layouts, body(): jnp.full((slot_total,), cells, jnp.int32).at[slot_index]  8.79 us
  transfers between devices with their start and end apart: 9, of which 2 were waited for; matrix products, arithmetic and copies ran while one was open for 3% of the time, Pallas kernels for 7%

profile of v1, /device:TPU:20, one launch (start us, length us, event | category | flops | bytes accessed | tf_op | source)
XLA Modules:
  0.0 227.5 jit_solution(6027983779049640615)
XLA Ops:
  1.2 1.4 reduce.5
  2.6 1.9 while.13
  4.6 0.7 compare_select_fusion
  5.3 8.8 %scatter_custom_fusion.cell_ref = s32[4096]{0:T(1024)} fusion(s32[2048]{0:T(1024)S(1)} %bitcast.72, s32[2048]{0:T(1024)} %act_ref.1, s32[]{:T(128)} %constant.14.clone.1), kind=kCustom, calls=%fused_computation.47 | custom fusion | bytes 16896 | tf_op jit(solution)/shard_map/scatter | solution.py:161
  14.1 26.6 %shard_map.104 = (f32[8192,128]{1,0:T(8,128)}, f32[4096,128]{1,0:T(8,128)}) custom-call(s32[4096]{0:T(1024)} %scatter_custom_fusion.cell_ref, f32[4096,128]{1,0:T(8,128)} %bitcast.63, f32[4096,128]{1,0:T(8,128)} %bitcast.64), custom_call_target="tpu_custom_call" | custom-call | tf_op jit(solution)/shard_map/pallas_call | solution.py:168
  40.7 52.6 %all_to_all.10 = f32[32,128,128]{2,1,0:T(8,128)S(1)} all-to-all(f32[32,128,128]{2,1,0:T(8,128)} %bitcast.65), channel_id=1, replica_groups=mesh['tile'=8,'inf'=4] {'tile','inf'}, dimensions={0} | all-to-all | bytes 4194304 | tf_op jit(solution)/shard_map/all_to_all | solution.py:177
  93.3 0.6 reduce_sum.36
  94.0 1.3 multiply_reduce_fusion
  95.3 1.4 subtract_multiply_fusion
  96.7 3.5 %fusion.31 = f32[4096,256]{1,0:T(8,128)S(1)} fusion(f32[4096,128]{1,0:T(8,128)S(1)} %bitcast.61, f32[1,128,256]{2,1,0:T(8,128)S(1)} %copy-done.3), kind=kOutput, calls=%fused_computation.40 | convolution fusion | flops 1610612736 | bytes 6422528 | tf_op jit(solution)/shard_map/dot_general | solution.py:30
  100.3 4.1 %fusion.16 = f32[4096,256]{1,0:T(8,128)S(1)} fusion(f32[4096,256]{1,0:T(8,128)S(1)} %fusion.31, f32[1,256,256]{2,1,0:T(8,128)S(1)} %copy-done.5), kind=kOutput, calls=%fused_computation.20 | convolution fusion | flops 3225419776 | bytes 8650752 | tf_op jit(solution)/shard_map/dot_general | solution.py:31
  104.4 4.6 %divide_multiply_fusion = f32[4096,256]{1,0:T(8,128)S(1)} fusion(f32[4096,256]{1,0:T(8,128)S(1)} %fusion.16, f32[1,256,256]{2,1,0:T(8,128)S(1)} %copy-done.6), kind=kOutput, calls=%fused_computation.13 | convolution fusion | flops 3229614080 | bytes 8650752 | tf_op jit(solution)/shard_map/dot_general | solution.py:32
  109.1 4.7 %fusion.29 = f32[32,128,128]{2,1,0:T(8,128)} fusion(f32[32,128,256]{2,1,0:T(8,128)S(1)} %bitcast.62, f32[1,256,128]{2,1,0:T(8,128)S(1)} %copy-done.4), kind=kOutput, calls=%fused_computation.38 | convolution fusion | flops 1610612736 | bytes 6422528 | tf_op jit(solution)/shard_map/dot_general | solution.py:33
  113.8 5.7 %all-to-all-start.1 = ((f32[32,128,128]{2,1,0:T(8,128)}), f32[32,128,128]{2,1,0:T(8,128)}, u32[]{:S(2)}, u32[]{:S(2)}) async-start(f32[32,128,128]{2,1,0:T(8,128)} %fusion.29), calls=%async_computation.1 | async-start | bytes 4194304 | tf_op jit(solution)/shard_map/all_to_all | solution.py:188
  119.5 1.1 fusion.38
  120.5 3.4 %collective-permute-start = (f32[4,128,128]{2,1,0:T(8,128)S(1)}, f32[4,128,128]{2,1,0:T(8,128)S(1)}, u32[]{:S(2)}, u32[]{:S(2)}) collective-permute-start(f32[4,128,128]{2,1,0:T(8,128)S(1)} %bitcast.67), channel_id=1, source_target_pairs={{0,4},{4,8},{8,12},{12,16},{16,20},{20,24},{24,28},{1,5},{5,9},{9,... | collective-permute-start | bytes 786440 | tf_op jit(solution)/shard_map/ppermute | solution.py:17
  123.9 3.4 %collective-permute-start.1 = (f32[4,128,128]{2,1,0:T(8,128)S(1)}, f32[4,128,128]{2,1,0:T(8,128)S(1)}, u32[]{:S(2)}, u32[]{:S(2)}) collective-permute-start(f32[4,128,128]{2,1,0:T(8,128)S(1)} %bitcast.66), channel_id=1, source_target_pairs={{4,0},{8,4},{12,8},{16,12},{20,16},{24,20},{28,24},{5,1},{9,5},{13... | collective-permute-start | bytes 786440 | tf_op jit(solution)/shard_map/ppermute | solution.py:18
  127.3 2.5 %collective-permute-start.4 = (f32[4,128]{1,0:T(4,128)S(1)}, f32[4,128]{1,0:T(4,128)S(1)}, u32[]{:S(2)}, u32[]{:S(2)}) collective-permute-start(f32[4,128]{1,0:T(4,128)S(1)} %get-tuple-element.71), channel_id=1, source_target_pairs={{0,4},{4,8},{8,12},{12,16},{16,20},{20,24},{24,28},{1,5},{5,9},{9,... | collective-permute-start | bytes 6152 | tf_op jit(solution)/shard_map/ppermute | solution.py:17
  129.8 4.3 %collective-permute-start.5 = (f32[4,128]{1,0:T(4,128)S(1)}, f32[4,128]{1,0:T(4,128)S(1)}, u32[]{:S(2)}, u32[]{:S(2)}) collective-permute-start(f32[4,128]{1,0:T(4,128)S(1)} %get-tuple-element.72), channel_id=1, source_target_pairs={{4,0},{8,4},{12,8},{16,12},{20,16},{24,20},{28,24},{5,1},{9,5},{13... | collective-permute-start | bytes 6152 | tf_op jit(solution)/shard_map/ppermute | solution.py:18
  134.1 39.0 %collective-permute-done.4 = f32[4,128]{1,0:T(4,128)S(1)} collective-permute-done((f32[4,128]{1,0:T(4,128)S(1)}, f32[4,128]{1,0:T(4,128)S(1)}, u32[]{:S(2)}, u32[]{:S(2)}) %collective-permute-start.4) | collective-permute-done | bytes 2080 | tf_op jit(solution)/shard_map/ppermute | solution.py:17
  173.1 0.7 copy-done
  173.8 1.1 pad_maximum_fusion.3
  174.9 1.9 collective-permute-start.2
  176.8 2.4 %collective-permute-start.3 = (f32[72,4,128]{2,1,0:T(4,128)S(1)}, f32[72,4,128]{2,1,0:T(4,128)S(1)}, u32[]{:S(2)}, u32[]{:S(2)}) collective-permute-start(f32[72,4,128]{2,1,0:T(4,128)S(1)} %get-tuple-element.66), channel_id=1, source_target_pairs={{0,1},{1,2},{2,3},{4,5},{5,6},{6,7},{8,9},{9,10},{10,11},{12,13},{... | collective-permute-start | bytes 442376 | tf_op jit(solution)/shard_map/ppermute | solution.py:17
  179.3 3.1 %collective-permute-start.6 = (f32[72,4]{1,0:T(8,128)S(1)}, f32[72,4]{1,0:T(8,128)S(1)}, u32[]{:S(2)}, u32[]{:S(2)}) collective-permute-start(f32[72,4]{1,0:T(8,128)S(1)} %get-tuple-element.69), channel_id=1, source_target_pairs={{1,0},{2,1},{3,2},{5,4},{6,5},{7,6},{9,8},{10,9},{11,10},{13,12},{... | collective-permute-start | bytes 3464 | tf_op jit(solution)/shard_map/ppermute | solution.py:18
  182.5 1.9 collective-permute-start.7
  184.4 0.6 add.50.slot_ref
  185.0 2.7 %collective-permute-done.7 = f32[72,4]{1,0:T(8,128)S(1)} collective-permute-done((f32[72,4]{1,0:T(8,128)S(1)}, f32[72,4]{1,0:T(8,128)S(1)}, u32[]{:S(2)}, u32[]{:S(2)}) %collective-permute-start.7) | collective-permute-done | bytes 1184 | tf_op jit(solution)/shard_map/ppermute | solution.py:17
  187.9 0.8 pad_maximum_fusion.yh_ref
  188.6 3.4 %broadcast_in_dim.16.c_ref = f32[72,136,128]{2,1,0:T(8,128)} broadcast(f32[72,136]{1,0:T(8,128)S(1)} %pad_maximum_fusion.4), dimensions={0,1} | broadcast | bytes 5052672 | tf_op jit(solution)/shard_map/broadcast_in_dim | solution.py:202
  192.1 15.3 %shard_map.105 = f32[64,128,128]{2,1,0:T(8,128)} custom-call(f32[64,128,128]{2,1,0:T(8,128)} %bitcast.59, f32[4,128,128]{2,1,0:T(8,128)} %copy-done, f32[4,128,128]{2,1,0:T(8,128)} %copy-done.1, f32[72,8,128]{2,1,0:T(8,128)} %pad_maximum_fusion.yh_ref, f32[72,136,128]{2,1,0:T(8,128)} %broadcast_in_dim.16.c_ref), custom_call_target="tpu_custom_call" | custom-call | tf_op jit(solution)/shard_map/pallas_call | solution.py:203
  207.3 20.1 %shard_map.106 = (f32[4096,128]{1,0:T(8,128)}, f32[4096,128]{1,0:T(8,128)}) custom-call(s32[2048]{0:T(1024)} %add.50.slot_ref, s32[2048]{0:T(1024)} %act_ref.1, f32[4096,128]{1,0:T(8,128)} %bitcast.12.r_ref, f32[8192,128]{1,0:T(8,128)} %bitcast.60), custom_call_target="tpu_custom_call" | custom-call | tf_op jit(solution)/shard_map/pallas_call | solution.py:214
  (50 shorter events, 2.6 us)
Async XLA Ops:
  93.3 3.4 %copy-start.3 = (f32[1,128,256]{2,1,0:T(8,128)S(1)}, f32[1,128,256]{2,1,0:T(8,128)}, u32[]{:S(2)}) copy-start(f32[1,128,256]{2,1,0:T(8,128)} %param.16) | copy-start | bytes 393220
  96.7 3.5 %copy-start.5 = (f32[1,256,256]{2,1,0:T(8,128)S(1)}, f32[1,256,256]{2,1,0:T(8,128)}, u32[]{:S(2)}) copy-start(f32[1,256,256]{2,1,0:T(8,128)} %param.17) | copy-start | bytes 786436
  100.3 4.2 %copy-start.6 = (f32[1,256,256]{2,1,0:T(8,128)S(1)}, f32[1,256,256]{2,1,0:T(8,128)}, u32[]{:S(2)}) copy-start(f32[1,256,256]{2,1,0:T(8,128)} %param.18) | copy-start | bytes 786436
  104.4 4.6 %copy-start.4 = (f32[1,256,128]{2,1,0:T(8,128)S(1)}, f32[1,256,128]{2,1,0:T(8,128)}, u32[]{:S(2)}) copy-start(f32[1,256,128]{2,1,0:T(8,128)} %param.19) | copy-start | bytes 393220
  113.8 13.5 %copy-start.2 = (f32[64,128]{1,0:T(8,128)S(1)}, f32[64,128]{1,0:T(8,128)}, u32[]{:S(2)}) copy-start(f32[64,128]{1,0:T(8,128)} %param.13) | copy-start | bytes 98308
  113.8 93.5 %all-to-all-start.1 = ((f32[32,128,128]{2,1,0:T(8,128)}), f32[32,128,128]{2,1,0:T(8,128)}, u32[]{:S(2)}, u32[]{:S(2)}) async-start(f32[32,128,128]{2,1,0:T(8,128)} %fusion.29), calls=%async_computation.1 | async-start | bytes 4194304 | tf_op jit(solution)/shard_map/all_to_all | solution.py:188
  120.5 52.5 %collective-permute-start = (f32[4,128,128]{2,1,0:T(8,128)S(1)}, f32[4,128,128]{2,1,0:T(8,128)S(1)}, u32[]{:S(2)}, u32[]{:S(2)}) collective-permute-start(f32[4,128,128]{2,1,0:T(8,128)S(1)} %bitcast.67), channel_id=1, source_target_pairs={{0,4},{4,8},{8,12},{12,16},{16,20},{20,24},{24,28},{1,5},{5,9},{9,... | collective-permute-start | bytes 786440 | tf_op jit(solution)/shard_map/ppermute | solution.py:17
  123.9 49.2 %collective-permute-start.1 = (f32[4,128,128]{2,1,0:T(8,128)S(1)}, f32[4,128,128]{2,1,0:T(8,128)S(1)}, u32[]{:S(2)}, u32[]{:S(2)}) collective-permute-start(f32[4,128,128]{2,1,0:T(8,128)S(1)} %bitcast.66), channel_id=1, source_target_pairs={{4,0},{8,4},{12,8},{16,12},{20,16},{24,20},{28,24},{5,1},{9,5},{13... | collective-permute-start | bytes 786440 | tf_op jit(solution)/shard_map/ppermute | solution.py:18
  127.3 45.7 %collective-permute-start.4 = (f32[4,128]{1,0:T(4,128)S(1)}, f32[4,128]{1,0:T(4,128)S(1)}, u32[]{:S(2)}, u32[]{:S(2)}) collective-permute-start(f32[4,128]{1,0:T(4,128)S(1)} %get-tuple-element.71), channel_id=1, source_target_pairs={{0,4},{4,8},{8,12},{12,16},{16,20},{20,24},{24,28},{1,5},{5,9},{9,... | collective-permute-start | bytes 6152 | tf_op jit(solution)/shard_map/ppermute | solution.py:17
  129.8 43.3 %collective-permute-start.5 = (f32[4,128]{1,0:T(4,128)S(1)}, f32[4,128]{1,0:T(4,128)S(1)}, u32[]{:S(2)}, u32[]{:S(2)}) collective-permute-start(f32[4,128]{1,0:T(4,128)S(1)} %get-tuple-element.72), channel_id=1, source_target_pairs={{4,0},{8,4},{12,8},{16,12},{20,16},{24,20},{28,24},{5,1},{9,5},{13... | collective-permute-start | bytes 6152 | tf_op jit(solution)/shard_map/ppermute | solution.py:18
  173.1 0.7 copy-start
  173.1 1.8 copy-start.1
  174.9 12.9 %collective-permute-start.2 = (f32[72,4,128]{2,1,0:T(4,128)S(1)}, f32[72,4,128]{2,1,0:T(4,128)S(1)}, u32[]{:S(2)}, u32[]{:S(2)}) collective-permute-start(f32[72,4,128]{2,1,0:T(4,128)S(1)} %get-tuple-element.65), channel_id=1, source_target_pairs={{1,0},{2,1},{3,2},{5,4},{6,5},{7,6},{9,8},{10,9},{11,10},{13,12},{... | collective-permute-start | bytes 442376 | tf_op jit(solution)/shard_map/ppermute | solution.py:18
  176.8 11.0 %collective-permute-start.3 = (f32[72,4,128]{2,1,0:T(4,128)S(1)}, f32[72,4,128]{2,1,0:T(4,128)S(1)}, u32[]{:S(2)}, u32[]{:S(2)}) collective-permute-start(f32[72,4,128]{2,1,0:T(4,128)S(1)} %get-tuple-element.66), channel_id=1, source_target_pairs={{0,1},{1,2},{2,3},{4,5},{5,6},{6,7},{8,9},{9,10},{10,11},{12,13},{... | collective-permute-start | bytes 442376 | tf_op jit(solution)/shard_map/ppermute | solution.py:17
  179.3 5.7 %collective-permute-start.6 = (f32[72,4]{1,0:T(8,128)S(1)}, f32[72,4]{1,0:T(8,128)S(1)}, u32[]{:S(2)}, u32[]{:S(2)}) collective-permute-start(f32[72,4]{1,0:T(8,128)S(1)} %get-tuple-element.69), channel_id=1, source_target_pairs={{1,0},{2,1},{3,2},{5,4},{6,5},{7,6},{9,8},{10,9},{11,10},{13,12},{... | collective-permute-start | bytes 3464 | tf_op jit(solution)/shard_map/ppermute | solution.py:18
  182.5 5.3 %collective-permute-start.7 = (f32[72,4]{1,0:T(8,128)S(1)}, f32[72,4]{1,0:T(8,128)S(1)}, u32[]{:S(2)}, u32[]{:S(2)}) collective-permute-start(f32[72,4]{1,0:T(8,128)S(1)} %get-tuple-element.70), channel_id=1, source_target_pairs={{0,1},{1,2},{2,3},{4,5},{5,6},{6,7},{8,9},{9,10},{10,11},{12,13},{... | collective-permute-start | bytes 3464 | tf_op jit(solution)/shard_map/ppermute | solution.py:17

commit v2 on v1

--- a/solution.py
+++ b/solution.py
@@ -33,11 +33,19 @@
     return jnp.dot(hidden, last_layer, precision=highest)
 
 
-def gather_kernel(cell_ref, u_ref, v_ref, st_ref, o_ref):
+def gather_kernel(slot_ref, act_ref, u_ref, v_ref, st_ref, o_ref):
     levels_x, width_y = u_ref.shape
     cells, features = st_ref.shape
     levels = features // 2
     width_x = levels_x // levels
+    chunk = 128
+
+    def clear(k, carry):
+        at = pl.ds(pl.multiple_of(k * chunk, chunk), chunk)
+        o_ref[at, :] = jnp.zeros((chunk, features), jnp.float32)
+        return carry
+
+    lax.fori_loop(0, o_ref.shape[0] // chunk, clear, 0)
 
     def transpose_tile(x, carry):
         a = u_ref[pl.ds(x, levels, stride=width_x), :]
@@ -48,14 +56,11 @@
 
     lax.fori_loop(0, width_x, transpose_tile, 0)
 
-    def pick(s, carry):
-        cell = cell_ref[s]
-        keep = (cell < cells).astype(jnp.float32)
-        row = st_ref[pl.ds(jnp.minimum(cell, cells - 1), 1), :]
-        o_ref[pl.ds(s, 1), :] = row * keep
-        return carry
-
-    lax.fori_loop(0, o_ref.shape[0], pick, 0, unroll=8)
+    def place(r, carry):
+        o_ref[pl.ds(slot_ref[r], 1), :] = st_ref[pl.ds(act_ref[r], 1), :]
+        return carry
+
+    lax.fori_loop(0, act_ref.shape[0], place, 0, unroll=8)
 
 
 def diffuse_kernel(st_ref, xb_ref, xa_ref, yh_ref, c_ref, f_ref, e_ref, a_ref):
@@ -158,9 +163,6 @@
 
     _, ranks = lax.scan(rank_step, jnp.zeros((devices_all,), jnp.float32), one_hot)
     slot_index = target * capacity + ranks.reshape(-1).astype(jnp.int32)
-    cell_of_slot = jnp.full((slot_total,), cells, jnp.int32).at[slot_index].set(
-        active_columns, unique_indices=True
-    )
     vmem = pl.BlockSpec(memory_space=pltpu.VMEM)
     smem = pl.BlockSpec(memory_space=pltpu.SMEM)
     u_rows = u_field.reshape(levels * width_x, width_y)
@@ -171,9 +173,9 @@
             jax.ShapeDtypeStruct((cells, features), jnp.float32),
             jax.ShapeDtypeStruct((slot_total, features), jnp.float32),
         ),
-        in_specs=[smem, vmem, vmem],
+        in_specs=[smem, smem, vmem, vmem],
         out_specs=(vmem, vmem),
-    )(cell_of_slot, u_rows, v_rows)
+    )(slot_index, active_columns, u_rows, v_rows)
     block = lax.all_to_all(
         outgoing.reshape(devices_all, capacity, features),
         ("tile", "inf"),
@@ -190,9 +192,25 @@
 
     depth = PASSES
     state_t = state_t.reshape(width_x, width_y, features)
-    x_before, x_after = halos(state_t, "tile", 0, depth)
-    extended = jnp.concatenate([x_before, state_t, x_after], axis=0)
-    y_before, y_after = halos(extended, "inf", 1, depth)
+    u_before, u_after = halos(u_field, "tile", 1, depth)
+    v_before, v_after = halos(v_field, "tile", 1, depth)
+    x_before = jnp.concatenate([u_before, v_before], axis=0).transpose(1, 2, 0)
+    x_after = jnp.concatenate([u_after, v_after], axis=0).transpose(1, 2, 0)
+
+    def edge_columns(start):
+        pieces = []
+        for field, before, after in ((u_field, u_before, u_after), (v_field, v_before, v_after)):
+            column = lambda a: lax.slice_in_dim(a, start, start + depth, axis=2)
+            pieces.append(
+                jnp.concatenate([column(before), column(field), column(after)], axis=1)
+            )
+        return jnp.concatenate(pieces, axis=0).transpose(1, 2, 0)
+
+    inf_count = lax.axis_size("inf")
+    up = [(i, i + 1) for i in range(inf_count - 1)]
+    down = [(j, i) for i, j in up]
+    y_before = lax.ppermute(edge_columns(width_y - depth), "inf", up)
+    y_after = lax.ppermute(edge_columns(0), "inf", down)
     y_halo = jnp.concatenate([y_after, y_before], axis=1)
     c_before, c_after = halos(diffusivity, "tile", 0, depth)
     c_ext = jnp.concatenate([c_before, diffusivity, c_after], axis=0)

time: 228 us -> 229 us (level)
  the two profiles are of different devices: /device:TPU:20 before, /device:TPU:11 now
where the time goes in v2:
time: 229 us; the launch traced here: 228 us
  Pallas kernels  53 us (23%)
  blocking collectives  52.4 us (23%)
  waiting for transfers between devices  35.9 us (16%)
  starting transfers between devices  34.9 us (15%)
  local copies, waits for them, and re-layouts  23.4 us (10%)
  matrix products  18.1 us (8%)
  other arithmetic  9.13 us (4%)
    all_to_all x1, blocking collectives, body(): lax.all_to_all(outgoing.reshape(devices_all, capacity, features), ('tile'...  52.4 us
    ppermute x4, waiting for transfers between devices, halos(): before = lax.ppermute(last, axis, up)  24.2 us
    pallas_call x1, Pallas kernels, body(): pl.pallas_call(finish_kernel, out_shape=(jax.ShapeDtypeStruct((levels * w...  20.1 us
    pallas_call x1, Pallas kernels, body(): pl.pallas_call(gather_kernel, out_shape=(jax.ShapeDtypeStruct((cells, fea...  17.7 us
    pallas_call x1, Pallas kernels, body(): pl.pallas_call(diffuse_kernel, out_shape=jax.ShapeDtypeStruct((width_x, w...  15.3 us
    ppermute x4, starting transfers between devices, halos(): before = lax.ppermute(last, axis, up)  14.6 us
    unnamed x30, local copies, waits for them, and re-layouts  12.5 us
    ppermute x4, starting transfers between devices, halos(): after = lax.ppermute(first, axis, down)  9.74 us
  transfers between devices with their start and end apart: 11, of which 4 were waited for; matrix products, arithmetic and copies ran while one was open for 11% of the time, Pallas kernels for 7%

profile of v2, /device:TPU:11, one launch (start us, length us, event | category | flops | bytes accessed | tf_op | source)
XLA Modules:
  0.0 228.0 jit_solution(11720383135164549251)
XLA Ops:
  1.2 1.4 fusion.46
  2.6 1.9 while.13
  5.1 17.7 %shard_map.104 = (f32[8192,128]{1,0:T(8,128)}, f32[4096,128]{1,0:T(8,128)}) custom-call(s32[2048]{0:T(1024)} %add.41.slot_ref, s32[2048]{0:T(1024)} %act_ref.3, f32[4096,128]{1,0:T(8,128)} %bitcast.57, f32[4096,128]{1,0:T(8,128)} %bitcast.58), custom_call_target="tpu_custom_call" | custom-call | tf_op jit(solution)/shard_map/pallas_call | solution.py:170
  22.8 52.4 %all_to_all.10 = f32[32,128,128]{2,1,0:T(8,128)S(1)} all-to-all(f32[32,128,128]{2,1,0:T(8,128)} %bitcast.63), channel_id=1, replica_groups=mesh['tile'=8,'inf'=4] {'tile','inf'}, dimensions={0} | all-to-all | bytes 4194304 | tf_op jit(solution)/shard_map/all_to_all | solution.py:179
  75.9 1.3 multiply_reduce_fusion
  77.2 1.2 subtract_multiply_fusion
  78.5 3.5 %fusion.31 = f32[4096,256]{1,0:T(8,128)S(1)} fusion(f32[4096,128]{1,0:T(8,128)S(1)} %bitcast.60, f32[1,128,256]{2,1,0:T(8,128)S(1)} %copy-done.5), kind=kOutput, calls=%fused_computation.40 | convolution fusion | flops 1610612736 | bytes 6422528 | tf_op jit(solution)/shard_map/dot_general | solution.py:30
  82.0 4.1 %fusion.16 = f32[4096,256]{1,0:T(8,128)S(1)} fusion(f32[4096,256]{1,0:T(8,128)S(1)} %fusion.31, f32[1,256,256]{2,1,0:T(8,128)S(1)} %copy-done.8), kind=kOutput, calls=%fused_computation.19 | convolution fusion | flops 3225419776 | bytes 8650752 | tf_op jit(solution)/shard_map/dot_general | solution.py:31
  86.1 4.6 %divide_multiply_fusion = f32[4096,256]{1,0:T(8,128)S(1)} fusion(f32[4096,256]{1,0:T(8,128)S(1)} %fusion.16, f32[1,256,256]{2,1,0:T(8,128)S(1)} %copy-done.9), kind=kOutput, calls=%fused_computation.12 | convolution fusion | flops 3229614080 | bytes 8650752 | tf_op jit(solution)/shard_map/dot_general | solution.py:32
  90.8 4.7 %fusion.29 = f32[32,128,128]{2,1,0:T(8,128)} fusion(f32[32,128,256]{2,1,0:T(8,128)S(1)} %bitcast.62, f32[1,256,128]{2,1,0:T(8,128)S(1)} %copy-done.6), kind=kOutput, calls=%fused_computation.38 | convolution fusion | flops 1610612736 | bytes 6422528 | tf_op jit(solution)/shard_map/dot_general | solution.py:33
  95.5 6.3 %all-to-all-start.1 = ((f32[32,128,128]{2,1,0:T(8,128)}), f32[32,128,128]{2,1,0:T(8,128)}, u32[]{:S(2)}, u32[]{:S(2)}) async-start(f32[32,128,128]{2,1,0:T(8,128)} %fusion.29), calls=%async_computation.1 | async-start | bytes 4194304 | tf_op jit(solution)/shard_map/all_to_all | solution.py:190
  101.8 3.1 %collective-permute-start.6 = (f32[4,128]{1,0:T(4,128)S(1)}, f32[4,128]{1,0:T(4,128)S(1)}, u32[]{:S(2)}, u32[]{:S(2)}) collective-permute-start(f32[4,128]{1,0:T(4,128)S(1)} %get-tuple-element.83), channel_id=1, source_target_pairs={{0,4},{4,8},{8,12},{12,16},{16,20},{20,24},{24,28},{1,5},{5,9},{9,... | collective-permute-start | bytes 6152 | tf_op jit(solution)/shard_map/ppermute | solution.py:17
  104.9 2.2 collective-permute-start.7
  108.3 4.0 %collective-permute-start.1 = (f32[64,4,128]{0,2,1:T(8,128)S(1)}, f32[64,4,128]{0,2,1:T(8,128)S(1)}, u32[]{:S(2)}, u32[]{:S(2)}) collective-permute-start(f32[64,4,128]{0,2,1:T(8,128)S(1)} %copy.20), channel_id=1, source_target_pairs={{0,4},{4,8},{8,12},{12,16},{16,20},{20,24},{24,28},{1,5},{5,9},{9,... | collective-permute-start | bytes 393224 | tf_op jit(solution)/shard_map/ppermute | solution.py:17
  113.2 1.9 collective-permute-start.3
  116.0 4.4 %collective-permute-start = (f32[64,4,128]{0,2,1:T(8,128)}, f32[64,4,128]{0,2,1:T(8,128)S(1)}, u32[]{:S(2)}, u32[]{:S(2)}) collective-permute-start(f32[64,4,128]{0,2,1:T(8,128)} %copy.19), channel_id=1, source_target_pairs={{0,4},{4,8},{8,12},{12,16},{16,20},{20,24},{24,28},{1,5},{5,9},{9,... | collective-permute-start | bytes 393224 | tf_op jit(solution)/shard_map/ppermute | solution.py:17
  120.4 2.8 %fusion.36 = (f32[64,64,4]{2,1,0:T(8,128)}, f32[64,64,4]{2,1,0:T(8,128)}) fusion(f32[64,64,128]{2,1,0:T(8,128)S(1)} %copy-done), kind=kLoop, calls=%fused_computation.51 | loop fusion | bytes 262144 | tf_op jit(solution)/shard_map/slice | solution.py:203
  123.2 24.2 %collective-permute-done.6 = f32[4,128]{1,0:T(4,128)S(1)} collective-permute-done((f32[4,128]{1,0:T(4,128)S(1)}, f32[4,128]{1,0:T(4,128)S(1)}, u32[]{:S(2)}, u32[]{:S(2)}) %collective-permute-start.6) | collective-permute-done | bytes 2080 | tf_op jit(solution)/shard_map/ppermute | solution.py:17
  149.1 3.7 %collective-permute-start.8 = (f32[72,4]{1,0:T(8,128)}, f32[72,4]{1,0:T(8,128)S(1)}, u32[]{:S(2)}, u32[]{:S(2)}) collective-permute-start(f32[72,4]{1,0:T(8,128)} %get-tuple-element.81), channel_id=1, source_target_pairs={{1,0},{2,1},{3,2},{5,4},{6,5},{7,6},{9,8},{10,9},{11,10},{13,12},{... | collective-permute-start | bytes 3464 | tf_op jit(solution)/shard_map/ppermute | solution.py:18
  152.8 3.1 %collective-permute-start.9 = (f32[72,4]{1,0:T(8,128)S(1)}, f32[72,4]{1,0:T(8,128)S(1)}, u32[]{:S(2)}, u32[]{:S(2)}) collective-permute-start(f32[72,4]{1,0:T(8,128)S(1)} %get-tuple-element.82), channel_id=1, source_target_pairs={{0,1},{1,2},{2,3},{4,5},{5,6},{6,7},{8,9},{9,10},{10,11},{12,13},{... | collective-permute-start | bytes 3464 | tf_op jit(solution)/shard_map/ppermute | solution.py:17
  155.9 2.8 %fusion.37 = (f32[64,64,4]{2,1,0:T(8,128)}, f32[64,64,4]{2,1,0:T(8,128)}) fusion(f32[64,64,128]{2,1,0:T(8,128)S(1)} %copy-done.1), kind=kLoop, calls=%fused_computation.52 | loop fusion | bytes 262144 | tf_op jit(solution)/shard_map/slice | solution.py:203
  159.6 2.7 %copy.23 = f32[64,64,4]{0,2,1:T(4,128)S(1)} copy(f32[64,64,4]{2,1,0:T(8,128)} %get-tuple-element.65) | data formatting | bytes 131072
  163.5 2.7 %copy.24 = f32[64,64,4]{0,2,1:T(4,128)S(1)} copy(f32[64,64,4]{2,1,0:T(8,128)} %get-tuple-element.67) | data formatting | bytes 131072
  166.2 2.7 %copy.26 = f32[64,64,4]{0,2,1:T(4,128)S(1)} copy(f32[64,64,4]{2,1,0:T(8,128)} %get-tuple-element.68) | data formatting | bytes 131072
  168.8 1.9 collective-permute-start.2
  171.6 8.2 %collective-permute-done.2 = f32[64,4,128]{0,2,1:T(8,128)S(1)} collective-permute-done((f32[64,4,128]{0,2,1:T(8,128)S(1)}, f32[64,4,128]{0,2,1:T(8,128)S(1)}, u32[]{:S(2)}, u32[]{:S(2)}) %collective-permute-start.2) | collective-permute-done | bytes 131104 | tf_op jit(solution)/shard_map/ppermute | solution.py:18
  179.9 1.9 collective-permute-start.5
  182.0 2.4 %collective-permute-start.4 = (f32[72,4,128]{2,1,0:T(4,128)S(1)}, f32[72,4,128]{2,1,0:T(4,128)S(1)}, u32[]{:S(2)}, u32[]{:S(2)}) collective-permute-start(f32[72,4,128]{2,1,0:T(4,128)S(1)} %maximum_bitcast_fusion.2), channel_id=1, source_target_pairs={{1,0},{2,1},{3,2},{5,4},{6,5},{7,6},{9,8},{10,9},{11,10},{13,12},{... | collective-permute-start | bytes 442376 | tf_op jit(solution)/shard_map/ppermute | solution.py:213
  186.1 2.4 %collective-permute-done.4 = f32[72,4,128]{2,1,0:T(4,128)S(1)} collective-permute-done((f32[72,4,128]{2,1,0:T(4,128)S(1)}, f32[72,4,128]{2,1,0:T(4,128)S(1)}, u32[]{:S(2)}, u32[]{:S(2)}) %collective-permute-start.4) | collective-permute-done | bytes 147488 | tf_op jit(solution)/shard_map/ppermute | solution.py:213
  189.2 3.4 %broadcast_in_dim.13.c_ref = f32[72,136,128]{2,1,0:T(8,128)} broadcast(f32[72,136]{1,0:T(8,128)S(1)} %pad_maximum_fusion.1), dimensions={0,1} | broadcast | bytes 5052672 | tf_op jit(solution)/shard_map/broadcast_in_dim | solution.py:220
  192.6 15.3 %shard_map.105 = f32[64,128,128]{2,1,0:T(8,128)} custom-call(f32[64,128,128]{2,1,0:T(8,128)} %bitcast.61, f32[4,128,128]{2,1,0:T(8,128)} %maximum_bitcast_fusion.xb_ref, f32[4,128,128]{2,1,0:T(8,128)} %maximum_bitcast_fusion.1.xa_ref, f32[72,8,128]{2,1,0:T(8,128)} %pad_maximum_fusion.yh_ref, f32[72,136,128]{2,1,0:T(8,128)} %broadcast_in_dim.13.c_ref), custom_call_target="tpu_custom_call" | custom-call | tf_op jit(solution)/shard_map/pallas_call | solution.py:221
  207.9 20.1 %shard_map.106 = (f32[4096,128]{1,0:T(8,128)}, f32[4096,128]{1,0:T(8,128)}) custom-call(s32[2048]{0:T(1024)} %add.41.slot_ref, s32[2048]{0:T(1024)} %act_ref.3, f32[4096,128]{1,0:T(8,128)} %bitcast.11.r_ref, f32[8192,128]{1,0:T(8,128)} %bitcast.59), custom_call_target="tpu_custom_call" | custom-call | tf_op jit(solution)/shard_map/pallas_call | solution.py:232
  (75 shorter events, 13.9 us)
Async XLA Ops:
  75.2 3.2 %copy-start.5 = (f32[1,128,256]{2,1,0:T(8,128)S(1)}, f32[1,128,256]{2,1,0:T(8,128)}, u32[]{:S(2)}) copy-start(f32[1,128,256]{2,1,0:T(8,128)} %param.16) | copy-start | bytes 393220
  78.4 3.5 %copy-start.8 = (f32[1,256,256]{2,1,0:T(8,128)S(1)}, f32[1,256,256]{2,1,0:T(8,128)}, u32[]{:S(2)}) copy-start(f32[1,256,256]{2,1,0:T(8,128)} %param.17) | copy-start | bytes 786436
  82.0 4.1 %copy-start.9 = (f32[1,256,256]{2,1,0:T(8,128)S(1)}, f32[1,256,256]{2,1,0:T(8,128)}, u32[]{:S(2)}) copy-start(f32[1,256,256]{2,1,0:T(8,128)} %param.18) | copy-start | bytes 786436
  86.1 4.6 %copy-start.6 = (f32[1,256,128]{2,1,0:T(8,128)S(1)}, f32[1,256,128]{2,1,0:T(8,128)}, u32[]{:S(2)}) copy-start(f32[1,256,128]{2,1,0:T(8,128)} %param.19) | copy-start | bytes 393220
  90.7 11.0 %copy-start.4 = (f32[64,128]{1,0:T(8,128)S(1)}, f32[64,128]{1,0:T(8,128)}, u32[]{:S(2)}) copy-start(f32[64,128]{1,0:T(8,128)} %param.13) | copy-start | bytes 98308
  95.5 19.6 %copy-start = (f32[64,64,128]{2,1,0:T(8,128)S(1)}, f32[64,64,128]{2,1,0:T(8,128)}, u32[]{:S(2)}) copy-start(f32[64,64,128]{2,1,0:T(8,128)} %param.11) | copy-start | bytes 6291460
  95.5 112.4 %all-to-all-start.1 = ((f32[32,128,128]{2,1,0:T(8,128)}), f32[32,128,128]{2,1,0:T(8,128)}, u32[]{:S(2)}, u32[]{:S(2)}) async-start(f32[32,128,128]{2,1,0:T(8,128)} %fusion.29), calls=%async_computation.1 | async-start | bytes 4194304 | tf_op jit(solution)/shard_map/all_to_all | solution.py:190
  101.8 45.6 %collective-permute-start.6 = (f32[4,128]{1,0:T(4,128)S(1)}, f32[4,128]{1,0:T(4,128)S(1)}, u32[]{:S(2)}, u32[]{:S(2)}) collective-permute-start(f32[4,128]{1,0:T(4,128)S(1)} %get-tuple-element.83), channel_id=1, source_target_pairs={{0,4},{4,8},{8,12},{12,16},{16,20},{20,24},{24,28},{1,5},{5,9},{9,... | collective-permute-start | bytes 6152 | tf_op jit(solution)/shard_map/ppermute | solution.py:17
  104.9 43.5 %collective-permute-start.7 = (f32[4,128]{1,0:T(4,128)S(1)}, f32[4,128]{1,0:T(4,128)S(1)}, u32[]{:S(2)}, u32[]{:S(2)}) collective-permute-start(f32[4,128]{1,0:T(4,128)S(1)} %get-tuple-element.84), channel_id=1, source_target_pairs={{4,0},{8,4},{12,8},{16,12},{20,16},{24,20},{28,24},{5,1},{9,5},{13... | collective-permute-start | bytes 6152 | tf_op jit(solution)/shard_map/ppermute | solution.py:18
  108.3 63.2 %collective-permute-start.1 = (f32[64,4,128]{0,2,1:T(8,128)S(1)}, f32[64,4,128]{0,2,1:T(8,128)S(1)}, u32[]{:S(2)}, u32[]{:S(2)}) collective-permute-start(f32[64,4,128]{0,2,1:T(8,128)S(1)} %copy.20), channel_id=1, source_target_pairs={{0,4},{4,8},{8,12},{12,16},{16,20},{20,24},{24,28},{1,5},{5,9},{9,... | collective-permute-start | bytes 393224 | tf_op jit(solution)/shard_map/ppermute | solution.py:17
  113.2 58.3 %collective-permute-start.3 = (f32[64,4,128]{0,2,1:T(8,128)}, f32[64,4,128]{0,2,1:T(8,128)S(1)}, u32[]{:S(2)}, u32[]{:S(2)}) collective-permute-start(f32[64,4,128]{0,2,1:T(8,128)} %copy.22), channel_id=1, source_target_pairs={{4,0},{8,4},{12,8},{16,12},{20,16},{24,20},{28,24},{5,1},{9,5},{13... | collective-permute-start | bytes 393224 | tf_op jit(solution)/shard_map/ppermute | solution.py:18
  116.0 39.9 %copy-start.1 = (f32[64,64,128]{2,1,0:T(8,128)S(1)}, f32[64,64,128]{2,1,0:T(8,128)}, u32[]{:S(2)}) copy-start(f32[64,64,128]{2,1,0:T(8,128)} %param.12) | copy-start | bytes 6291460
  116.0 55.5 %collective-permute-start = (f32[64,4,128]{0,2,1:T(8,128)}, f32[64,4,128]{0,2,1:T(8,128)S(1)}, u32[]{:S(2)}, u32[]{:S(2)}) collective-permute-start(f32[64,4,128]{0,2,1:T(8,128)} %copy.19), channel_id=1, source_target_pairs={{0,4},{4,8},{8,12},{12,16},{16,20},{20,24},{24,28},{1,5},{5,9},{9,... | collective-permute-start | bytes 393224 | tf_op jit(solution)/shard_map/ppermute | solution.py:17
  148.5 0.6 copy-start.7
  149.1 19.8 %collective-permute-start.8 = (f32[72,4]{1,0:T(8,128)}, f32[72,4]{1,0:T(8,128)S(1)}, u32[]{:S(2)}, u32[]{:S(2)}) collective-permute-start(f32[72,4]{1,0:T(8,128)} %get-tuple-element.81), channel_id=1, source_target_pairs={{1,0},{2,1},{3,2},{5,4},{6,5},{7,6},{9,8},{10,9},{11,10},{13,12},{... | collective-permute-start | bytes 3464 | tf_op jit(solution)/shard_map/ppermute | solution.py:18
  152.8 9.4 %copy-start.2 = (f32[64,64,4]{2,1,0:T(8,128)S(1)}, f32[64,64,4]{2,1,0:T(8,128)}, u32[]{:S(2)}) copy-start(f32[64,64,4]{2,1,0:T(8,128)} %get-tuple-element.66) | copy-start | bytes 196612
  152.8 17.9 %collective-permute-start.9 = (f32[72,4]{1,0:T(8,128)S(1)}, f32[72,4]{1,0:T(8,128)S(1)}, u32[]{:S(2)}, u32[]{:S(2)}) collective-permute-start(f32[72,4]{1,0:T(8,128)S(1)} %get-tuple-element.82), channel_id=1, source_target_pairs={{0,1},{1,2},{2,3},{4,5},{5,6},{6,7},{8,9},{9,10},{10,11},{12,13},{... | collective-permute-start | bytes 3464 | tf_op jit(solution)/shard_map/ppermute | solution.py:17
  163.4 5.4 %copy-start.3 = (f32[64,4,128]{0,2,1:T(8,128)S(1)}, f32[64,4,128]{0,2,1:T(8,128)}, u32[]{:S(2)}) copy-start(f32[64,4,128]{0,2,1:T(8,128)} %copy.21) | copy-start | bytes 393220
  168.8 10.9 %collective-permute-start.2 = (f32[64,4,128]{0,2,1:T(8,128)S(1)}, f32[64,4,128]{0,2,1:T(8,128)S(1)}, u32[]{:S(2)}, u32[]{:S(2)}) collective-permute-start(f32[64,4,128]{0,2,1:T(8,128)S(1)} %copy-done.3), channel_id=1, source_target_pairs={{4,0},{8,4},{12,8},{16,12},{20,16},{24,20},{28,24},{5,1},{9,5},{13... | collective-permute-start | bytes 393224 | tf_op jit(solution)/shard_map/ppermute | solution.py:18
  179.9 6.2 %collective-permute-start.5 = (f32[72,4,128]{2,1,0:T(4,128)S(1)}, f32[72,4,128]{2,1,0:T(4,128)S(1)}, u32[]{:S(2)}, u32[]{:S(2)}) collective-permute-start(f32[72,4,128]{2,1,0:T(4,128)S(1)} %maximum_bitcast_fusion.3), channel_id=1, source_target_pairs={{0,1},{1,2},{2,3},{4,5},{5,6},{6,7},{8,9},{9,10},{10,11},{12,13},{... | collective-permute-start | bytes 442376 | tf_op jit(solution)/shard_map/ppermute | solution.py:212
  182.0 6.5 %collective-permute-start.4 = (f32[72,4,128]{2,1,0:T(4,128)S(1)}, f32[72,4,128]{2,1,0:T(4,128)S(1)}, u32[]{:S(2)}, u32[]{:S(2)}) collective-permute-start(f32[72,4,128]{2,1,0:T(4,128)S(1)} %maximum_bitcast_fusion.2), channel_id=1, source_target_pairs={{1,0},{2,1},{3,2},{5,4},{6,5},{7,6},{9,8},{10,9},{11,10},{13,12},{... | collective-permute-start | bytes 442376 | tf_op jit(solution)/shard_map/ppermute | solution.py:213

commit v3 on v2

--- a/solution.py
+++ b/solution.py
@@ -26,7 +26,7 @@
 
 
 def network_rows(rows, first_layer, second_layer, third_layer, last_layer):
-    highest = lax.Precision.HIGHEST
+    highest = lax.Precision.HIGH
     hidden = jax.nn.silu(jnp.dot(rows, first_layer, precision=highest))
     hidden = jax.nn.silu(jnp.dot(hidden, second_layer, precision=highest))
     hidden = jax.nn.silu(jnp.dot(hidden, third_layer, precision=highest))
@@ -165,33 +165,7 @@
     slot_index = target * capacity + ranks.reshape(-1).astype(jnp.int32)
     vmem = pl.BlockSpec(memory_space=pltpu.VMEM)
     smem = pl.BlockSpec(memory_space=pltpu.SMEM)
-    u_rows = u_field.reshape(levels * width_x, width_y)
-    v_rows = v_field.reshape(levels * width_x, width_y)
-    state_t, outgoing = pl.pallas_call(
-        gather_kernel,
-        out_shape=(
-            jax.ShapeDtypeStruct((cells, features), jnp.float32),
-            jax.ShapeDtypeStruct((slot_total, features), jnp.float32),
-        ),
-        in_specs=[smem, smem, vmem, vmem],
-        out_specs=(vmem, vmem),
-    )(slot_index, active_columns, u_rows, v_rows)
-    block = lax.all_to_all(
-        outgoing.reshape(devices_all, capacity, features),
-        ("tile", "inf"),
-        split_axis=0,
-        concat_axis=0,
-        tiled=True,
-    )
-    block_shape = block.shape
-    rows = standardize(block.reshape(-1, features))
-    result = network_rows(rows, first_layer[0], second_layer[0], third_layer[0], last_layer[0])
-    answered = result.reshape(block_shape)
-    returned = lax.all_to_all(answered, ("tile", "inf"), split_axis=0, concat_axis=0, tiled=True)
-    returned_rows = returned.reshape(slot_total, features)
-
     depth = PASSES
-    state_t = state_t.reshape(width_x, width_y, features)
     u_before, u_after = halos(u_field, "tile", 1, depth)
     v_before, v_after = halos(v_field, "tile", 1, depth)
     x_before = jnp.concatenate([u_before, v_before], axis=0).transpose(1, 2, 0)
@@ -218,6 +192,35 @@
     c_ext = jnp.concatenate([c_ext, c_after, c_before], axis=1)
     rows_ext, ylen = c_ext.shape
     coeff = jnp.broadcast_to(c_ext[:, :, None], (rows_ext, ylen, features))
+    u_rows = u_field.reshape(levels * width_x, width_y)
+    v_rows = v_field.reshape(levels * width_x, width_y)
+    state_t, outgoing = pl.pallas_call(
+        gather_kernel,
+        out_shape=(
+            jax.ShapeDtypeStruct((cells, features), jnp.float32),
+            jax.ShapeDtypeStruct((slot_total, features), jnp.float32),
+        ),
+        in_specs=[smem, smem, vmem, vmem],
+        out_specs=(vmem, vmem),
+    )(slot_index, active_columns, u_rows, v_rows)
+    outgoing, x_before, x_after, y_halo, coeff = lax.optimization_barrier(
+        (outgoing, x_before, x_after, y_halo, coeff)
+    )
+    state_t = state_t.reshape(width_x, width_y, features)
+    block = lax.all_to_all(
+        outgoing.reshape(devices_all, capacity, features),
+        ("tile", "inf"),
+        split_axis=0,
+        concat_axis=0,
+        tiled=True,
+    )
+    block_shape = block.shape
+    rows = standardize(block.reshape(-1, features))
+    result = network_rows(rows, first_layer[0], second_layer[0], third_layer[0], last_layer[0])
+    answered = result.reshape(block_shape)
+    returned = lax.all_to_all(answered, ("tile", "inf"), split_axis=0, concat_axis=0, tiled=True)
+    returned_rows = returned.reshape(slot_total, features)
+
     diffused = pl.pallas_call(
         diffuse_kernel,
         out_shape=jax.ShapeDtypeStruct((width_x, width_y, features), jnp.float32),

time: 229 us -> 233 us (1.017)
  the two profiles are of different devices: /device:TPU:11 before, /device:TPU:0 now
where the time goes in v3:
time: 233 us; the launch traced here: 232 us
  blocking collectives  56.8 us (24%)
  Pallas kernels  53.1 us (23%)
  waiting for transfers between devices  43.7 us (19%)
  starting transfers between devices  30 us (13%)
  local copies, waits for them, and re-layouts  28.3 us (12%)
  matrix products  11 us (5%)
  other arithmetic  8.44 us (4%)
    all_to_all x1, blocking collectives, body(): lax.all_to_all(outgoing.reshape(devices_all, capacity, features), ('tile'...  56.8 us
    all_to_all x1, waiting for transfers between devices, body(): lax.all_to_all(answered, ('tile', 'inf'), split_axis=0, concat_axis=0, ti...  33.4 us
    pallas_call x1, Pallas kernels, body(): pl.pallas_call(finish_kernel, out_shape=(jax.ShapeDtypeStruct((levels * w...  20.1 us
    pallas_call x1, Pallas kernels, body(): pl.pallas_call(gather_kernel, out_shape=(jax.ShapeDtypeStruct((cells, fea...  17.7 us
    ppermute x4, starting transfers between devices, halos(): before = lax.ppermute(last, axis, up)  17.4 us
    pallas_call x1, Pallas kernels, body(): pl.pallas_call(diffuse_kernel, out_shape=jax.ShapeDtypeStruct((width_x, w...  15.3 us
    unnamed x38, local copies, waits for them, and re-layouts  13.1 us
    ppermute x4, waiting for transfers between devices, halos(): after = lax.ppermute(first, axis, down)  10 us
  transfers between devices with their start and end apart: 11, of which 3 were waited for; matrix products, arithmetic and copies ran while one was open for 13% of the time, Pallas kernels for 14%

profile of v3, /device:TPU:0, one launch (start us, length us, event | category | flops | bytes accessed | tf_op | source)
XLA Modules:
  0.0 232.4 jit_solution(149013756251069302)
XLA Ops:
  1.5 4.9 %collective-permute-start.6 = (f32[4,128]{1,0:T(4,128)S(1)}, f32[4,128]{1,0:T(4,128)S(1)}, u32[]{:S(2)}, u32[]{:S(2)}) collective-permute-start(f32[4,128]{1,0:T(4,128)S(1)} %get-tuple-element.93), channel_id=1, source_target_pairs={{0,4},{4,8},{8,12},{12,16},{16,20},{20,24},{24,28},{1,5},{5,9},{9,... | collective-permute-start | bytes 6152 | tf_op jit(solution)/shard_map/ppermute | solution.py:17
  6.4 1.3 collective-permute-start.7
  8.9 4.6 %collective-permute-start.1 = (f32[64,4,128]{0,2,1:T(8,128)S(1)}, f32[64,4,128]{0,2,1:T(8,128)S(1)}, u32[]{:S(2)}, u32[]{:S(2)}) collective-permute-start(f32[64,4,128]{0,2,1:T(8,128)S(1)} %copy.20), channel_id=1, source_target_pairs={{0,4},{4,8},{8,12},{12,16},{16,20},{20,24},{24,28},{1,5},{5,9},{9,... | collective-permute-start | bytes 393224 | tf_op jit(solution)/shard_map/ppermute | solution.py:17
  14.3 1.3 collective-permute-start.3
  17.5 5.0 %collective-permute-start = (f32[64,4,128]{0,2,1:T(8,128)}, f32[64,4,128]{0,2,1:T(8,128)S(1)}, u32[]{:S(2)}, u32[]{:S(2)}) collective-permute-start(f32[64,4,128]{0,2,1:T(8,128)} %copy.19), channel_id=1, source_target_pairs={{0,4},{4,8},{8,12},{12,16},{16,20},{20,24},{24,28},{1,5},{5,9},{9,... | collective-permute-start | bytes 393224 | tf_op jit(solution)/shard_map/ppermute | solution.py:17
  22.6 2.8 %fusion.36 = (f32[64,64,4]{2,1,0:T(8,128)}, f32[64,64,4]{2,1,0:T(8,128)}) fusion(f32[64,64,128]{2,1,0:T(8,128)S(1)} %copy-done), kind=kLoop, calls=%fused_computation.51 | loop fusion | bytes 262144 | tf_op jit(solution)/shard_map/slice | solution.py:177
  25.8 1.2 fusion.46
  27.1 1.9 while.13
  29.1 5.1 %fusion.37 = (f32[64,64,4]{2,1,0:T(8,128)}, f32[64,64,4]{2,1,0:T(8,128)}) fusion(f32[64,64,128]{2,1,0:T(8,128)} %param.12), kind=kLoop, calls=%fused_computation.52 | loop fusion | bytes 262144 | tf_op jit(solution)/shard_map/slice | solution.py:177
  34.9 1.3 collective-permute-start.8
  36.2 3.0 %collective-permute-start.9 = (f32[72,4]{1,0:T(8,128)S(1)}, f32[72,4]{1,0:T(8,128)S(1)}, u32[]{:S(2)}, u32[]{:S(2)}) collective-permute-start(f32[72,4]{1,0:T(8,128)S(1)} %get-tuple-element.92), channel_id=1, source_target_pairs={{0,1},{1,2},{2,3},{4,5},{5,6},{6,7},{8,9},{9,10},{10,11},{12,13},{... | collective-permute-start | bytes 3464 | tf_op jit(solution)/shard_map/ppermute | solution.py:17
  40.7 2.7 %copy.23 = f32[64,64,4]{0,2,1:T(4,128)S(1)} copy(f32[64,64,4]{2,1,0:T(8,128)} %get-tuple-element.75) | data formatting | bytes 131072
  43.4 1.2 copy.25
  44.6 2.7 %copy.24 = f32[64,64,4]{0,2,1:T(4,128)S(1)} copy(f32[64,64,4]{2,1,0:T(8,128)} %get-tuple-element.77) | data formatting | bytes 131072
  47.3 2.7 %copy.26 = f32[64,64,4]{0,2,1:T(4,128)S(1)} copy(f32[64,64,4]{2,1,0:T(8,128)} %get-tuple-element.78) | data formatting | bytes 131072
  50.6 17.7 %shard_map.104 = (f32[8192,128]{1,0:T(8,128)}, f32[4096,128]{1,0:T(8,128)}) custom-call(s32[2048]{0:T(1024)} %add.41.slot_ref, s32[2048]{0:T(1024)} %act_ref.3, f32[4096,128]{1,0:T(8,128)} %bitcast.57, f32[4096,128]{1,0:T(8,128)} %bitcast.58), custom_call_target="tpu_custom_call" | custom-call | tf_op jit(solution)/shard_map/pallas_call | solution.py:197
  68.2 1.4 collective-permute-start.2
  69.9 10.0 %collective-permute-done.2 = f32[64,4,128]{0,2,1:T(8,128)S(1)} collective-permute-done((f32[64,4,128]{0,2,1:T(8,128)S(1)}, f32[64,4,128]{0,2,1:T(8,128)S(1)}, u32[]{:S(2)}, u32[]{:S(2)}) %collective-permute-start.2) | collective-permute-done | bytes 131104 | tf_op jit(solution)/shard_map/ppermute | solution.py:18
  80.0 2.2 collective-permute-start.5
  82.4 1.3 collective-permute-start.4
  86.4 3.4 %broadcast_in_dim.13.c_ref = f32[72,136,128]{2,1,0:T(8,128)} broadcast(f32[72,136]{1,0:T(8,128)S(1)} %pad_maximum_fusion.1), dimensions={0,1} | broadcast | bytes 5052672 | tf_op jit(solution)/shard_map/broadcast_in_dim | solution.py:194
  89.8 56.8 %all_to_all.10 = f32[32,128,128]{2,1,0:T(8,128)S(1)} all-to-all(f32[32,128,128]{2,1,0:T(8,128)S(1)} %bitcast.63), channel_id=1, replica_groups=mesh['tile'=8,'inf'=4] {'tile','inf'}, dimensions={0} | all-to-all | bytes 4194304 | tf_op jit(solution)/shard_map/all_to_all | solution.py:210
  147.3 1.3 multiply_reduce_fusion
  148.6 1.2 subtract_multiply_fusion
  149.9 1.8 fusion.31
  151.7 2.4 %fusion.16 = f32[4096,256]{1,0:T(8,128)S(1)} fusion(f32[4096,256]{1,0:T(8,128)S(1)} %fusion.31, f32[1,256,256]{2,1,0:T(8,128)S(1)} %copy-done.12), kind=kOutput, calls=%fused_computation.19 | convolution fusion | flops 1614807040 | bytes 8650752 | tf_op jit(solution)/shard_map/dot_general | solution.py:31
  154.1 2.6 %divide_multiply_fusion = f32[4096,256]{1,0:T(8,128)S(1)} fusion(f32[4096,256]{1,0:T(8,128)S(1)} %fusion.16, f32[1,256,256]{2,1,0:T(8,128)S(1)} %copy-done.13), kind=kOutput, calls=%fused_computation.12 | convolution fusion | flops 1619001344 | bytes 8650752 | tf_op jit(solution)/shard_map/dot_general | solution.py:32
  156.7 3.1 %fusion.29 = f32[32,128,128]{2,1,0:T(8,128)} fusion(f32[32,128,256]{2,1,0:T(8,128)S(1)} %bitcast.62, f32[1,256,128]{2,1,0:T(8,128)S(1)} %copy-done.6), kind=kOutput, calls=%fused_computation.38 | convolution fusion | flops 805306368 | bytes 6422528 | tf_op jit(solution)/shard_map/dot_general | solution.py:33
  159.8 3.8 %all-to-all-start.1 = ((f32[32,128,128]{2,1,0:T(8,128)}), f32[32,128,128]{2,1,0:T(8,128)}, u32[]{:S(2)}, u32[]{:S(2)}) async-start(f32[32,128,128]{2,1,0:T(8,128)} %fusion.29), calls=%async_computation.1 | async-start | bytes 4194304 | tf_op jit(solution)/shard_map/all_to_all | solution.py:221
  163.6 15.3 %shard_map.105 = f32[64,128,128]{2,1,0:T(8,128)} custom-call(f32[64,128,128]{2,1,0:T(8,128)} %bitcast.61, f32[4,128,128]{2,1,0:T(8,128)} %maximum_bitcast_fusion.xb_ref, f32[4,128,128]{2,1,0:T(8,128)} %maximum_bitcast_fusion.1.xa_ref, f32[72,8,128]{2,1,0:T(8,128)} %pad_maximum_fusion.yh_ref, f32[72,136,128]{2,1,0:T(8,128)} %broadcast_in_dim.13.c_ref), custom_call_target="tpu_custom_call" | custom-call | tf_op jit(solution)/shard_map/pallas_call | solution.py:224
  178.9 33.4 %all-to-all-done.1 = f32[32,128,128]{2,1,0:T(8,128)} async-done(((f32[32,128,128]{2,1,0:T(8,128)}), f32[32,128,128]{2,1,0:T(8,128)}, u32[]{:S(2)}, u32[]{:S(2)}) %all-to-all-start.1) | async-done | bytes 2097184 | tf_op jit(solution)/shard_map/all_to_all | solution.py:221
  212.3 20.1 %shard_map.106 = (f32[4096,128]{1,0:T(8,128)}, f32[4096,128]{1,0:T(8,128)}) custom-call(s32[2048]{0:T(1024)} %add.41.slot_ref, s32[2048]{0:T(1024)} %act_ref.3, f32[4096,128]{1,0:T(8,128)} %bitcast.15.r_ref, f32[8192,128]{1,0:T(8,128)} %bitcast.59), custom_call_target="tpu_custom_call" | custom-call | tf_op jit(solution)/shard_map/pallas_call | solution.py:235
  (83 shorter events, 13.8 us)
Async XLA Ops:
  0.6 21.9 %copy-start = (f32[64,64,128]{2,1,0:T(8,128)S(1)}, f32[64,64,128]{2,1,0:T(8,128)}, u32[]{:S(2)}) copy-start(f32[64,64,128]{2,1,0:T(8,128)} %param.11) | copy-start | bytes 6291460
  1.5 32.7 %collective-permute-start.6 = (f32[4,128]{1,0:T(4,128)S(1)}, f32[4,128]{1,0:T(4,128)S(1)}, u32[]{:S(2)}, u32[]{:S(2)}) collective-permute-start(f32[4,128]{1,0:T(4,128)S(1)} %get-tuple-element.93), channel_id=1, source_target_pairs={{0,4},{4,8},{8,12},{12,16},{16,20},{20,24},{24,28},{1,5},{5,9},{9,... | collective-permute-start | bytes 6152 | tf_op jit(solution)/shard_map/ppermute | solution.py:17
  6.4 27.9 %collective-permute-start.7 = (f32[4,128]{1,0:T(4,128)S(1)}, f32[4,128]{1,0:T(4,128)S(1)}, u32[]{:S(2)}, u32[]{:S(2)}) collective-permute-start(f32[4,128]{1,0:T(4,128)S(1)} %get-tuple-element.94), channel_id=1, source_target_pairs={{4,0},{8,4},{12,8},{16,12},{20,16},{24,20},{28,24},{5,1},{9,5},{13... | collective-permute-start | bytes 6152 | tf_op jit(solution)/shard_map/ppermute | solution.py:18
  8.9 60.9 %collective-permute-start.1 = (f32[64,4,128]{0,2,1:T(8,128)S(1)}, f32[64,4,128]{0,2,1:T(8,128)S(1)}, u32[]{:S(2)}, u32[]{:S(2)}) collective-permute-start(f32[64,4,128]{0,2,1:T(8,128)S(1)} %copy.20), channel_id=1, source_target_pairs={{0,4},{4,8},{8,12},{12,16},{16,20},{20,24},{24,28},{1,5},{5,9},{9,... | collective-permute-start | bytes 393224 | tf_op jit(solution)/shard_map/ppermute | solution.py:17
  14.3 55.5 %collective-permute-start.3 = (f32[64,4,128]{0,2,1:T(8,128)}, f32[64,4,128]{0,2,1:T(8,128)S(1)}, u32[]{:S(2)}, u32[]{:S(2)}) collective-permute-start(f32[64,4,128]{0,2,1:T(8,128)} %copy.22), channel_id=1, source_target_pairs={{4,0},{8,4},{12,8},{16,12},{20,16},{24,20},{28,24},{5,1},{9,5},{13... | collective-permute-start | bytes 393224 | tf_op jit(solution)/shard_map/ppermute | solution.py:18
  17.5 52.3 %collective-permute-start = (f32[64,4,128]{0,2,1:T(8,128)}, f32[64,4,128]{0,2,1:T(8,128)S(1)}, u32[]{:S(2)}, u32[]{:S(2)}) collective-permute-start(f32[64,4,128]{0,2,1:T(8,128)} %copy.19), channel_id=1, source_target_pairs={{0,4},{4,8},{8,12},{12,16},{16,20},{20,24},{24,28},{1,5},{5,9},{9,... | collective-permute-start | bytes 393224 | tf_op jit(solution)/shard_map/ppermute | solution.py:17
  22.6 3.3 %copy-start.11 = (s32[2048,1]{0,1:T(1,128)S(1)}, s32[2048,1]{0,1:T(1,128)}, u32[]{:S(2)}) copy-start(s32[2048,1]{0,1:T(1,128)} %param.15) | copy-start | bytes 24580
  29.1 5.2 %copy-start.4 = (f32[64,128]{1,0:T(8,128)S(1)}, f32[64,128]{1,0:T(8,128)}, u32[]{:S(2)}) copy-start(f32[64,128]{1,0:T(8,128)} %param.13) | copy-start | bytes 98308
  29.1 14.3 %copy-start.1 = (f32[64,64,4]{2,1,0:T(8,128)S(1)}, f32[64,64,4]{2,1,0:T(8,128)}, u32[]{:S(2)}) copy-start(f32[64,64,4]{2,1,0:T(8,128)} %get-tuple-element.76) | copy-start | bytes 196612
  34.2 0.6 copy-start.9
  34.9 33.3 %collective-permute-start.8 = (f32[72,4]{1,0:T(8,128)}, f32[72,4]{1,0:T(8,128)S(1)}, u32[]{:S(2)}, u32[]{:S(2)}) collective-permute-start(f32[72,4]{1,0:T(8,128)} %get-tuple-element.91), channel_id=1, source_target_pairs={{1,0},{2,1},{3,2},{5,4},{6,5},{7,6},{9,8},{10,9},{11,10},{13,12},{... | collective-permute-start | bytes 3464 | tf_op jit(solution)/shard_map/ppermute | solution.py:18
  36.2 33.5 %collective-permute-start.9 = (f32[72,4]{1,0:T(8,128)S(1)}, f32[72,4]{1,0:T(8,128)S(1)}, u32[]{:S(2)}, u32[]{:S(2)}) collective-permute-start(f32[72,4]{1,0:T(8,128)S(1)} %get-tuple-element.92), channel_id=1, source_target_pairs={{0,1},{1,2},{2,3},{4,5},{5,6},{6,7},{8,9},{9,10},{10,11},{12,13},{... | collective-permute-start | bytes 3464 | tf_op jit(solution)/shard_map/ppermute | solution.py:17
  44.5 5.4 %copy-start.7 = (s32[2048,1]{0,1:T(1,128)S(1)}, s32[2048,1]{0,1:T(1,128)}, u32[]{:S(2)}) copy-start(s32[2048,1]{0,1:T(1,128)} %get-tuple-element.96) | copy-start | bytes 24580
  44.6 5.4 %copy-start.8 = (s32[1,4,4,128]{3,1,2,0:T(4,128)S(1)}, s32[1,4,4,128]{3,1,2,0:T(4,128)}, u32[]{:S(2)}) copy-start(s32[1,4,4,128]{3,1,2,0:T(4,128)} %copy.27) | copy-start | bytes 24580
  44.6 23.7 %copy-start.3 = (f32[64,4,128]{0,2,1:T(8,128)S(1)}, f32[64,4,128]{0,2,1:T(8,128)}, u32[]{:S(2)}) copy-start(f32[64,4,128]{0,2,1:T(8,128)} %copy.21) | copy-start | bytes 393220
  44.6 25.1 %copy-start.10 = (f32[4,128]{1,0:T(4,128)S(1)}, f32[4,128]{1,0:T(4,128)}, u32[]{:S(2)}) copy-start(f32[4,128]{1,0:T(4,128)} %copy-done.9) | copy-start | bytes 6148
  68.2 21.6 %copy-start.2 = (f32[4096,128]{1,0:T(8,128)S(1)}, f32[4096,128]{1,0:T(8,128)}, u32[]{:S(2)}) copy-start(f32[4096,128]{1,0:T(8,128)} %get-tuple-element.40) | copy-start | bytes 6291460
  68.2 11.6 %collective-permute-start.2 = (f32[64,4,128]{0,2,1:T(8,128)S(1)}, f32[64,4,128]{0,2,1:T(8,128)S(1)}, u32[]{:S(2)}, u32[]{:S(2)}) collective-permute-start(f32[64,4,128]{0,2,1:T(8,128)S(1)} %copy-done.3), channel_id=1, source_target_pairs={{4,0},{8,4},{12,8},{16,12},{20,16},{24,20},{28,24},{5,1},{9,5},{13... | collective-permute-start | bytes 393224 | tf_op jit(solution)/shard_map/ppermute | solution.py:18
  80.0 5.4 %collective-permute-start.5 = (f32[72,4,128]{2,1,0:T(4,128)S(1)}, f32[72,4,128]{2,1,0:T(4,128)S(1)}, u32[]{:S(2)}, u32[]{:S(2)}) collective-permute-start(f32[72,4,128]{2,1,0:T(4,128)S(1)} %maximum_bitcast_fusion.3), channel_id=1, source_target_pairs={{0,1},{1,2},{2,3},{4,5},{5,6},{6,7},{8,9},{9,10},{10,11},{12,13},{... | collective-permute-start | bytes 442376 | tf_op jit(solution)/shard_map/ppermute | solution.py:186
  82.4 3.3 %collective-permute-start.4 = (f32[72,4,128]{2,1,0:T(4,128)S(1)}, f32[72,4,128]{2,1,0:T(4,128)S(1)}, u32[]{:S(2)}, u32[]{:S(2)}) collective-permute-start(f32[72,4,128]{2,1,0:T(4,128)S(1)} %maximum_bitcast_fusion.2), channel_id=1, source_target_pairs={{1,0},{2,1},{3,2},{5,4},{6,5},{7,6},{9,8},{10,9},{11,10},{13,12},{... | collective-permute-start | bytes 442376 | tf_op jit(solution)/shard_map/ppermute | solution.py:187
  146.6 3.2 %copy-start.5 = (f32[1,128,256]{2,1,0:T(8,128)S(1)}, f32[1,128,256]{2,1,0:T(8,128)}, u32[]{:S(2)}) copy-start(f32[1,128,256]{2,1,0:T(8,128)} %param.16) | copy-start | bytes 393220
  149.8 1.8 copy-start.12
  151.7 2.4 %copy-start.13 = (f32[1,256,256]{2,1,0:T(8,128)S(1)}, f32[1,256,256]{2,1,0:T(8,128)}, u32[]{:S(2)}) copy-start(f32[1,256,256]{2,1,0:T(8,128)} %param.18) | copy-start | bytes 786436
  154.1 2.6 %copy-start.6 = (f32[1,256,128]{2,1,0:T(8,128)S(1)}, f32[1,256,128]{2,1,0:T(8,128)}, u32[]{:S(2)}) copy-start(f32[1,256,128]{2,1,0:T(8,128)} %param.19) | copy-start | bytes 393220
  159.8 52.5 %all-to-all-start.1 = ((f32[32,128,128]{2,1,0:T(8,128)}), f32[32,128,128]{2,1,0:T(8,128)}, u32[]{:S(2)}, u32[]{:S(2)}) async-start(f32[32,128,128]{2,1,0:T(8,128)} %fusion.29), calls=%async_computation.1 | async-start | bytes 4194304 | tf_op jit(solution)/shard_map/all_to_all | solution.py:221

commit v4 on v2

--- a/solution.py
+++ b/solution.py
@@ -19,6 +19,46 @@
     return before, after
 
 
+def stencil_inputs(state_t, diffusivity, depth):
+    width_x, width_y, features = state_t.shape
+    pad_rows = lambda c: jnp.pad(c, ((0, width_y - c.shape[0]), (0, 0)))[None]
+
+    def x_piece(start):
+        rows = lax.slice_in_dim(diffusivity, start, start + depth, axis=0)
+        return jnp.concatenate(
+            [lax.slice_in_dim(state_t, start, start + depth, axis=0), pad_rows(rows)], axis=0
+        )
+
+    tile_count = lax.axis_size("tile")
+    up = [(i, i + 1) for i in range(tile_count - 1)]
+    down = [(j, i) for i, j in up]
+    before = lax.ppermute(x_piece(width_x - depth), "tile", up)
+    after = lax.ppermute(x_piece(0), "tile", down)
+    x_before, x_after = before[:depth], after[:depth]
+    c_rows = jnp.concatenate([before[depth, :depth], diffusivity, after[depth, :depth]], axis=0)
+    extended = jnp.concatenate([x_before, state_t, x_after], axis=0)
+
+    def y_piece(start):
+        rows = lax.slice_in_dim(extended, start, start + depth, axis=1)
+        cols = lax.slice_in_dim(c_rows, start, start + depth, axis=1).T
+        cols = jnp.pad(cols, ((0, 0), (0, features - cols.shape[1])))
+        return jnp.concatenate([rows, cols[None]], axis=0)
+
+    inf_count = lax.axis_size("inf")
+    up = [(i, i + 1) for i in range(inf_count - 1)]
+    down = [(j, i) for i, j in up]
+    before = lax.ppermute(y_piece(width_y - depth), "inf", up)
+    after = lax.ppermute(y_piece(0), "inf", down)
+    rows_ext = extended.shape[0]
+    y_halo = jnp.concatenate([after[:rows_ext], before[:rows_ext]], axis=1)
+    c_ext = jnp.concatenate(
+        [c_rows, after[rows_ext, :, :rows_ext].T, before[rows_ext, :, :rows_ext].T], axis=1
+    )
+    ylen = c_ext.shape[1]
+    coeff = jnp.broadcast_to(c_ext[:, :, None], (rows_ext, ylen, features))
+    return x_before, x_after, y_halo, coeff
+
+
 def standardize(rows):
     center = jnp.mean(rows, axis=-1, keepdims=True)
     spread = jnp.mean(jnp.square(rows - center), axis=-1, keepdims=True)
@@ -26,7 +66,7 @@
 
 
 def network_rows(rows, first_layer, second_layer, third_layer, last_layer):
-    highest = lax.Precision.HIGHEST
+    highest = lax.Precision.HIGH
     hidden = jax.nn.silu(jnp.dot(rows, first_layer, precision=highest))
     hidden = jax.nn.silu(jnp.dot(hidden, second_layer, precision=highest))
     hidden = jax.nn.silu(jnp.dot(hidden, third_layer, precision=highest))
@@ -184,40 +224,19 @@
         tiled=True,
     )
     block_shape = block.shape
+    block, state_t = lax.optimization_barrier((block, state_t))
+    state_t = state_t.reshape(width_x, width_y, features)
+    x_before, x_after, y_halo, coeff = stencil_inputs(state_t, diffusivity, PASSES)
     rows = standardize(block.reshape(-1, features))
     result = network_rows(rows, first_layer[0], second_layer[0], third_layer[0], last_layer[0])
     answered = result.reshape(block_shape)
+    answered, x_before, x_after, y_halo, coeff = lax.optimization_barrier(
+        (answered, x_before, x_after, y_halo, coeff)
+    )
     returned = lax.all_to_all(answered, ("tile", "inf"), split_axis=0, concat_axis=0, tiled=True)
     returned_rows = returned.reshape(slot_total, features)
 
-    depth = PASSES
-    state_t = state_t.reshape(width_x, width_y, features)
-    u_before, u_after = halos(u_field, "tile", 1, depth)
-    v_before, v_after = halos(v_field, "tile", 1, depth)
-    x_before = jnp.concatenate([u_before, v_before], axis=0).transpose(1, 2, 0)
-    x_after = jnp.concatenate([u_after, v_after], axis=0).transpose(1, 2, 0)
-
-    def edge_columns(start):
-        pieces = []
-        for field, before, after in ((u_field, u_before, u_after), (v_field, v_before, v_after)):
-            column = lambda a: lax.slice_in_dim(a, start, start + depth, axis=2)
-            pieces.append(
-                jnp.concatenate([column(before), column(field), column(after)], axis=1)
-            )
-        return jnp.concatenate(pieces, axis=0).transpose(1, 2, 0)
-
-    inf_count = lax.axis_size("inf")
-    up = [(i, i + 1) for i in range(inf_count - 1)]
-    down = [(j, i) for i, j in up]
-    y_before = lax.ppermute(edge_columns(width_y - depth), "inf", up)
-    y_after = lax.ppermute(edge_columns(0), "inf", down)
-    y_halo = jnp.concatenate([y_after, y_before], axis=1)
-    c_before, c_after = halos(diffusivity, "tile", 0, depth)
-    c_ext = jnp.concatenate([c_before, diffusivity, c_after], axis=0)
-    c_before, c_after = halos(c_ext, "inf", 1, depth)
-    c_ext = jnp.concatenate([c_ext, c_after, c_before], axis=1)
-    rows_ext, ylen = c_ext.shape
-    coeff = jnp.broadcast_to(c_ext[:, :, None], (rows_ext, ylen, features))
+    rows_ext, ylen = coeff.shape[:2]
     diffused = pl.pallas_call(
         diffuse_kernel,
         out_shape=jax.ShapeDtypeStruct((width_x, width_y, features), jnp.float32),

time: 229 us -> 194 us (0.85)
  the two profiles are of different devices: /device:TPU:11 before, /device:TPU:0 now
where the time goes in v4:
time: 194 us; the launch traced here: 193 us
  waiting for transfers between devices  87.1 us (45%)
  Pallas kernels  53.1 us (27%)
  starting transfers between devices  24.8 us (13%)
  matrix products  12.4 us (6%)
  other arithmetic  8.37 us (4%)
  local copies, waits for them, and re-layouts  6.43 us (3%)
    all_to_all x1, waiting for transfers between devices, body(): lax.all_to_all(outgoing.reshape(devices_all, capacity, features), ('tile'...  48.6 us
    all_to_all x1, waiting for transfers between devices, body(): lax.all_to_all(answered, ('tile', 'inf'), split_axis=0, concat_axis=0, ti...  33.4 us
    pallas_call x1, Pallas kernels, body(): pl.pallas_call(finish_kernel, out_shape=(jax.ShapeDtypeStruct((levels * w...  20.1 us
    pallas_call x1, Pallas kernels, body(): pl.pallas_call(gather_kernel, out_shape=(jax.ShapeDtypeStruct((cells, fea...  17.7 us
    pallas_call x1, Pallas kernels, body(): pl.pallas_call(diffuse_kernel, out_shape=jax.ShapeDtypeStruct((width_x, w...  15.3 us
    all_to_all x1, starting transfers between devices, body(): lax.all_to_all(answered, ('tile', 'inf'), split_axis=0, concat_axis=0, ti...  8.47 us
    all_to_all x1, starting transfers between devices, body(): lax.all_to_all(outgoing.reshape(devices_all, capacity, features), ('tile'...  7.33 us
    ppermute x1, waiting for transfers between devices, stencil_inputs(): before = lax.ppermute(x_piece(width_x - depth), 'tile', up)  4.13 us
  transfers between devices with their start and end apart: 6, of which 4 were waited for; matrix products, arithmetic and copies ran while one was open for 6% of the time, Pallas kernels for 8%

profile of v4, /device:TPU:0, one launch (start us, length us, event | category | flops | bytes accessed | tf_op | source)
XLA Modules:
  0.0 193.2 jit_solution(14958387875853096343)
XLA Ops:
  0.6 0.5 broadcast.60
  1.2 1.4 fusion.41
  2.6 1.9 %while.13 = (s32[]{:T(128)}, f32[32]{0:T(128)S(1)}, f32[4,512]{1,0:T(4,128)S(1)}, bf16[4,512,32]{1,2,0:T(8,128)(2,1)S(1)}, s32[]{:T(128)}, /*index=5*/s32[]{:T(128)}) while((s32[]{:T(128)}, f32[32]{0:T(128)S(1)}, f32[4,512]{1,0:T(4,128)S(1)}, bf16[4,512,32]{1,2,0:T(8,128)(2,1)S(1)}, s32[]{:T(128)}, /*index=5*/s32[]{:T(128)}) %tuple.39), condition=%wide.region_3.4_spmd.clone, body=%wide.region_0.3_spmd.clone.sunk | while | flops 17399332 | bytes 106719 | solution.py:204
  2.7 0.3 fusion.51
  3.2 0.3 fusion.51
  3.7 0.3 fusion.51
  4.5 0.6 add.49.slot_ref
  5.2 17.7 %shard_map.104 = (f32[8192,128]{1,0:T(8,128)}, f32[4096,128]{1,0:T(8,128)}) custom-call(s32[2048]{0:T(1024)} %add.49.slot_ref, s32[2048]{0:T(1024)} %act_ref.3, f32[4096,128]{1,0:T(8,128)} %bitcast.80, f32[4096,128]{1,0:T(8,128)} %bitcast.81), custom_call_target="tpu_custom_call" | custom-call | tf_op jit(solution)/shard_map/pallas_call | solution.py:210
  22.8 7.3 %all-to-all-start = ((f32[32,128,128]{2,1,0:T(8,128)}), f32[32,128,128]{2,1,0:T(8,128)S(1)}, u32[]{:S(2)}, u32[]{:S(2)}) async-start(f32[32,128,128]{2,1,0:T(8,128)} %bitcast.82), calls=%async_computation | async-start | bytes 4194304 | tf_op jit(solution)/shard_map/all_to_all | solution.py:219
  30.3 48.6 %all-to-all-done = f32[32,128,128]{2,1,0:T(8,128)S(1)} async-done(((f32[32,128,128]{2,1,0:T(8,128)}), f32[32,128,128]{2,1,0:T(8,128)S(1)}, u32[]{:S(2)}, u32[]{:S(2)}) %all-to-all-start) | async-done | bytes 2097184 | tf_op jit(solution)/shard_map/all_to_all | solution.py:219
  78.9 0.6 reduce_sum.36
  79.5 1.3 multiply_reduce_fusion
  80.8 1.2 subtract_multiply_fusion
  82.1 1.1 fusion.39
  83.2 3.4 %collective-permute-start = (f32[5,128,128]{2,1,0:T(8,128)S(1)}, f32[5,128,128]{2,1,0:T(8,128)S(1)}, u32[]{:S(2)}, u32[]{:S(2)}) collective-permute-start(f32[5,128,128]{2,1,0:T(8,128)S(1)} %pad_maximum_fusion), channel_id=1, source_target_pairs={{0,4},{4,8},{8,12},{12,16},{16,20},{20,24},{24,28},{1,5},{5,9},{9,... | collective-permute-start | bytes 983048 | tf_op jit(solution)/shard_map/ppermute | solution.py:35
  86.6 1.3 collective-permute-start.1
  88.0 1.8 fusion.33
  89.8 2.4 %fusion.16 = f32[4096,256]{1,0:T(8,128)S(1)} fusion(f32[4096,256]{1,0:T(8,128)S(1)} %fusion.33, f32[1,256,256]{2,1,0:T(8,128)S(1)} %copy-done.6), kind=kOutput, calls=%fused_computation.19 | convolution fusion | flops 1614807040 | bytes 8650752 | tf_op jit(solution)/shard_map/dot_general | solution.py:71
  92.2 4.0 %divide_multiply_fusion = f32[4096,256]{1,0:T(8,128)} fusion(f32[4096,256]{1,0:T(8,128)S(1)} %fusion.16, f32[1,256,256]{2,1,0:T(8,128)S(1)} %copy-done.7), kind=kOutput, calls=%fused_computation.12 | convolution fusion | flops 1619001344 | bytes 8650752 | tf_op jit(solution)/shard_map/dot_general | solution.py:72
  96.1 4.1 %collective-permute-done = f32[5,128,128]{2,1,0:T(8,128)S(1)} collective-permute-done((f32[5,128,128]{2,1,0:T(8,128)S(1)}, f32[5,128,128]{2,1,0:T(8,128)S(1)}, u32[]{:S(2)}, u32[]{:S(2)}) %collective-permute-start) | collective-permute-done | bytes 327712 | tf_op jit(solution)/shard_map/ppermute | solution.py:35
  100.7 0.7 copy-done.1
  101.3 1.7 fusion.30
  103.0 1.3 collective-permute-start.2
  104.3 3.1 %fusion.31 = f32[32,128,128]{2,1,0:T(8,128)} fusion(f32[32,128,256]{2,1,0:T(8,128)S(1)} %bitcast.79, f32[1,256,128]{2,1,0:T(8,128)S(1)} %copy-done.4), kind=kOutput, calls=%fused_computation.42 | convolution fusion | flops 805306368 | bytes 6422528 | tf_op jit(solution)/shard_map/dot_general | solution.py:73
  107.5 3.0 %collective-permute-start.3 = (f32[73,4,128]{2,1,0:T(4,128)S(1)}, f32[73,4,128]{2,1,0:T(4,128)S(1)}, u32[]{:S(2)}, u32[]{:S(2)}) collective-permute-start(f32[73,4,128]{2,1,0:T(4,128)S(1)} %get-tuple-element.80), channel_id=1, source_target_pairs={{0,1},{1,2},{2,3},{4,5},{5,6},{6,7},{8,9},{9,10},{10,11},{12,13},{... | collective-permute-start | bytes 448520 | tf_op jit(solution)/shard_map/ppermute | solution.py:50
  110.5 1.0 collective-permute-done.3
  111.7 0.8 pad_maximum_fusion.2.yh_ref
  112.5 3.4 %broadcast_in_dim.40.c_ref = f32[72,136,128]{2,1,0:T(8,128)} broadcast(f32[72,136]{1,0:T(8,128)S(1)} %copy.14), dimensions={0,1} | broadcast | bytes 5052672 | tf_op jit(solution)/shard_map/broadcast_in_dim | solution.py:58
  115.9 8.5 %all-to-all-start.1 = ((f32[32,128,128]{2,1,0:T(8,128)}), f32[32,128,128]{2,1,0:T(8,128)}, u32[]{:S(2)}, u32[]{:S(2)}) async-start(f32[32,128,128]{2,1,0:T(8,128)} %fusion.31), calls=%async_computation.1 | async-start | bytes 4194304 | tf_op jit(solution)/shard_map/all_to_all | solution.py:236
  124.4 15.3 %shard_map.105 = f32[64,128,128]{2,1,0:T(8,128)} custom-call(f32[64,128,128]{2,1,0:T(8,128)} %bitcast.76, f32[4,128,128]{2,1,0:T(8,128)} %copy-done.1, f32[4,128,128]{2,1,0:T(8,128)} %copy-done.2, f32[72,8,128]{2,1,0:T(8,128)} %pad_maximum_fusion.2.yh_ref, f32[72,136,128]{2,1,0:T(8,128)} %broadcast_in_dim.40.c_ref), custom_call_target="tpu_custom_call" | custom-call | tf_op jit(solution)/shard_map/pallas_call | solution.py:240
  139.6 33.4 %all-to-all-done.1 = f32[32,128,128]{2,1,0:T(8,128)} async-done(((f32[32,128,128]{2,1,0:T(8,128)}), f32[32,128,128]{2,1,0:T(8,128)}, u32[]{:S(2)}, u32[]{:S(2)}) %all-to-all-start.1) | async-done | bytes 2097184 | tf_op jit(solution)/shard_map/all_to_all | solution.py:236
  173.1 20.1 %shard_map.106 = (f32[4096,128]{1,0:T(8,128)}, f32[4096,128]{1,0:T(8,128)}) custom-call(s32[2048]{0:T(1024)} %add.49.slot_ref, s32[2048]{0:T(1024)} %act_ref.3, f32[4096,128]{1,0:T(8,128)} %bitcast.26.r_ref, f32[8192,128]{1,0:T(8,128)} %bitcast.77), custom_call_target="tpu_custom_call" | custom-call | tf_op jit(solution)/shard_map/pallas_call | solution.py:251
  (58 shorter events, 1.8 us)
Async XLA Ops:
  5.2 25.0 %copy-start.5 = (f32[64,128]{1,0:T(8,128)S(1)}, f32[64,128]{1,0:T(8,128)}, u32[]{:S(2)}) copy-start(f32[64,128]{1,0:T(8,128)} %param.13) | copy-start | bytes 98308
  22.8 56.0 %all-to-all-start = ((f32[32,128,128]{2,1,0:T(8,128)}), f32[32,128,128]{2,1,0:T(8,128)S(1)}, u32[]{:S(2)}, u32[]{:S(2)}) async-start(f32[32,128,128]{2,1,0:T(8,128)} %bitcast.82), calls=%async_computation | async-start | bytes 4194304 | tf_op jit(solution)/shard_map/all_to_all | solution.py:219
  79.5 8.4 %copy-start.3 = (f32[1,128,256]{2,1,0:T(8,128)S(1)}, f32[1,128,256]{2,1,0:T(8,128)}, u32[]{:S(2)}) copy-start(f32[1,128,256]{2,1,0:T(8,128)} %param.16) | copy-start | bytes 393220
  82.1 7.7 %copy-start.6 = (f32[1,256,256]{2,1,0:T(8,128)S(1)}, f32[1,256,256]{2,1,0:T(8,128)}, u32[]{:S(2)}) copy-start(f32[1,256,256]{2,1,0:T(8,128)} %param.17) | copy-start | bytes 786436
  83.2 17.0 %collective-permute-start = (f32[5,128,128]{2,1,0:T(8,128)S(1)}, f32[5,128,128]{2,1,0:T(8,128)S(1)}, u32[]{:S(2)}, u32[]{:S(2)}) collective-permute-start(f32[5,128,128]{2,1,0:T(8,128)S(1)} %pad_maximum_fusion), channel_id=1, source_target_pairs={{0,4},{4,8},{8,12},{12,16},{16,20},{20,24},{24,28},{1,5},{5,9},{9,... | collective-permute-start | bytes 983048 | tf_op jit(solution)/shard_map/ppermute | solution.py:35
  86.6 13.7 %collective-permute-start.1 = (f32[5,128,128]{2,1,0:T(8,128)S(1)}, f32[5,128,128]{2,1,0:T(8,128)S(1)}, u32[]{:S(2)}, u32[]{:S(2)}) collective-permute-start(f32[5,128,128]{2,1,0:T(8,128)S(1)} %pad_maximum_fusion.1), channel_id=1, source_target_pairs={{4,0},{8,4},{12,8},{16,12},{20,16},{24,20},{28,24},{5,1},{9,5},{13... | collective-permute-start | bytes 983048 | tf_op jit(solution)/shard_map/ppermute | solution.py:36
  89.8 2.4 %copy-start.7 = (f32[1,256,256]{2,1,0:T(8,128)S(1)}, f32[1,256,256]{2,1,0:T(8,128)}, u32[]{:S(2)}) copy-start(f32[1,256,256]{2,1,0:T(8,128)} %param.18) | copy-start | bytes 786436
  96.1 8.2 %copy-start.4 = (f32[1,256,128]{2,1,0:T(8,128)S(1)}, f32[1,256,128]{2,1,0:T(8,128)}, u32[]{:S(2)}) copy-start(f32[1,256,128]{2,1,0:T(8,128)} %param.19) | copy-start | bytes 393220
  100.5 3.8 %copy-start = (f32[4096,256]{1,0:T(8,128)S(1)}, f32[4096,256]{1,0:T(8,128)}, u32[]{:S(2)}) copy-start(f32[4096,256]{1,0:T(8,128)} %divide_multiply_fusion) | copy-start | bytes 12582916
  100.6 0.7 copy-start.1
  100.7 2.3 %copy-start.2 = (f32[4,128,128]{2,1,0:T(8,128)}, f32[4,128,128]{2,1,0:T(8,128)S(1)}, u32[]{:S(2)}) copy-start(f32[4,128,128]{2,1,0:T(8,128)S(1)} %slice.73.xa_ref) | copy-start | bytes 786436
  103.0 7.5 %collective-permute-start.2 = (f32[73,4,128]{2,1,0:T(4,128)S(1)}, f32[73,4,128]{2,1,0:T(4,128)S(1)}, u32[]{:S(2)}, u32[]{:S(2)}) collective-permute-start(f32[73,4,128]{2,1,0:T(4,128)S(1)} %get-tuple-element.79), channel_id=1, source_target_pairs={{1,0},{2,1},{3,2},{5,4},{6,5},{7,6},{9,8},{10,9},{11,10},{13,12},{... | collective-permute-start | bytes 448520 | tf_op jit(solution)/shard_map/ppermute | solution.py:51
  107.5 4.0 %collective-permute-start.3 = (f32[73,4,128]{2,1,0:T(4,128)S(1)}, f32[73,4,128]{2,1,0:T(4,128)S(1)}, u32[]{:S(2)}, u32[]{:S(2)}) collective-permute-start(f32[73,4,128]{2,1,0:T(4,128)S(1)} %get-tuple-element.80), channel_id=1, source_target_pairs={{0,1},{1,2},{2,3},{4,5},{5,6},{6,7},{8,9},{9,10},{10,11},{12,13},{... | collective-permute-start | bytes 448520 | tf_op jit(solution)/shard_map/ppermute | solution.py:50
  115.9 57.2 %all-to-all-start.1 = ((f32[32,128,128]{2,1,0:T(8,128)}), f32[32,128,128]{2,1,0:T(8,128)}, u32[]{:S(2)}, u32[]{:S(2)}) async-start(f32[32,128,128]{2,1,0:T(8,128)} %fusion.31), calls=%async_computation.1 | async-start | bytes 4194304 | tf_op jit(solution)/shard_map/all_to_all | solution.py:236

commit v5 on v4

--- a/solution.py
+++ b/solution.py
@@ -19,7 +19,7 @@
     return before, after
 
 
-def stencil_inputs(state_t, diffusivity, depth):
+def stencil_start(state_t, diffusivity, depth):
     width_x, width_y, features = state_t.shape
     pad_rows = lambda c: jnp.pad(c, ((0, width_y - c.shape[0]), (0, 0)))[None]
 
@@ -34,6 +34,11 @@
     down = [(j, i) for i, j in up]
     before = lax.ppermute(x_piece(width_x - depth), "tile", up)
     after = lax.ppermute(x_piece(0), "tile", down)
+    return before, after
+
+
+def stencil_finish(state_t, diffusivity, before, after, depth):
+    width_x, width_y, features = state_t.shape
     x_before, x_after = before[:depth], after[:depth]
     c_rows = jnp.concatenate([before[depth, :depth], diffusivity, after[depth, :depth]], axis=0)
     extended = jnp.concatenate([x_before, state_t, x_after], axis=0)
@@ -216,6 +221,11 @@
         in_specs=[smem, smem, vmem, vmem],
         out_specs=(vmem, vmem),
     )(slot_index, active_columns, u_rows, v_rows)
+    state_t = state_t.reshape(width_x, width_y, features)
+    x_from_before, x_from_after = stencil_start(state_t, diffusivity, PASSES)
+    outgoing, x_from_before, x_from_after = lax.optimization_barrier(
+        (outgoing, x_from_before, x_from_after)
+    )
     block = lax.all_to_all(
         outgoing.reshape(devices_all, capacity, features),
         ("tile", "inf"),
@@ -224,18 +234,9 @@
         tiled=True,
     )
     block_shape = block.shape
-    block, state_t = lax.optimization_barrier((block, state_t))
-    state_t = state_t.reshape(width_x, width_y, features)
-    x_before, x_after, y_halo, coeff = stencil_inputs(state_t, diffusivity, PASSES)
-    rows = standardize(block.reshape(-1, features))
-    result = network_rows(rows, first_layer[0], second_layer[0], third_layer[0], last_layer[0])
-    answered = result.reshape(block_shape)
-    answered, x_before, x_after, y_halo, coeff = lax.optimization_barrier(
-        (answered, x_before, x_after, y_halo, coeff)
-    )
-    returned = lax.all_to_all(answered, ("tile", "inf"), split_axis=0, concat_axis=0, tiled=True)
-    returned_rows = returned.reshape(slot_total, features)
-
+    x_before, x_after, y_halo, coeff = stencil_finish(
+        state_t, diffusivity, x_from_before, x_from_after, PASSES
+    )
     rows_ext, ylen = coeff.shape[:2]
     diffused = pl.pallas_call(
         diffuse_kernel,
@@ -248,6 +249,13 @@
         ],
         compiler_params=pltpu.CompilerParams(vmem_limit_bytes=100 * 1024 * 1024),
     )(state_t, x_before, x_after, y_halo, coeff)
+    block, diffused = lax.optimization_barrier((block, diffused))
+    rows = standardize(block.reshape(-1, features))
+    result = network_rows(rows, first_layer[0], second_layer[0], third_layer[0], last_layer[0])
+    answered = result.reshape(block_shape)
+    returned = lax.all_to_all(answered, ("tile", "inf"), split_axis=0, concat_axis=0, tiled=True)
+    returned_rows = returned.reshape(slot_total, features)
+
     u_next, v_next = pl.pallas_call(
         finish_kernel,
         out_shape=(

time: 194 us -> 188 us (0.969)
  blocking collectives: 0 us -> 52.6 us
  waiting for transfers between devices: 87.1 us -> 35.4 us
  starting transfers between devices: 24.8 us -> 17.5 us
  other arithmetic: 8.37 us -> 11.8 us
  matrix products: 12.4 us -> 9.66 us
    all_to_all x0 -> x1, blocking collectives: none -> 52.6 us  [body(): lax.all_to_all(answered, ('tile', 'inf'), split_axis=0, concat_axis=0, ti...]
    all_to_all x1 -> x0, waiting for transfers between devices: 33.4 us -> none  [body(): lax.all_to_all(answered, ('tile', 'inf'), split_axis=0, concat_axis=0, ti...]
    all_to_all x1, waiting for transfers between devices: 48.6 us -> 21.8 us  [body(): lax.all_to_all(outgoing.reshape(devices_all, capacity, features), ('tile'...]
    ppermute x4, waiting for transfers between devices: 5.1 us -> 13.6 us  [the longest x1 12.6 us: stencil_start(): before = lax.ppermute(x_piece(width_x - depth), 'tile', up)]
    all_to_all x1 -> x0, starting transfers between devices: 8.47 us -> none  [body(): lax.all_to_all(answered, ('tile', 'inf'), split_axis=0, concat_axis=0, ti...]
  transfers between devices with their start and end apart: 6 -> 5, of which waited for: 4 -> 3; matrix products, arithmetic and copies ran while one was open for 6% -> 3% of each run, Pallas kernels for 8% -> 8%
where the time goes in v5:
time: 188 us
  Pallas kernels  53 us (28%)
  blocking collectives  52.6 us (28%)
  waiting for transfers between devices  35.4 us (19%)
  starting transfers between devices  17.5 us (9%)
  other arithmetic  11.8 us (6%)
  matrix products  9.66 us (5%)
  local copies, waits for them, and re-layouts  6.77 us (4%)
    all_to_all x1, blocking collectives, body(): lax.all_to_all(answered, ('tile', 'inf'), split_axis=0, concat_axis=0, ti...  52.6 us
    all_to_all x1, waiting for transfers between devices, body(): lax.all_to_all(outgoing.reshape(devices_all, capacity, features), ('tile'...  21.8 us
    pallas_call x1, Pallas kernels, body(): pl.pallas_call(finish_kernel, out_shape=(jax.ShapeDtypeStruct((levels * w...  20.1 us
    pallas_call x1, Pallas kernels, body(): pl.pallas_call(gather_kernel, out_shape=(jax.ShapeDtypeStruct((cells, fea...  17.7 us
    pallas_call x1, Pallas kernels, body(): pl.pallas_call(diffuse_kernel, out_shape=jax.ShapeDtypeStruct((width_x, w...  15.2 us
    ppermute x1, waiting for transfers between devices, stencil_start(): before = lax.ppermute(x_piece(width_x - depth), 'tile', up)  12.6 us
    all_to_all x1, starting transfers between devices, body(): lax.all_to_all(outgoing.reshape(devices_all, capacity, features), ('tile'...  6.94 us
    ppermute x1, starting transfers between devices, stencil_start(): before = lax.ppermute(x_piece(width_x - depth), 'tile', up)  4.89 us
  transfers between devices with their start and end apart: 5, of which 3 were waited for; matrix products, arithmetic and copies ran while one was open for 3% of the time, Pallas kernels for 8%

profile of v5, /device:TPU:0, one launch (start us, length us, event | category | flops | bytes accessed | tf_op | source)
XLA Modules:
  0.0 187.7 jit_solution(784192957514556646)
XLA Ops:
  0.6 0.7 fusion.40
  1.4 0.5 broadcast.60
  1.9 1.4 fusion.41
  3.3 1.9 %while.13 = (s32[]{:T(128)}, f32[32]{0:T(128)S(1)}, f32[4,512]{1,0:T(4,128)S(1)}, bf16[4,512,32]{1,2,0:T(8,128)(2,1)S(1)}, s32[]{:T(128)}, /*index=5*/s32[]{:T(128)}) while((s32[]{:T(128)}, f32[32]{0:T(128)S(1)}, f32[4,512]{1,0:T(4,128)S(1)}, bf16[4,512,32]{1,2,0:T(8,128)(2,1)S(1)}, s32[]{:T(128)}, /*index=5*/s32[]{:T(128)}) %tuple.39), condition=%wide.region_3.4_spmd.clone, body=%wide.region_0.3_spmd.clone.sunk | while | flops 17399332 | bytes 106719 | solution.py:209
  3.4 0.3 fusion.51
  3.9 0.3 fusion.51
  4.4 0.3 fusion.51
  5.3 0.6 add.49.slot_ref
  5.9 17.7 %shard_map.104 = (f32[8192,128]{1,0:T(8,128)}, f32[4096,128]{1,0:T(8,128)}) custom-call(s32[2048]{0:T(1024)} %add.49.slot_ref, s32[2048]{0:T(1024)} %act_ref.3, f32[4096,128]{1,0:T(8,128)} %bitcast.81, f32[4096,128]{1,0:T(8,128)} %bitcast.82), custom_call_target="tpu_custom_call" | custom-call | tf_op jit(solution)/shard_map/pallas_call | solution.py:215
  23.5 1.1 fusion.39
  24.6 4.9 %collective-permute-start = (f32[5,128,128]{2,1,0:T(8,128)S(1)}, f32[5,128,128]{2,1,0:T(8,128)S(1)}, u32[]{:S(2)}, u32[]{:S(2)}) collective-permute-start(f32[5,128,128]{2,1,0:T(8,128)S(1)} %pad_maximum_fusion), channel_id=1, source_target_pairs={{0,4},{4,8},{8,12},{12,16},{16,20},{20,24},{24,28},{1,5},{5,9},{9,... | collective-permute-start | bytes 983048 | tf_op jit(solution)/shard_map/ppermute | solution.py:35
  29.6 1.3 collective-permute-start.1
  30.9 12.6 %collective-permute-done = f32[5,128,128]{2,1,0:T(8,128)S(1)} collective-permute-done((f32[5,128,128]{2,1,0:T(8,128)S(1)}, f32[5,128,128]{2,1,0:T(8,128)S(1)}, u32[]{:S(2)}, u32[]{:S(2)}) %collective-permute-start) | collective-permute-done | bytes 327712 | tf_op jit(solution)/shard_map/ppermute | solution.py:35
  43.5 6.9 %all-to-all-start = ((f32[32,128,128]{2,1,0:T(8,128)}), f32[32,128,128]{2,1,0:T(8,128)}, u32[]{:S(2)}, u32[]{:S(2)}) async-start(f32[32,128,128]{2,1,0:T(8,128)} %bitcast.83), calls=%async_computation | async-start | bytes 4194304 | tf_op jit(solution)/shard_map/all_to_all | solution.py:229
  51.0 0.3 copy-done
  51.3 1.1 fusion.30
  52.4 1.3 collective-permute-start.2
  53.7 3.0 %collective-permute-start.3 = (f32[73,4,128]{2,1,0:T(4,128)S(1)}, f32[73,4,128]{2,1,0:T(4,128)S(1)}, u32[]{:S(2)}, u32[]{:S(2)}) collective-permute-start(f32[73,4,128]{2,1,0:T(4,128)S(1)} %get-tuple-element.76), channel_id=1, source_target_pairs={{0,1},{1,2},{2,3},{4,5},{5,6},{6,7},{8,9},{9,10},{10,11},{12,13},{... | collective-permute-start | bytes 448520 | tf_op jit(solution)/shard_map/ppermute | solution.py:55
  56.8 1.0 collective-permute-done.3
  58.0 0.8 pad_maximum_fusion.2.yh_ref
  58.7 3.4 %broadcast_in_dim.40.c_ref = f32[72,136,128]{2,1,0:T(8,128)} broadcast(f32[72,136]{1,0:T(8,128)S(1)} %copy.14), dimensions={0,1} | broadcast | bytes 5052672 | tf_op jit(solution)/shard_map/broadcast_in_dim | solution.py:63
  62.1 15.2 %shard_map.105 = f32[64,128,128]{2,1,0:T(8,128)} custom-call(f32[64,128,128]{2,1,0:T(8,128)} %bitcast.76, f32[4,128,128]{2,1,0:T(8,128)} %copy-done, f32[4,128,128]{2,1,0:T(8,128)} %copy-done.1, f32[72,8,128]{2,1,0:T(8,128)} %pad_maximum_fusion.2.yh_ref, f32[72,136,128]{2,1,0:T(8,128)} %broadcast_in_dim.40.c_ref), custom_call_target="tpu_custom_call" | custom-call | tf_op jit(solution)/shard_map/pallas_call | solution.py:241
  77.3 21.8 %all-to-all-done = f32[32,128,128]{2,1,0:T(8,128)} async-done(((f32[32,128,128]{2,1,0:T(8,128)}), f32[32,128,128]{2,1,0:T(8,128)}, u32[]{:S(2)}, u32[]{:S(2)}) %all-to-all-start) | async-done | bytes 2097184 | tf_op jit(solution)/shard_map/all_to_all | solution.py:229
  99.1 2.2 %reduce_sum.36 = f32[32,128]{1,0:T(8,128)S(1)} reduce(f32[32,128,128]{2,1,0:T(8,128)} %all-to-all-done, f32[]{:T(128)} %constant.27.clone.1), dimensions={2}, to_apply=%region_4.5 | reduce | flops 520192 | bytes 2113540 | tf_op jit(solution)/shard_map/reduce_sum | solution.py:68
  101.4 2.5 %multiply_reduce_fusion = f32[32,128]{1,0:T(8,128)S(1)} fusion(f32[32,128,128]{2,1,0:T(8,128)} %all-to-all-done, f32[32,128]{1,0:T(8,128)S(1)} %broadcast_multiply_fusion), kind=kLoop, calls=%fused_computation.27 | loop fusion | flops 1568768 | bytes 2129920 | tf_op jit(solution)/shard_map/reduce_sum | solution.py:69
  103.9 2.5 %subtract_multiply_fusion = f32[32,128,128]{2,1,0:T(8,128)S(1)} fusion(f32[32,128,128]{2,1,0:T(8,128)} %all-to-all-done, f32[32,128]{1,0:T(8,128)S(1)} %add_rsqrt_fusion, f32[32,128]{1,0:T(8,128)S(1)} %broadcast_multiply_fusion), kind=kLoop, calls=%fused_computation.28 | loop fusion | flops 1048576 | bytes 4227072 | tf_op jit(solution)/shard_map/mul | solution.py:70
  106.4 1.8 fusion.33
  108.2 2.4 %fusion.16 = f32[4096,256]{1,0:T(8,128)S(1)} fusion(f32[4096,256]{1,0:T(8,128)S(1)} %fusion.33, f32[1,256,256]{2,1,0:T(8,128)S(1)} %copy-done.5), kind=kOutput, calls=%fused_computation.19 | convolution fusion | flops 1614807040 | bytes 8650752 | tf_op jit(solution)/shard_map/dot_general | solution.py:76
  110.6 2.6 %divide_multiply_fusion = f32[4096,256]{1,0:T(8,128)S(1)} fusion(f32[4096,256]{1,0:T(8,128)S(1)} %fusion.16, f32[1,256,256]{2,1,0:T(8,128)S(1)} %copy-done.6), kind=kOutput, calls=%fused_computation.12 | convolution fusion | flops 1619001344 | bytes 8650752 | tf_op jit(solution)/shard_map/dot_general | solution.py:77
  113.2 1.8 fusion.31
  115.0 52.6 %all_to_all.10 = f32[32,128,128]{2,1,0:T(8,128)} all-to-all(f32[32,128,128]{2,1,0:T(8,128)S(1)} %fusion.31), channel_id=1, replica_groups=mesh['tile'=8,'inf'=4] {'tile','inf'}, dimensions={0} | all-to-all | bytes 4194304 | tf_op jit(solution)/shard_map/all_to_all | solution.py:256
  167.6 20.1 %shard_map.106 = (f32[4096,128]{1,0:T(8,128)}, f32[4096,128]{1,0:T(8,128)}) custom-call(s32[2048]{0:T(1024)} %add.49.slot_ref, s32[2048]{0:T(1024)} %act_ref.3, f32[4096,128]{1,0:T(8,128)} %bitcast.78, f32[8192,128]{1,0:T(8,128)} %bitcast.77), custom_call_target="tpu_custom_call" | custom-call | tf_op jit(solution)/shard_map/pallas_call | solution.py:259
  (55 shorter events, 1.8 us)
Async XLA Ops:
  23.5 26.9 %copy-start.4 = (f32[64,128]{1,0:T(8,128)S(1)}, f32[64,128]{1,0:T(8,128)}, u32[]{:S(2)}) copy-start(f32[64,128]{1,0:T(8,128)} %param.13) | copy-start | bytes 98308
  24.6 18.9 %collective-permute-start = (f32[5,128,128]{2,1,0:T(8,128)S(1)}, f32[5,128,128]{2,1,0:T(8,128)S(1)}, u32[]{:S(2)}, u32[]{:S(2)}) collective-permute-start(f32[5,128,128]{2,1,0:T(8,128)S(1)} %pad_maximum_fusion), channel_id=1, source_target_pairs={{0,4},{4,8},{8,12},{12,16},{16,20},{20,24},{24,28},{1,5},{5,9},{9,... | collective-permute-start | bytes 983048 | tf_op jit(solution)/shard_map/ppermute | solution.py:35
  29.6 13.9 %collective-permute-start.1 = (f32[5,128,128]{2,1,0:T(8,128)S(1)}, f32[5,128,128]{2,1,0:T(8,128)S(1)}, u32[]{:S(2)}, u32[]{:S(2)}) collective-permute-start(f32[5,128,128]{2,1,0:T(8,128)S(1)} %pad_maximum_fusion.1), channel_id=1, source_target_pairs={{4,0},{8,4},{12,8},{16,12},{20,16},{24,20},{28,24},{5,1},{9,5},{13... | collective-permute-start | bytes 983048 | tf_op jit(solution)/shard_map/ppermute | solution.py:36
  43.5 55.6 %all-to-all-start = ((f32[32,128,128]{2,1,0:T(8,128)}), f32[32,128,128]{2,1,0:T(8,128)}, u32[]{:S(2)}, u32[]{:S(2)}) async-start(f32[32,128,128]{2,1,0:T(8,128)} %bitcast.83), calls=%async_computation | async-start | bytes 4194304 | tf_op jit(solution)/shard_map/all_to_all | solution.py:229
  50.6 0.7 copy-start
  50.6 1.8 copy-start.1
  52.4 4.3 %collective-permute-start.2 = (f32[73,4,128]{2,1,0:T(4,128)S(1)}, f32[73,4,128]{2,1,0:T(4,128)S(1)}, u32[]{:S(2)}, u32[]{:S(2)}) collective-permute-start(f32[73,4,128]{2,1,0:T(4,128)S(1)} %get-tuple-element.75), channel_id=1, source_target_pairs={{1,0},{2,1},{3,2},{5,4},{6,5},{7,6},{9,8},{10,9},{11,10},{13,12},{... | collective-permute-start | bytes 448520 | tf_op jit(solution)/shard_map/ppermute | solution.py:56
  53.7 4.0 %collective-permute-start.3 = (f32[73,4,128]{2,1,0:T(4,128)S(1)}, f32[73,4,128]{2,1,0:T(4,128)S(1)}, u32[]{:S(2)}, u32[]{:S(2)}) collective-permute-start(f32[73,4,128]{2,1,0:T(4,128)S(1)} %get-tuple-element.76), channel_id=1, source_target_pairs={{0,1},{1,2},{2,3},{4,5},{5,6},{6,7},{8,9},{9,10},{10,11},{12,13},{... | collective-permute-start | bytes 448520 | tf_op jit(solution)/shard_map/ppermute | solution.py:55
  77.3 29.0 %copy-start.2 = (f32[1,128,256]{2,1,0:T(8,128)S(1)}, f32[1,128,256]{2,1,0:T(8,128)}, u32[]{:S(2)}) copy-start(f32[1,128,256]{2,1,0:T(8,128)} %param.16) | copy-start | bytes 393220
  106.4 1.8 copy-start.5
  108.2 2.4 %copy-start.6 = (f32[1,256,256]{2,1,0:T(8,128)S(1)}, f32[1,256,256]{2,1,0:T(8,128)}, u32[]{:S(2)}) copy-start(f32[1,256,256]{2,1,0:T(8,128)} %param.18) | copy-start | bytes 786436
  110.6 2.6 %copy-start.3 = (f32[1,256,128]{2,1,0:T(8,128)S(1)}, f32[1,256,128]{2,1,0:T(8,128)}, u32[]{:S(2)}) copy-start(f32[1,256,128]{2,1,0:T(8,128)} %param.19) | copy-start | bytes 393220

commit v6 on v5

--- a/solution.py
+++ b/solution.py
@@ -19,15 +19,12 @@
     return before, after
 
 
-def stencil_start(state_t, diffusivity, depth):
-    width_x, width_y, features = state_t.shape
-    pad_rows = lambda c: jnp.pad(c, ((0, width_y - c.shape[0]), (0, 0)))[None]
+def stencil_start(u_field, v_field, diffusivity, depth):
+    width_x = u_field.shape[1]
 
     def x_piece(start):
-        rows = lax.slice_in_dim(diffusivity, start, start + depth, axis=0)
-        return jnp.concatenate(
-            [lax.slice_in_dim(state_t, start, start + depth, axis=0), pad_rows(rows)], axis=0
-        )
+        rows = lambda a: lax.slice_in_dim(a, start, start + depth, axis=a.ndim - 2)
+        return jnp.concatenate([rows(u_field), rows(v_field), rows(diffusivity)[None]], axis=0)
 
     tile_count = lax.axis_size("tile")
     up = [(i, i + 1) for i in range(tile_count - 1)]
@@ -39,8 +36,9 @@
 
 def stencil_finish(state_t, diffusivity, before, after, depth):
     width_x, width_y, features = state_t.shape
-    x_before, x_after = before[:depth], after[:depth]
-    c_rows = jnp.concatenate([before[depth, :depth], diffusivity, after[depth, :depth]], axis=0)
+    x_before = before[:features].transpose(1, 2, 0)
+    x_after = after[:features].transpose(1, 2, 0)
+    c_rows = jnp.concatenate([before[features], diffusivity, after[features]], axis=0)
     extended = jnp.concatenate([x_before, state_t, x_after], axis=0)
 
     def y_piece(start):
@@ -210,6 +208,7 @@
     slot_index = target * capacity + ranks.reshape(-1).astype(jnp.int32)
     vmem = pl.BlockSpec(memory_space=pltpu.VMEM)
     smem = pl.BlockSpec(memory_space=pltpu.SMEM)
+    x_from_before, x_from_after = stencil_start(u_field, v_field, diffusivity, PASSES)
     u_rows = u_field.reshape(levels * width_x, width_y)
     v_rows = v_field.reshape(levels * width_x, width_y)
     state_t, outgoing = pl.pallas_call(
@@ -222,7 +221,6 @@
         out_specs=(vmem, vmem),
     )(slot_index, active_columns, u_rows, v_rows)
     state_t = state_t.reshape(width_x, width_y, features)
-    x_from_before, x_from_after = stencil_start(state_t, diffusivity, PASSES)
     outgoing, x_from_before, x_from_after = lax.optimization_barrier(
         (outgoing, x_from_before, x_from_after)
     )

time: 188 us -> 177 us (0.941)
  waiting for transfers between devices: 35.4 us -> 20.7 us
  local copies, waits for them, and re-layouts: 6.77 us -> 10.6 us
    ppermute x1, waiting for transfers between devices: 12.6 us -> 0.01 us  [stencil_start(): before = lax.ppermute(x_piece(width_x - depth), 'tile', up)]
    all_to_all x1, waiting for transfers between devices: 21.8 us -> 19.9 us  [body(): lax.all_to_all(outgoing.reshape(devices_all, capacity, features), ('tile'...]
  transfers between devices with their start and end apart: 5 -> 5, of which waited for: 3 -> 2; matrix products, arithmetic and copies ran while one was open for 3% -> 7% of each run, Pallas kernels for 8% -> 19%
where the time goes in v6:
time: 177 us
  Pallas kernels  53 us (30%)
  blocking collectives  52.6 us (30%)
  waiting for transfers between devices  20.7 us (12%)
  starting transfers between devices  17.8 us (10%)
  other arithmetic  11.5 us (6%)
  local copies, waits for them, and re-layouts  10.6 us (6%)
  matrix products  9.66 us (5%)
    all_to_all x1, blocking collectives, body(): lax.all_to_all(answered, ('tile', 'inf'), split_axis=0, concat_axis=0, ti...  52.6 us
    pallas_call x1, Pallas kernels, body(): pl.pallas_call(finish_kernel, out_shape=(jax.ShapeDtypeStruct((levels * w...  20.1 us
    all_to_all x1, waiting for transfers between devices, body(): lax.all_to_all(outgoing.reshape(devices_all, capacity, features), ('tile'...  19.9 us
    pallas_call x1, Pallas kernels, body(): pl.pallas_call(gather_kernel, out_shape=(jax.ShapeDtypeStruct((cells, fea...  17.7 us
    pallas_call x1, Pallas kernels, body(): pl.pallas_call(diffuse_kernel, out_shape=jax.ShapeDtypeStruct((width_x, w...  15.2 us
    all_to_all x1, starting transfers between devices, body(): lax.all_to_all(outgoing.reshape(devices_all, capacity, features), ('tile'...  7.14 us
    ppermute x1, starting transfers between devices, stencil_start(): before = lax.ppermute(x_piece(width_x - depth), 'tile', up)  4.9 us
  transfers between devices with their start and end apart: 5, of which 2 were waited for; matrix products, arithmetic and copies ran while one was open for 7% of the time, Pallas kernels for 19%

profile of v6, /device:TPU:0, one launch (start us, length us, event | category | flops | bytes accessed | tf_op | source)
XLA Modules:
  0.0 177.0 jit_solution(13756667472068620125)
XLA Ops:
  0.6 0.7 slice_bitcast_fusion.4
  1.5 1.1 fusion.39
  2.7 1.1 fusion.40
  4.2 4.9 %collective-permute-start = (f32[129,4,128]{0,2,1:T(8,128)S(1)}, f32[129,4,128]{0,2,1:T(8,128)S(1)}, u32[]{:S(2)}, u32[]{:S(2)}) collective-permute-start(f32[129,4,128]{0,2,1:T(8,128)S(1)} %pad_maximum_fusion), channel_id=1, source_target_pairs={{0,4},{4,8},{8,12},{12,16},{16,20},{20,24},{24,28},{1,5},{5,9},{9,... | collective-permute-start | bytes 792584 | tf_op jit(solution)/shard_map/ppermute | solution.py:32
  9.7 1.3 collective-permute-start.1
  11.1 0.5 broadcast.56
  11.6 0.7 fusion.41
  12.3 1.9 %while.13 = (s32[]{:T(128)}, f32[32]{0:T(128)S(1)}, f32[4,512]{1,0:T(4,128)S(1)}, bf16[4,512,32]{1,2,0:T(8,128)(2,1)S(1)}, s32[]{:T(128)}, /*index=5*/s32[]{:T(128)}) while((s32[]{:T(128)}, f32[32]{0:T(128)S(1)}, f32[4,512]{1,0:T(4,128)S(1)}, bf16[4,512,32]{1,2,0:T(8,128)(2,1)S(1)}, s32[]{:T(128)}, /*index=5*/s32[]{:T(128)}) %tuple.41), condition=%wide.region_3.4_spmd.clone, body=%wide.region_0.3_spmd.clone.sunk | while | flops 17399332 | bytes 106719 | solution.py:207
  12.4 0.3 fusion.51
  14.3 0.6 add.45.slot_ref
  14.9 17.7 %shard_map.104 = (f32[8192,128]{1,0:T(8,128)}, f32[4096,128]{1,0:T(8,128)}) custom-call(s32[2048]{0:T(1024)} %add.45.slot_ref, s32[2048]{0:T(1024)} %act_ref.3, f32[4096,128]{1,0:T(8,128)} %bitcast.81, f32[4096,128]{1,0:T(8,128)} %bitcast.82), custom_call_target="tpu_custom_call" | custom-call | tf_op jit(solution)/shard_map/pallas_call | solution.py:214
  32.6 7.1 %all-to-all-start = ((f32[32,128,128]{2,1,0:T(8,128)}), f32[32,128,128]{2,1,0:T(8,128)}, u32[]{:S(2)}, u32[]{:S(2)}) async-start(f32[32,128,128]{2,1,0:T(8,128)} %bitcast.83), calls=%async_computation | async-start | bytes 4194304 | tf_op jit(solution)/shard_map/all_to_all | solution.py:227
  39.8 0.9 copy.29
  40.7 0.9 copy.30
  41.8 0.7 copy-done
  42.4 1.1 fusion.30
  43.5 1.3 collective-permute-start.2
  44.8 3.2 %collective-permute-start.3 = (f32[73,4,128]{2,1,0:T(4,128)S(1)}, f32[73,4,128]{2,1,0:T(4,128)S(1)}, u32[]{:S(2)}, u32[]{:S(2)}) collective-permute-start(f32[73,4,128]{2,1,0:T(4,128)S(1)} %get-tuple-element.76), channel_id=1, source_target_pairs={{0,1},{1,2},{2,3},{4,5},{5,6},{6,7},{8,9},{9,10},{10,11},{12,13},{... | collective-permute-start | bytes 448520 | tf_op jit(solution)/shard_map/ppermute | solution.py:53
  48.1 0.8 collective-permute-done.3
  49.1 0.8 pad_maximum_fusion.2.yh_ref
  49.9 3.4 %broadcast_in_dim.40.c_ref = f32[72,136,128]{2,1,0:T(8,128)} broadcast(f32[72,136]{1,0:T(8,128)S(1)} %copy.28), dimensions={0,1} | broadcast | bytes 5052672 | tf_op jit(solution)/shard_map/broadcast_in_dim | solution.py:61
  53.3 15.2 %shard_map.105 = f32[64,128,128]{2,1,0:T(8,128)} custom-call(f32[64,128,128]{2,1,0:T(8,128)} %bitcast.76, f32[4,128,128]{2,1,0:T(8,128)} %copy-done.1, f32[4,128,128]{2,1,0:T(8,128)} %copy-done, f32[72,8,128]{2,1,0:T(8,128)} %pad_maximum_fusion.2.yh_ref, f32[72,136,128]{2,1,0:T(8,128)} %broadcast_in_dim.40.c_ref), custom_call_target="tpu_custom_call" | custom-call | tf_op jit(solution)/shard_map/pallas_call | solution.py:239
  68.5 19.9 %all-to-all-done = f32[32,128,128]{2,1,0:T(8,128)} async-done(((f32[32,128,128]{2,1,0:T(8,128)}), f32[32,128,128]{2,1,0:T(8,128)}, u32[]{:S(2)}, u32[]{:S(2)}) %all-to-all-start) | async-done | bytes 2097184 | tf_op jit(solution)/shard_map/all_to_all | solution.py:227
  88.4 2.2 %reduce_sum.36 = f32[32,128]{1,0:T(8,128)S(1)} reduce(f32[32,128,128]{2,1,0:T(8,128)} %all-to-all-done, f32[]{:T(128)} %constant.27.clone.1), dimensions={2}, to_apply=%region_4.5 | reduce | flops 520192 | bytes 2113540 | tf_op jit(solution)/shard_map/reduce_sum | solution.py:66
  90.6 2.5 %multiply_reduce_fusion = f32[32,128]{1,0:T(8,128)S(1)} fusion(f32[32,128,128]{2,1,0:T(8,128)} %all-to-all-done, f32[32,128]{1,0:T(8,128)S(1)} %broadcast_multiply_fusion), kind=kLoop, calls=%fused_computation.27 | loop fusion | flops 1568768 | bytes 2129920 | tf_op jit(solution)/shard_map/reduce_sum | solution.py:67
  93.2 2.5 %subtract_multiply_fusion = f32[32,128,128]{2,1,0:T(8,128)S(1)} fusion(f32[32,128,128]{2,1,0:T(8,128)} %all-to-all-done, f32[32,128]{1,0:T(8,128)S(1)} %add_rsqrt_fusion, f32[32,128]{1,0:T(8,128)S(1)} %broadcast_multiply_fusion), kind=kLoop, calls=%fused_computation.28 | loop fusion | flops 1048576 | bytes 4227072 | tf_op jit(solution)/shard_map/mul | solution.py:68
  95.7 1.8 %fusion.33 = f32[4096,256]{1,0:T(8,128)S(1)} fusion(f32[4096,128]{1,0:T(8,128)S(1)} %bitcast.79, f32[1,128,256]{2,1,0:T(8,128)S(1)} %copy-done.2), kind=kOutput, calls=%fused_computation.46 | convolution fusion | flops 805306368 | bytes 6422528 | tf_op jit(solution)/shard_map/dot_general | solution.py:73
  97.5 2.4 %fusion.16 = f32[4096,256]{1,0:T(8,128)S(1)} fusion(f32[4096,256]{1,0:T(8,128)S(1)} %fusion.33, f32[1,256,256]{2,1,0:T(8,128)S(1)} %copy-done.6), kind=kOutput, calls=%fused_computation.19 | convolution fusion | flops 1614807040 | bytes 8650752 | tf_op jit(solution)/shard_map/dot_general | solution.py:74
  99.9 2.6 %divide_multiply_fusion = f32[4096,256]{1,0:T(8,128)S(1)} fusion(f32[4096,256]{1,0:T(8,128)S(1)} %fusion.16, f32[1,256,256]{2,1,0:T(8,128)S(1)} %copy-done.7), kind=kOutput, calls=%fused_computation.12 | convolution fusion | flops 1619001344 | bytes 8650752 | tf_op jit(solution)/shard_map/dot_general | solution.py:75
  102.5 1.8 %fusion.31 = f32[32,128,128]{2,1,0:T(8,128)S(1)} fusion(f32[32,128,256]{2,1,0:T(8,128)S(1)} %bitcast.80, f32[1,256,128]{2,1,0:T(8,128)S(1)} %copy-done.3), kind=kOutput, calls=%fused_computation.44 | convolution fusion | flops 805306368 | bytes 6422528 | tf_op jit(solution)/shard_map/dot_general | solution.py:76
  104.3 52.6 %all_to_all.10 = f32[32,128,128]{2,1,0:T(8,128)} all-to-all(f32[32,128,128]{2,1,0:T(8,128)S(1)} %fusion.31), channel_id=1, replica_groups=mesh['tile'=8,'inf'=4] {'tile','inf'}, dimensions={0} | all-to-all | bytes 4194304 | tf_op jit(solution)/shard_map/all_to_all | solution.py:254
  156.9 20.1 %shard_map.106 = (f32[4096,128]{1,0:T(8,128)}, f32[4096,128]{1,0:T(8,128)}) custom-call(s32[2048]{0:T(1024)} %add.45.slot_ref, s32[2048]{0:T(1024)} %act_ref.3, f32[4096,128]{1,0:T(8,128)} %bitcast.78, f32[8192,128]{1,0:T(8,128)} %bitcast.77), custom_call_target="tpu_custom_call" | custom-call | tf_op jit(solution)/shard_map/pallas_call | solution.py:257
  (61 shorter events, 3.4 us)
Async XLA Ops:
  0.6 10.9 %copy-start.5 = (s32[2048,1]{0,1:T(1,128)S(1)}, s32[2048,1]{0,1:T(1,128)}, u32[]{:S(2)}) copy-start(s32[2048,1]{0,1:T(1,128)} %param.15) | copy-start | bytes 24580
  4.2 28.4 %collective-permute-start = (f32[129,4,128]{0,2,1:T(8,128)S(1)}, f32[129,4,128]{0,2,1:T(8,128)S(1)}, u32[]{:S(2)}, u32[]{:S(2)}) collective-permute-start(f32[129,4,128]{0,2,1:T(8,128)S(1)} %pad_maximum_fusion), channel_id=1, source_target_pairs={{0,4},{4,8},{8,12},{12,16},{16,20},{20,24},{24,28},{1,5},{5,9},{9,... | collective-permute-start | bytes 792584 | tf_op jit(solution)/shard_map/ppermute | solution.py:32
  9.7 22.8 %collective-permute-start.1 = (f32[129,4,128]{0,2,1:T(8,128)S(1)}, f32[129,4,128]{0,2,1:T(8,128)S(1)}, u32[]{:S(2)}, u32[]{:S(2)}) collective-permute-start(f32[129,4,128]{0,2,1:T(8,128)S(1)} %pad_maximum_fusion.1), channel_id=1, source_target_pairs={{4,0},{8,4},{12,8},{16,12},{20,16},{24,20},{28,24},{5,1},{9,5},{13... | collective-permute-start | bytes 792584 | tf_op jit(solution)/shard_map/ppermute | solution.py:33
  14.9 24.8 %copy-start.4 = (f32[64,128]{1,0:T(8,128)S(1)}, f32[64,128]{1,0:T(8,128)}, u32[]{:S(2)}) copy-start(f32[64,128]{1,0:T(8,128)} %param.13) | copy-start | bytes 98308
  32.6 55.8 %all-to-all-start = ((f32[32,128,128]{2,1,0:T(8,128)}), f32[32,128,128]{2,1,0:T(8,128)}, u32[]{:S(2)}, u32[]{:S(2)}) async-start(f32[32,128,128]{2,1,0:T(8,128)} %bitcast.83), calls=%async_computation | async-start | bytes 4194304 | tf_op jit(solution)/shard_map/all_to_all | solution.py:227
  41.7 0.7 copy-start
  41.7 1.8 %copy-start.1 = (f32[4,128,128]{2,1,0:T(8,128)}, f32[4,128,128]{2,1,0:T(8,128)S(1)}, u32[]{:S(2)}) copy-start(f32[4,128,128]{2,1,0:T(8,128)S(1)} %get-tuple-element.88.xb_ref) | copy-start | bytes 786436
  43.5 4.5 %collective-permute-start.2 = (f32[73,4,128]{2,1,0:T(4,128)S(1)}, f32[73,4,128]{2,1,0:T(4,128)S(1)}, u32[]{:S(2)}, u32[]{:S(2)}) collective-permute-start(f32[73,4,128]{2,1,0:T(4,128)S(1)} %get-tuple-element.75), channel_id=1, source_target_pairs={{1,0},{2,1},{3,2},{5,4},{6,5},{7,6},{9,8},{10,9},{11,10},{13,12},{... | collective-permute-start | bytes 448520 | tf_op jit(solution)/shard_map/ppermute | solution.py:54
  44.8 4.0 %collective-permute-start.3 = (f32[73,4,128]{2,1,0:T(4,128)S(1)}, f32[73,4,128]{2,1,0:T(4,128)S(1)}, u32[]{:S(2)}, u32[]{:S(2)}) collective-permute-start(f32[73,4,128]{2,1,0:T(4,128)S(1)} %get-tuple-element.76), channel_id=1, source_target_pairs={{0,1},{1,2},{2,3},{4,5},{5,6},{6,7},{8,9},{9,10},{10,11},{12,13},{... | collective-permute-start | bytes 448520 | tf_op jit(solution)/shard_map/ppermute | solution.py:53
  68.5 27.1 %copy-start.2 = (f32[1,128,256]{2,1,0:T(8,128)S(1)}, f32[1,128,256]{2,1,0:T(8,128)}, u32[]{:S(2)}) copy-start(f32[1,128,256]{2,1,0:T(8,128)} %param.16) | copy-start | bytes 393220
  95.6 1.8 %copy-start.6 = (f32[1,256,256]{2,1,0:T(8,128)S(1)}, f32[1,256,256]{2,1,0:T(8,128)}, u32[]{:S(2)}) copy-start(f32[1,256,256]{2,1,0:T(8,128)} %param.17) | copy-start | bytes 786436
  97.5 2.4 %copy-start.7 = (f32[1,256,256]{2,1,0:T(8,128)S(1)}, f32[1,256,256]{2,1,0:T(8,128)}, u32[]{:S(2)}) copy-start(f32[1,256,256]{2,1,0:T(8,128)} %param.18) | copy-start | bytes 786436
  99.9 2.6 %copy-start.3 = (f32[1,256,128]{2,1,0:T(8,128)S(1)}, f32[1,256,128]{2,1,0:T(8,128)}, u32[]{:S(2)}) copy-start(f32[1,256,128]{2,1,0:T(8,128)} %param.19) | copy-start | bytes 393220

commit v7 on v6

--- a/solution.py
+++ b/solution.py
@@ -205,7 +205,23 @@
         return (counts + jnp.sum(wide_piece, axis=0), rank)
 
     _, ranks = lax.scan(rank_step, jnp.zeros((devices_all,), jnp.float32), one_hot)
-    slot_index = target * capacity + ranks.reshape(-1).astype(jnp.int32)
+    tile_count, inf_count = lax.axis_size("tile"), lax.axis_size("inf")
+    half_tiles = tile_count // 2
+    my_half = lax.axis_index("tile") // half_tiles
+    target_tile = target // inf_count
+    place = (target_tile % half_tiles) * inf_count + target % inf_count
+    kind = (target_tile // half_tiles != my_half).astype(jnp.int32)
+    pair_slots = 2 * capacity
+    slot_index = place * pair_slots + kind * capacity + ranks.reshape(-1).astype(jnp.int32)
+    groups = [
+        [t * inf_count + i for t in range(h * half_tiles, (h + 1) * half_tiles) for i in range(inf_count)]
+        for h in range(2)
+    ]
+    group_size = half_tiles * inf_count
+    swap = [(t, (t + half_tiles) % tile_count) for t in range(tile_count)]
+    mirrored = [
+        lax.ppermute(w[0], "tile", swap) for w in (first_layer, second_layer, third_layer, last_layer)
+    ]
     vmem = pl.BlockSpec(memory_space=pltpu.VMEM)
     smem = pl.BlockSpec(memory_space=pltpu.SMEM)
     x_from_before, x_from_after = stencil_start(u_field, v_field, diffusivity, PASSES)
@@ -221,15 +237,16 @@
         out_specs=(vmem, vmem),
     )(slot_index, active_columns, u_rows, v_rows)
     state_t = state_t.reshape(width_x, width_y, features)
-    outgoing, x_from_before, x_from_after = lax.optimization_barrier(
-        (outgoing, x_from_before, x_from_after)
+    outgoing, x_from_before, x_from_after, mirrored = lax.optimization_barrier(
+        (outgoing, x_from_before, x_from_after, mirrored)
     )
     block = lax.all_to_all(
-        outgoing.reshape(devices_all, capacity, features),
+        outgoing.reshape(group_size, pair_slots, features),
         ("tile", "inf"),
         split_axis=0,
         concat_axis=0,
         tiled=True,
+        axis_index_groups=groups,
     )
     block_shape = block.shape
     x_before, x_after, y_halo, coeff = stencil_finish(
@@ -248,10 +265,22 @@
         compiler_params=pltpu.CompilerParams(vmem_limit_bytes=100 * 1024 * 1024),
     )(state_t, x_before, x_after, y_halo, coeff)
     block, diffused = lax.optimization_barrier((block, diffused))
-    rows = standardize(block.reshape(-1, features))
-    result = network_rows(rows, first_layer[0], second_layer[0], third_layer[0], last_layer[0])
-    answered = result.reshape(block_shape)
-    returned = lax.all_to_all(answered, ("tile", "inf"), split_axis=0, concat_axis=0, tiled=True)
+    own_rows = standardize(block[:, :capacity].reshape(-1, features))
+    own = network_rows(own_rows, first_layer[0], second_layer[0], third_layer[0], last_layer[0])
+    other_rows = standardize(block[:, capacity:].reshape(-1, features))
+    other = network_rows(other_rows, *mirrored)
+    answered = jnp.concatenate(
+        [own.reshape(group_size, capacity, features), other.reshape(group_size, capacity, features)],
+        axis=1,
+    )
+    returned = lax.all_to_all(
+        answered,
+        ("tile", "inf"),
+        split_axis=0,
+        concat_axis=0,
+        tiled=True,
+        axis_index_groups=groups,
+    )
     returned_rows = returned.reshape(slot_total, features)
 
     u_next, v_next = pl.pallas_call(

time: 177 us -> 171 us (0.966)
  waiting for transfers between devices: 20.7 us -> 15 us
  blocking collectives: 52.6 us -> 47 us
  starting transfers between devices: 17.8 us -> 20.5 us
    all_to_all x1, waiting for transfers between devices: 19.9 us -> 1.49 us  [body(): lax.all_to_all(outgoing.reshape(group_size, pair_slots, features), ('tile...]
    ppermute x0 -> x4, waiting for transfers between devices: none -> 12.5 us  [body(): lax.ppermute(w[0], 'tile', swap)]
    ppermute x0 -> x4, starting transfers between devices: none -> 7.06 us  [body(): lax.ppermute(w[0], 'tile', swap)]
    all_to_all x1, blocking collectives: 52.6 us -> 47 us  [body(): lax.all_to_all(answered, ('tile', 'inf'), split_axis=0, concat_axis=0, ti...]
    all_to_all x1, starting transfers between devices: 7.14 us -> 4.44 us  [body(): lax.all_to_all(outgoing.reshape(group_size, pair_slots, features), ('tile...]
  transfers between devices with their start and end apart: 5 -> 9, of which waited for: 2 -> 4; matrix products, arithmetic and copies ran while one was open for 7% -> 9% of each run, Pallas kernels for 19% -> 19%
where the time goes in v7:
time: 171 us
  Pallas kernels  53 us (31%)
  blocking collectives  47 us (27%)
  starting transfers between devices  20.5 us (12%)
  waiting for transfers between devices  15 us (9%)
  other arithmetic  12.1 us (7%)
  matrix products  11.3 us (7%)
  local copies, waits for them, and re-layouts  10.7 us (6%)
    all_to_all x1, blocking collectives, body(): lax.all_to_all(answered, ('tile', 'inf'), split_axis=0, concat_axis=0, ti...  47 us
    pallas_call x1, Pallas kernels, body(): pl.pallas_call(finish_kernel, out_shape=(jax.ShapeDtypeStruct((levels * w...  20.1 us
    pallas_call x1, Pallas kernels, body(): pl.pallas_call(gather_kernel, out_shape=(jax.ShapeDtypeStruct((cells, fea...  17.7 us
    pallas_call x1, Pallas kernels, body(): pl.pallas_call(diffuse_kernel, out_shape=jax.ShapeDtypeStruct((width_x, w...  15.2 us
    ppermute x4, waiting for transfers between devices, body(): lax.ppermute(w[0], 'tile', swap)  12.5 us
    ppermute x4, starting transfers between devices, body(): lax.ppermute(w[0], 'tile', swap)  7.06 us
    all_to_all x1, starting transfers between devices, body(): lax.all_to_all(outgoing.reshape(group_size, pair_slots, features), ('tile...  4.44 us
    ppermute x1, starting transfers between devices, stencil_start(): before = lax.ppermute(x_piece(width_x - depth), 'tile', up)  3.43 us
  transfers between devices with their start and end apart: 9, of which 4 were waited for; matrix products, arithmetic and copies ran while one was open for 9% of the time, Pallas kernels for 19%

profile of v7, /device:TPU:0, one launch (start us, length us, event | category | flops | bytes accessed | tf_op | source)
XLA Modules:
  0.0 170.9 jit_solution(150698561102541658)
XLA Ops:
  0.6 4.1 %collective-permute-start.5 = (f32[256,128]{1,0:T(8,128)}, f32[256,128]{1,0:T(8,128)}, u32[]{:S(2)}, u32[]{:S(2)}) collective-permute-start(f32[256,128]{1,0:T(8,128)} %bitcast.104), channel_id=1, source_target_pairs={{0,16},{4,20},{8,24},{12,28},{16,0},{20,4},{24,8},{28,12},{1,17},{... | collective-permute-start | bytes 393224 | tf_op jit(solution)/shard_map/ppermute | solution.py:223
  4.8 2.8 %collective-permute-start.3 = (f32[256,256]{1,0:T(8,128)}, f32[256,256]{1,0:T(8,128)S(1)}, u32[]{:S(2)}, u32[]{:S(2)}) collective-permute-start(f32[256,256]{1,0:T(8,128)} %bitcast.110), channel_id=1, source_target_pairs={{0,16},{4,20},{8,24},{12,28},{16,0},{20,4},{24,8},{28,12},{1,17},{... | collective-permute-start | bytes 786440 | tf_op jit(solution)/shard_map/ppermute | solution.py:223
  8.5 1.1 fusion.74
  9.8 1.1 fusion.75
  11.2 3.4 %collective-permute-start = (f32[129,4,128]{0,2,1:T(8,128)S(1)}, f32[129,4,128]{0,2,1:T(8,128)S(1)}, u32[]{:S(2)}, u32[]{:S(2)}) collective-permute-start(f32[129,4,128]{0,2,1:T(8,128)S(1)} %pad_maximum_fusion.1), channel_id=1, source_target_pairs={{0,4},{4,8},{8,12},{12,16},{16,20},{20,24},{24,28},{1,5},{5,9},{9,... | collective-permute-start | bytes 792584 | tf_op jit(solution)/shard_map/ppermute | solution.py:32
  15.3 1.3 collective-permute-start.1
  17.9 1.9 %while.13 = (s32[]{:T(128)}, f32[32]{0:T(128)S(1)}, f32[4,512]{1,0:T(4,128)S(1)}, bf16[4,512,32]{1,2,0:T(8,128)(2,1)S(1)}, s32[]{:T(128)}, /*index=5*/s32[]{:T(128)}) while((s32[]{:T(128)}, f32[32]{0:T(128)S(1)}, f32[4,512]{1,0:T(4,128)S(1)}, bf16[4,512,32]{1,2,0:T(8,128)(2,1)S(1)}, s32[]{:T(128)}, /*index=5*/s32[]{:T(128)}) %tuple.44), condition=%wide.region_3.4_spmd.clone, body=%wide.region_0.3_spmd.clone.sunk | while | flops 17399332 | bytes 106719 | solution.py:207
  19.9 3.7 %collective-permute-done.5 = f32[256,128]{1,0:T(8,128)} collective-permute-done((f32[256,128]{1,0:T(8,128)}, f32[256,128]{1,0:T(8,128)}, u32[]{:S(2)}, u32[]{:S(2)}) %collective-permute-start.5) | collective-permute-done | bytes 131104 | tf_op jit(solution)/shard_map/ppermute | solution.py:223
  24.2 17.7 %shard_map.104 = (f32[8192,128]{1,0:T(8,128)}, f32[4096,128]{1,0:T(8,128)}) custom-call(s32[2048]{0:T(1024)} %fusion.57.slot_ref, s32[2048]{0:T(1024)} %act_ref.3, f32[4096,128]{1,0:T(8,128)} %bitcast.94, f32[4096,128]{1,0:T(8,128)} %bitcast.95), custom_call_target="tpu_custom_call" | custom-call | tf_op jit(solution)/shard_map/pallas_call | solution.py:230
  41.9 8.8 %collective-permute-done.2 = f32[128,256]{1,0:T(8,128)S(1)} collective-permute-done((f32[128,256]{1,0:T(8,128)S(1)}, f32[128,256]{1,0:T(8,128)S(1)}, u32[]{:S(2)}, u32[]{:S(2)}) %collective-permute-start.2) | collective-permute-done | bytes 131104 | tf_op jit(solution)/shard_map/ppermute | solution.py:223
  51.5 4.4 %all-to-all-start = ((f32[16,256,128]{2,1,0:T(8,128)}), f32[16,256,128]{2,1,0:T(8,128)}, u32[]{:S(2)}, u32[]{:S(2)}) async-start(f32[16,256,128]{2,1,0:T(8,128)} %bitcast.96), calls=%async_computation | async-start | bytes 4194304 | tf_op jit(solution)/shard_map/all_to_all | solution.py:243
  56.1 0.9 copy.29
  58.0 1.3 fusion.50
  59.3 1.3 collective-permute-start.6
  60.6 3.0 %collective-permute-start.7 = (f32[73,4,128]{2,1,0:T(4,128)S(1)}, f32[73,4,128]{2,1,0:T(4,128)S(1)}, u32[]{:S(2)}, u32[]{:S(2)}) collective-permute-start(f32[73,4,128]{2,1,0:T(4,128)S(1)} %get-tuple-element.86), channel_id=1, source_target_pairs={{0,1},{1,2},{2,3},{4,5},{5,6},{6,7},{8,9},{9,10},{10,11},{12,13},{... | collective-permute-start | bytes 448520 | tf_op jit(solution)/shard_map/ppermute | solution.py:53
  63.7 1.0 collective-permute-done.7
  65.6 3.4 %broadcast_in_dim.42.c_ref = f32[72,136,128]{2,1,0:T(8,128)} broadcast(f32[72,136]{1,0:T(8,128)S(1)} %copy.28), dimensions={0,1} | broadcast | bytes 5052672 | tf_op jit(solution)/shard_map/broadcast_in_dim | solution.py:61
  69.0 15.2 %shard_map.105 = f32[64,128,128]{2,1,0:T(8,128)} custom-call(f32[64,128,128]{2,1,0:T(8,128)} %bitcast.90, f32[4,128,128]{2,1,0:T(8,128)} %copy-done.1, f32[4,128,128]{2,1,0:T(8,128)} %copy-done, f32[72,8,128]{2,1,0:T(8,128)} %pad_maximum_fusion.3.yh_ref, f32[72,136,128]{2,1,0:T(8,128)} %broadcast_in_dim.42.c_ref), custom_call_target="tpu_custom_call" | custom-call | tf_op jit(solution)/shard_map/pallas_call | solution.py:256
  84.2 1.5 all-to-all-done
  85.7 1.6 slice_reduce_fusion
  87.3 2.5 %multiply_reduce_fusion.1 = (f32[16,128]{1,0:T(8,128)S(1)}, f32[16,128]{1,0:T(8,128)S(1)}) fusion(f32[16,256,128]{2,1,0:T(8,128)} %all-to-all-done, f32[16,128]{1,0:T(8,128)S(1)} %broadcast_multiply_fusion.1), kind=kLoop, calls=%fused_computation.52 | loop fusion | flops 1044480 | bytes 2121728 | tf_op jit(solution)/shard_map/reduce_sum | solution.py:67
  89.8 2.7 %subtract_multiply_fusion = (f32[16,128,128]{2,1,0:T(8,128)S(1)}, f32[16,128]{1,0:T(8,128)S(1)}, f32[16,128,128]{2,1,0:T(8,128)S(1)}) fusion(f32[16,256,128]{2,1,0:T(8,128)} %all-to-all-done, f32[16,128]{1,0:T(8,128)S(1)} %add_rsqrt_fusion, f32[16,128]{1,0:T(8,128)S(1)} %broadcast_multiply_fusion.1, f32[16,128]{1,0:T(8,128)S(1)} %get-tuple-element.99), kind=kLoop, calls=%fused_computation.53 | loop fusion | flops 1308672 | bytes 4227072 | tf_op jit(solution)/shard_map/mul | solution.py:68
  92.6 1.0 fusion.65
  93.6 1.3 fusion.36
  94.8 1.3 divide_multiply_fusion
  96.2 1.0 fusion.51
  97.8 1.0 fusion.76
  98.8 1.3 fusion.22
  100.1 1.3 fusion.16
  101.4 2.2 %fusion.10 = f32[2048,128]{1,0:T(8,128)S(1)} fusion(f32[256,128]{1,0:T(8,128)} %collective-permute-done.5, f32[2048,256]{1,0:T(8,128)S(1)} %fusion.16), kind=kOutput, calls=%fused_computation.13 | convolution fusion | flops 404750336 | bytes 3276800 | tf_op jit(solution)/shard_map/dot_general | solution.py:76
  103.8 47.0 %all_to_all.10 = f32[16,256,128]{2,1,0:T(8,128)} all-to-all(f32[16,256,128]{2,1,0:T(8,128)S(1)} %pad_maximum_fusion), channel_id=1, replica_groups={{0,1,2,3,4,5,6,7,8,9,10,11,12,13,14,15},{16,17,18,19,20,21,22,23,24,25,..., dimensions={0} | all-to-all | bytes 4194304 | tf_op jit(solution)/shard_map/all_to_all | solution.py:276
  150.8 20.1 %shard_map.106 = (f32[4096,128]{1,0:T(8,128)}, f32[4096,128]{1,0:T(8,128)}) custom-call(s32[2048]{0:T(1024)} %fusion.57.slot_ref, s32[2048]{0:T(1024)} %act_ref.3, f32[4096,128]{1,0:T(8,128)} %bitcast.92, f32[8192,128]{1,0:T(8,128)} %bitcast.91), custom_call_target="tpu_custom_call" | custom-call | tf_op jit(solution)/shard_map/pallas_call | solution.py:286
  (91 shorter events, 9.5 us)
Async XLA Ops:
  0.6 22.9 %collective-permute-start.5 = (f32[256,128]{1,0:T(8,128)}, f32[256,128]{1,0:T(8,128)}, u32[]{:S(2)}, u32[]{:S(2)}) collective-permute-start(f32[256,128]{1,0:T(8,128)} %bitcast.104), channel_id=1, source_target_pairs={{0,16},{4,20},{8,24},{12,28},{16,0},{20,4},{24,8},{28,12},{1,17},{... | collective-permute-start | bytes 393224 | tf_op jit(solution)/shard_map/ppermute | solution.py:223
  4.8 45.9 %collective-permute-start.4 = (f32[256,256]{1,0:T(8,128)}, f32[256,256]{1,0:T(8,128)S(1)}, u32[]{:S(2)}, u32[]{:S(2)}) collective-permute-start(f32[256,256]{1,0:T(8,128)} %bitcast.111), channel_id=1, source_target_pairs={{0,16},{4,20},{8,24},{12,28},{16,0},{20,4},{24,8},{28,12},{1,17},{... | collective-permute-start | bytes 786440 | tf_op jit(solution)/shard_map/ppermute | solution.py:223
  4.8 45.8 %collective-permute-start.3 = (f32[256,256]{1,0:T(8,128)}, f32[256,256]{1,0:T(8,128)S(1)}, u32[]{:S(2)}, u32[]{:S(2)}) collective-permute-start(f32[256,256]{1,0:T(8,128)} %bitcast.110), channel_id=1, source_target_pairs={{0,16},{4,20},{8,24},{12,28},{16,0},{20,4},{24,8},{28,12},{1,17},{... | collective-permute-start | bytes 786440 | tf_op jit(solution)/shard_map/ppermute | solution.py:223
  10.9 6.3 %copy-start.8 = (s32[2048,1]{0,1:T(1,128)S(1)}, s32[2048,1]{0,1:T(1,128)}, u32[]{:S(2)}) copy-start(s32[2048,1]{0,1:T(1,128)} %param.15) | copy-start | bytes 24580
  11.2 39.5 %collective-permute-start = (f32[129,4,128]{0,2,1:T(8,128)S(1)}, f32[129,4,128]{0,2,1:T(8,128)S(1)}, u32[]{:S(2)}, u32[]{:S(2)}) collective-permute-start(f32[129,4,128]{0,2,1:T(8,128)S(1)} %pad_maximum_fusion.1), channel_id=1, source_target_pairs={{0,4},{4,8},{8,12},{12,16},{16,20},{20,24},{24,28},{1,5},{5,9},{9,... | collective-permute-start | bytes 792584 | tf_op jit(solution)/shard_map/ppermute | solution.py:32
  15.0 8.6 %copy-start.2 = (f32[1,128,256]{2,1,0:T(8,128)S(1)}, f32[1,128,256]{2,1,0:T(8,128)}, u32[]{:S(2)}) copy-start(f32[1,128,256]{2,1,0:T(8,128)} %param.16) | copy-start | bytes 393220
  15.3 35.4 %collective-permute-start.1 = (f32[129,4,128]{0,2,1:T(8,128)S(1)}, f32[129,4,128]{0,2,1:T(8,128)S(1)}, u32[]{:S(2)}, u32[]{:S(2)}) collective-permute-start(f32[129,4,128]{0,2,1:T(8,128)S(1)} %pad_maximum_fusion.2), channel_id=1, source_target_pairs={{4,0},{8,4},{12,8},{16,12},{20,16},{24,20},{28,24},{5,1},{9,5},{13... | collective-permute-start | bytes 792584 | tf_op jit(solution)/shard_map/ppermute | solution.py:33
  23.6 27.1 %collective-permute-start.2 = (f32[128,256]{1,0:T(8,128)S(1)}, f32[128,256]{1,0:T(8,128)S(1)}, u32[]{:S(2)}, u32[]{:S(2)}) collective-permute-start(f32[128,256]{1,0:T(8,128)S(1)} %bitcast.103), channel_id=1, source_target_pairs={{0,16},{4,20},{8,24},{12,28},{16,0},{20,4},{24,8},{28,12},{1,17},{... | collective-permute-start | bytes 393224 | tf_op jit(solution)/shard_map/ppermute | solution.py:223
  50.6 0.7 copy-start.5
  50.7 0.7 copy-start.11
  50.7 0.8 copy-start.13
  50.7 5.2 %copy-start.7 = (f32[64,128]{1,0:T(8,128)S(1)}, f32[64,128]{1,0:T(8,128)}, u32[]{:S(2)}) copy-start(f32[64,128]{1,0:T(8,128)} %param.13) | copy-start | bytes 98308
  51.5 34.2 %all-to-all-start = ((f32[16,256,128]{2,1,0:T(8,128)}), f32[16,256,128]{2,1,0:T(8,128)}, u32[]{:S(2)}, u32[]{:S(2)}) async-start(f32[16,256,128]{2,1,0:T(8,128)} %bitcast.96), calls=%async_computation | async-start | bytes 4194304 | tf_op jit(solution)/shard_map/all_to_all | solution.py:243
  58.0 1.3 copy-start
  58.0 1.3 copy-start.1
  59.3 4.3 %collective-permute-start.6 = (f32[73,4,128]{2,1,0:T(4,128)S(1)}, f32[73,4,128]{2,1,0:T(4,128)S(1)}, u32[]{:S(2)}, u32[]{:S(2)}) collective-permute-start(f32[73,4,128]{2,1,0:T(4,128)S(1)} %get-tuple-element.85), channel_id=1, source_target_pairs={{1,0},{2,1},{3,2},{5,4},{6,5},{7,6},{9,8},{10,9},{11,10},{13,12},{... | collective-permute-start | bytes 448520 | tf_op jit(solution)/shard_map/ppermute | solution.py:54
  60.6 4.0 %collective-permute-start.7 = (f32[73,4,128]{2,1,0:T(4,128)S(1)}, f32[73,4,128]{2,1,0:T(4,128)S(1)}, u32[]{:S(2)}, u32[]{:S(2)}) collective-permute-start(f32[73,4,128]{2,1,0:T(4,128)S(1)} %get-tuple-element.86), channel_id=1, source_target_pairs={{0,1},{1,2},{2,3},{4,5},{5,6},{6,7},{8,9},{9,10},{10,11},{12,13},{... | collective-permute-start | bytes 448520 | tf_op jit(solution)/shard_map/ppermute | solution.py:53
  89.8 2.8 %copy-start.3 = (f32[1,128,256]{2,1,0:T(8,128)S(1)}, f32[1,128,256]{2,1,0:T(8,128)}, u32[]{:S(2)}) copy-start(f32[1,128,256]{2,1,0:T(8,128)} %param.16) | copy-start | bytes 393220
  92.5 1.0 copy-start.9
  93.5 1.3 copy-start.10
  94.8 1.3 copy-start.4
  96.2 1.6 copy-start.6
  97.8 1.0 copy-start.14
  98.8 1.3 copy-start.12

commit v8 on v7

--- a/solution.py
+++ b/solution.py
@@ -237,8 +237,8 @@
         out_specs=(vmem, vmem),
     )(slot_index, active_columns, u_rows, v_rows)
     state_t = state_t.reshape(width_x, width_y, features)
-    outgoing, x_from_before, x_from_after, mirrored = lax.optimization_barrier(
-        (outgoing, x_from_before, x_from_after, mirrored)
+    outgoing, x_from_before, x_from_after = lax.optimization_barrier(
+        (outgoing, x_from_before, x_from_after)
     )
     block = lax.all_to_all(
         outgoing.reshape(group_size, pair_slots, features),
@@ -252,6 +252,27 @@
     x_before, x_after, y_halo, coeff = stencil_finish(
         state_t, diffusivity, x_from_before, x_from_after, PASSES
     )
+    block, mirrored, x_before, x_after, y_halo, coeff = lax.optimization_barrier(
+        (block, mirrored, x_before, x_after, y_halo, coeff)
+    )
+    own_rows = standardize(block[:, :capacity].reshape(-1, features))
+    own = network_rows(own_rows, first_layer[0], second_layer[0], third_layer[0], last_layer[0])
+    other_rows = standardize(block[:, capacity:].reshape(-1, features))
+    other = network_rows(other_rows, *mirrored)
+    answered = jnp.concatenate(
+        [own.reshape(group_size, capacity, features), other.reshape(group_size, capacity, features)],
+        axis=1,
+    )
+    returned = lax.all_to_all(
+        answered,
+        ("tile", "inf"),
+        split_axis=0,
+        concat_axis=0,
+        tiled=True,
+        axis_index_groups=groups,
+    )
+    returned_rows = returned.reshape(slot_total, features)
+
     rows_ext, ylen = coeff.shape[:2]
     diffused = pl.pallas_call(
         diffuse_kernel,
@@ -264,25 +285,6 @@
         ],
         compiler_params=pltpu.CompilerParams(vmem_limit_bytes=100 * 1024 * 1024),
     )(state_t, x_before, x_after, y_halo, coeff)
-    block, diffused = lax.optimization_barrier((block, diffused))
-    own_rows = standardize(block[:, :capacity].reshape(-1, features))
-    own = network_rows(own_rows, first_layer[0], second_layer[0], third_layer[0], last_layer[0])
-    other_rows = standardize(block[:, capacity:].reshape(-1, features))
-    other = network_rows(other_rows, *mirrored)
-    answered = jnp.concatenate(
-        [own.reshape(group_size, capacity, features), other.reshape(group_size, capacity, features)],
-        axis=1,
-    )
-    returned = lax.all_to_all(
-        answered,
-        ("tile", "inf"),
-        split_axis=0,
-        concat_axis=0,
-        tiled=True,
-        axis_index_groups=groups,
-    )
-    returned_rows = returned.reshape(slot_total, features)
-
     u_next, v_next = pl.pallas_call(
         finish_kernel,
         out_shape=(

time: 171 us -> 162 us (0.947)
  blocking collectives: 47 us -> 0 us
  waiting for transfers between devices: 15 us -> 44 us
  starting transfers between devices: 20.5 us -> 27.6 us
  other arithmetic: 12.1 us -> 9.17 us
  matrix products: 11.3 us -> 14.2 us
    all_to_all x1 -> x0, blocking collectives: 47 us -> none  [body(): lax.all_to_all(answered, ('tile', 'inf'), split_axis=0, concat_axis=0, ti...]
    all_to_all x0 -> x1, waiting for transfers between devices: none -> 14.4 us  [body(): lax.all_to_all(answered, ('tile', 'inf'), split_axis=0, concat_axis=0, ti...]
    ppermute x4, waiting for transfers between devices: 12.5 us -> 25.1 us  [body(): lax.ppermute(w[0], 'tile', swap)]
    all_to_all x0 -> x1, starting transfers between devices: none -> 5.21 us  [body(): lax.all_to_all(answered, ('tile', 'inf'), split_axis=0, concat_axis=0, ti...]
    ppermute x1, waiting for transfers between devices: 0.01 us -> 4.51 us  [stencil_finish(): after = lax.ppermute(y_piece(0), 'inf', down)]
    dot_general x2, matrix products: 2.58 us -> 4.48 us  [network_rows(): hidden = jax.nn.silu(jnp.dot(hidden, third_layer, precision=highest))]
  transfers between devices with their start and end apart: 9 -> 10, of which waited for: 4 -> 4; matrix products, arithmetic and copies ran while one was open for 9% -> 7% of each run, Pallas kernels for 19% -> 20%
where the time goes in v8:
time: 162 us; the launch traced here: 161 us
  Pallas kernels  53 us (33%)
  waiting for transfers between devices  44 us (27%)
  starting transfers between devices  27.6 us (17%)
  matrix products  14.2 us (9%)
  local copies, waits for them, and re-layouts  11.8 us (7%)
  other arithmetic  9.17 us (6%)
    ppermute x4, waiting for transfers between devices, body(): lax.ppermute(w[0], 'tile', swap)  25.1 us
    pallas_call x1, Pallas kernels, body(): pl.pallas_call(finish_kernel, out_shape=(jax.ShapeDtypeStruct((levels * w...  20.1 us
    pallas_call x1, Pallas kernels, body(): pl.pallas_call(gather_kernel, out_shape=(jax.ShapeDtypeStruct((cells, fea...  17.7 us
    pallas_call x1, Pallas kernels, body(): pl.pallas_call(diffuse_kernel, out_shape=jax.ShapeDtypeStruct((width_x, w...  15.3 us
    all_to_all x1, waiting for transfers between devices, body(): lax.all_to_all(answered, ('tile', 'inf'), split_axis=0, concat_axis=0, ti...  14.4 us
    ppermute x4, starting transfers between devices, body(): lax.ppermute(w[0], 'tile', swap)  6.45 us
    all_to_all x1, starting transfers between devices, body(): lax.all_to_all(outgoing.reshape(group_size, pair_slots, features), ('tile...  5.97 us
    all_to_all x1, starting transfers between devices, body(): lax.all_to_all(answered, ('tile', 'inf'), split_axis=0, concat_axis=0, ti...  5.21 us
  transfers between devices with their start and end apart: 10, of which 4 were waited for; matrix products, arithmetic and copies ran while one was open for 7% of the time, Pallas kernels for 20%

profile of v8, /device:TPU:0, one launch (start us, length us, event | category | flops | bytes accessed | tf_op | source)
XLA Modules:
  0.0 161.1 jit_solution(11529976302621219314)
XLA Ops:
  1.5 1.1 fusion.75
  2.7 1.1 fusion.74
  4.2 4.9 %collective-permute-start = (f32[129,4,128]{0,2,1:T(8,128)S(1)}, f32[129,4,128]{0,2,1:T(8,128)S(1)}, u32[]{:S(2)}, u32[]{:S(2)}) collective-permute-start(f32[129,4,128]{0,2,1:T(8,128)S(1)} %pad_maximum_fusion.1), channel_id=1, source_target_pairs={{0,4},{4,8},{8,12},{12,16},{16,20},{20,24},{24,28},{1,5},{5,9},{9,... | collective-permute-start | bytes 792584 | tf_op jit(solution)/shard_map/ppermute | solution.py:32
  9.7 1.3 collective-permute-start.1
  12.3 1.9 %while.13 = (s32[]{:T(128)}, f32[32]{0:T(128)S(1)}, f32[4,512]{1,0:T(4,128)S(1)}, bf16[4,512,32]{1,2,0:T(8,128)(2,1)S(1)}, s32[]{:T(128)}, /*index=5*/s32[]{:T(128)}) while((s32[]{:T(128)}, f32[32]{0:T(128)S(1)}, f32[4,512]{1,0:T(4,128)S(1)}, bf16[4,512,32]{1,2,0:T(8,128)(2,1)S(1)}, s32[]{:T(128)}, /*index=5*/s32[]{:T(128)}) %tuple.44), condition=%wide.region_3.4_spmd.clone, body=%wide.region_0.3_spmd.clone.sunk | while | flops 17399332 | bytes 106719 | solution.py:207
  14.9 17.7 %shard_map.104 = (f32[8192,128]{1,0:T(8,128)}, f32[4096,128]{1,0:T(8,128)}) custom-call(s32[2048]{0:T(1024)} %fusion.57.slot_ref, s32[2048]{0:T(1024)} %act_ref.3, f32[4096,128]{1,0:T(8,128)} %bitcast.93, f32[4096,128]{1,0:T(8,128)} %bitcast.94), custom_call_target="tpu_custom_call" | custom-call | tf_op jit(solution)/shard_map/pallas_call | solution.py:230
  32.6 6.0 %all-to-all-start = ((f32[16,256,128]{2,1,0:T(8,128)}), f32[16,256,128]{2,1,0:T(8,128)S(1)}, u32[]{:S(2)}, u32[]{:S(2)}) async-start(f32[16,256,128]{2,1,0:T(8,128)} %bitcast.95), calls=%async_computation | async-start | bytes 4194304 | tf_op jit(solution)/shard_map/all_to_all | solution.py:243
  38.7 1.0 slice.70
  41.5 1.0 slice_bitcast_fusion
  42.6 1.3 fusion.50
  43.9 2.3 %collective-permute-start.7 = (f32[73,4,128]{2,1,0:T(4,128)S(1)}, f32[73,4,128]{2,1,0:T(4,128)S(1)}, u32[]{:S(2)}, u32[]{:S(2)}) collective-permute-start(f32[73,4,128]{2,1,0:T(4,128)S(1)} %get-tuple-element.92), channel_id=1, source_target_pairs={{0,1},{1,2},{2,3},{4,5},{5,6},{6,7},{8,9},{9,10},{10,11},{12,13},{... | collective-permute-start | bytes 448520 | tf_op jit(solution)/shard_map/ppermute | solution.py:53
  46.2 3.4 %collective-permute-start.2 = (f32[128,256]{1,0:T(8,128)S(1)}, f32[128,256]{1,0:T(8,128)S(1)}, u32[]{:S(2)}, u32[]{:S(2)}) collective-permute-start(f32[128,256]{1,0:T(8,128)S(1)} %bitcast.102), channel_id=1, source_target_pairs={{0,16},{4,20},{8,24},{12,28},{16,0},{20,4},{24,8},{28,12},{1,17},{... | collective-permute-start | bytes 393224 | tf_op jit(solution)/shard_map/ppermute | solution.py:223
  49.8 2.8 %collective-permute-start.4 = (f32[256,256]{1,0:T(8,128)}, f32[256,256]{1,0:T(8,128)}, u32[]{:S(2)}, u32[]{:S(2)}) collective-permute-start(f32[256,256]{1,0:T(8,128)} %bitcast.8), channel_id=1, source_target_pairs={{0,16},{4,20},{8,24},{12,28},{16,0},{20,4},{24,8},{28,12},{1,17},{... | collective-permute-start | bytes 786440 | tf_op jit(solution)/shard_map/ppermute | solution.py:223
  52.7 1.5 collective-permute-start.6
  54.2 4.5 %collective-permute-done.6 = f32[73,4,128]{2,1,0:T(4,128)S(1)} collective-permute-done((f32[73,4,128]{2,1,0:T(4,128)S(1)}, f32[73,4,128]{2,1,0:T(4,128)S(1)}, u32[]{:S(2)}, u32[]{:S(2)}) %collective-permute-start.6) | collective-permute-done | bytes 149536 | tf_op jit(solution)/shard_map/ppermute | solution.py:54
  59.7 8.5 %collective-permute-done.2 = f32[128,256]{1,0:T(8,128)S(1)} collective-permute-done((f32[128,256]{1,0:T(8,128)S(1)}, f32[128,256]{1,0:T(8,128)S(1)}, u32[]{:S(2)}, u32[]{:S(2)}) %collective-permute-start.2) | collective-permute-done | bytes 131104 | tf_op jit(solution)/shard_map/ppermute | solution.py:223
  68.2 16.6 %collective-permute-done.5 = f32[256,128]{1,0:T(8,128)} collective-permute-done((f32[256,128]{1,0:T(8,128)S(1)}, f32[256,128]{1,0:T(8,128)}, u32[]{:S(2)}, u32[]{:S(2)}) %collective-permute-start.5) | collective-permute-done | bytes 131104 | tf_op jit(solution)/shard_map/ppermute | solution.py:223
  84.8 3.4 %broadcast_in_dim.42.c_ref = f32[72,136,128]{2,1,0:T(8,128)} broadcast(f32[72,136]{1,0:T(8,128)S(1)} %copy.28), dimensions={0,1} | broadcast | bytes 5052672 | tf_op jit(solution)/shard_map/broadcast_in_dim | solution.py:61
  89.5 1.3 subtract_multiply_fusion
  90.8 1.0 fusion.65
  91.8 1.3 fusion.36
  93.1 2.3 %divide_multiply_fusion = f32[2048,256]{1,0:T(8,128)S(1)} fusion(f32[2048,256]{1,0:T(8,128)S(1)} %fusion.36, f32[1,256,256]{2,1,0:T(8,128)} %param.18), kind=kOutput, calls=%fused_computation.31 | convolution fusion | flops 809500672 | bytes 4456448 | tf_op jit(solution)/shard_map/dot_general | solution.py:75
  95.4 1.0 fusion.51
  97.0 1.0 fusion.76
  98.0 2.2 %fusion.22 = f32[2048,256]{1,0:T(8,128)S(1)} fusion(f32[256,256]{1,0:T(8,128)} %collective-permute-done.3, f32[2048,256]{1,0:T(8,128)S(1)} %fusion.76), kind=kOutput, calls=%fused_computation.25 | convolution fusion | flops 807403520 | bytes 4456448 | tf_op jit(solution)/shard_map/dot_general | solution.py:74
  100.2 2.2 %fusion.16 = f32[2048,256]{1,0:T(8,128)S(1)} fusion(f32[256,256]{1,0:T(8,128)} %collective-permute-done.4, f32[2048,256]{1,0:T(8,128)S(1)} %fusion.22), kind=kOutput, calls=%fused_computation.19 | convolution fusion | flops 807403520 | bytes 4456448 | tf_op jit(solution)/shard_map/dot_general | solution.py:75
  102.4 2.2 %fusion.10 = f32[2048,128]{1,0:T(8,128)S(1)} fusion(f32[256,128]{1,0:T(8,128)} %collective-permute-done.5, f32[2048,256]{1,0:T(8,128)S(1)} %fusion.16), kind=kOutput, calls=%fused_computation.13 | convolution fusion | flops 404750336 | bytes 3276800 | tf_op jit(solution)/shard_map/dot_general | solution.py:76
  104.6 1.5 pad_maximum_fusion
  106.1 5.2 %all-to-all-start.1 = ((f32[16,256,128]{2,1,0:T(8,128)}), f32[16,256,128]{2,1,0:T(8,128)}, u32[]{:S(2)}, u32[]{:S(2)}) async-start(f32[16,256,128]{2,1,0:T(8,128)} %pad_maximum_fusion), calls=%async_computation.1 | async-start | bytes 4194304 | tf_op jit(solution)/shard_map/all_to_all | solution.py:266
  111.3 15.3 %shard_map.105 = f32[64,128,128]{2,1,0:T(8,128)} custom-call(f32[64,128,128]{2,1,0:T(8,128)} %bitcast.90, f32[4,128,128]{2,1,0:T(8,128)} %copy-done.1, f32[4,128,128]{2,1,0:T(8,128)} %copy-done, f32[72,8,128]{2,1,0:T(8,128)} %pad_maximum_fusion.3.yh_ref, f32[72,136,128]{2,1,0:T(8,128)} %broadcast_in_dim.42.c_ref), custom_call_target="tpu_custom_call" | custom-call | tf_op jit(solution)/shard_map/pallas_call | solution.py:277
  126.5 14.4 %all-to-all-done.1 = f32[16,256,128]{2,1,0:T(8,128)} async-done(((f32[16,256,128]{2,1,0:T(8,128)}), f32[16,256,128]{2,1,0:T(8,128)}, u32[]{:S(2)}, u32[]{:S(2)}) %all-to-all-start.1) | async-done | bytes 2097184 | tf_op jit(solution)/shard_map/all_to_all | solution.py:266
  141.0 20.1 %shard_map.106 = (f32[4096,128]{1,0:T(8,128)}, f32[4096,128]{1,0:T(8,128)}) custom-call(s32[2048]{0:T(1024)} %fusion.57.slot_ref, s32[2048]{0:T(1024)} %act_ref.3, f32[4096,128]{1,0:T(8,128)} %bitcast.30.r_ref, f32[8192,128]{1,0:T(8,128)} %bitcast.91), custom_call_target="tpu_custom_call" | custom-call | tf_op jit(solution)/shard_map/pallas_call | solution.py:288
  (76 shorter events, 10.6 us)
Async XLA Ops:
  3.8 7.8 %copy-start.5 = (s32[2048,1]{0,1:T(1,128)S(1)}, s32[2048,1]{0,1:T(1,128)}, u32[]{:S(2)}) copy-start(s32[2048,1]{0,1:T(1,128)} %param.15) | copy-start | bytes 24580
  4.2 28.4 %collective-permute-start = (f32[129,4,128]{0,2,1:T(8,128)S(1)}, f32[129,4,128]{0,2,1:T(8,128)S(1)}, u32[]{:S(2)}, u32[]{:S(2)}) collective-permute-start(f32[129,4,128]{0,2,1:T(8,128)S(1)} %pad_maximum_fusion.1), channel_id=1, source_target_pairs={{0,4},{4,8},{8,12},{12,16},{16,20},{20,24},{24,28},{1,5},{5,9},{9,... | collective-permute-start | bytes 792584 | tf_op jit(solution)/shard_map/ppermute | solution.py:32
  9.7 22.8 %collective-permute-start.1 = (f32[129,4,128]{0,2,1:T(8,128)S(1)}, f32[129,4,128]{0,2,1:T(8,128)}, u32[]{:S(2)}, u32[]{:S(2)}) collective-permute-start(f32[129,4,128]{0,2,1:T(8,128)S(1)} %pad_maximum_fusion.2), channel_id=1, source_target_pairs={{4,0},{8,4},{12,8},{16,12},{20,16},{24,20},{28,24},{5,1},{9,5},{13... | collective-permute-start | bytes 792584 | tf_op jit(solution)/shard_map/ppermute | solution.py:33
  32.6 6.0 %copy-start.4 = (f32[64,128]{1,0:T(8,128)S(1)}, f32[64,128]{1,0:T(8,128)}, u32[]{:S(2)}) copy-start(f32[64,128]{1,0:T(8,128)} %param.13) | copy-start | bytes 98308
  32.6 52.2 %all-to-all-start = ((f32[16,256,128]{2,1,0:T(8,128)}), f32[16,256,128]{2,1,0:T(8,128)S(1)}, u32[]{:S(2)}, u32[]{:S(2)}) async-start(f32[16,256,128]{2,1,0:T(8,128)} %bitcast.95), calls=%async_computation | async-start | bytes 4194304 | tf_op jit(solution)/shard_map/all_to_all | solution.py:243
  42.5 1.4 copy-start
  42.5 1.4 copy-start.1
  42.5 3.7 %copy-start.2 = (f32[1,128,256]{2,1,0:T(8,128)S(1)}, f32[1,128,256]{2,1,0:T(8,128)}, u32[]{:S(2)}) copy-start(f32[1,128,256]{2,1,0:T(8,128)} %param.16) | copy-start | bytes 393220
  42.5 7.1 %copy-start.6 = (f32[1,256,256]{2,1,0:T(8,128)S(1)}, f32[1,256,256]{2,1,0:T(8,128)}, u32[]{:S(2)}) copy-start(f32[1,256,256]{2,1,0:T(8,128)} %param.17) | copy-start | bytes 786436
  42.5 10.1 %copy-start.3 = (f32[1,256,128]{2,1,0:T(8,128)S(1)}, f32[1,256,128]{2,1,0:T(8,128)}, u32[]{:S(2)}) copy-start(f32[1,256,128]{2,1,0:T(8,128)} %param.19) | copy-start | bytes 393220
  43.9 8.8 %collective-permute-start.7 = (f32[73,4,128]{2,1,0:T(4,128)S(1)}, f32[73,4,128]{2,1,0:T(4,128)S(1)}, u32[]{:S(2)}, u32[]{:S(2)}) collective-permute-start(f32[73,4,128]{2,1,0:T(4,128)S(1)} %get-tuple-element.92), channel_id=1, source_target_pairs={{0,1},{1,2},{2,3},{4,5},{5,6},{6,7},{8,9},{9,10},{10,11},{12,13},{... | collective-permute-start | bytes 448520 | tf_op jit(solution)/shard_map/ppermute | solution.py:53
  46.2 21.9 %collective-permute-start.2 = (f32[128,256]{1,0:T(8,128)S(1)}, f32[128,256]{1,0:T(8,128)S(1)}, u32[]{:S(2)}, u32[]{:S(2)}) collective-permute-start(f32[128,256]{1,0:T(8,128)S(1)} %bitcast.102), channel_id=1, source_target_pairs={{0,16},{4,20},{8,24},{12,28},{16,0},{20,4},{24,8},{28,12},{1,17},{... | collective-permute-start | bytes 393224 | tf_op jit(solution)/shard_map/ppermute | solution.py:223
  49.7 35.1 %collective-permute-start.3 = (f32[256,256]{1,0:T(8,128)S(1)}, f32[256,256]{1,0:T(8,128)}, u32[]{:S(2)}, u32[]{:S(2)}) collective-permute-start(f32[256,256]{1,0:T(8,128)S(1)} %bitcast.109), channel_id=1, source_target_pairs={{0,16},{4,20},{8,24},{12,28},{16,0},{20,4},{24,8},{28,12},{1,17},{... | collective-permute-start | bytes 786440 | tf_op jit(solution)/shard_map/ppermute | solution.py:223
  49.8 35.0 %collective-permute-start.4 = (f32[256,256]{1,0:T(8,128)}, f32[256,256]{1,0:T(8,128)}, u32[]{:S(2)}, u32[]{:S(2)}) collective-permute-start(f32[256,256]{1,0:T(8,128)} %bitcast.8), channel_id=1, source_target_pairs={{0,16},{4,20},{8,24},{12,28},{16,0},{20,4},{24,8},{28,12},{1,17},{... | collective-permute-start | bytes 786440 | tf_op jit(solution)/shard_map/ppermute | solution.py:223
  52.6 32.2 %collective-permute-start.5 = (f32[256,128]{1,0:T(8,128)S(1)}, f32[256,128]{1,0:T(8,128)}, u32[]{:S(2)}, u32[]{:S(2)}) collective-permute-start(f32[256,128]{1,0:T(8,128)S(1)} %bitcast.103), channel_id=1, source_target_pairs={{0,16},{4,20},{8,24},{12,28},{16,0},{20,4},{24,8},{28,12},{1,17},{... | collective-permute-start | bytes 393224 | tf_op jit(solution)/shard_map/ppermute | solution.py:223
  52.7 6.0 %collective-permute-start.6 = (f32[73,4,128]{2,1,0:T(4,128)S(1)}, f32[73,4,128]{2,1,0:T(4,128)S(1)}, u32[]{:S(2)}, u32[]{:S(2)}) collective-permute-start(f32[73,4,128]{2,1,0:T(4,128)S(1)} %get-tuple-element.91), channel_id=1, source_target_pairs={{1,0},{2,1},{3,2},{5,4},{6,5},{7,6},{9,8},{10,9},{11,10},{13,12},{... | collective-permute-start | bytes 448520 | tf_op jit(solution)/shard_map/ppermute | solution.py:54
  106.1 34.9 %all-to-all-start.1 = ((f32[16,256,128]{2,1,0:T(8,128)}), f32[16,256,128]{2,1,0:T(8,128)}, u32[]{:S(2)}, u32[]{:S(2)}) async-start(f32[16,256,128]{2,1,0:T(8,128)} %pad_maximum_fusion), calls=%async_computation.1 | async-start | bytes 4194304 | tf_op jit(solution)/shard_map/all_to_all | solution.py:266

commit v9 on v8

--- a/solution.py
+++ b/solution.py
@@ -5,18 +5,8 @@
 from jax.experimental.pallas import tpu as pltpu
 from jax.sharding import PartitionSpec as P
 
+
 PASSES = 4
-
-
-def halos(x, axis, dim, width):
-    count, length = (lax.axis_size(axis), x.shape[dim])
-    up = [(i, i + 1) for i in range(count - 1)]
-    down = [(j, i) for i, j in up]
-    last = lax.slice_in_dim(x, length - width, length, axis=dim)
-    first = lax.slice_in_dim(x, 0, width, axis=dim)
-    before = lax.ppermute(last, axis, up)
-    after = lax.ppermute(first, axis, down)
-    return before, after
 
 
 def stencil_start(u_field, v_field, diffusivity, depth):
@@ -35,7 +25,7 @@
 
 
 def stencil_finish(state_t, diffusivity, before, after, depth):
-    width_x, width_y, features = state_t.shape
+    _, width_y, features = state_t.shape
     x_before = before[:features].transpose(1, 2, 0)
     x_after = after[:features].transpose(1, 2, 0)
     c_rows = jnp.concatenate([before[features], diffusivity, after[features]], axis=0)
@@ -78,7 +68,7 @@
 
 def gather_kernel(slot_ref, act_ref, u_ref, v_ref, st_ref, o_ref):
     levels_x, width_y = u_ref.shape
-    cells, features = st_ref.shape
+    _, features = st_ref.shape
     levels = features // 2
     width_x = levels_x // levels
     chunk = 128
@@ -141,7 +131,7 @@
 
 def finish_kernel(slot_ref, act_ref, r_ref, f_ref, uo_ref, vo_ref, d_ref):
     levels_x, width_y = uo_ref.shape
-    cells, features = f_ref.shape
+    _, features = f_ref.shape
     levels = features // 2
     width_x = levels_x // levels
 
@@ -168,7 +158,7 @@
     lax.fori_loop(0, width_x, transpose_tile, 0)
 
 
-def body(
+def step(
     u_field,
     v_field,
     diffusivity,
@@ -220,7 +210,8 @@
     group_size = half_tiles * inf_count
     swap = [(t, (t + half_tiles) % tile_count) for t in range(tile_count)]
     mirrored = [
-        lax.ppermute(w[0], "tile", swap) for w in (first_layer, second_layer, third_layer, last_layer)
+        lax.ppermute(w[0], "tile", swap)
+        for w in (first_layer, second_layer, third_layer, last_layer)
     ]
     vmem = pl.BlockSpec(memory_space=pltpu.VMEM)
     smem = pl.BlockSpec(memory_space=pltpu.SMEM)
@@ -248,7 +239,6 @@
         tiled=True,
         axis_index_groups=groups,
     )
-    block_shape = block.shape
     x_before, x_after, y_halo, coeff = stencil_finish(
         state_t, diffusivity, x_from_before, x_from_after, PASSES
     )
@@ -311,4 +301,4 @@
         P(("tile", "inf"), None, None),
     )
     out_specs = (P(None, "tile", "inf"), P(None, "tile", "inf"))
-    return jax.shard_map(body, mesh=mesh, in_specs=in_specs, out_specs=out_specs, check_vma=False)
+    return jax.shard_map(step, mesh=mesh, in_specs=in_specs, out_specs=out_specs, check_vma=False)

time: 162 us -> 162 us (level)
  no operation moved by 1% of the time
where the time goes in v9:
time: 162 us; the launch traced here: 161 us
  Pallas kernels  53 us (33%)
  waiting for transfers between devices  44 us (27%)
  starting transfers between devices  27.6 us (17%)
  matrix products  14.2 us (9%)
  local copies, waits for them, and re-layouts  11.8 us (7%)
  other arithmetic  9.17 us (6%)
    ppermute x4, waiting for transfers between devices, step(): lax.ppermute(w[0], 'tile', swap)  25.1 us
    pallas_call x1, Pallas kernels, step(): pl.pallas_call(finish_kernel, out_shape=(jax.ShapeDtypeStruct((levels * w...  20.1 us
    pallas_call x1, Pallas kernels, step(): pl.pallas_call(gather_kernel, out_shape=(jax.ShapeDtypeStruct((cells, fea...  17.7 us
    pallas_call x1, Pallas kernels, step(): pl.pallas_call(diffuse_kernel, out_shape=jax.ShapeDtypeStruct((width_x, w...  15.3 us
    all_to_all x1, waiting for transfers between devices, step(): lax.all_to_all(answered, ('tile', 'inf'), split_axis=0, concat_axis=0, ti...  14.4 us
    ppermute x4, starting transfers between devices, step(): lax.ppermute(w[0], 'tile', swap)  6.45 us
    all_to_all x1, starting transfers between devices, step(): lax.all_to_all(outgoing.reshape(group_size, pair_slots, features), ('tile...  5.97 us
    all_to_all x1, starting transfers between devices, step(): lax.all_to_all(answered, ('tile', 'inf'), split_axis=0, concat_axis=0, ti...  5.21 us
  transfers between devices with their start and end apart: 10, of which 4 were waited for; matrix products, arithmetic and copies ran while one was open for 7% of the time, Pallas kernels for 20%

profile of v9, /device:TPU:0, one launch (start us, length us, event | category | flops | bytes accessed | tf_op | source)
XLA Modules:
  0.0 161.1 jit_solution(11529976302621219314)
XLA Ops:
  1.5 1.1 fusion.75
  2.7 1.1 fusion.74
  4.2 4.9 %collective-permute-start = (f32[129,4,128]{0,2,1:T(8,128)S(1)}, f32[129,4,128]{0,2,1:T(8,128)S(1)}, u32[]{:S(2)}, u32[]{:S(2)}) collective-permute-start(f32[129,4,128]{0,2,1:T(8,128)S(1)} %pad_maximum_fusion.1), channel_id=1, source_target_pairs={{0,4},{4,8},{8,12},{12,16},{16,20},{20,24},{24,28},{1,5},{5,9},{9,... | collective-permute-start | bytes 792584 | tf_op jit(solution)/shard_map/ppermute | solution.py:22
  9.7 1.3 collective-permute-start.1
  12.3 1.9 %while.13 = (s32[]{:T(128)}, f32[32]{0:T(128)S(1)}, f32[4,512]{1,0:T(4,128)S(1)}, bf16[4,512,32]{1,2,0:T(8,128)(2,1)S(1)}, s32[]{:T(128)}, /*index=5*/s32[]{:T(128)}) while((s32[]{:T(128)}, f32[32]{0:T(128)S(1)}, f32[4,512]{1,0:T(4,128)S(1)}, bf16[4,512,32]{1,2,0:T(8,128)(2,1)S(1)}, s32[]{:T(128)}, /*index=5*/s32[]{:T(128)}) %tuple.44), condition=%wide.region_3.4_spmd.clone, body=%wide.region_0.3_spmd.clone.sunk | while | flops 17399332 | bytes 106719 | solution.py:197
  14.9 17.7 %shard_map.104 = (f32[8192,128]{1,0:T(8,128)}, f32[4096,128]{1,0:T(8,128)}) custom-call(s32[2048]{0:T(1024)} %fusion.57.slot_ref, s32[2048]{0:T(1024)} %act_ref.3, f32[4096,128]{1,0:T(8,128)} %bitcast.93, f32[4096,128]{1,0:T(8,128)} %bitcast.94), custom_call_target="tpu_custom_call" | custom-call | tf_op jit(solution)/shard_map/pallas_call | solution.py:221
  32.6 6.0 %all-to-all-start = ((f32[16,256,128]{2,1,0:T(8,128)}), f32[16,256,128]{2,1,0:T(8,128)S(1)}, u32[]{:S(2)}, u32[]{:S(2)}) async-start(f32[16,256,128]{2,1,0:T(8,128)} %bitcast.95), calls=%async_computation | async-start | bytes 4194304 | tf_op jit(solution)/shard_map/all_to_all | solution.py:234
  38.7 1.0 slice.70
  41.5 1.0 slice_bitcast_fusion
  42.6 1.3 fusion.50
  43.9 2.3 %collective-permute-start.7 = (f32[73,4,128]{2,1,0:T(4,128)S(1)}, f32[73,4,128]{2,1,0:T(4,128)S(1)}, u32[]{:S(2)}, u32[]{:S(2)}) collective-permute-start(f32[73,4,128]{2,1,0:T(4,128)S(1)} %get-tuple-element.92), channel_id=1, source_target_pairs={{0,1},{1,2},{2,3},{4,5},{5,6},{6,7},{8,9},{9,10},{10,11},{12,13},{... | collective-permute-start | bytes 448520 | tf_op jit(solution)/shard_map/ppermute | solution.py:43
  46.2 3.4 %collective-permute-start.2 = (f32[128,256]{1,0:T(8,128)S(1)}, f32[128,256]{1,0:T(8,128)S(1)}, u32[]{:S(2)}, u32[]{:S(2)}) collective-permute-start(f32[128,256]{1,0:T(8,128)S(1)} %bitcast.102), channel_id=1, source_target_pairs={{0,16},{4,20},{8,24},{12,28},{16,0},{20,4},{24,8},{28,12},{1,17},{... | collective-permute-start | bytes 393224 | tf_op jit(solution)/shard_map/ppermute | solution.py:213
  49.8 2.8 %collective-permute-start.4 = (f32[256,256]{1,0:T(8,128)}, f32[256,256]{1,0:T(8,128)}, u32[]{:S(2)}, u32[]{:S(2)}) collective-permute-start(f32[256,256]{1,0:T(8,128)} %bitcast.8), channel_id=1, source_target_pairs={{0,16},{4,20},{8,24},{12,28},{16,0},{20,4},{24,8},{28,12},{1,17},{... | collective-permute-start | bytes 786440 | tf_op jit(solution)/shard_map/ppermute | solution.py:213
  52.7 1.5 collective-permute-start.6
  54.2 4.5 %collective-permute-done.6 = f32[73,4,128]{2,1,0:T(4,128)S(1)} collective-permute-done((f32[73,4,128]{2,1,0:T(4,128)S(1)}, f32[73,4,128]{2,1,0:T(4,128)S(1)}, u32[]{:S(2)}, u32[]{:S(2)}) %collective-permute-start.6) | collective-permute-done | bytes 149536 | tf_op jit(solution)/shard_map/ppermute | solution.py:44
  59.7 8.5 %collective-permute-done.2 = f32[128,256]{1,0:T(8,128)S(1)} collective-permute-done((f32[128,256]{1,0:T(8,128)S(1)}, f32[128,256]{1,0:T(8,128)S(1)}, u32[]{:S(2)}, u32[]{:S(2)}) %collective-permute-start.2) | collective-permute-done | bytes 131104 | tf_op jit(solution)/shard_map/ppermute | solution.py:213
  68.2 16.6 %collective-permute-done.5 = f32[256,128]{1,0:T(8,128)} collective-permute-done((f32[256,128]{1,0:T(8,128)S(1)}, f32[256,128]{1,0:T(8,128)}, u32[]{:S(2)}, u32[]{:S(2)}) %collective-permute-start.5) | collective-permute-done | bytes 131104 | tf_op jit(solution)/shard_map/ppermute | solution.py:213
  84.8 3.4 %broadcast_in_dim.42.c_ref = f32[72,136,128]{2,1,0:T(8,128)} broadcast(f32[72,136]{1,0:T(8,128)S(1)} %copy.28), dimensions={0,1} | broadcast | bytes 5052672 | tf_op jit(solution)/shard_map/broadcast_in_dim | solution.py:51
  89.5 1.3 subtract_multiply_fusion
  90.8 1.0 fusion.65
  91.8 1.3 fusion.36
  93.1 2.3 %divide_multiply_fusion = f32[2048,256]{1,0:T(8,128)S(1)} fusion(f32[2048,256]{1,0:T(8,128)S(1)} %fusion.36, f32[1,256,256]{2,1,0:T(8,128)} %param.18), kind=kOutput, calls=%fused_computation.31 | convolution fusion | flops 809500672 | bytes 4456448 | tf_op jit(solution)/shard_map/dot_general | solution.py:65
  95.4 1.0 fusion.51
  97.0 1.0 fusion.76
  98.0 2.2 %fusion.22 = f32[2048,256]{1,0:T(8,128)S(1)} fusion(f32[256,256]{1,0:T(8,128)} %collective-permute-done.3, f32[2048,256]{1,0:T(8,128)S(1)} %fusion.76), kind=kOutput, calls=%fused_computation.25 | convolution fusion | flops 807403520 | bytes 4456448 | tf_op jit(solution)/shard_map/dot_general | solution.py:64
  100.2 2.2 %fusion.16 = f32[2048,256]{1,0:T(8,128)S(1)} fusion(f32[256,256]{1,0:T(8,128)} %collective-permute-done.4, f32[2048,256]{1,0:T(8,128)S(1)} %fusion.22), kind=kOutput, calls=%fused_computation.19 | convolution fusion | flops 807403520 | bytes 4456448 | tf_op jit(solution)/shard_map/dot_general | solution.py:65
  102.4 2.2 %fusion.10 = f32[2048,128]{1,0:T(8,128)S(1)} fusion(f32[256,128]{1,0:T(8,128)} %collective-permute-done.5, f32[2048,256]{1,0:T(8,128)S(1)} %fusion.16), kind=kOutput, calls=%fused_computation.13 | convolution fusion | flops 404750336 | bytes 3276800 | tf_op jit(solution)/shard_map/dot_general | solution.py:66
  104.6 1.5 pad_maximum_fusion
  106.1 5.2 %all-to-all-start.1 = ((f32[16,256,128]{2,1,0:T(8,128)}), f32[16,256,128]{2,1,0:T(8,128)}, u32[]{:S(2)}, u32[]{:S(2)}) async-start(f32[16,256,128]{2,1,0:T(8,128)} %pad_maximum_fusion), calls=%async_computation.1 | async-start | bytes 4194304 | tf_op jit(solution)/shard_map/all_to_all | solution.py:256
  111.3 15.3 %shard_map.105 = f32[64,128,128]{2,1,0:T(8,128)} custom-call(f32[64,128,128]{2,1,0:T(8,128)} %bitcast.90, f32[4,128,128]{2,1,0:T(8,128)} %copy-done.1, f32[4,128,128]{2,1,0:T(8,128)} %copy-done, f32[72,8,128]{2,1,0:T(8,128)} %pad_maximum_fusion.3.yh_ref, f32[72,136,128]{2,1,0:T(8,128)} %broadcast_in_dim.42.c_ref), custom_call_target="tpu_custom_call" | custom-call | tf_op jit(solution)/shard_map/pallas_call | solution.py:267
  126.5 14.4 %all-to-all-done.1 = f32[16,256,128]{2,1,0:T(8,128)} async-done(((f32[16,256,128]{2,1,0:T(8,128)}), f32[16,256,128]{2,1,0:T(8,128)}, u32[]{:S(2)}, u32[]{:S(2)}) %all-to-all-start.1) | async-done | bytes 2097184 | tf_op jit(solution)/shard_map/all_to_all | solution.py:256
  141.0 20.1 %shard_map.106 = (f32[4096,128]{1,0:T(8,128)}, f32[4096,128]{1,0:T(8,128)}) custom-call(s32[2048]{0:T(1024)} %fusion.57.slot_ref, s32[2048]{0:T(1024)} %act_ref.3, f32[4096,128]{1,0:T(8,128)} %bitcast.30.r_ref, f32[8192,128]{1,0:T(8,128)} %bitcast.91), custom_call_target="tpu_custom_call" | custom-call | tf_op jit(solution)/shard_map/pallas_call | solution.py:278
  (76 shorter events, 10.6 us)
Async XLA Ops:
  3.8 7.8 %copy-start.5 = (s32[2048,1]{0,1:T(1,128)S(1)}, s32[2048,1]{0,1:T(1,128)}, u32[]{:S(2)}) copy-start(s32[2048,1]{0,1:T(1,128)} %param.15) | copy-start | bytes 24580
  4.2 28.4 %collective-permute-start = (f32[129,4,128]{0,2,1:T(8,128)S(1)}, f32[129,4,128]{0,2,1:T(8,128)S(1)}, u32[]{:S(2)}, u32[]{:S(2)}) collective-permute-start(f32[129,4,128]{0,2,1:T(8,128)S(1)} %pad_maximum_fusion.1), channel_id=1, source_target_pairs={{0,4},{4,8},{8,12},{12,16},{16,20},{20,24},{24,28},{1,5},{5,9},{9,... | collective-permute-start | bytes 792584 | tf_op jit(solution)/shard_map/ppermute | solution.py:22
  9.7 22.8 %collective-permute-start.1 = (f32[129,4,128]{0,2,1:T(8,128)S(1)}, f32[129,4,128]{0,2,1:T(8,128)}, u32[]{:S(2)}, u32[]{:S(2)}) collective-permute-start(f32[129,4,128]{0,2,1:T(8,128)S(1)} %pad_maximum_fusion.2), channel_id=1, source_target_pairs={{4,0},{8,4},{12,8},{16,12},{20,16},{24,20},{28,24},{5,1},{9,5},{13... | collective-permute-start | bytes 792584 | tf_op jit(solution)/shard_map/ppermute | solution.py:23
  32.6 6.0 %copy-start.4 = (f32[64,128]{1,0:T(8,128)S(1)}, f32[64,128]{1,0:T(8,128)}, u32[]{:S(2)}) copy-start(f32[64,128]{1,0:T(8,128)} %param.13) | copy-start | bytes 98308
  32.6 52.2 %all-to-all-start = ((f32[16,256,128]{2,1,0:T(8,128)}), f32[16,256,128]{2,1,0:T(8,128)S(1)}, u32[]{:S(2)}, u32[]{:S(2)}) async-start(f32[16,256,128]{2,1,0:T(8,128)} %bitcast.95), calls=%async_computation | async-start | bytes 4194304 | tf_op jit(solution)/shard_map/all_to_all | solution.py:234
  42.5 1.4 copy-start
  42.5 1.4 copy-start.1
  42.5 3.7 %copy-start.2 = (f32[1,128,256]{2,1,0:T(8,128)S(1)}, f32[1,128,256]{2,1,0:T(8,128)}, u32[]{:S(2)}) copy-start(f32[1,128,256]{2,1,0:T(8,128)} %param.16) | copy-start | bytes 393220
  42.5 7.1 %copy-start.6 = (f32[1,256,256]{2,1,0:T(8,128)S(1)}, f32[1,256,256]{2,1,0:T(8,128)}, u32[]{:S(2)}) copy-start(f32[1,256,256]{2,1,0:T(8,128)} %param.17) | copy-start | bytes 786436
  42.5 10.1 %copy-start.3 = (f32[1,256,128]{2,1,0:T(8,128)S(1)}, f32[1,256,128]{2,1,0:T(8,128)}, u32[]{:S(2)}) copy-start(f32[1,256,128]{2,1,0:T(8,128)} %param.19) | copy-start | bytes 393220
  43.9 8.8 %collective-permute-start.7 = (f32[73,4,128]{2,1,0:T(4,128)S(1)}, f32[73,4,128]{2,1,0:T(4,128)S(1)}, u32[]{:S(2)}, u32[]{:S(2)}) collective-permute-start(f32[73,4,128]{2,1,0:T(4,128)S(1)} %get-tuple-element.92), channel_id=1, source_target_pairs={{0,1},{1,2},{2,3},{4,5},{5,6},{6,7},{8,9},{9,10},{10,11},{12,13},{... | collective-permute-start | bytes 448520 | tf_op jit(solution)/shard_map/ppermute | solution.py:43
  46.2 21.9 %collective-permute-start.2 = (f32[128,256]{1,0:T(8,128)S(1)}, f32[128,256]{1,0:T(8,128)S(1)}, u32[]{:S(2)}, u32[]{:S(2)}) collective-permute-start(f32[128,256]{1,0:T(8,128)S(1)} %bitcast.102), channel_id=1, source_target_pairs={{0,16},{4,20},{8,24},{12,28},{16,0},{20,4},{24,8},{28,12},{1,17},{... | collective-permute-start | bytes 393224 | tf_op jit(solution)/shard_map/ppermute | solution.py:213
  49.7 35.1 %collective-permute-start.3 = (f32[256,256]{1,0:T(8,128)S(1)}, f32[256,256]{1,0:T(8,128)}, u32[]{:S(2)}, u32[]{:S(2)}) collective-permute-start(f32[256,256]{1,0:T(8,128)S(1)} %bitcast.109), channel_id=1, source_target_pairs={{0,16},{4,20},{8,24},{12,28},{16,0},{20,4},{24,8},{28,12},{1,17},{... | collective-permute-start | bytes 786440 | tf_op jit(solution)/shard_map/ppermute | solution.py:213
  49.8 35.0 %collective-permute-start.4 = (f32[256,256]{1,0:T(8,128)}, f32[256,256]{1,0:T(8,128)}, u32[]{:S(2)}, u32[]{:S(2)}) collective-permute-start(f32[256,256]{1,0:T(8,128)} %bitcast.8), channel_id=1, source_target_pairs={{0,16},{4,20},{8,24},{12,28},{16,0},{20,4},{24,8},{28,12},{1,17},{... | collective-permute-start | bytes 786440 | tf_op jit(solution)/shard_map/ppermute | solution.py:213
  52.6 32.2 %collective-permute-start.5 = (f32[256,128]{1,0:T(8,128)S(1)}, f32[256,128]{1,0:T(8,128)}, u32[]{:S(2)}, u32[]{:S(2)}) collective-permute-start(f32[256,128]{1,0:T(8,128)S(1)} %bitcast.103), channel_id=1, source_target_pairs={{0,16},{4,20},{8,24},{12,28},{16,0},{20,4},{24,8},{28,12},{1,17},{... | collective-permute-start | bytes 393224 | tf_op jit(solution)/shard_map/ppermute | solution.py:213
  52.7 6.0 %collective-permute-start.6 = (f32[73,4,128]{2,1,0:T(4,128)S(1)}, f32[73,4,128]{2,1,0:T(4,128)S(1)}, u32[]{:S(2)}, u32[]{:S(2)}) collective-permute-start(f32[73,4,128]{2,1,0:T(4,128)S(1)} %get-tuple-element.91), channel_id=1, source_target_pairs={{1,0},{2,1},{3,2},{5,4},{6,5},{7,6},{9,8},{10,9},{11,10},{13,12},{... | collective-permute-start | bytes 448520 | tf_op jit(solution)/shard_map/ppermute | solution.py:44
  106.1 34.9 %all-to-all-start.1 = ((f32[16,256,128]{2,1,0:T(8,128)}), f32[16,256,128]{2,1,0:T(8,128)}, u32[]{:S(2)}, u32[]{:S(2)}) async-start(f32[16,256,128]{2,1,0:T(8,128)} %pad_maximum_fusion), calls=%async_computation.1 | async-start | bytes 4194304 | tf_op jit(solution)/shard_map/all_to_all | solution.py:256

commit v10 on v8

--- a/solution.py
+++ b/solution.py
@@ -252,8 +252,8 @@
     x_before, x_after, y_halo, coeff = stencil_finish(
         state_t, diffusivity, x_from_before, x_from_after, PASSES
     )
-    block, mirrored, x_before, x_after, y_halo, coeff = lax.optimization_barrier(
-        (block, mirrored, x_before, x_after, y_halo, coeff)
+    block, x_before, x_after, y_halo = lax.optimization_barrier(
+        (block, x_before, x_after, y_halo)
     )
     own_rows = standardize(block[:, :capacity].reshape(-1, features))
     own = network_rows(own_rows, first_layer[0], second_layer[0], third_layer[0], last_layer[0])

time: 162 us -> 155 us (0.957)
  waiting for transfers between devices: 44 us -> 36.9 us
    all_to_all x1, waiting for transfers between devices: 0.01 us -> 26.1 us  [body(): lax.all_to_all(outgoing.reshape(group_size, pair_slots, features), ('tile...]
    ppermute x4, waiting for transfers between devices: 25.1 us -> 0.01 us  [body(): lax.ppermute(w[0], 'tile', swap)]
    ppermute x1, waiting for transfers between devices: 4.51 us -> 0.01 us  [stencil_finish(): after = lax.ppermute(y_piece(0), 'inf', down)]
    all_to_all x1, waiting for transfers between devices: 14.4 us -> 10.8 us  [body(): lax.all_to_all(answered, ('tile', 'inf'), split_axis=0, concat_axis=0, ti...]
  transfers between devices with their start and end apart: 10 -> 10, of which waited for: 4 -> 2; matrix products, arithmetic and copies ran while one was open for 7% -> 18% of each run, Pallas kernels for 20% -> 21%
where the time goes in v10:
time: 155 us; the launch traced here: 154 us
  Pallas kernels  53 us (34%)
  waiting for transfers between devices  36.9 us (24%)
  starting transfers between devices  27.7 us (18%)
  matrix products  14.2 us (9%)
  local copies, waits for them, and re-layouts  11.8 us (8%)
  other arithmetic  9.18 us (6%)
    all_to_all x1, waiting for transfers between devices, body(): lax.all_to_all(outgoing.reshape(group_size, pair_slots, features), ('tile...  26.1 us
    pallas_call x1, Pallas kernels, body(): pl.pallas_call(finish_kernel, out_shape=(jax.ShapeDtypeStruct((levels * w...  20.1 us
    pallas_call x1, Pallas kernels, body(): pl.pallas_call(gather_kernel, out_shape=(jax.ShapeDtypeStruct((cells, fea...  17.7 us
    pallas_call x1, Pallas kernels, body(): pl.pallas_call(diffuse_kernel, out_shape=jax.ShapeDtypeStruct((width_x, w...  15.3 us
    all_to_all x1, waiting for transfers between devices, body(): lax.all_to_all(answered, ('tile', 'inf'), split_axis=0, concat_axis=0, ti...  10.8 us
    ppermute x4, starting transfers between devices, body(): lax.ppermute(w[0], 'tile', swap)  6.45 us
    all_to_all x1, starting transfers between devices, body(): lax.all_to_all(outgoing.reshape(group_size, pair_slots, features), ('tile...  5.97 us
    ppermute x1, starting transfers between devices, stencil_start(): before = lax.ppermute(x_piece(width_x - depth), 'tile', up)  4.9 us
  transfers between devices with their start and end apart: 10, of which 2 were waited for; matrix products, arithmetic and copies ran while one was open for 18% of the time, Pallas kernels for 21%

profile of v10, /device:TPU:0, one launch (start us, length us, event | category | flops | bytes accessed | tf_op | source)
XLA Modules:
  0.0 154.1 jit_solution(10325914199635664764)
XLA Ops:
  1.5 1.1 fusion.74
  2.7 1.1 fusion.75
  4.2 4.9 %collective-permute-start = (f32[129,4,128]{0,2,1:T(8,128)S(1)}, f32[129,4,128]{0,2,1:T(8,128)S(1)}, u32[]{:S(2)}, u32[]{:S(2)}) collective-permute-start(f32[129,4,128]{0,2,1:T(8,128)S(1)} %pad_maximum_fusion.1), channel_id=1, source_target_pairs={{0,4},{4,8},{8,12},{12,16},{16,20},{20,24},{24,28},{1,5},{5,9},{9,... | collective-permute-start | bytes 792584 | tf_op jit(solution)/shard_map/ppermute | solution.py:32
  9.7 1.3 collective-permute-start.1
  12.3 1.9 %while.13 = (s32[]{:T(128)}, f32[32]{0:T(128)S(1)}, f32[4,512]{1,0:T(4,128)S(1)}, bf16[4,512,32]{1,2,0:T(8,128)(2,1)S(1)}, s32[]{:T(128)}, /*index=5*/s32[]{:T(128)}) while((s32[]{:T(128)}, f32[32]{0:T(128)S(1)}, f32[4,512]{1,0:T(4,128)S(1)}, bf16[4,512,32]{1,2,0:T(8,128)(2,1)S(1)}, s32[]{:T(128)}, /*index=5*/s32[]{:T(128)}) %tuple.44), condition=%wide.region_3.4_spmd.clone, body=%wide.region_0.3_spmd.clone.sunk | while | flops 17399332 | bytes 106719 | solution.py:207
  14.9 17.7 %shard_map.104 = (f32[8192,128]{1,0:T(8,128)}, f32[4096,128]{1,0:T(8,128)}) custom-call(s32[2048]{0:T(1024)} %fusion.57.slot_ref, s32[2048]{0:T(1024)} %act_ref.3, f32[4096,128]{1,0:T(8,128)} %bitcast.93, f32[4096,128]{1,0:T(8,128)} %bitcast.94), custom_call_target="tpu_custom_call" | custom-call | tf_op jit(solution)/shard_map/pallas_call | solution.py:230
  32.6 6.0 %all-to-all-start = ((f32[16,256,128]{2,1,0:T(8,128)}), f32[16,256,128]{2,1,0:T(8,128)S(1)}, u32[]{:S(2)}, u32[]{:S(2)}) async-start(f32[16,256,128]{2,1,0:T(8,128)} %bitcast.95), calls=%async_computation | async-start | bytes 4194304 | tf_op jit(solution)/shard_map/all_to_all | solution.py:243
  38.7 0.9 copy.29
  39.6 1.0 slice.70
  41.5 1.0 slice_bitcast_fusion
  42.6 1.3 fusion.50
  43.9 1.3 collective-permute-start.2
  45.2 3.2 %collective-permute-start.3 = (f32[73,4,128]{2,1,0:T(4,128)S(1)}, f32[73,4,128]{2,1,0:T(4,128)S(1)}, u32[]{:S(2)}, u32[]{:S(2)}) collective-permute-start(f32[73,4,128]{2,1,0:T(4,128)S(1)} %get-tuple-element.82), channel_id=1, source_target_pairs={{0,1},{1,2},{2,3},{4,5},{5,6},{6,7},{8,9},{9,10},{10,11},{12,13},{... | collective-permute-start | bytes 448520 | tf_op jit(solution)/shard_map/ppermute | solution.py:53
  48.5 3.4 %collective-permute-start.7 = (f32[256,128]{1,0:T(8,128)S(1)}, f32[256,128]{1,0:T(8,128)}, u32[]{:S(2)}, u32[]{:S(2)}) collective-permute-start(f32[256,128]{1,0:T(8,128)S(1)} %bitcast.103), channel_id=1, source_target_pairs={{0,16},{4,20},{8,24},{12,28},{16,0},{20,4},{24,8},{28,12},{1,17},{... | collective-permute-start | bytes 393224 | tf_op jit(solution)/shard_map/ppermute | solution.py:223
  52.0 2.8 %collective-permute-start.6 = (f32[256,256]{1,0:T(8,128)}, f32[256,256]{1,0:T(8,128)}, u32[]{:S(2)}, u32[]{:S(2)}) collective-permute-start(f32[256,256]{1,0:T(8,128)} %bitcast.18), channel_id=1, source_target_pairs={{0,16},{4,20},{8,24},{12,28},{16,0},{20,4},{24,8},{28,12},{1,17},{... | collective-permute-start | bytes 786440 | tf_op jit(solution)/shard_map/ppermute | solution.py:223
  55.7 26.1 %all-to-all-done = f32[16,256,128]{2,1,0:T(8,128)S(1)} async-done(((f32[16,256,128]{2,1,0:T(8,128)}), f32[16,256,128]{2,1,0:T(8,128)S(1)}, u32[]{:S(2)}, u32[]{:S(2)}) %all-to-all-start) | async-done | bytes 2097184 | tf_op jit(solution)/shard_map/all_to_all | solution.py:243
  82.2 0.9 multiply_reduce_fusion.1
  83.1 1.3 subtract_multiply_fusion
  84.5 1.0 fusion.65
  85.5 1.3 fusion.36
  86.7 2.3 %divide_multiply_fusion = f32[2048,256]{1,0:T(8,128)S(1)} fusion(f32[2048,256]{1,0:T(8,128)S(1)} %fusion.36, f32[1,256,256]{2,1,0:T(8,128)} %param.18), kind=kOutput, calls=%fused_computation.31 | convolution fusion | flops 809500672 | bytes 4456448 | tf_op jit(solution)/shard_map/dot_general | solution.py:75
  89.6 1.0 fusion.76
  90.6 2.2 %fusion.22 = f32[2048,256]{1,0:T(8,128)S(1)} fusion(f32[256,256]{1,0:T(8,128)} %collective-permute-done.5, f32[2048,256]{1,0:T(8,128)S(1)} %fusion.76), kind=kOutput, calls=%fused_computation.25 | convolution fusion | flops 807403520 | bytes 4456448 | tf_op jit(solution)/shard_map/dot_general | solution.py:74
  92.8 2.2 %fusion.16 = f32[2048,256]{1,0:T(8,128)S(1)} fusion(f32[256,256]{1,0:T(8,128)} %collective-permute-done.6, f32[2048,256]{1,0:T(8,128)S(1)} %fusion.22), kind=kOutput, calls=%fused_computation.19 | convolution fusion | flops 807403520 | bytes 4456448 | tf_op jit(solution)/shard_map/dot_general | solution.py:75
  95.0 1.0 fusion.51
  96.0 2.2 %fusion.10 = f32[2048,128]{1,0:T(8,128)S(1)} fusion(f32[256,128]{1,0:T(8,128)} %collective-permute-done.7, f32[2048,256]{1,0:T(8,128)S(1)} %fusion.16), kind=kOutput, calls=%fused_computation.13 | convolution fusion | flops 404750336 | bytes 3276800 | tf_op jit(solution)/shard_map/dot_general | solution.py:76
  98.2 1.5 pad_maximum_fusion
  99.7 4.5 %all-to-all-start.1 = ((f32[16,256,128]{2,1,0:T(8,128)}), f32[16,256,128]{2,1,0:T(8,128)}, u32[]{:S(2)}, u32[]{:S(2)}) async-start(f32[16,256,128]{2,1,0:T(8,128)} %pad_maximum_fusion), calls=%async_computation.1 | async-start | bytes 4194304 | tf_op jit(solution)/shard_map/all_to_all | solution.py:266
  104.5 3.4 %broadcast_in_dim.42.c_ref = f32[72,136,128]{2,1,0:T(8,128)} broadcast(f32[72,136]{1,0:T(8,128)S(1)} %copy.28), dimensions={0,1} | broadcast | bytes 5052672 | tf_op jit(solution)/shard_map/broadcast_in_dim | solution.py:61
  107.9 15.3 %shard_map.105 = f32[64,128,128]{2,1,0:T(8,128)} custom-call(f32[64,128,128]{2,1,0:T(8,128)} %bitcast.90, f32[4,128,128]{2,1,0:T(8,128)} %copy-done.1, f32[4,128,128]{2,1,0:T(8,128)} %copy-done, f32[72,8,128]{2,1,0:T(8,128)} %pad_maximum_fusion.3.yh_ref, f32[72,136,128]{2,1,0:T(8,128)} %broadcast_in_dim.42.c_ref), custom_call_target="tpu_custom_call" | custom-call | tf_op jit(solution)/shard_map/pallas_call | solution.py:277
  123.2 10.8 %all-to-all-done.1 = f32[16,256,128]{2,1,0:T(8,128)} async-done(((f32[16,256,128]{2,1,0:T(8,128)}), f32[16,256,128]{2,1,0:T(8,128)}, u32[]{:S(2)}, u32[]{:S(2)}) %all-to-all-start.1) | async-done | bytes 2097184 | tf_op jit(solution)/shard_map/all_to_all | solution.py:266
  134.0 20.1 %shard_map.106 = (f32[4096,128]{1,0:T(8,128)}, f32[4096,128]{1,0:T(8,128)}) custom-call(s32[2048]{0:T(1024)} %fusion.57.slot_ref, s32[2048]{0:T(1024)} %act_ref.3, f32[4096,128]{1,0:T(8,128)} %bitcast.26.r_ref, f32[8192,128]{1,0:T(8,128)} %bitcast.91), custom_call_target="tpu_custom_call" | custom-call | tf_op jit(solution)/shard_map/pallas_call | solution.py:288
  (76 shorter events, 8.9 us)
Async XLA Ops:
  3.8 7.8 %copy-start.5 = (s32[2048,1]{0,1:T(1,128)S(1)}, s32[2048,1]{0,1:T(1,128)}, u32[]{:S(2)}) copy-start(s32[2048,1]{0,1:T(1,128)} %param.15) | copy-start | bytes 24580
  4.2 28.4 %collective-permute-start = (f32[129,4,128]{0,2,1:T(8,128)S(1)}, f32[129,4,128]{0,2,1:T(8,128)S(1)}, u32[]{:S(2)}, u32[]{:S(2)}) collective-permute-start(f32[129,4,128]{0,2,1:T(8,128)S(1)} %pad_maximum_fusion.1), channel_id=1, source_target_pairs={{0,4},{4,8},{8,12},{12,16},{16,20},{20,24},{24,28},{1,5},{5,9},{9,... | collective-permute-start | bytes 792584 | tf_op jit(solution)/shard_map/ppermute | solution.py:32
  9.7 22.8 %collective-permute-start.1 = (f32[129,4,128]{0,2,1:T(8,128)S(1)}, f32[129,4,128]{0,2,1:T(8,128)}, u32[]{:S(2)}, u32[]{:S(2)}) collective-permute-start(f32[129,4,128]{0,2,1:T(8,128)S(1)} %pad_maximum_fusion.2), channel_id=1, source_target_pairs={{4,0},{8,4},{12,8},{16,12},{20,16},{24,20},{28,24},{5,1},{9,5},{13... | collective-permute-start | bytes 792584 | tf_op jit(solution)/shard_map/ppermute | solution.py:33
  32.6 6.0 %copy-start.4 = (f32[64,128]{1,0:T(8,128)S(1)}, f32[64,128]{1,0:T(8,128)}, u32[]{:S(2)}) copy-start(f32[64,128]{1,0:T(8,128)} %param.13) | copy-start | bytes 98308
  32.6 49.3 %all-to-all-start = ((f32[16,256,128]{2,1,0:T(8,128)}), f32[16,256,128]{2,1,0:T(8,128)S(1)}, u32[]{:S(2)}, u32[]{:S(2)}) async-start(f32[16,256,128]{2,1,0:T(8,128)} %bitcast.95), calls=%async_computation | async-start | bytes 4194304 | tf_op jit(solution)/shard_map/all_to_all | solution.py:243
  42.5 1.4 copy-start
  42.5 1.4 copy-start.1
  42.5 5.9 %copy-start.3 = (f32[1,256,128]{2,1,0:T(8,128)S(1)}, f32[1,256,128]{2,1,0:T(8,128)}, u32[]{:S(2)}) copy-start(f32[1,256,128]{2,1,0:T(8,128)} %param.19) | copy-start | bytes 393220
  42.5 9.4 %copy-start.2 = (f32[1,128,256]{2,1,0:T(8,128)S(1)}, f32[1,128,256]{2,1,0:T(8,128)}, u32[]{:S(2)}) copy-start(f32[1,128,256]{2,1,0:T(8,128)} %param.16) | copy-start | bytes 393220
  42.6 12.3 %copy-start.6 = (f32[1,256,256]{2,1,0:T(8,128)S(1)}, f32[1,256,256]{2,1,0:T(8,128)}, u32[]{:S(2)}) copy-start(f32[1,256,256]{2,1,0:T(8,128)} %param.17) | copy-start | bytes 786436
  43.9 10.9 %collective-permute-start.2 = (f32[73,4,128]{2,1,0:T(4,128)S(1)}, f32[73,4,128]{2,1,0:T(4,128)S(1)}, u32[]{:S(2)}, u32[]{:S(2)}) collective-permute-start(f32[73,4,128]{2,1,0:T(4,128)S(1)} %get-tuple-element.81), channel_id=1, source_target_pairs={{1,0},{2,1},{3,2},{5,4},{6,5},{7,6},{9,8},{10,9},{11,10},{13,12},{... | collective-permute-start | bytes 448520 | tf_op jit(solution)/shard_map/ppermute | solution.py:54
  45.2 9.7 %collective-permute-start.3 = (f32[73,4,128]{2,1,0:T(4,128)S(1)}, f32[73,4,128]{2,1,0:T(4,128)S(1)}, u32[]{:S(2)}, u32[]{:S(2)}) collective-permute-start(f32[73,4,128]{2,1,0:T(4,128)S(1)} %get-tuple-element.82), channel_id=1, source_target_pairs={{0,1},{1,2},{2,3},{4,5},{5,6},{6,7},{8,9},{9,10},{10,11},{12,13},{... | collective-permute-start | bytes 448520 | tf_op jit(solution)/shard_map/ppermute | solution.py:53
  48.5 47.6 %collective-permute-start.7 = (f32[256,128]{1,0:T(8,128)S(1)}, f32[256,128]{1,0:T(8,128)}, u32[]{:S(2)}, u32[]{:S(2)}) collective-permute-start(f32[256,128]{1,0:T(8,128)S(1)} %bitcast.103), channel_id=1, source_target_pairs={{0,16},{4,20},{8,24},{12,28},{16,0},{20,4},{24,8},{28,12},{1,17},{... | collective-permute-start | bytes 393224 | tf_op jit(solution)/shard_map/ppermute | solution.py:223
  51.9 37.7 %collective-permute-start.4 = (f32[128,256]{1,0:T(8,128)S(1)}, f32[128,256]{1,0:T(8,128)S(1)}, u32[]{:S(2)}, u32[]{:S(2)}) collective-permute-start(f32[128,256]{1,0:T(8,128)S(1)} %bitcast.102), channel_id=1, source_target_pairs={{0,16},{4,20},{8,24},{12,28},{16,0},{20,4},{24,8},{28,12},{1,17},{... | collective-permute-start | bytes 393224 | tf_op jit(solution)/shard_map/ppermute | solution.py:223
  52.0 40.8 %collective-permute-start.6 = (f32[256,256]{1,0:T(8,128)}, f32[256,256]{1,0:T(8,128)}, u32[]{:S(2)}, u32[]{:S(2)}) collective-permute-start(f32[256,256]{1,0:T(8,128)} %bitcast.18), channel_id=1, source_target_pairs={{0,16},{4,20},{8,24},{12,28},{16,0},{20,4},{24,8},{28,12},{1,17},{... | collective-permute-start | bytes 786440 | tf_op jit(solution)/shard_map/ppermute | solution.py:223
  54.8 35.8 %collective-permute-start.5 = (f32[256,256]{1,0:T(8,128)S(1)}, f32[256,256]{1,0:T(8,128)}, u32[]{:S(2)}, u32[]{:S(2)}) collective-permute-start(f32[256,256]{1,0:T(8,128)S(1)} %bitcast.109), channel_id=1, source_target_pairs={{0,16},{4,20},{8,24},{12,28},{16,0},{20,4},{24,8},{28,12},{1,17},{... | collective-permute-start | bytes 786440 | tf_op jit(solution)/shard_map/ppermute | solution.py:223
  99.7 34.3 %all-to-all-start.1 = ((f32[16,256,128]{2,1,0:T(8,128)}), f32[16,256,128]{2,1,0:T(8,128)}, u32[]{:S(2)}, u32[]{:S(2)}) async-start(f32[16,256,128]{2,1,0:T(8,128)} %pad_maximum_fusion), calls=%async_computation.1 | async-start | bytes 4194304 | tf_op jit(solution)/shard_map/all_to_all | solution.py:266

commit v11 on v10

--- a/solution.py
+++ b/solution.py
@@ -76,12 +76,24 @@
     return jnp.dot(hidden, last_layer, precision=highest)
 
 
-def gather_kernel(slot_ref, act_ref, u_ref, v_ref, st_ref, o_ref):
-    levels_x, width_y = u_ref.shape
-    cells, features = st_ref.shape
-    levels = features // 2
-    width_x = levels_x // levels
+def gather_kernel(slot_ref, act_ref, u_hbm, v_hbm, st_ref, o_ref, buf, sems):
+    levels = u_hbm.shape[0]
+    width_x, features, width_y = buf.shape
     chunk = 128
+
+    def copies(x):
+        at = pl.ds(pl.multiple_of(x * width_y, width_y), width_y)
+        return (
+            pltpu.make_async_copy(u_hbm.at[:, at], buf.at[x, pl.ds(0, levels), :], sems.at[0, x]),
+            pltpu.make_async_copy(v_hbm.at[:, at], buf.at[x, pl.ds(levels, levels), :], sems.at[1, x]),
+        )
+
+    def start(x, carry):
+        for copy in copies(x):
+            copy.start()
+        return carry
+
+    lax.fori_loop(0, width_x, start, 0)
 
     def clear(k, carry):
         at = pl.ds(pl.multiple_of(k * chunk, chunk), chunk)
@@ -91,10 +103,9 @@
     lax.fori_loop(0, o_ref.shape[0] // chunk, clear, 0)
 
     def transpose_tile(x, carry):
-        a = u_ref[pl.ds(x, levels, stride=width_x), :]
-        b = v_ref[pl.ds(x, levels, stride=width_x), :]
-        tile = jnp.concatenate([a, b], axis=0)
-        st_ref[pl.ds(pl.multiple_of(x * width_y, width_y), width_y), :] = tile.T
+        for copy in copies(x):
+            copy.wait()
+        st_ref[pl.ds(pl.multiple_of(x * width_y, width_y), width_y), :] = buf[x].T
         return carry
 
     lax.fori_loop(0, width_x, transpose_tile, 0)
@@ -139,33 +150,45 @@
         sweep(src, dst, p, p == PASSES - 1)
 
 
-def finish_kernel(slot_ref, act_ref, r_ref, f_ref, uo_ref, vo_ref, d_ref):
-    levels_x, width_y = uo_ref.shape
-    cells, features = f_ref.shape
-    levels = features // 2
-    width_x = levels_x // levels
-
-    def copy_tile(x, carry):
+def finish_kernel(slot_ref, act_ref, r_ref, f_ref, uo_hbm, vo_hbm, d_ref, obuf, sems):
+    levels = uo_hbm.shape[0]
+    width_x, features, width_y = obuf.shape
+
+    def clear(x, carry):
         at = pl.ds(pl.multiple_of(x * width_y, width_y), width_y)
-        d_ref[at, :] = f_ref[at, :]
-        return carry
-
-    lax.fori_loop(0, width_x, copy_tile, 0)
+        d_ref[at, :] = jnp.zeros((width_y, features), jnp.float32)
+        return carry
+
+    lax.fori_loop(0, width_x, clear, 0)
 
     def place(r, carry):
-        at = pl.ds(act_ref[r], 1)
-        d_ref[at, :] = d_ref[at, :] + r_ref[pl.ds(slot_ref[r], 1), :]
+        d_ref[pl.ds(act_ref[r], 1), :] = r_ref[pl.ds(slot_ref[r], 1), :]
         return carry
 
     lax.fori_loop(0, act_ref.shape[0], place, 0, unroll=8)
 
+    def copies(x):
+        at = pl.ds(pl.multiple_of(x * width_y, width_y), width_y)
+        return (
+            pltpu.make_async_copy(obuf.at[x, pl.ds(0, levels), :], uo_hbm.at[:, at], sems.at[0, x]),
+            pltpu.make_async_copy(obuf.at[x, pl.ds(levels, levels), :], vo_hbm.at[:, at], sems.at[1, x]),
+        )
+
     def transpose_tile(x, carry):
-        tile = d_ref[pl.ds(pl.multiple_of(x * width_y, width_y), width_y), :].T
-        uo_ref[pl.ds(x, levels, stride=width_x), :] = tile[:levels]
-        vo_ref[pl.ds(x, levels, stride=width_x), :] = tile[levels:]
+        at = pl.ds(pl.multiple_of(x * width_y, width_y), width_y)
+        obuf[x] = (f_ref[at, :] + d_ref[at, :]).T
+        for copy in copies(x):
+            copy.start()
         return carry
 
     lax.fori_loop(0, width_x, transpose_tile, 0)
+
+    def finish(x, carry):
+        for copy in copies(x):
+            copy.wait()
+        return carry
+
+    lax.fori_loop(0, width_x, finish, 0)
 
 
 def body(
@@ -225,16 +248,21 @@
     vmem = pl.BlockSpec(memory_space=pltpu.VMEM)
     smem = pl.BlockSpec(memory_space=pltpu.SMEM)
     x_from_before, x_from_after = stencil_start(u_field, v_field, diffusivity, PASSES)
-    u_rows = u_field.reshape(levels * width_x, width_y)
-    v_rows = v_field.reshape(levels * width_x, width_y)
+    u_rows = u_field.reshape(levels, cells)
+    v_rows = v_field.reshape(levels, cells)
+    hbm = pl.BlockSpec(memory_space=pl.ANY)
     state_t, outgoing = pl.pallas_call(
         gather_kernel,
         out_shape=(
             jax.ShapeDtypeStruct((cells, features), jnp.float32),
             jax.ShapeDtypeStruct((slot_total, features), jnp.float32),
         ),
-        in_specs=[smem, smem, vmem, vmem],
+        in_specs=[smem, smem, hbm, hbm],
         out_specs=(vmem, vmem),
+        scratch_shapes=[
+            pltpu.VMEM((width_x, features, width_y), jnp.float32),
+            pltpu.SemaphoreType.DMA((2, width_x)),
+        ],
     )(slot_index, active_columns, u_rows, v_rows)
     state_t = state_t.reshape(width_x, width_y, features)
     outgoing, x_from_before, x_from_after = lax.optimization_barrier(
@@ -288,12 +316,16 @@
     u_next, v_next = pl.pallas_call(
         finish_kernel,
         out_shape=(
-            jax.ShapeDtypeStruct((levels * width_x, width_y), jnp.float32),
-            jax.ShapeDtypeStruct((levels * width_x, width_y), jnp.float32),
+            jax.ShapeDtypeStruct((levels, cells), jnp.float32),
+            jax.ShapeDtypeStruct((levels, cells), jnp.float32),
         ),
         in_specs=[smem, smem, vmem, vmem],
-        out_specs=(vmem, vmem),
-        scratch_shapes=[pltpu.VMEM((cells, features), jnp.float32)],
+        out_specs=(hbm, hbm),
+        scratch_shapes=[
+            pltpu.VMEM((cells, features), jnp.float32),
+            pltpu.VMEM((width_x, features, width_y), jnp.float32),
+            pltpu.SemaphoreType.DMA((2, width_x)),
+        ],
     )(slot_index, active_columns, returned_rows, diffused.reshape(cells, features))
     return (u_next.reshape(u_field.shape), v_next.reshape(v_field.shape))
 

time: 155 us -> 161 us (1.039)
  local copies, waits for them, and re-layouts: 11.8 us -> 24.7 us
  Pallas kernels: 53 us -> 46.4 us
    reshape x0 -> x1, local copies, waits for them, and re-layouts: none -> 6.85 us  [body(): v_rows = v_field.reshape(levels, cells)]
    unnamed x21 -> x29, local copies, waits for them, and re-layouts: 1.18 us -> 7.09 us
    pallas_call x1, Pallas kernels: 20.1 us -> 15.3 us  [body(): pl.pallas_call(finish_kernel, out_shape=(jax.ShapeDtypeStruct((levels, ce...]
    pallas_call x1, Pallas kernels: 17.7 us -> 15.8 us  [body(): pl.pallas_call(gather_kernel, out_shape=(jax.ShapeDtypeStruct((cells, fea...]
  transfers between devices with their start and end apart: 10 -> 10, of which waited for: 2 -> 2; matrix products, arithmetic and copies ran while one was open for 18% -> 22% of each run, Pallas kernels for 21% -> 19%
where the time goes in v11:
time: 161 us
  Pallas kernels  46.4 us (29%)
  waiting for transfers between devices  37.4 us (23%)
  starting transfers between devices  27 us (17%)
  local copies, waits for them, and re-layouts  24.7 us (15%)
  matrix products  13.3 us (8%)
  other arithmetic  10.7 us (7%)
    all_to_all x1, waiting for transfers between devices, body(): lax.all_to_all(outgoing.reshape(group_size, pair_slots, features), ('tile...  26.6 us
    pallas_call x1, Pallas kernels, body(): pl.pallas_call(gather_kernel, out_shape=(jax.ShapeDtypeStruct((cells, fea...  15.8 us
    pallas_call x1, Pallas kernels, body(): pl.pallas_call(finish_kernel, out_shape=(jax.ShapeDtypeStruct((levels, ce...  15.3 us
    pallas_call x1, Pallas kernels, body(): pl.pallas_call(diffuse_kernel, out_shape=jax.ShapeDtypeStruct((width_x, w...  15.3 us
    all_to_all x1, waiting for transfers between devices, body(): lax.all_to_all(answered, ('tile', 'inf'), split_axis=0, concat_axis=0, ti...  10.8 us
    unnamed x29, local copies, waits for them, and re-layouts  7.09 us
    reshape x1, local copies, waits for them, and re-layouts, body(): v_rows = v_field.reshape(levels, cells)  6.85 us
    all_to_all x1, starting transfers between devices, body(): lax.all_to_all(outgoing.reshape(group_size, pair_slots, features), ('tile...  5.96 us
  transfers between devices with their start and end apart: 10, of which 2 were waited for; matrix products, arithmetic and copies ran while one was open for 22% of the time, Pallas kernels for 19%

profile of v11, /device:TPU:0, one launch (start us, length us, event | category | flops | bytes accessed | tf_op | source)
XLA Modules:
  0.0 160.8 jit_solution(2323730716966676107)
XLA Ops:
  1.5 1.1 fusion.74
  2.7 1.1 fusion.75
  4.0 1.0 pad_maximum_fusion.1
  5.0 4.9 %collective-permute-start = (f32[129,4,128]{0,2,1:T(8,128)}, f32[129,4,128]{0,2,1:T(8,128)S(1)}, u32[]{:S(2)}, u32[]{:S(2)}) collective-permute-start(f32[129,4,128]{0,2,1:T(8,128)} %pad_maximum_fusion.1), channel_id=1, source_target_pairs={{0,4},{4,8},{8,12},{12,16},{16,20},{20,24},{24,28},{1,5},{5,9},{9,... | collective-permute-start | bytes 792584 | tf_op jit(solution)/shard_map/ppermute | solution.py:32
  10.3 1.0 pad_maximum_fusion.2
  11.3 1.3 collective-permute-start.1
  13.9 1.9 %while.13 = (s32[]{:T(128)}, f32[32]{0:T(128)S(1)}, f32[4,512]{1,0:T(4,128)S(1)}, bf16[4,512,32]{1,2,0:T(8,128)(2,1)S(1)}, s32[]{:T(128)}, /*index=5*/s32[]{:T(128)}) while((s32[]{:T(128)}, f32[32]{0:T(128)S(1)}, f32[4,512]{1,0:T(4,128)S(1)}, bf16[4,512,32]{1,2,0:T(8,128)(2,1)S(1)}, s32[]{:T(128)}, /*index=5*/s32[]{:T(128)}) %tuple.43), condition=%wide.region_3.4_spmd.clone, body=%wide.region_0.3_spmd.clone.sunk | while | flops 17399332 | bytes 106719 | solution.py:230
  15.8 6.9 %copy_bitcast_fusion = (f32[64,8192]{1,0:T(8,128)}, f32[64,8192]{1,0:T(8,128)}) fusion(f32[8,8,64,128]{3,2,1,0:T(8,128)S(1)} %bitcast.99, f32[8,8,64,128]{3,2,1,0:T(8,128)} %bitcast.100), kind=kLoop, calls=%fused_computation.12 | loop fusion | bytes 8388608 | tf_op jit(solution)/shard_map/reshape | solution.py:252
  23.3 15.8 %shard_map.104 = (f32[8192,128]{1,0:T(8,128)}, f32[4096,128]{1,0:T(8,128)}) custom-call(s32[2048]{0:T(1024)} %fusion.57.slot_ref, s32[2048]{0:T(1024)} %act_ref.3, f32[64,8192]{1,0:T(8,128)} %get-tuple-element.97.u_hbm, f32[64,8192]{1,0:T(8,128)} %get-tuple-element.96.v_hbm), custom_call_target="tpu_custom_call" | custom-call | tf_op jit(solution)/shard_map/pallas_call | solution.py:254
  40.0 6.0 %all-to-all-start = ((f32[16,256,128]{2,1,0:T(8,128)}), f32[16,256,128]{2,1,0:T(8,128)S(1)}, u32[]{:S(2)}, u32[]{:S(2)}) async-start(f32[16,256,128]{2,1,0:T(8,128)} %bitcast.101), calls=%async_computation | async-start | bytes 4194304 | tf_op jit(solution)/shard_map/all_to_all | solution.py:271
  48.9 1.1 slice_bitcast_fusion.xa_ref
  50.1 1.2 fusion.50
  51.3 1.3 collective-permute-start.2
  52.6 3.2 %collective-permute-start.3 = (f32[73,4,128]{2,1,0:T(4,128)S(1)}, f32[73,4,128]{2,1,0:T(4,128)S(1)}, u32[]{:S(2)}, u32[]{:S(2)}) collective-permute-start(f32[73,4,128]{2,1,0:T(4,128)S(1)} %get-tuple-element.82), channel_id=1, source_target_pairs={{0,1},{1,2},{2,3},{4,5},{5,6},{6,7},{8,9},{9,10},{10,11},{12,13},{... | collective-permute-start | bytes 448520 | tf_op jit(solution)/shard_map/ppermute | solution.py:53
  55.9 2.7 %collective-permute-start.7 = (f32[256,128]{1,0:T(8,128)S(1)}, f32[256,128]{1,0:T(8,128)S(1)}, u32[]{:S(2)}, u32[]{:S(2)}) collective-permute-start(f32[256,128]{1,0:T(8,128)S(1)} %bitcast.113), channel_id=1, source_target_pairs={{0,16},{4,20},{8,24},{12,28},{16,0},{20,4},{24,8},{28,12},{1,17},{... | collective-permute-start | bytes 393224 | tf_op jit(solution)/shard_map/ppermute | solution.py:246
  58.9 2.6 %collective-permute-start.6 = (f32[256,256]{1,0:T(8,128)}, f32[256,256]{1,0:T(8,128)}, u32[]{:S(2)}, u32[]{:S(2)}) collective-permute-start(f32[256,256]{1,0:T(8,128)} %bitcast.16), channel_id=1, source_target_pairs={{0,16},{4,20},{8,24},{12,28},{16,0},{20,4},{24,8},{28,12},{1,17},{... | collective-permute-start | bytes 786440 | tf_op jit(solution)/shard_map/ppermute | solution.py:246
  62.6 26.6 %all-to-all-done = f32[16,256,128]{2,1,0:T(8,128)S(1)} async-done(((f32[16,256,128]{2,1,0:T(8,128)}), f32[16,256,128]{2,1,0:T(8,128)S(1)}, u32[]{:S(2)}, u32[]{:S(2)}) %all-to-all-start) | async-done | bytes 2097184 | tf_op jit(solution)/shard_map/all_to_all | solution.py:271
  90.5 1.3 subtract_multiply_fusion
  92.8 1.3 fusion.36
  94.1 2.3 %divide_multiply_fusion = f32[2048,256]{1,0:T(8,128)S(1)} fusion(f32[2048,256]{1,0:T(8,128)S(1)} %fusion.36, f32[1,256,256]{2,1,0:T(8,128)} %param.18), kind=kOutput, calls=%fused_computation.33 | convolution fusion | flops 809500672 | bytes 4456448 | tf_op jit(solution)/shard_map/dot_general | solution.py:75
  98.0 2.2 %fusion.22 = f32[2048,256]{1,0:T(8,128)S(1)} fusion(f32[256,256]{1,0:T(8,128)} %collective-permute-done.5, f32[2048,256]{1,0:T(8,128)S(1)} %fusion.76), kind=kOutput, calls=%fused_computation.27 | convolution fusion | flops 807403520 | bytes 4456448 | tf_op jit(solution)/shard_map/dot_general | solution.py:74
  100.2 2.2 %fusion.16 = f32[2048,256]{1,0:T(8,128)S(1)} fusion(f32[256,256]{1,0:T(8,128)} %collective-permute-done.6, f32[2048,256]{1,0:T(8,128)S(1)} %fusion.22), kind=kOutput, calls=%fused_computation.21 | convolution fusion | flops 807403520 | bytes 4456448 | tf_op jit(solution)/shard_map/dot_general | solution.py:75
  102.4 1.0 fusion.51
  103.4 1.3 fusion.10
  104.7 1.5 pad_maximum_fusion
  106.2 4.4 %all-to-all-start.1 = ((f32[16,256,128]{2,1,0:T(8,128)}), f32[16,256,128]{2,1,0:T(8,128)}, u32[]{:S(2)}, u32[]{:S(2)}) async-start(f32[16,256,128]{2,1,0:T(8,128)} %pad_maximum_fusion), calls=%async_computation.1 | async-start | bytes 4194304 | tf_op jit(solution)/shard_map/all_to_all | solution.py:294
  110.9 3.4 %broadcast_in_dim.42.c_ref = f32[72,136,128]{2,1,0:T(8,128)} broadcast(f32[72,136]{1,0:T(8,128)S(1)} %copy.28), dimensions={0,1} | broadcast | bytes 5052672 | tf_op jit(solution)/shard_map/broadcast_in_dim | solution.py:61
  114.3 15.3 %shard_map.105 = f32[64,128,128]{2,1,0:T(8,128)} custom-call(f32[64,128,128]{2,1,0:T(8,128)} %bitcast.96, f32[4,128,128]{2,1,0:T(8,128)} %copy-done.1, f32[4,128,128]{2,1,0:T(8,128)} %copy-done.2, f32[72,8,128]{2,1,0:T(8,128)} %pad_maximum_fusion.3.yh_ref, f32[72,136,128]{2,1,0:T(8,128)} %broadcast_in_dim.42.c_ref), custom_call_target="tpu_custom_call" | custom-call | tf_op jit(solution)/shard_map/pallas_call | solution.py:305
  129.6 10.8 %all-to-all-done.1 = f32[16,256,128]{2,1,0:T(8,128)} async-done(((f32[16,256,128]{2,1,0:T(8,128)}), f32[16,256,128]{2,1,0:T(8,128)}, u32[]{:S(2)}, u32[]{:S(2)}) %all-to-all-start.1) | async-done | bytes 2097184 | tf_op jit(solution)/shard_map/all_to_all | solution.py:294
  140.3 15.3 %shard_map.106 = (f32[64,8192]{1,0:T(8,128)}, f32[64,8192]{1,0:T(8,128)}) custom-call(s32[2048]{0:T(1024)} %fusion.57.slot_ref, s32[2048]{0:T(1024)} %act_ref.3, f32[4096,128]{1,0:T(8,128)} %bitcast.24.r_ref, f32[8192,128]{1,0:T(8,128)} %bitcast.97), custom_call_target="tpu_custom_call" | custom-call | tf_op jit(solution)/shard_map/pallas_call | solution.py:316
  155.7 3.4 %copy.38 = f32[8,8,64,128]{3,2,1,0:T(8,128)} copy(f32[8,8,64,128]{3,1,2,0:T(8,128)} %bitcast.106) | data formatting | bytes 4194304
  159.1 1.7 %copy.39 = f32[8,8,64,128]{3,2,1,0:T(8,128)} copy(f32[8,8,64,128]{3,1,2,0:T(8,128)S(1)} %bitcast.105) | data formatting | bytes 4194304
  (87 shorter events, 14.4 us)
Async XLA Ops:
  3.8 9.3 %copy-start.8 = (s32[2048,1]{0,1:T(1,128)S(1)}, s32[2048,1]{0,1:T(1,128)}, u32[]{:S(2)}) copy-start(s32[2048,1]{0,1:T(1,128)} %param.15) | copy-start | bytes 24580
  5.0 34.2 %collective-permute-start = (f32[129,4,128]{0,2,1:T(8,128)}, f32[129,4,128]{0,2,1:T(8,128)S(1)}, u32[]{:S(2)}, u32[]{:S(2)}) collective-permute-start(f32[129,4,128]{0,2,1:T(8,128)} %pad_maximum_fusion.1), channel_id=1, source_target_pairs={{0,4},{4,8},{8,12},{12,16},{16,20},{20,24},{24,28},{1,5},{5,9},{9,... | collective-permute-start | bytes 792584 | tf_op jit(solution)/shard_map/ppermute | solution.py:32
  10.2 5.7 %copy-start = (f32[64,64,128]{2,1,0:T(8,128)S(1)}, f32[64,64,128]{2,1,0:T(8,128)}, u32[]{:S(2)}) copy-start(f32[64,64,128]{2,1,0:T(8,128)} %param.12) | copy-start | bytes 6291460
  11.3 27.9 %collective-permute-start.1 = (f32[129,4,128]{0,2,1:T(8,128)}, f32[129,4,128]{0,2,1:T(8,128)S(1)}, u32[]{:S(2)}, u32[]{:S(2)}) collective-permute-start(f32[129,4,128]{0,2,1:T(8,128)} %pad_maximum_fusion.2), channel_id=1, source_target_pairs={{4,0},{8,4},{12,8},{16,12},{20,16},{24,20},{28,24},{5,1},{9,5},{13... | collective-permute-start | bytes 792584 | tf_op jit(solution)/shard_map/ppermute | solution.py:33
  39.2 0.8 copy-start.4
  39.2 6.8 %copy-start.7 = (f32[64,128]{1,0:T(8,128)S(1)}, f32[64,128]{1,0:T(8,128)}, u32[]{:S(2)}) copy-start(f32[64,128]{1,0:T(8,128)} %param.13) | copy-start | bytes 98308
  40.0 49.2 %all-to-all-start = ((f32[16,256,128]{2,1,0:T(8,128)}), f32[16,256,128]{2,1,0:T(8,128)S(1)}, u32[]{:S(2)}, u32[]{:S(2)}) async-start(f32[16,256,128]{2,1,0:T(8,128)} %bitcast.101), calls=%async_computation | async-start | bytes 4194304 | tf_op jit(solution)/shard_map/all_to_all | solution.py:271
  48.9 2.4 %copy-start.1 = (f32[4,128,128]{2,1,0:T(8,128)}, f32[4,128,128]{2,1,0:T(8,128)S(1)}, u32[]{:S(2)}) copy-start(f32[4,128,128]{2,1,0:T(8,128)S(1)} %slice_bitcast_fusion.1.xb_ref) | copy-start | bytes 786436
  50.0 1.3 copy-start.2
  50.0 5.8 %copy-start.6 = (f32[1,256,128]{2,1,0:T(8,128)S(1)}, f32[1,256,128]{2,1,0:T(8,128)}, u32[]{:S(2)}) copy-start(f32[1,256,128]{2,1,0:T(8,128)} %param.19) | copy-start | bytes 393220
  50.0 8.5 %copy-start.5 = (f32[1,128,256]{2,1,0:T(8,128)S(1)}, f32[1,128,256]{2,1,0:T(8,128)}, u32[]{:S(2)}) copy-start(f32[1,128,256]{2,1,0:T(8,128)} %param.16) | copy-start | bytes 393220
  50.0 11.4 %copy-start.9 = (f32[1,256,256]{2,1,0:T(8,128)S(1)}, f32[1,256,256]{2,1,0:T(8,128)}, u32[]{:S(2)}) copy-start(f32[1,256,256]{2,1,0:T(8,128)} %param.17) | copy-start | bytes 786436
  51.3 10.2 %collective-permute-start.2 = (f32[73,4,128]{2,1,0:T(4,128)S(1)}, f32[73,4,128]{2,1,0:T(4,128)S(1)}, u32[]{:S(2)}, u32[]{:S(2)}) collective-permute-start(f32[73,4,128]{2,1,0:T(4,128)S(1)} %get-tuple-element.81), channel_id=1, source_target_pairs={{1,0},{2,1},{3,2},{5,4},{6,5},{7,6},{9,8},{10,9},{11,10},{13,12},{... | collective-permute-start | bytes 448520 | tf_op jit(solution)/shard_map/ppermute | solution.py:54
  52.6 9.2 %collective-permute-start.3 = (f32[73,4,128]{2,1,0:T(4,128)S(1)}, f32[73,4,128]{2,1,0:T(4,128)S(1)}, u32[]{:S(2)}, u32[]{:S(2)}) collective-permute-start(f32[73,4,128]{2,1,0:T(4,128)S(1)} %get-tuple-element.82), channel_id=1, source_target_pairs={{0,1},{1,2},{2,3},{4,5},{5,6},{6,7},{8,9},{9,10},{10,11},{12,13},{... | collective-permute-start | bytes 448520 | tf_op jit(solution)/shard_map/ppermute | solution.py:53
  55.9 47.6 %collective-permute-start.7 = (f32[256,128]{1,0:T(8,128)S(1)}, f32[256,128]{1,0:T(8,128)S(1)}, u32[]{:S(2)}, u32[]{:S(2)}) collective-permute-start(f32[256,128]{1,0:T(8,128)S(1)} %bitcast.113), channel_id=1, source_target_pairs={{0,16},{4,20},{8,24},{12,28},{16,0},{20,4},{24,8},{28,12},{1,17},{... | collective-permute-start | bytes 393224 | tf_op jit(solution)/shard_map/ppermute | solution.py:246
  58.5 38.4 %collective-permute-start.4 = (f32[128,256]{1,0:T(8,128)S(1)}, f32[128,256]{1,0:T(8,128)S(1)}, u32[]{:S(2)}, u32[]{:S(2)}) collective-permute-start(f32[128,256]{1,0:T(8,128)S(1)} %bitcast.112), channel_id=1, source_target_pairs={{0,16},{4,20},{8,24},{12,28},{16,0},{20,4},{24,8},{28,12},{1,17},{... | collective-permute-start | bytes 393224 | tf_op jit(solution)/shard_map/ppermute | solution.py:246
  58.9 41.4 %collective-permute-start.6 = (f32[256,256]{1,0:T(8,128)}, f32[256,256]{1,0:T(8,128)}, u32[]{:S(2)}, u32[]{:S(2)}) collective-permute-start(f32[256,256]{1,0:T(8,128)} %bitcast.16), channel_id=1, source_target_pairs={{0,16},{4,20},{8,24},{12,28},{16,0},{20,4},{24,8},{28,12},{1,17},{... | collective-permute-start | bytes 786440 | tf_op jit(solution)/shard_map/ppermute | solution.py:246
  61.5 36.5 %collective-permute-start.5 = (f32[256,256]{1,0:T(8,128)S(1)}, f32[256,256]{1,0:T(8,128)}, u32[]{:S(2)}, u32[]{:S(2)}) collective-permute-start(f32[256,256]{1,0:T(8,128)S(1)} %bitcast.117), channel_id=1, source_target_pairs={{0,16},{4,20},{8,24},{12,28},{16,0},{20,4},{24,8},{28,12},{1,17},{... | collective-permute-start | bytes 786440 | tf_op jit(solution)/shard_map/ppermute | solution.py:246
  106.2 34.1 %all-to-all-start.1 = ((f32[16,256,128]{2,1,0:T(8,128)}), f32[16,256,128]{2,1,0:T(8,128)}, u32[]{:S(2)}, u32[]{:S(2)}) async-start(f32[16,256,128]{2,1,0:T(8,128)} %pad_maximum_fusion), calls=%async_computation.1 | async-start | bytes 4194304 | tf_op jit(solution)/shard_map/all_to_all | solution.py:294
  155.6 3.4 %copy-start.3 = (f32[64,8192]{1,0:T(8,128)S(1)}, f32[64,8192]{1,0:T(8,128)}, u32[]{:S(2)}) copy-start(f32[64,8192]{1,0:T(8,128)} %get-tuple-element.51) | copy-start | bytes 6291460

commit v12 on v11

--- a/solution.py
+++ b/solution.py
@@ -82,10 +82,9 @@
     chunk = 128
 
     def copies(x):
-        at = pl.ds(pl.multiple_of(x * width_y, width_y), width_y)
         return (
-            pltpu.make_async_copy(u_hbm.at[:, at], buf.at[x, pl.ds(0, levels), :], sems.at[0, x]),
-            pltpu.make_async_copy(v_hbm.at[:, at], buf.at[x, pl.ds(levels, levels), :], sems.at[1, x]),
+            pltpu.make_async_copy(u_hbm.at[:, x, :], buf.at[x, pl.ds(0, levels), :], sems.at[0, x]),
+            pltpu.make_async_copy(v_hbm.at[:, x, :], buf.at[x, pl.ds(levels, levels), :], sems.at[1, x]),
         )
 
     def start(x, carry):
@@ -168,10 +167,9 @@
     lax.fori_loop(0, act_ref.shape[0], place, 0, unroll=8)
 
     def copies(x):
-        at = pl.ds(pl.multiple_of(x * width_y, width_y), width_y)
         return (
-            pltpu.make_async_copy(obuf.at[x, pl.ds(0, levels), :], uo_hbm.at[:, at], sems.at[0, x]),
-            pltpu.make_async_copy(obuf.at[x, pl.ds(levels, levels), :], vo_hbm.at[:, at], sems.at[1, x]),
+            pltpu.make_async_copy(obuf.at[x, pl.ds(0, levels), :], uo_hbm.at[:, x, :], sems.at[0, x]),
+            pltpu.make_async_copy(obuf.at[x, pl.ds(levels, levels), :], vo_hbm.at[:, x, :], sems.at[1, x]),
         )
 
     def transpose_tile(x, carry):
@@ -248,8 +246,6 @@
     vmem = pl.BlockSpec(memory_space=pltpu.VMEM)
     smem = pl.BlockSpec(memory_space=pltpu.SMEM)
     x_from_before, x_from_after = stencil_start(u_field, v_field, diffusivity, PASSES)
-    u_rows = u_field.reshape(levels, cells)
-    v_rows = v_field.reshape(levels, cells)
     hbm = pl.BlockSpec(memory_space=pl.ANY)
     state_t, outgoing = pl.pallas_call(
         gather_kernel,
@@ -263,7 +259,7 @@
             pltpu.VMEM((width_x, features, width_y), jnp.float32),
             pltpu.SemaphoreType.DMA((2, width_x)),
         ],
-    )(slot_index, active_columns, u_rows, v_rows)
+    )(slot_index, active_columns, u_field, v_field)
     state_t = state_t.reshape(width_x, width_y, features)
     outgoing, x_from_before, x_from_after = lax.optimization_barrier(
         (outgoing, x_from_before, x_from_after)
@@ -316,8 +312,8 @@
     u_next, v_next = pl.pallas_call(
         finish_kernel,
         out_shape=(
-            jax.ShapeDtypeStruct((levels, cells), jnp.float32),
-            jax.ShapeDtypeStruct((levels, cells), jnp.float32),
+            jax.ShapeDtypeStruct(u_field.shape, jnp.float32),
+            jax.ShapeDtypeStruct(v_field.shape, jnp.float32),
         ),
         in_specs=[smem, smem, vmem, vmem],
         out_specs=(hbm, hbm),
@@ -327,7 +323,7 @@
             pltpu.SemaphoreType.DMA((2, width_x)),
         ],
     )(slot_index, active_columns, returned_rows, diffused.reshape(cells, features))
-    return (u_next.reshape(u_field.shape), v_next.reshape(v_field.shape))
+    return (u_next, v_next)
 
 
 def solution(mesh):

time: 161 us -> 149 us (0.925)
  local copies, waits for them, and re-layouts: 24.7 us -> 11.8 us
    reshape x1 -> x0, local copies, waits for them, and re-layouts: 6.85 us -> none  [body(): v_rows = v_field.reshape(levels, cells)]
    unnamed x29 -> x21, local copies, waits for them, and re-layouts: 7.09 us -> 1.18 us
  transfers between devices with their start and end apart: 10 -> 10, of which waited for: 2 -> 3; matrix products, arithmetic and copies ran while one was open for 22% -> 19% of each run, Pallas kernels for 19% -> 21%
where the time goes in v12:
time: 149 us; the launch traced here: 148 us
  Pallas kernels  46.5 us (31%)
  waiting for transfers between devices  38 us (26%)
  starting transfers between devices  27.2 us (18%)
  matrix products  14.2 us (10%)
  local copies, waits for them, and re-layouts  11.8 us (8%)
  other arithmetic  9.19 us (6%)
    all_to_all x1, waiting for transfers between devices, body(): lax.all_to_all(outgoing.reshape(group_size, pair_slots, features), ('tile...  26.6 us
    pallas_call x1, Pallas kernels, body(): pl.pallas_call(gather_kernel, out_shape=(jax.ShapeDtypeStruct((cells, fea...  16 us
    pallas_call x1, Pallas kernels, body(): pl.pallas_call(finish_kernel, out_shape=(jax.ShapeDtypeStruct(u_field.sha...  15.3 us
    pallas_call x1, Pallas kernels, body(): pl.pallas_call(diffuse_kernel, out_shape=jax.ShapeDtypeStruct((width_x, w...  15.3 us
    all_to_all x1, waiting for transfers between devices, body(): lax.all_to_all(answered, ('tile', 'inf'), split_axis=0, concat_axis=0, ti...  10.8 us
    all_to_all x1, starting transfers between devices, body(): lax.all_to_all(outgoing.reshape(group_size, pair_slots, features), ('tile...  6.04 us
    ppermute x4, starting transfers between devices, body(): lax.ppermute(w[0], 'tile', swap)  5.92 us
    ppermute x1, starting transfers between devices, stencil_start(): before = lax.ppermute(x_piece(width_x - depth), 'tile', up)  4.9 us
  transfers between devices with their start and end apart: 10, of which 3 were waited for; matrix products, arithmetic and copies ran while one was open for 19% of the time, Pallas kernels for 21%

profile of v12, /device:TPU:0, one launch (start us, length us, event | category | flops | bytes accessed | tf_op | source)
XLA Modules:
  0.0 148.3 jit_solution(13772496585831251403)
XLA Ops:
  1.5 1.1 fusion.74
  2.7 1.1 fusion.75
  4.2 4.9 %collective-permute-start = (f32[129,4,128]{0,2,1:T(8,128)S(1)}, f32[129,4,128]{0,2,1:T(8,128)S(1)}, u32[]{:S(2)}, u32[]{:S(2)}) collective-permute-start(f32[129,4,128]{0,2,1:T(8,128)S(1)} %pad_maximum_fusion.1), channel_id=1, source_target_pairs={{0,4},{4,8},{8,12},{12,16},{16,20},{20,24},{24,28},{1,5},{5,9},{9,... | collective-permute-start | bytes 792584 | tf_op jit(solution)/shard_map/ppermute | solution.py:32
  9.7 1.3 collective-permute-start.1
  12.3 1.9 %while.13 = (s32[]{:T(128)}, f32[32]{0:T(128)S(1)}, f32[4,512]{1,0:T(4,128)S(1)}, bf16[4,512,32]{1,2,0:T(8,128)(2,1)S(1)}, s32[]{:T(128)}, /*index=5*/s32[]{:T(128)}) while((s32[]{:T(128)}, f32[32]{0:T(128)S(1)}, f32[4,512]{1,0:T(4,128)S(1)}, bf16[4,512,32]{1,2,0:T(8,128)(2,1)S(1)}, s32[]{:T(128)}, /*index=5*/s32[]{:T(128)}) %tuple.42), condition=%wide.region_3.4_spmd.clone, body=%wide.region_0.3_spmd.clone.sunk | while | flops 17399332 | bytes 106719 | solution.py:228
  14.9 16.0 %shard_map.104 = (f32[8192,128]{1,0:T(8,128)}, f32[4096,128]{1,0:T(8,128)}) custom-call(s32[2048]{0:T(1024)} %fusion.57.slot_ref, s32[2048]{0:T(1024)} %act_ref.3, f32[64,64,128]{2,1,0:T(8,128)} %u_hbm.1, f32[64,64,128]{2,1,0:T(8,128)} %v_hbm.1), custom_call_target="tpu_custom_call" | custom-call | tf_op jit(solution)/shard_map/pallas_call | solution.py:250
  31.5 6.0 %all-to-all-start = ((f32[16,256,128]{2,1,0:T(8,128)}), f32[16,256,128]{2,1,0:T(8,128)S(1)}, u32[]{:S(2)}, u32[]{:S(2)}) async-start(f32[16,256,128]{2,1,0:T(8,128)} %bitcast.89), calls=%async_computation | async-start | bytes 4194304 | tf_op jit(solution)/shard_map/all_to_all | solution.py:267
  37.6 0.9 copy.29
  38.5 1.0 slice.70
  40.4 1.0 slice_bitcast_fusion
  41.5 1.3 fusion.50
  42.8 1.3 collective-permute-start.2
  44.1 3.2 %collective-permute-start.3 = (f32[73,4,128]{2,1,0:T(4,128)S(1)}, f32[73,4,128]{2,1,0:T(4,128)S(1)}, u32[]{:S(2)}, u32[]{:S(2)}) collective-permute-start(f32[73,4,128]{2,1,0:T(4,128)S(1)} %get-tuple-element.78), channel_id=1, source_target_pairs={{0,1},{1,2},{2,3},{4,5},{5,6},{6,7},{8,9},{9,10},{10,11},{12,13},{... | collective-permute-start | bytes 448520 | tf_op jit(solution)/shard_map/ppermute | solution.py:53
  47.4 2.8 %collective-permute-start.7 = (f32[256,128]{1,0:T(8,128)S(1)}, f32[256,128]{1,0:T(8,128)}, u32[]{:S(2)}, u32[]{:S(2)}) collective-permute-start(f32[256,128]{1,0:T(8,128)S(1)} %bitcast.97), channel_id=1, source_target_pairs={{0,16},{4,20},{8,24},{12,28},{16,0},{20,4},{24,8},{28,12},{1,17},{... | collective-permute-start | bytes 393224 | tf_op jit(solution)/shard_map/ppermute | solution.py:244
  50.4 2.7 %collective-permute-start.6 = (f32[256,256]{1,0:T(8,128)}, f32[256,256]{1,0:T(8,128)}, u32[]{:S(2)}, u32[]{:S(2)}) collective-permute-start(f32[256,256]{1,0:T(8,128)} %bitcast.16), channel_id=1, source_target_pairs={{0,16},{4,20},{8,24},{12,28},{16,0},{20,4},{24,8},{28,12},{1,17},{... | collective-permute-start | bytes 786440 | tf_op jit(solution)/shard_map/ppermute | solution.py:244
  54.1 26.6 %all-to-all-done = f32[16,256,128]{2,1,0:T(8,128)S(1)} async-done(((f32[16,256,128]{2,1,0:T(8,128)}), f32[16,256,128]{2,1,0:T(8,128)S(1)}, u32[]{:S(2)}, u32[]{:S(2)}) %all-to-all-start) | async-done | bytes 2097184 | tf_op jit(solution)/shard_map/all_to_all | solution.py:267
  81.1 0.9 multiply_reduce_fusion.1
  82.1 1.3 subtract_multiply_fusion
  83.4 1.0 fusion.65
  84.4 1.3 fusion.36
  85.6 2.3 %divide_multiply_fusion = f32[2048,256]{1,0:T(8,128)S(1)} fusion(f32[2048,256]{1,0:T(8,128)S(1)} %fusion.36, f32[1,256,256]{2,1,0:T(8,128)} %param.18), kind=kOutput, calls=%fused_computation.31 | convolution fusion | flops 809500672 | bytes 4456448 | tf_op jit(solution)/shard_map/dot_general | solution.py:75
  88.5 1.0 fusion.76
  89.5 2.2 %fusion.22 = f32[2048,256]{1,0:T(8,128)S(1)} fusion(f32[256,256]{1,0:T(8,128)} %collective-permute-done.5, f32[2048,256]{1,0:T(8,128)S(1)} %fusion.76), kind=kOutput, calls=%fused_computation.25 | convolution fusion | flops 807403520 | bytes 4456448 | tf_op jit(solution)/shard_map/dot_general | solution.py:74
  91.8 2.2 %fusion.16 = f32[2048,256]{1,0:T(8,128)S(1)} fusion(f32[256,256]{1,0:T(8,128)} %collective-permute-done.6, f32[2048,256]{1,0:T(8,128)S(1)} %fusion.22), kind=kOutput, calls=%fused_computation.19 | convolution fusion | flops 807403520 | bytes 4456448 | tf_op jit(solution)/shard_map/dot_general | solution.py:75
  94.0 1.0 fusion.51
  95.0 2.2 %fusion.10 = f32[2048,128]{1,0:T(8,128)S(1)} fusion(f32[256,128]{1,0:T(8,128)} %collective-permute-done.7, f32[2048,256]{1,0:T(8,128)S(1)} %fusion.16), kind=kOutput, calls=%fused_computation.13 | convolution fusion | flops 404750336 | bytes 3276800 | tf_op jit(solution)/shard_map/dot_general | solution.py:76
  97.2 1.5 pad_maximum_fusion
  98.6 4.5 %all-to-all-start.1 = ((f32[16,256,128]{2,1,0:T(8,128)}), f32[16,256,128]{2,1,0:T(8,128)}, u32[]{:S(2)}, u32[]{:S(2)}) async-start(f32[16,256,128]{2,1,0:T(8,128)} %pad_maximum_fusion), calls=%async_computation.1 | async-start | bytes 4194304 | tf_op jit(solution)/shard_map/all_to_all | solution.py:290
  103.4 3.4 %broadcast_in_dim.42.c_ref = f32[72,136,128]{2,1,0:T(8,128)} broadcast(f32[72,136]{1,0:T(8,128)S(1)} %copy.28), dimensions={0,1} | broadcast | bytes 5052672 | tf_op jit(solution)/shard_map/broadcast_in_dim | solution.py:61
  106.8 15.3 %shard_map.105 = f32[64,128,128]{2,1,0:T(8,128)} custom-call(f32[64,128,128]{2,1,0:T(8,128)} %bitcast.86, f32[4,128,128]{2,1,0:T(8,128)} %copy-done.1, f32[4,128,128]{2,1,0:T(8,128)} %copy-done, f32[72,8,128]{2,1,0:T(8,128)} %pad_maximum_fusion.3.yh_ref, f32[72,136,128]{2,1,0:T(8,128)} %broadcast_in_dim.42.c_ref), custom_call_target="tpu_custom_call" | custom-call | tf_op jit(solution)/shard_map/pallas_call | solution.py:301
  122.1 10.8 %all-to-all-done.1 = f32[16,256,128]{2,1,0:T(8,128)} async-done(((f32[16,256,128]{2,1,0:T(8,128)}), f32[16,256,128]{2,1,0:T(8,128)}, u32[]{:S(2)}, u32[]{:S(2)}) %all-to-all-start.1) | async-done | bytes 2097184 | tf_op jit(solution)/shard_map/all_to_all | solution.py:290
  132.9 15.3 %shard_map.106 = (f32[64,64,128]{2,1,0:T(8,128)}, f32[64,64,128]{2,1,0:T(8,128)}) custom-call(s32[2048]{0:T(1024)} %fusion.57.slot_ref, s32[2048]{0:T(1024)} %act_ref.3, f32[4096,128]{1,0:T(8,128)} %bitcast.24.r_ref, f32[8192,128]{1,0:T(8,128)} %bitcast.87), custom_call_target="tpu_custom_call" | custom-call | tf_op jit(solution)/shard_map/pallas_call | solution.py:312
  (76 shorter events, 9.6 us)
Async XLA Ops:
  3.8 7.8 %copy-start.5 = (s32[2048,1]{0,1:T(1,128)S(1)}, s32[2048,1]{0,1:T(1,128)}, u32[]{:S(2)}) copy-start(s32[2048,1]{0,1:T(1,128)} %param.15) | copy-start | bytes 24580
  4.2 27.3 %collective-permute-start = (f32[129,4,128]{0,2,1:T(8,128)S(1)}, f32[129,4,128]{0,2,1:T(8,128)S(1)}, u32[]{:S(2)}, u32[]{:S(2)}) collective-permute-start(f32[129,4,128]{0,2,1:T(8,128)S(1)} %pad_maximum_fusion.1), channel_id=1, source_target_pairs={{0,4},{4,8},{8,12},{12,16},{16,20},{20,24},{24,28},{1,5},{5,9},{9,... | collective-permute-start | bytes 792584 | tf_op jit(solution)/shard_map/ppermute | solution.py:32
  9.7 21.7 %collective-permute-start.1 = (f32[129,4,128]{0,2,1:T(8,128)S(1)}, f32[129,4,128]{0,2,1:T(8,128)}, u32[]{:S(2)}, u32[]{:S(2)}) collective-permute-start(f32[129,4,128]{0,2,1:T(8,128)S(1)} %pad_maximum_fusion.2), channel_id=1, source_target_pairs={{4,0},{8,4},{12,8},{16,12},{20,16},{24,20},{28,24},{5,1},{9,5},{13... | collective-permute-start | bytes 792584 | tf_op jit(solution)/shard_map/ppermute | solution.py:33
  31.5 6.0 %copy-start.4 = (f32[64,128]{1,0:T(8,128)S(1)}, f32[64,128]{1,0:T(8,128)}, u32[]{:S(2)}) copy-start(f32[64,128]{1,0:T(8,128)} %param.13) | copy-start | bytes 98308
  31.5 49.3 %all-to-all-start = ((f32[16,256,128]{2,1,0:T(8,128)}), f32[16,256,128]{2,1,0:T(8,128)S(1)}, u32[]{:S(2)}, u32[]{:S(2)}) async-start(f32[16,256,128]{2,1,0:T(8,128)} %bitcast.89), calls=%async_computation | async-start | bytes 4194304 | tf_op jit(solution)/shard_map/all_to_all | solution.py:267
  41.4 1.4 copy-start
  41.4 1.4 copy-start.1
  41.5 5.9 %copy-start.3 = (f32[1,256,128]{2,1,0:T(8,128)S(1)}, f32[1,256,128]{2,1,0:T(8,128)}, u32[]{:S(2)}) copy-start(f32[1,256,128]{2,1,0:T(8,128)} %param.19) | copy-start | bytes 393220
  41.5 8.7 %copy-start.2 = (f32[1,128,256]{2,1,0:T(8,128)S(1)}, f32[1,128,256]{2,1,0:T(8,128)}, u32[]{:S(2)}) copy-start(f32[1,128,256]{2,1,0:T(8,128)} %param.16) | copy-start | bytes 393220
  41.5 11.6 %copy-start.6 = (f32[1,256,256]{2,1,0:T(8,128)S(1)}, f32[1,256,256]{2,1,0:T(8,128)}, u32[]{:S(2)}) copy-start(f32[1,256,256]{2,1,0:T(8,128)} %param.17) | copy-start | bytes 786436
  42.8 10.3 %collective-permute-start.2 = (f32[73,4,128]{2,1,0:T(4,128)S(1)}, f32[73,4,128]{2,1,0:T(4,128)S(1)}, u32[]{:S(2)}, u32[]{:S(2)}) collective-permute-start(f32[73,4,128]{2,1,0:T(4,128)S(1)} %get-tuple-element.77), channel_id=1, source_target_pairs={{1,0},{2,1},{3,2},{5,4},{6,5},{7,6},{9,8},{10,9},{11,10},{13,12},{... | collective-permute-start | bytes 448520 | tf_op jit(solution)/shard_map/ppermute | solution.py:54
  44.1 9.2 %collective-permute-start.3 = (f32[73,4,128]{2,1,0:T(4,128)S(1)}, f32[73,4,128]{2,1,0:T(4,128)S(1)}, u32[]{:S(2)}, u32[]{:S(2)}) collective-permute-start(f32[73,4,128]{2,1,0:T(4,128)S(1)} %get-tuple-element.78), channel_id=1, source_target_pairs={{0,1},{1,2},{2,3},{4,5},{5,6},{6,7},{8,9},{9,10},{10,11},{12,13},{... | collective-permute-start | bytes 448520 | tf_op jit(solution)/shard_map/ppermute | solution.py:53
  47.4 47.6 %collective-permute-start.7 = (f32[256,128]{1,0:T(8,128)S(1)}, f32[256,128]{1,0:T(8,128)}, u32[]{:S(2)}, u32[]{:S(2)}) collective-permute-start(f32[256,128]{1,0:T(8,128)S(1)} %bitcast.97), channel_id=1, source_target_pairs={{0,16},{4,20},{8,24},{12,28},{16,0},{20,4},{24,8},{28,12},{1,17},{... | collective-permute-start | bytes 393224 | tf_op jit(solution)/shard_map/ppermute | solution.py:244
  50.2 38.3 %collective-permute-start.4 = (f32[128,256]{1,0:T(8,128)S(1)}, f32[128,256]{1,0:T(8,128)S(1)}, u32[]{:S(2)}, u32[]{:S(2)}) collective-permute-start(f32[128,256]{1,0:T(8,128)S(1)} %bitcast.96), channel_id=1, source_target_pairs={{0,16},{4,20},{8,24},{12,28},{16,0},{20,4},{24,8},{28,12},{1,17},{... | collective-permute-start | bytes 393224 | tf_op jit(solution)/shard_map/ppermute | solution.py:244
  50.4 41.4 %collective-permute-start.6 = (f32[256,256]{1,0:T(8,128)}, f32[256,256]{1,0:T(8,128)}, u32[]{:S(2)}, u32[]{:S(2)}) collective-permute-start(f32[256,256]{1,0:T(8,128)} %bitcast.16), channel_id=1, source_target_pairs={{0,16},{4,20},{8,24},{12,28},{16,0},{20,4},{24,8},{28,12},{1,17},{... | collective-permute-start | bytes 786440 | tf_op jit(solution)/shard_map/ppermute | solution.py:244
  53.1 36.4 %collective-permute-start.5 = (f32[256,256]{1,0:T(8,128)S(1)}, f32[256,256]{1,0:T(8,128)}, u32[]{:S(2)}, u32[]{:S(2)}) collective-permute-start(f32[256,256]{1,0:T(8,128)S(1)} %bitcast.101), channel_id=1, source_target_pairs={{0,16},{4,20},{8,24},{12,28},{16,0},{20,4},{24,8},{28,12},{1,17},{... | collective-permute-start | bytes 786440 | tf_op jit(solution)/shard_map/ppermute | solution.py:244
  98.6 34.2 %all-to-all-start.1 = ((f32[16,256,128]{2,1,0:T(8,128)}), f32[16,256,128]{2,1,0:T(8,128)}, u32[]{:S(2)}, u32[]{:S(2)}) async-start(f32[16,256,128]{2,1,0:T(8,128)} %pad_maximum_fusion), calls=%async_computation.1 | async-start | bytes 4194304 | tf_op jit(solution)/shard_map/all_to_all | solution.py:290

commit v13 on v12

--- a/solution.py
+++ b/solution.py
@@ -233,7 +233,8 @@
     place = (target_tile % half_tiles) * inf_count + target % inf_count
     kind = (target_tile // half_tiles != my_half).astype(jnp.int32)
     pair_slots = 2 * capacity
-    slot_index = place * pair_slots + kind * capacity + ranks.reshape(-1).astype(jnp.int32)
+    group_size = half_tiles * inf_count
+    slot_index = (kind * group_size + place) * capacity + ranks.reshape(-1).astype(jnp.int32)
     groups = [
         [t * inf_count + i for t in range(h * half_tiles, (h + 1) * half_tiles) for i in range(inf_count)]
         for h in range(2)
@@ -264,37 +265,25 @@
     outgoing, x_from_before, x_from_after = lax.optimization_barrier(
         (outgoing, x_from_before, x_from_after)
     )
-    block = lax.all_to_all(
-        outgoing.reshape(group_size, pair_slots, features),
-        ("tile", "inf"),
-        split_axis=0,
-        concat_axis=0,
-        tiled=True,
-        axis_index_groups=groups,
-    )
-    block_shape = block.shape
+    exchange = lambda a: lax.all_to_all(
+        a, ("tile", "inf"), split_axis=0, concat_axis=0, tiled=True, axis_index_groups=groups
+    )
+    halves = outgoing.reshape(2, group_size, capacity, features)
+    block_own = exchange(halves[0])
+    block_other = exchange(halves[1])
     x_before, x_after, y_halo, coeff = stencil_finish(
         state_t, diffusivity, x_from_before, x_from_after, PASSES
     )
-    block, x_before, x_after, y_halo = lax.optimization_barrier(
-        (block, x_before, x_after, y_halo)
-    )
-    own_rows = standardize(block[:, :capacity].reshape(-1, features))
+    block_own, x_before, x_after, y_halo = lax.optimization_barrier(
+        (block_own, x_before, x_after, y_halo)
+    )
+    own_rows = standardize(block_own.reshape(-1, features))
     own = network_rows(own_rows, first_layer[0], second_layer[0], third_layer[0], last_layer[0])
-    other_rows = standardize(block[:, capacity:].reshape(-1, features))
+    returned_own = exchange(own.reshape(group_size, capacity, features))
+    other_rows = standardize(block_other.reshape(-1, features))
     other = network_rows(other_rows, *mirrored)
-    answered = jnp.concatenate(
-        [own.reshape(group_size, capacity, features), other.reshape(group_size, capacity, features)],
-        axis=1,
-    )
-    returned = lax.all_to_all(
-        answered,
-        ("tile", "inf"),
-        split_axis=0,
-        concat_axis=0,
-        tiled=True,
-        axis_index_groups=groups,
-    )
+    returned_other = exchange(other.reshape(group_size, capacity, features))
+    returned = jnp.concatenate([returned_own, returned_other], axis=0)
     returned_rows = returned.reshape(slot_total, features)
 
     rows_ext, ylen = coeff.shape[:2]

time: 149 us -> 172 us (1.15)
  waiting for transfers between devices: 38 us -> 47.1 us
  starting transfers between devices: 27.2 us -> 35.1 us
  matrix products: 14.2 us -> 17.1 us
    ppermute x4, waiting for transfers between devices: 0.01 us -> 28.4 us  [body(): lax.ppermute(w[0], 'tile', swap)]
    all_to_all x2 -> x4, waiting for transfers between devices: 37.4 us -> 18.1 us  [body(): lax.all_to_all(a, ('tile', 'inf'), split_axis=0, concat_axis=0, tiled=Tru...]
    all_to_all x2 -> x4, starting transfers between devices: 10.6 us -> 18.5 us  [body(): lax.all_to_all(a, ('tile', 'inf'), split_axis=0, concat_axis=0, tiled=Tru...]
    slice x0 -> x1, local copies, waits for them, and re-layouts: none -> 3 us  [body(): block_own = exchange(halves[0])]
    dot_general x2, matrix products: 3.19 us -> 5.13 us  [network_rows(): return jnp.dot(hidden, last_layer, precision=highest)]
  transfers between devices with their start and end apart: 10 -> 12, of which waited for: 3 -> 5; matrix products, arithmetic and copies ran while one was open for 19% -> 16% of each run, Pallas kernels for 21% -> 18%
where the time goes in v13:
time: 172 us; the launch traced here: 171 us
  waiting for transfers between devices  47.1 us (27%)
  Pallas kernels  46.5 us (27%)
  starting transfers between devices  35.1 us (20%)
  matrix products  17.1 us (10%)
  local copies, waits for them, and re-layouts  12.9 us (8%)
  other arithmetic  10.8 us (6%)
    ppermute x4, waiting for transfers between devices, body(): lax.ppermute(w[0], 'tile', swap)  28.4 us
    all_to_all x4, starting transfers between devices, body(): lax.all_to_all(a, ('tile', 'inf'), split_axis=0, concat_axis=0, tiled=Tru...  18.5 us
    all_to_all x4, waiting for transfers between devices, body(): lax.all_to_all(a, ('tile', 'inf'), split_axis=0, concat_axis=0, tiled=Tru...  18.1 us
    pallas_call x1, Pallas kernels, body(): pl.pallas_call(gather_kernel, out_shape=(jax.ShapeDtypeStruct((cells, fea...  16 us
    pallas_call x1, Pallas kernels, body(): pl.pallas_call(finish_kernel, out_shape=(jax.ShapeDtypeStruct(u_field.sha...  15.3 us
    pallas_call x1, Pallas kernels, body(): pl.pallas_call(diffuse_kernel, out_shape=jax.ShapeDtypeStruct((width_x, w...  15.3 us
    ppermute x4, starting transfers between devices, body(): lax.ppermute(w[0], 'tile', swap)  5.92 us
    dot_general x2, matrix products, network_rows(): return jnp.dot(hidden, last_layer, precision=highest)  5.13 us
  transfers between devices with their start and end apart: 12, of which 5 were waited for; matrix products, arithmetic and copies ran while one was open for 16% of the time, Pallas kernels for 18%

profile of v13, /device:TPU:0, one launch (start us, length us, event | category | flops | bytes accessed | tf_op | source)
XLA Modules:
  0.0 170.9 jit_solution(13351275059112635776)
XLA Ops:
  1.5 1.1 fusion.75
  2.7 1.1 fusion.76
  4.2 4.9 %collective-permute-start = (f32[129,4,128]{0,2,1:T(8,128)S(1)}, f32[129,4,128]{0,2,1:T(8,128)S(1)}, u32[]{:S(2)}, u32[]{:S(2)}) collective-permute-start(f32[129,4,128]{0,2,1:T(8,128)S(1)} %pad_maximum_fusion.1), channel_id=1, source_target_pairs={{0,4},{4,8},{8,12},{12,16},{16,20},{20,24},{24,28},{1,5},{5,9},{9,... | collective-permute-start | bytes 792584 | tf_op jit(solution)/shard_map/ppermute | solution.py:32
  9.7 1.3 collective-permute-start.1
  12.3 1.9 %while.13 = (s32[]{:T(128)}, f32[32]{0:T(128)S(1)}, f32[4,512]{1,0:T(4,128)S(1)}, bf16[4,512,32]{1,2,0:T(8,128)(2,1)S(1)}, s32[]{:T(128)}, /*index=5*/s32[]{:T(128)}) while((s32[]{:T(128)}, f32[32]{0:T(128)S(1)}, f32[4,512]{1,0:T(4,128)S(1)}, bf16[4,512,32]{1,2,0:T(8,128)(2,1)S(1)}, s32[]{:T(128)}, /*index=5*/s32[]{:T(128)}) %tuple.40), condition=%wide.region_3.4_spmd.clone, body=%wide.region_0.3_spmd.clone.sunk | while | flops 17399332 | bytes 106719 | solution.py:228
  14.9 16.0 %shard_map.104 = (f32[8192,128]{1,0:T(8,128)}, f32[4096,128]{1,0:T(8,128)}) custom-call(s32[2048]{0:T(1024)} %fusion.58.slot_ref, s32[2048]{0:T(1024)} %act_ref.3, f32[64,64,128]{2,1,0:T(8,128)} %u_hbm.1, f32[64,64,128]{2,1,0:T(8,128)} %v_hbm.1), custom_call_target="tpu_custom_call" | custom-call | tf_op jit(solution)/shard_map/pallas_call | solution.py:251
  31.5 3.0 %fusion.74 = (f32[2048,128]{1,0:T(8,128)}, f32[2048,128]{1,0:T(8,128)}) fusion(f32[4096,128]{1,0:T(8,128)} %get-tuple-element.40), kind=kLoop, calls=%fused_computation.117 | loop fusion | bytes 4194304 | tf_op jit(solution)/shard_map/slice | solution.py:272
  34.5 6.0 %all-to-all-start.2 = ((f32[16,128,128]{2,1,0:T(8,128)}), f32[16,128,128]{2,1,0:T(8,128)S(1)}, u32[]{:S(2)}, u32[]{:S(2)}) async-start(f32[16,128,128]{2,1,0:T(8,128)} %bitcast.20), calls=%async_computation.2 | async-start | bytes 2097152 | tf_op jit(solution)/shard_map/all_to_all | solution.py:268
  42.5 1.3 fusion.50
  43.8 1.4 collective-permute-start.2
  45.2 3.0 %collective-permute-start.3 = (f32[73,4,128]{2,1,0:T(4,128)S(1)}, f32[73,4,128]{2,1,0:T(4,128)S(1)}, u32[]{:S(2)}, u32[]{:S(2)}) collective-permute-start(f32[73,4,128]{2,1,0:T(4,128)S(1)} %get-tuple-element.76), channel_id=1, source_target_pairs={{0,1},{1,2},{2,3},{4,5},{5,6},{6,7},{8,9},{9,10},{10,11},{12,13},{... | collective-permute-start | bytes 448520 | tf_op jit(solution)/shard_map/ppermute | solution.py:53
  48.3 8.3 %all-to-all-done.2 = f32[16,128,128]{2,1,0:T(8,128)S(1)} async-done(((f32[16,128,128]{2,1,0:T(8,128)}), f32[16,128,128]{2,1,0:T(8,128)S(1)}, u32[]{:S(2)}, u32[]{:S(2)}) %all-to-all-start.2) | async-done | bytes 1048608 | tf_op jit(solution)/shard_map/all_to_all | solution.py:268
  56.6 3.7 %all-to-all-start = ((f32[16,128,128]{2,1,0:T(8,128)}), f32[16,128,128]{2,1,0:T(8,128)S(1)}, u32[]{:S(2)}, u32[]{:S(2)}) async-start(f32[16,128,128]{2,1,0:T(8,128)} %bitcast.3), calls=%async_computation | async-start | bytes 2097152 | tf_op jit(solution)/shard_map/all_to_all | solution.py:268
  60.3 2.6 %collective-permute-start.7 = (f32[256,128]{1,0:T(8,128)S(1)}, f32[256,128]{1,0:T(8,128)}, u32[]{:S(2)}, u32[]{:S(2)}) collective-permute-start(f32[256,128]{1,0:T(8,128)S(1)} %bitcast.97), channel_id=1, source_target_pairs={{0,16},{4,20},{8,24},{12,28},{16,0},{20,4},{24,8},{28,12},{1,17},{... | collective-permute-start | bytes 393224 | tf_op jit(solution)/shard_map/ppermute | solution.py:245
  63.3 2.6 %collective-permute-start.6 = (f32[256,256]{1,0:T(8,128)}, f32[256,256]{1,0:T(8,128)}, u32[]{:S(2)}, u32[]{:S(2)}) collective-permute-start(f32[256,256]{1,0:T(8,128)} %bitcast.102), channel_id=1, source_target_pairs={{0,16},{4,20},{8,24},{12,28},{16,0},{20,4},{24,8},{28,12},{1,17},{... | collective-permute-start | bytes 786440 | tf_op jit(solution)/shard_map/ppermute | solution.py:245
  68.6 9.8 %collective-permute-done.4 = f32[128,256]{1,0:T(8,128)S(1)} collective-permute-done((f32[128,256]{1,0:T(8,128)S(1)}, f32[128,256]{1,0:T(8,128)S(1)}, u32[]{:S(2)}, u32[]{:S(2)}) %collective-permute-start.4) | collective-permute-done | bytes 131104 | tf_op jit(solution)/shard_map/ppermute | solution.py:245
  78.5 1.0 fusion.77
  79.4 18.5 %collective-permute-done.5 = f32[256,256]{1,0:T(8,128)} collective-permute-done((f32[256,256]{1,0:T(8,128)S(1)}, f32[256,256]{1,0:T(8,128)}, u32[]{:S(2)}, u32[]{:S(2)}) %collective-permute-start.5) | collective-permute-done | bytes 262176 | tf_op jit(solution)/shard_map/ppermute | solution.py:245
  98.0 3.5 %fusion.22 = f32[2048,256]{1,0:T(8,128)} fusion(f32[256,256]{1,0:T(8,128)} %collective-permute-done.5, f32[2048,256]{1,0:T(8,128)S(1)} %fusion.77), kind=kOutput, calls=%fused_computation.25 | convolution fusion | flops 807403520 | bytes 4456448 | tf_op jit(solution)/shard_map/dot_general | solution.py:74
  101.9 2.9 %fusion.16 = f32[2048,256]{1,0:T(8,128)S(1)} fusion(f32[256,256]{1,0:T(8,128)} %collective-permute-done.6, f32[2048,256]{1,0:T(8,128)} %fusion.22), kind=kOutput, calls=%fused_computation.19 | convolution fusion | flops 807403520 | bytes 4456448 | tf_op jit(solution)/shard_map/dot_general | solution.py:75
  105.4 3.2 %fusion.10 = f32[2048,128]{1,0:T(8,128)} fusion(f32[256,128]{1,0:T(8,128)} %collective-permute-done.7, f32[2048,256]{1,0:T(8,128)S(1)} %fusion.16), kind=kOutput, calls=%fused_computation.13 | convolution fusion | flops 404750336 | bytes 3276800 | tf_op jit(solution)/shard_map/dot_general | solution.py:76
  108.5 4.5 %all-to-all-start.3 = ((f32[16,128,128]{2,1,0:T(8,128)}), f32[16,128,128]{2,1,0:T(8,128)}, u32[]{:S(2)}, u32[]{:S(2)}) async-start(f32[16,128,128]{2,1,0:T(8,128)} %bitcast.24), calls=%async_computation.3 | async-start | bytes 2097152 | tf_op jit(solution)/shard_map/all_to_all | solution.py:268
  113.7 1.0 fusion.65
  114.7 1.3 fusion.36
  116.0 1.3 divide_multiply_fusion
  117.3 2.0 %fusion.51 = f32[16,128,128]{2,1,0:T(8,128)} fusion(f32[16,128,256]{2,1,0:T(8,128)S(1)} %bitcast.91, f32[1,256,128]{2,1,0:T(8,128)S(1)} %copy-done.3), kind=kOutput, calls=%fused_computation.67 | convolution fusion | flops 402653184 | bytes 3276800 | tf_op jit(solution)/shard_map/dot_general | solution.py:76
  119.3 9.8 %all-to-all-done.3 = f32[16,128,128]{2,1,0:T(8,128)} async-done(((f32[16,128,128]{2,1,0:T(8,128)}), f32[16,128,128]{2,1,0:T(8,128)}, u32[]{:S(2)}, u32[]{:S(2)}) %all-to-all-start.3) | async-done | bytes 1048608 | tf_op jit(solution)/shard_map/all_to_all | solution.py:268
  129.1 4.3 %all-to-all-start.1 = ((f32[16,128,128]{2,1,0:T(8,128)}), f32[16,128,128]{2,1,0:T(8,128)}, u32[]{:S(2)}, u32[]{:S(2)}) async-start(f32[16,128,128]{2,1,0:T(8,128)} %fusion.51), calls=%async_computation.1 | async-start | bytes 2097152 | tf_op jit(solution)/shard_map/all_to_all | solution.py:268
  133.7 3.4 %broadcast_in_dim.42.c_ref = f32[72,136,128]{2,1,0:T(8,128)} broadcast(f32[72,136]{1,0:T(8,128)S(1)} %copy.28), dimensions={0,1} | broadcast | bytes 5052672 | tf_op jit(solution)/shard_map/broadcast_in_dim | solution.py:61
  137.1 15.3 %shard_map.105 = f32[64,128,128]{2,1,0:T(8,128)} custom-call(f32[64,128,128]{2,1,0:T(8,128)} %bitcast.87, f32[4,128,128]{2,1,0:T(8,128)} %copy-done.1, f32[4,128,128]{2,1,0:T(8,128)} %copy-done, f32[72,8,128]{2,1,0:T(8,128)} %pad_maximum_fusion.3.yh_ref, f32[72,136,128]{2,1,0:T(8,128)} %broadcast_in_dim.42.c_ref), custom_call_target="tpu_custom_call" | custom-call | tf_op jit(solution)/shard_map/pallas_call | solution.py:290
  152.3 3.1 %pad_maximum_fusion = f32[32,128,128]{2,1,0:T(8,128)} fusion(f32[16,128,128]{2,1,0:T(8,128)} %all-to-all-done.3, f32[16,128,128]{2,1,0:T(8,128)} %all-to-all-done.1), kind=kLoop, calls=%fused_computation.12 | loop fusion | flops 524288 | bytes 4194304 | tf_op jit(solution)/shard_map/concatenate | solution.py:286
  155.4 15.3 %shard_map.106 = (f32[64,64,128]{2,1,0:T(8,128)}, f32[64,64,128]{2,1,0:T(8,128)}) custom-call(s32[2048]{0:T(1024)} %fusion.58.slot_ref, s32[2048]{0:T(1024)} %act_ref.3, f32[4096,128]{1,0:T(8,128)} %bitcast.89, f32[8192,128]{1,0:T(8,128)} %bitcast.88), custom_call_target="tpu_custom_call" | custom-call | tf_op jit(solution)/shard_map/pallas_call | solution.py:301
  (85 shorter events, 13.2 us)
Async XLA Ops:
  3.8 7.8 %copy-start.5 = (s32[2048,1]{0,1:T(1,128)S(1)}, s32[2048,1]{0,1:T(1,128)}, u32[]{:S(2)}) copy-start(s32[2048,1]{0,1:T(1,128)} %param.15) | copy-start | bytes 24580
  4.2 27.3 %collective-permute-start = (f32[129,4,128]{0,2,1:T(8,128)S(1)}, f32[129,4,128]{0,2,1:T(8,128)S(1)}, u32[]{:S(2)}, u32[]{:S(2)}) collective-permute-start(f32[129,4,128]{0,2,1:T(8,128)S(1)} %pad_maximum_fusion.1), channel_id=1, source_target_pairs={{0,4},{4,8},{8,12},{12,16},{16,20},{20,24},{24,28},{1,5},{5,9},{9,... | collective-permute-start | bytes 792584 | tf_op jit(solution)/shard_map/ppermute | solution.py:32
  9.7 21.7 %collective-permute-start.1 = (f32[129,4,128]{0,2,1:T(8,128)S(1)}, f32[129,4,128]{0,2,1:T(8,128)S(1)}, u32[]{:S(2)}, u32[]{:S(2)}) collective-permute-start(f32[129,4,128]{0,2,1:T(8,128)S(1)} %pad_maximum_fusion.2), channel_id=1, source_target_pairs={{4,0},{8,4},{12,8},{16,12},{20,16},{24,20},{28,24},{5,1},{9,5},{13... | collective-permute-start | bytes 792584 | tf_op jit(solution)/shard_map/ppermute | solution.py:33
  34.5 6.0 %copy-start.4 = (f32[64,128]{1,0:T(8,128)S(1)}, f32[64,128]{1,0:T(8,128)}, u32[]{:S(2)}) copy-start(f32[64,128]{1,0:T(8,128)} %param.13) | copy-start | bytes 98308
  34.5 22.1 %all-to-all-start.2 = ((f32[16,128,128]{2,1,0:T(8,128)}), f32[16,128,128]{2,1,0:T(8,128)S(1)}, u32[]{:S(2)}, u32[]{:S(2)}) async-start(f32[16,128,128]{2,1,0:T(8,128)} %bitcast.20), calls=%async_computation.2 | async-start | bytes 2097152 | tf_op jit(solution)/shard_map/all_to_all | solution.py:268
  42.5 1.3 copy-start
  42.5 1.3 copy-start.1
  43.8 16.5 %copy-start.3 = (f32[1,256,128]{2,1,0:T(8,128)S(1)}, f32[1,256,128]{2,1,0:T(8,128)}, u32[]{:S(2)}) copy-start(f32[1,256,128]{2,1,0:T(8,128)} %param.19) | copy-start | bytes 393220
  43.8 19.1 %copy-start.2 = (f32[1,128,256]{2,1,0:T(8,128)S(1)}, f32[1,128,256]{2,1,0:T(8,128)}, u32[]{:S(2)}) copy-start(f32[1,128,256]{2,1,0:T(8,128)} %param.16) | copy-start | bytes 393220
  43.8 22.0 %copy-start.6 = (f32[1,256,256]{2,1,0:T(8,128)S(1)}, f32[1,256,256]{2,1,0:T(8,128)}, u32[]{:S(2)}) copy-start(f32[1,256,256]{2,1,0:T(8,128)} %param.17) | copy-start | bytes 786436
  43.8 22.0 %collective-permute-start.2 = (f32[73,4,128]{2,1,0:T(4,128)S(1)}, f32[73,4,128]{2,1,0:T(4,128)S(1)}, u32[]{:S(2)}, u32[]{:S(2)}) collective-permute-start(f32[73,4,128]{2,1,0:T(4,128)S(1)} %get-tuple-element.75), channel_id=1, source_target_pairs={{1,0},{2,1},{3,2},{5,4},{6,5},{7,6},{9,8},{10,9},{11,10},{13,12},{... | collective-permute-start | bytes 448520 | tf_op jit(solution)/shard_map/ppermute | solution.py:54
  45.2 21.0 %collective-permute-start.3 = (f32[73,4,128]{2,1,0:T(4,128)S(1)}, f32[73,4,128]{2,1,0:T(4,128)S(1)}, u32[]{:S(2)}, u32[]{:S(2)}) collective-permute-start(f32[73,4,128]{2,1,0:T(4,128)S(1)} %get-tuple-element.76), channel_id=1, source_target_pairs={{0,1},{1,2},{2,3},{4,5},{5,6},{6,7},{8,9},{9,10},{10,11},{12,13},{... | collective-permute-start | bytes 448520 | tf_op jit(solution)/shard_map/ppermute | solution.py:53
  56.6 44.9 %all-to-all-start = ((f32[16,128,128]{2,1,0:T(8,128)}), f32[16,128,128]{2,1,0:T(8,128)S(1)}, u32[]{:S(2)}, u32[]{:S(2)}) async-start(f32[16,128,128]{2,1,0:T(8,128)} %bitcast.3), calls=%async_computation | async-start | bytes 2097152 | tf_op jit(solution)/shard_map/all_to_all | solution.py:268
  60.3 45.1 %collective-permute-start.7 = (f32[256,128]{1,0:T(8,128)S(1)}, f32[256,128]{1,0:T(8,128)}, u32[]{:S(2)}, u32[]{:S(2)}) collective-permute-start(f32[256,128]{1,0:T(8,128)S(1)} %bitcast.97), channel_id=1, source_target_pairs={{0,16},{4,20},{8,24},{12,28},{16,0},{20,4},{24,8},{28,12},{1,17},{... | collective-permute-start | bytes 393224 | tf_op jit(solution)/shard_map/ppermute | solution.py:245
  62.9 15.5 %collective-permute-start.4 = (f32[128,256]{1,0:T(8,128)S(1)}, f32[128,256]{1,0:T(8,128)S(1)}, u32[]{:S(2)}, u32[]{:S(2)}) collective-permute-start(f32[128,256]{1,0:T(8,128)S(1)} %bitcast.96), channel_id=1, source_target_pairs={{0,16},{4,20},{8,24},{12,28},{16,0},{20,4},{24,8},{28,12},{1,17},{... | collective-permute-start | bytes 393224 | tf_op jit(solution)/shard_map/ppermute | solution.py:245
  63.3 38.6 %collective-permute-start.6 = (f32[256,256]{1,0:T(8,128)}, f32[256,256]{1,0:T(8,128)}, u32[]{:S(2)}, u32[]{:S(2)}) collective-permute-start(f32[256,256]{1,0:T(8,128)} %bitcast.102), channel_id=1, source_target_pairs={{0,16},{4,20},{8,24},{12,28},{16,0},{20,4},{24,8},{28,12},{1,17},{... | collective-permute-start | bytes 786440 | tf_op jit(solution)/shard_map/ppermute | solution.py:245
  65.8 32.1 %collective-permute-start.5 = (f32[256,256]{1,0:T(8,128)S(1)}, f32[256,256]{1,0:T(8,128)}, u32[]{:S(2)}, u32[]{:S(2)}) collective-permute-start(f32[256,256]{1,0:T(8,128)S(1)} %bitcast.101), channel_id=1, source_target_pairs={{0,16},{4,20},{8,24},{12,28},{16,0},{20,4},{24,8},{28,12},{1,17},{... | collective-permute-start | bytes 786440 | tf_op jit(solution)/shard_map/ppermute | solution.py:245
  108.5 20.5 %all-to-all-start.3 = ((f32[16,128,128]{2,1,0:T(8,128)}), f32[16,128,128]{2,1,0:T(8,128)}, u32[]{:S(2)}, u32[]{:S(2)}) async-start(f32[16,128,128]{2,1,0:T(8,128)} %bitcast.24), calls=%async_computation.3 | async-start | bytes 2097152 | tf_op jit(solution)/shard_map/all_to_all | solution.py:268
  114.7 1.3 copy-start.7
  129.1 23.3 %all-to-all-start.1 = ((f32[16,128,128]{2,1,0:T(8,128)}), f32[16,128,128]{2,1,0:T(8,128)}, u32[]{:S(2)}, u32[]{:S(2)}) async-start(f32[16,128,128]{2,1,0:T(8,128)} %fusion.51), calls=%async_computation.1 | async-start | bytes 2097152 | tf_op jit(solution)/shard_map/all_to_all | solution.py:268

commit v14 on v12

--- a/solution.py
+++ b/solution.py
@@ -114,6 +114,13 @@
         return carry
 
     lax.fori_loop(0, act_ref.shape[0], place, 0, unroll=8)
+
+    def normalize(k, carry):
+        at = pl.ds(pl.multiple_of(k * chunk, chunk), chunk)
+        o_ref[at, :] = standardize(o_ref[at, :])
+        return carry
+
+    lax.fori_loop(0, o_ref.shape[0] // chunk, normalize, 0)
 
 
 def diffuse_kernel(st_ref, xb_ref, xa_ref, yh_ref, c_ref, f_ref, e_ref, a_ref):
@@ -279,9 +286,9 @@
     block, x_before, x_after, y_halo = lax.optimization_barrier(
         (block, x_before, x_after, y_halo)
     )
-    own_rows = standardize(block[:, :capacity].reshape(-1, features))
+    own_rows = block[:, :capacity].reshape(-1, features)
     own = network_rows(own_rows, first_layer[0], second_layer[0], third_layer[0], last_layer[0])
-    other_rows = standardize(block[:, capacity:].reshape(-1, features))
+    other_rows = block[:, capacity:].reshape(-1, features)
     other = network_rows(other_rows, *mirrored)
     answered = jnp.concatenate(
         [own.reshape(group_size, capacity, features), other.reshape(group_size, capacity, features)],

time: 149 us -> 151 us (1.013)
  Pallas kernels: 46.5 us -> 52.1 us
  other arithmetic: 9.19 us -> 6.01 us
    pallas_call x1, Pallas kernels: 16 us -> 21.5 us  [body(): pl.pallas_call(gather_kernel, out_shape=(jax.ShapeDtypeStruct((cells, fea...]
    mul x2 -> x0, other arithmetic: 1.91 us -> none  [standardize(): return (rows - center) * lax.rsqrt(spread + 1e-05)]
  transfers between devices with their start and end apart: 10 -> 10, of which waited for: 3 -> 2; matrix products, arithmetic and copies ran while one was open for 19% -> 17% of each run, Pallas kernels for 21% -> 24%
where the time goes in v14:
time: 151 us
  Pallas kernels  52.1 us (35%)
  waiting for transfers between devices  36.9 us (24%)
  starting transfers between devices  27.8 us (18%)
  matrix products  14.2 us (9%)
  local copies, waits for them, and re-layouts  12 us (8%)
  other arithmetic  6.01 us (4%)
    all_to_all x1, waiting for transfers between devices, body(): lax.all_to_all(outgoing.reshape(group_size, pair_slots, features), ('tile...  26.1 us
    pallas_call x1, Pallas kernels, body(): pl.pallas_call(gather_kernel, out_shape=(jax.ShapeDtypeStruct((cells, fea...  21.5 us
    pallas_call x1, Pallas kernels, body(): pl.pallas_call(finish_kernel, out_shape=(jax.ShapeDtypeStruct(u_field.sha...  15.3 us
    pallas_call x1, Pallas kernels, body(): pl.pallas_call(diffuse_kernel, out_shape=jax.ShapeDtypeStruct((width_x, w...  15.3 us
    all_to_all x1, waiting for transfers between devices, body(): lax.all_to_all(answered, ('tile', 'inf'), split_axis=0, concat_axis=0, ti...  10.8 us
    ppermute x4, starting transfers between devices, body(): lax.ppermute(w[0], 'tile', swap)  6.45 us
    all_to_all x1, starting transfers between devices, body(): lax.all_to_all(outgoing.reshape(group_size, pair_slots, features), ('tile...  5.97 us
    ppermute x1, starting transfers between devices, stencil_start(): before = lax.ppermute(x_piece(width_x - depth), 'tile', up)  4.9 us
  transfers between devices with their start and end apart: 10, of which 2 were waited for; matrix products, arithmetic and copies ran while one was open for 17% of the time, Pallas kernels for 24%

profile of v14, /device:TPU:0, one launch (start us, length us, event | category | flops | bytes accessed | tf_op | source)
XLA Modules:
  0.0 150.5 jit_solution(6807453838770488463)
XLA Ops:
  1.5 1.1 fusion.73
  2.7 1.1 fusion.74
  4.2 4.9 %collective-permute-start = (f32[129,4,128]{0,2,1:T(8,128)S(1)}, f32[129,4,128]{0,2,1:T(8,128)S(1)}, u32[]{:S(2)}, u32[]{:S(2)}) collective-permute-start(f32[129,4,128]{0,2,1:T(8,128)S(1)} %pad_maximum_fusion.1), channel_id=1, source_target_pairs={{0,4},{4,8},{8,12},{12,16},{16,20},{20,24},{24,28},{1,5},{5,9},{9,... | collective-permute-start | bytes 792584 | tf_op jit(solution)/shard_map/ppermute | solution.py:32
  9.7 1.3 collective-permute-start.1
  12.3 1.9 %while.13 = (s32[]{:T(128)}, f32[32]{0:T(128)S(1)}, f32[4,512]{1,0:T(4,128)S(1)}, bf16[4,512,32]{1,2,0:T(8,128)(2,1)S(1)}, s32[]{:T(128)}, /*index=5*/s32[]{:T(128)}) while((s32[]{:T(128)}, f32[32]{0:T(128)S(1)}, f32[4,512]{1,0:T(4,128)S(1)}, bf16[4,512,32]{1,2,0:T(8,128)(2,1)S(1)}, s32[]{:T(128)}, /*index=5*/s32[]{:T(128)}) %tuple.39), condition=%wide.region_3.4_spmd.clone, body=%wide.region_0.3_spmd.clone.sunk | while | flops 17399332 | bytes 106719 | solution.py:235
  14.9 21.5 %shard_map.104 = (f32[8192,128]{1,0:T(8,128)}, f32[4096,128]{1,0:T(8,128)}) custom-call(s32[2048]{0:T(1024)} %fusion.56.slot_ref, s32[2048]{0:T(1024)} %act_ref.3, f32[64,64,128]{2,1,0:T(8,128)} %u_hbm.1, f32[64,64,128]{2,1,0:T(8,128)} %v_hbm.1), custom_call_target="tpu_custom_call" | custom-call | tf_op jit(solution)/shard_map/pallas_call | solution.py:257
  36.5 6.0 %all-to-all-start = ((f32[16,256,128]{2,1,0:T(8,128)}), f32[16,256,128]{2,1,0:T(8,128)S(1)}, u32[]{:S(2)}, u32[]{:S(2)}) async-start(f32[16,256,128]{2,1,0:T(8,128)} %bitcast.83), calls=%async_computation | async-start | bytes 4194304 | tf_op jit(solution)/shard_map/all_to_all | solution.py:274
  42.6 0.9 copy.29
  43.5 1.0 slice.70
  44.4 0.9 copy.30
  45.4 1.0 slice_bitcast_fusion
  46.4 1.3 fusion.49
  47.8 1.3 collective-permute-start.2
  49.1 3.2 %collective-permute-start.3 = (f32[73,4,128]{2,1,0:T(4,128)S(1)}, f32[73,4,128]{2,1,0:T(4,128)S(1)}, u32[]{:S(2)}, u32[]{:S(2)}) collective-permute-start(f32[73,4,128]{2,1,0:T(4,128)S(1)} %get-tuple-element.76), channel_id=1, source_target_pairs={{0,1},{1,2},{2,3},{4,5},{5,6},{6,7},{8,9},{9,10},{10,11},{12,13},{... | collective-permute-start | bytes 448520 | tf_op jit(solution)/shard_map/ppermute | solution.py:53
  52.3 3.4 %collective-permute-start.7 = (f32[256,128]{1,0:T(8,128)S(1)}, f32[256,128]{1,0:T(8,128)}, u32[]{:S(2)}, u32[]{:S(2)}) collective-permute-start(f32[256,128]{1,0:T(8,128)S(1)} %bitcast.91), channel_id=1, source_target_pairs={{0,16},{4,20},{8,24},{12,28},{16,0},{20,4},{24,8},{28,12},{1,17},{... | collective-permute-start | bytes 393224 | tf_op jit(solution)/shard_map/ppermute | solution.py:251
  55.9 2.8 %collective-permute-start.6 = (f32[256,256]{1,0:T(8,128)}, f32[256,256]{1,0:T(8,128)}, u32[]{:S(2)}, u32[]{:S(2)}) collective-permute-start(f32[256,256]{1,0:T(8,128)} %bitcast.16), channel_id=1, source_target_pairs={{0,16},{4,20},{8,24},{12,28},{16,0},{20,4},{24,8},{28,12},{1,17},{... | collective-permute-start | bytes 786440 | tf_op jit(solution)/shard_map/ppermute | solution.py:251
  58.8 0.8 pad_maximum_fusion.3.yh_ref
  59.6 26.1 %all-to-all-done = f32[16,256,128]{2,1,0:T(8,128)S(1)} async-done(((f32[16,256,128]{2,1,0:T(8,128)}), f32[16,256,128]{2,1,0:T(8,128)S(1)}, u32[]{:S(2)}, u32[]{:S(2)}) %all-to-all-start) | async-done | bytes 2097184 | tf_op jit(solution)/shard_map/all_to_all | solution.py:274
  85.9 1.0 fusion.64
  86.9 1.3 fusion.36
  88.2 2.3 %divide_multiply_fusion = f32[2048,256]{1,0:T(8,128)S(1)} fusion(f32[2048,256]{1,0:T(8,128)S(1)} %fusion.36, f32[1,256,256]{2,1,0:T(8,128)} %param.18), kind=kOutput, calls=%fused_computation.31 | convolution fusion | flops 809500672 | bytes 4456448 | tf_op jit(solution)/shard_map/dot_general | solution.py:75
  90.5 1.0 fusion.75
  91.5 2.2 %fusion.22 = f32[2048,256]{1,0:T(8,128)S(1)} fusion(f32[256,256]{1,0:T(8,128)} %collective-permute-done.5, f32[2048,256]{1,0:T(8,128)S(1)} %fusion.75), kind=kOutput, calls=%fused_computation.25 | convolution fusion | flops 807403520 | bytes 4456448 | tf_op jit(solution)/shard_map/dot_general | solution.py:74
  93.7 2.2 %fusion.16 = f32[2048,256]{1,0:T(8,128)S(1)} fusion(f32[256,256]{1,0:T(8,128)} %collective-permute-done.6, f32[2048,256]{1,0:T(8,128)S(1)} %fusion.22), kind=kOutput, calls=%fused_computation.19 | convolution fusion | flops 807403520 | bytes 4456448 | tf_op jit(solution)/shard_map/dot_general | solution.py:75
  95.9 1.0 fusion.50
  96.9 2.2 %fusion.10 = f32[2048,128]{1,0:T(8,128)S(1)} fusion(f32[256,128]{1,0:T(8,128)} %collective-permute-done.7, f32[2048,256]{1,0:T(8,128)S(1)} %fusion.16), kind=kOutput, calls=%fused_computation.13 | convolution fusion | flops 404750336 | bytes 3276800 | tf_op jit(solution)/shard_map/dot_general | solution.py:76
  99.1 1.5 pad_maximum_fusion
  100.6 4.7 %all-to-all-start.1 = ((f32[16,256,128]{2,1,0:T(8,128)}), f32[16,256,128]{2,1,0:T(8,128)}, u32[]{:S(2)}, u32[]{:S(2)}) async-start(f32[16,256,128]{2,1,0:T(8,128)} %pad_maximum_fusion), calls=%async_computation.1 | async-start | bytes 4194304 | tf_op jit(solution)/shard_map/all_to_all | solution.py:297
  105.5 3.4 %broadcast_in_dim.38.c_ref = f32[72,136,128]{2,1,0:T(8,128)} broadcast(f32[72,136]{1,0:T(8,128)S(1)} %copy.28), dimensions={0,1} | broadcast | bytes 5052672 | tf_op jit(solution)/shard_map/broadcast_in_dim | solution.py:61
  108.9 15.3 %shard_map.105 = f32[64,128,128]{2,1,0:T(8,128)} custom-call(f32[64,128,128]{2,1,0:T(8,128)} %bitcast.79, f32[4,128,128]{2,1,0:T(8,128)} %copy-done.1, f32[4,128,128]{2,1,0:T(8,128)} %copy-done, f32[72,8,128]{2,1,0:T(8,128)} %pad_maximum_fusion.3.yh_ref, f32[72,136,128]{2,1,0:T(8,128)} %broadcast_in_dim.38.c_ref), custom_call_target="tpu_custom_call" | custom-call | tf_op jit(solution)/shard_map/pallas_call | solution.py:308
  124.2 10.8 %all-to-all-done.1 = f32[16,256,128]{2,1,0:T(8,128)} async-done(((f32[16,256,128]{2,1,0:T(8,128)}), f32[16,256,128]{2,1,0:T(8,128)}, u32[]{:S(2)}, u32[]{:S(2)}) %all-to-all-start.1) | async-done | bytes 2097184 | tf_op jit(solution)/shard_map/all_to_all | solution.py:297
  135.0 15.3 %shard_map.106 = (f32[64,64,128]{2,1,0:T(8,128)}, f32[64,64,128]{2,1,0:T(8,128)}) custom-call(s32[2048]{0:T(1024)} %fusion.56.slot_ref, s32[2048]{0:T(1024)} %act_ref.3, f32[4096,128]{1,0:T(8,128)} %bitcast.22.r_ref, f32[8192,128]{1,0:T(8,128)} %bitcast.80), custom_call_target="tpu_custom_call" | custom-call | tf_op jit(solution)/shard_map/pallas_call | solution.py:319
  (69 shorter events, 6.5 us)
Async XLA Ops:
  3.8 7.8 %copy-start.5 = (s32[2048,1]{0,1:T(1,128)S(1)}, s32[2048,1]{0,1:T(1,128)}, u32[]{:S(2)}) copy-start(s32[2048,1]{0,1:T(1,128)} %param.15) | copy-start | bytes 24580
  4.2 32.3 %collective-permute-start = (f32[129,4,128]{0,2,1:T(8,128)S(1)}, f32[129,4,128]{0,2,1:T(8,128)S(1)}, u32[]{:S(2)}, u32[]{:S(2)}) collective-permute-start(f32[129,4,128]{0,2,1:T(8,128)S(1)} %pad_maximum_fusion.1), channel_id=1, source_target_pairs={{0,4},{4,8},{8,12},{12,16},{16,20},{20,24},{24,28},{1,5},{5,9},{9,... | collective-permute-start | bytes 792584 | tf_op jit(solution)/shard_map/ppermute | solution.py:32
  9.7 26.7 %collective-permute-start.1 = (f32[129,4,128]{0,2,1:T(8,128)S(1)}, f32[129,4,128]{0,2,1:T(8,128)}, u32[]{:S(2)}, u32[]{:S(2)}) collective-permute-start(f32[129,4,128]{0,2,1:T(8,128)S(1)} %pad_maximum_fusion.2), channel_id=1, source_target_pairs={{4,0},{8,4},{12,8},{16,12},{20,16},{24,20},{28,24},{5,1},{9,5},{13... | collective-permute-start | bytes 792584 | tf_op jit(solution)/shard_map/ppermute | solution.py:33
  36.5 6.0 %copy-start.4 = (f32[64,128]{1,0:T(8,128)S(1)}, f32[64,128]{1,0:T(8,128)}, u32[]{:S(2)}) copy-start(f32[64,128]{1,0:T(8,128)} %param.13) | copy-start | bytes 98308
  36.5 49.3 %all-to-all-start = ((f32[16,256,128]{2,1,0:T(8,128)}), f32[16,256,128]{2,1,0:T(8,128)S(1)}, u32[]{:S(2)}, u32[]{:S(2)}) async-start(f32[16,256,128]{2,1,0:T(8,128)} %bitcast.83), calls=%async_computation | async-start | bytes 4194304 | tf_op jit(solution)/shard_map/all_to_all | solution.py:274
  46.4 1.4 copy-start
  46.4 1.4 copy-start.1
  46.4 5.9 %copy-start.3 = (f32[1,256,128]{2,1,0:T(8,128)S(1)}, f32[1,256,128]{2,1,0:T(8,128)}, u32[]{:S(2)}) copy-start(f32[1,256,128]{2,1,0:T(8,128)} %param.19) | copy-start | bytes 393220
  46.4 9.4 %copy-start.2 = (f32[1,128,256]{2,1,0:T(8,128)S(1)}, f32[1,128,256]{2,1,0:T(8,128)}, u32[]{:S(2)}) copy-start(f32[1,128,256]{2,1,0:T(8,128)} %param.16) | copy-start | bytes 393220
  46.4 12.3 %copy-start.6 = (f32[1,256,256]{2,1,0:T(8,128)S(1)}, f32[1,256,256]{2,1,0:T(8,128)}, u32[]{:S(2)}) copy-start(f32[1,256,256]{2,1,0:T(8,128)} %param.17) | copy-start | bytes 786436
  47.8 10.9 %collective-permute-start.2 = (f32[73,4,128]{2,1,0:T(4,128)S(1)}, f32[73,4,128]{2,1,0:T(4,128)S(1)}, u32[]{:S(2)}, u32[]{:S(2)}) collective-permute-start(f32[73,4,128]{2,1,0:T(4,128)S(1)} %get-tuple-element.75), channel_id=1, source_target_pairs={{1,0},{2,1},{3,2},{5,4},{6,5},{7,6},{9,8},{10,9},{11,10},{13,12},{... | collective-permute-start | bytes 448520 | tf_op jit(solution)/shard_map/ppermute | solution.py:54
  49.1 9.7 %collective-permute-start.3 = (f32[73,4,128]{2,1,0:T(4,128)S(1)}, f32[73,4,128]{2,1,0:T(4,128)S(1)}, u32[]{:S(2)}, u32[]{:S(2)}) collective-permute-start(f32[73,4,128]{2,1,0:T(4,128)S(1)} %get-tuple-element.76), channel_id=1, source_target_pairs={{0,1},{1,2},{2,3},{4,5},{5,6},{6,7},{8,9},{9,10},{10,11},{12,13},{... | collective-permute-start | bytes 448520 | tf_op jit(solution)/shard_map/ppermute | solution.py:53
  52.3 44.6 %collective-permute-start.7 = (f32[256,128]{1,0:T(8,128)S(1)}, f32[256,128]{1,0:T(8,128)}, u32[]{:S(2)}, u32[]{:S(2)}) collective-permute-start(f32[256,128]{1,0:T(8,128)S(1)} %bitcast.91), channel_id=1, source_target_pairs={{0,16},{4,20},{8,24},{12,28},{16,0},{20,4},{24,8},{28,12},{1,17},{... | collective-permute-start | bytes 393224 | tf_op jit(solution)/shard_map/ppermute | solution.py:251
  55.8 34.7 %collective-permute-start.4 = (f32[128,256]{1,0:T(8,128)S(1)}, f32[128,256]{1,0:T(8,128)S(1)}, u32[]{:S(2)}, u32[]{:S(2)}) collective-permute-start(f32[128,256]{1,0:T(8,128)S(1)} %bitcast.90), channel_id=1, source_target_pairs={{0,16},{4,20},{8,24},{12,28},{16,0},{20,4},{24,8},{28,12},{1,17},{... | collective-permute-start | bytes 393224 | tf_op jit(solution)/shard_map/ppermute | solution.py:251
  55.9 37.8 %collective-permute-start.6 = (f32[256,256]{1,0:T(8,128)}, f32[256,256]{1,0:T(8,128)}, u32[]{:S(2)}, u32[]{:S(2)}) collective-permute-start(f32[256,256]{1,0:T(8,128)} %bitcast.16), channel_id=1, source_target_pairs={{0,16},{4,20},{8,24},{12,28},{16,0},{20,4},{24,8},{28,12},{1,17},{... | collective-permute-start | bytes 786440 | tf_op jit(solution)/shard_map/ppermute | solution.py:251
  58.7 32.8 %collective-permute-start.5 = (f32[256,256]{1,0:T(8,128)S(1)}, f32[256,256]{1,0:T(8,128)}, u32[]{:S(2)}, u32[]{:S(2)}) collective-permute-start(f32[256,256]{1,0:T(8,128)S(1)} %bitcast.95), channel_id=1, source_target_pairs={{0,16},{4,20},{8,24},{12,28},{16,0},{20,4},{24,8},{28,12},{1,17},{... | collective-permute-start | bytes 786440 | tf_op jit(solution)/shard_map/ppermute | solution.py:251
  100.6 34.4 %all-to-all-start.1 = ((f32[16,256,128]{2,1,0:T(8,128)}), f32[16,256,128]{2,1,0:T(8,128)}, u32[]{:S(2)}, u32[]{:S(2)}) async-start(f32[16,256,128]{2,1,0:T(8,128)} %pad_maximum_fusion), calls=%async_computation.1 | async-start | bytes 4194304 | tf_op jit(solution)/shard_map/all_to_all | solution.py:297

commit v15 on v12

--- a/solution.py
+++ b/solution.py
@@ -19,7 +19,7 @@
     return before, after
 
 
-def stencil_start(u_field, v_field, diffusivity, depth):
+def stencil_start(u_field, v_field, diffusivity, depth, after_this):
     width_x = u_field.shape[1]
 
     def x_piece(start):
@@ -29,9 +29,12 @@
     tile_count = lax.axis_size("tile")
     up = [(i, i + 1) for i in range(tile_count - 1)]
     down = [(j, i) for i, j in up]
-    before = lax.ppermute(x_piece(width_x - depth), "tile", up)
-    after = lax.ppermute(x_piece(0), "tile", down)
-    return before, after
+    after_this, last, first = lax.optimization_barrier(
+        (after_this, x_piece(width_x - depth), x_piece(0))
+    )
+    before = lax.ppermute(last, "tile", up)
+    after = lax.ppermute(first, "tile", down)
+    return after_this, before, after
 
 
 def stencil_finish(state_t, diffusivity, before, after, depth):
@@ -245,7 +248,6 @@
     ]
     vmem = pl.BlockSpec(memory_space=pltpu.VMEM)
     smem = pl.BlockSpec(memory_space=pltpu.SMEM)
-    x_from_before, x_from_after = stencil_start(u_field, v_field, diffusivity, PASSES)
     hbm = pl.BlockSpec(memory_space=pl.ANY)
     state_t, outgoing = pl.pallas_call(
         gather_kernel,
@@ -261,8 +263,8 @@
         ],
     )(slot_index, active_columns, u_field, v_field)
     state_t = state_t.reshape(width_x, width_y, features)
-    outgoing, x_from_before, x_from_after = lax.optimization_barrier(
-        (outgoing, x_from_before, x_from_after)
+    outgoing, x_from_before, x_from_after = stencil_start(
+        u_field, v_field, diffusivity, PASSES, outgoing
     )
     block = lax.all_to_all(
         outgoing.reshape(group_size, pair_slots, features),

time: 149 us -> 188 us (1.26)
  waiting for transfers between devices: 38 us -> 74.9 us
  local copies, waits for them, and re-layouts: 11.8 us -> 13.8 us
    ppermute x2, waiting for transfers between devices: 0.58 us -> 40.8 us  [the longest x1 40.8 us: stencil_start(): before = lax.ppermute(last, 'tile', up)]
    all_to_all x1, waiting for transfers between devices: 26.6 us -> 0.01 us  [body(): lax.all_to_all(outgoing.reshape(group_size, pair_slots, features), ('tile...]
    ppermute x4, waiting for transfers between devices: 0.01 us -> 23.2 us  [body(): lax.ppermute(w[0], 'tile', swap)]
  transfers between devices with their start and end apart: 10 -> 10, of which waited for: 3 -> 4; matrix products, arithmetic and copies ran while one was open for 19% -> 13% of each run, Pallas kernels for 21% -> 8%
where the time goes in v15:
time: 188 us; the launch traced here: 187 us
  waiting for transfers between devices  74.9 us (40%)
  Pallas kernels  46.5 us (25%)
  starting transfers between devices  27.2 us (14%)
  local copies, waits for them, and re-layouts  13.8 us (7%)
  matrix products  13.3 us (7%)
  other arithmetic  9.74 us (5%)
    ppermute x1, waiting for transfers between devices, stencil_start(): before = lax.ppermute(last, 'tile', up)  40.8 us
    ppermute x4, waiting for transfers between devices, body(): lax.ppermute(w[0], 'tile', swap)  23.2 us
    pallas_call x1, Pallas kernels, body(): pl.pallas_call(gather_kernel, out_shape=(jax.ShapeDtypeStruct((cells, fea...  16 us
    pallas_call x1, Pallas kernels, body(): pl.pallas_call(finish_kernel, out_shape=(jax.ShapeDtypeStruct(u_field.sha...  15.3 us
    pallas_call x1, Pallas kernels, body(): pl.pallas_call(diffuse_kernel, out_shape=jax.ShapeDtypeStruct((width_x, w...  15.3 us
    all_to_all x1, waiting for transfers between devices, body(): lax.all_to_all(answered, ('tile', 'inf'), split_axis=0, concat_axis=0, ti...  10.8 us
    all_to_all x1, starting transfers between devices, body(): lax.all_to_all(outgoing.reshape(group_size, pair_slots, features), ('tile...  6.33 us
    ppermute x4, starting transfers between devices, body(): lax.ppermute(w[0], 'tile', swap)  6.06 us
  transfers between devices with their start and end apart: 10, of which 4 were waited for; matrix products, arithmetic and copies ran while one was open for 13% of the time, Pallas kernels for 8%

profile of v15, /device:TPU:0, one launch (start us, length us, event | category | flops | bytes accessed | tf_op | source)
XLA Modules:
  0.0 186.8 jit_solution(9552944636840845687)
XLA Ops:
  1.9 1.4 reduce.7
  3.3 1.9 %while.13 = (s32[]{:T(128)}, f32[32]{0:T(128)S(1)}, f32[4,512]{1,0:T(4,128)S(1)}, bf16[4,512,32]{1,2,0:T(8,128)(2,1)S(1)}, s32[]{:T(128)}, /*index=5*/s32[]{:T(128)}) while((s32[]{:T(128)}, f32[32]{0:T(128)S(1)}, f32[4,512]{1,0:T(4,128)S(1)}, bf16[4,512,32]{1,2,0:T(8,128)(2,1)S(1)}, s32[]{:T(128)}, /*index=5*/s32[]{:T(128)}) %tuple.41), condition=%wide.region_3.4_spmd.clone, body=%wide.region_0.3_spmd.clone.sunk | while | flops 17399332 | bytes 106719 | solution.py:231
  5.6 1.1 fusion.74
  7.0 1.1 fusion.75
  9.0 16.0 %shard_map.104 = (f32[8192,128]{1,0:T(8,128)}, f32[4096,128]{1,0:T(8,128)}) custom-call(s32[2048]{0:T(1024)} %fusion.57.slot_ref, s32[2048]{0:T(1024)} %act_ref.3, f32[64,64,128]{2,1,0:T(8,128)} %u_hbm.1, f32[64,64,128]{2,1,0:T(8,128)} %v_hbm.1), custom_call_target="tpu_custom_call" | custom-call | tf_op jit(solution)/shard_map/pallas_call | solution.py:252
  25.3 6.3 %all-to-all-start = ((f32[16,256,128]{2,1,0:T(8,128)}), f32[16,256,128]{2,1,0:T(8,128)S(1)}, u32[]{:S(2)}, u32[]{:S(2)}) async-start(f32[16,256,128]{2,1,0:T(8,128)} %bitcast.89), calls=%async_computation | async-start | bytes 4194304 | tf_op jit(solution)/shard_map/all_to_all | solution.py:269
  31.6 4.6 %collective-permute-start = (f32[129,4,128]{0,2,1:T(8,128)S(1)}, f32[129,4,128]{0,2,1:T(8,128)}, u32[]{:S(2)}, u32[]{:S(2)}) collective-permute-start(f32[129,4,128]{0,2,1:T(8,128)S(1)} %get-tuple-element.41), channel_id=1, source_target_pairs={{0,4},{4,8},{8,12},{12,16},{16,20},{20,24},{24,28},{1,5},{5,9},{9,... | collective-permute-start | bytes 792584 | tf_op jit(solution)/shard_map/ppermute | solution.py:35
  36.3 1.3 collective-permute-start.1
  37.6 40.8 %collective-permute-done = f32[129,4,128]{0,2,1:T(8,128)} collective-permute-done((f32[129,4,128]{0,2,1:T(8,128)S(1)}, f32[129,4,128]{0,2,1:T(8,128)}, u32[]{:S(2)}, u32[]{:S(2)}) %collective-permute-start) | collective-permute-done | bytes 264224 | tf_op jit(solution)/shard_map/ppermute | solution.py:35
  83.2 1.1 slice_bitcast_fusion.xa_ref
  84.4 1.3 fusion.50
  85.6 1.3 collective-permute-start.2
  86.9 3.2 %collective-permute-start.3 = (f32[73,4,128]{2,1,0:T(4,128)S(1)}, f32[73,4,128]{2,1,0:T(4,128)S(1)}, u32[]{:S(2)}, u32[]{:S(2)}) collective-permute-start(f32[73,4,128]{2,1,0:T(4,128)S(1)} %get-tuple-element.78), channel_id=1, source_target_pairs={{0,1},{1,2},{2,3},{4,5},{5,6},{6,7},{8,9},{9,10},{10,11},{12,13},{... | collective-permute-start | bytes 448520 | tf_op jit(solution)/shard_map/ppermute | solution.py:56
  90.2 3.1 %collective-permute-start.7 = (f32[256,128]{1,0:T(8,128)S(1)}, f32[256,128]{1,0:T(8,128)}, u32[]{:S(2)}, u32[]{:S(2)}) collective-permute-start(f32[256,128]{1,0:T(8,128)S(1)} %bitcast.97), channel_id=1, source_target_pairs={{0,16},{4,20},{8,24},{12,28},{16,0},{20,4},{24,8},{28,12},{1,17},{... | collective-permute-start | bytes 393224 | tf_op jit(solution)/shard_map/ppermute | solution.py:247
  93.3 2.8 %collective-permute-start.6 = (f32[256,256]{1,0:T(8,128)S(1)}, f32[256,256]{1,0:T(8,128)}, u32[]{:S(2)}, u32[]{:S(2)}) collective-permute-start(f32[256,256]{1,0:T(8,128)S(1)} %bitcast.102), channel_id=1, source_target_pairs={{0,16},{4,20},{8,24},{12,28},{16,0},{20,4},{24,8},{28,12},{1,17},{... | collective-permute-start | bytes 786440 | tf_op jit(solution)/shard_map/ppermute | solution.py:247
  98.4 1.3 subtract_multiply_fusion
  99.7 1.0 fusion.65
  100.7 1.3 fusion.36
  102.0 1.3 divide_multiply_fusion
  103.9 12.9 %collective-permute-done.4 = f32[128,256]{1,0:T(8,128)S(1)} collective-permute-done((f32[128,256]{1,0:T(8,128)S(1)}, f32[128,256]{1,0:T(8,128)S(1)}, u32[]{:S(2)}, u32[]{:S(2)}) %collective-permute-start.4) | collective-permute-done | bytes 131104 | tf_op jit(solution)/shard_map/ppermute | solution.py:247
  116.8 1.0 fusion.76
  117.8 10.4 %collective-permute-done.5 = f32[256,256]{1,0:T(8,128)} collective-permute-done((f32[256,256]{1,0:T(8,128)S(1)}, f32[256,256]{1,0:T(8,128)}, u32[]{:S(2)}, u32[]{:S(2)}) %collective-permute-start.5) | collective-permute-done | bytes 262176 | tf_op jit(solution)/shard_map/ppermute | solution.py:247
  128.1 2.2 %fusion.22 = f32[2048,256]{1,0:T(8,128)S(1)} fusion(f32[256,256]{1,0:T(8,128)} %collective-permute-done.5, f32[2048,256]{1,0:T(8,128)S(1)} %fusion.76), kind=kOutput, calls=%fused_computation.25 | convolution fusion | flops 807403520 | bytes 4456448 | tf_op jit(solution)/shard_map/dot_general | solution.py:77
  130.3 2.2 %fusion.16 = f32[2048,256]{1,0:T(8,128)S(1)} fusion(f32[256,256]{1,0:T(8,128)} %collective-permute-done.6, f32[2048,256]{1,0:T(8,128)S(1)} %fusion.22), kind=kOutput, calls=%fused_computation.19 | convolution fusion | flops 807403520 | bytes 4456448 | tf_op jit(solution)/shard_map/dot_general | solution.py:78
  132.6 1.0 fusion.51
  133.6 2.2 %fusion.10 = f32[2048,128]{1,0:T(8,128)S(1)} fusion(f32[256,128]{1,0:T(8,128)} %collective-permute-done.7, f32[2048,256]{1,0:T(8,128)S(1)} %fusion.16), kind=kOutput, calls=%fused_computation.13 | convolution fusion | flops 404750336 | bytes 3276800 | tf_op jit(solution)/shard_map/dot_general | solution.py:79
  135.8 1.5 pad_maximum_fusion
  137.2 4.4 %all-to-all-start.1 = ((f32[16,256,128]{2,1,0:T(8,128)}), f32[16,256,128]{2,1,0:T(8,128)}, u32[]{:S(2)}, u32[]{:S(2)}) async-start(f32[16,256,128]{2,1,0:T(8,128)} %pad_maximum_fusion), calls=%async_computation.1 | async-start | bytes 4194304 | tf_op jit(solution)/shard_map/all_to_all | solution.py:292
  141.9 3.4 %broadcast_in_dim.42.c_ref = f32[72,136,128]{2,1,0:T(8,128)} broadcast(f32[72,136]{1,0:T(8,128)S(1)} %copy.28), dimensions={0,1} | broadcast | bytes 5052672 | tf_op jit(solution)/shard_map/broadcast_in_dim | solution.py:64
  145.3 15.3 %shard_map.105 = f32[64,128,128]{2,1,0:T(8,128)} custom-call(f32[64,128,128]{2,1,0:T(8,128)} %bitcast.86, f32[4,128,128]{2,1,0:T(8,128)} %copy-done, f32[4,128,128]{2,1,0:T(8,128)} %copy-done.1, f32[72,8,128]{2,1,0:T(8,128)} %pad_maximum_fusion.3.yh_ref, f32[72,136,128]{2,1,0:T(8,128)} %broadcast_in_dim.42.c_ref), custom_call_target="tpu_custom_call" | custom-call | tf_op jit(solution)/shard_map/pallas_call | solution.py:303
  160.6 10.8 %all-to-all-done.1 = f32[16,256,128]{2,1,0:T(8,128)} async-done(((f32[16,256,128]{2,1,0:T(8,128)}), f32[16,256,128]{2,1,0:T(8,128)}, u32[]{:S(2)}, u32[]{:S(2)}) %all-to-all-start.1) | async-done | bytes 2097184 | tf_op jit(solution)/shard_map/all_to_all | solution.py:292
  171.4 15.3 %shard_map.106 = (f32[64,64,128]{2,1,0:T(8,128)}, f32[64,64,128]{2,1,0:T(8,128)}) custom-call(s32[2048]{0:T(1024)} %fusion.57.slot_ref, s32[2048]{0:T(1024)} %act_ref.3, f32[4096,128]{1,0:T(8,128)} %bitcast.24.r_ref, f32[8192,128]{1,0:T(8,128)} %bitcast.87), custom_call_target="tpu_custom_call" | custom-call | tf_op jit(solution)/shard_map/pallas_call | solution.py:314
  (79 shorter events, 12.8 us)
Async XLA Ops:
  5.2 3.1 %copy-start.5 = (s32[2048,1]{0,1:T(1,128)S(1)}, s32[2048,1]{0,1:T(1,128)}, u32[]{:S(2)}) copy-start(s32[2048,1]{0,1:T(1,128)} %param.15) | copy-start | bytes 24580
  25.3 12.2 %copy-start.4 = (f32[64,128]{1,0:T(8,128)S(1)}, f32[64,128]{1,0:T(8,128)}, u32[]{:S(2)}) copy-start(f32[64,128]{1,0:T(8,128)} %param.13) | copy-start | bytes 98308
  25.3 71.8 %all-to-all-start = ((f32[16,256,128]{2,1,0:T(8,128)}), f32[16,256,128]{2,1,0:T(8,128)S(1)}, u32[]{:S(2)}, u32[]{:S(2)}) async-start(f32[16,256,128]{2,1,0:T(8,128)} %bitcast.89), calls=%async_computation | async-start | bytes 4194304 | tf_op jit(solution)/shard_map/all_to_all | solution.py:269
  31.6 46.8 %collective-permute-start = (f32[129,4,128]{0,2,1:T(8,128)S(1)}, f32[129,4,128]{0,2,1:T(8,128)}, u32[]{:S(2)}, u32[]{:S(2)}) collective-permute-start(f32[129,4,128]{0,2,1:T(8,128)S(1)} %get-tuple-element.41), channel_id=1, source_target_pairs={{0,4},{4,8},{8,12},{12,16},{16,20},{20,24},{24,28},{1,5},{5,9},{9,... | collective-permute-start | bytes 792584 | tf_op jit(solution)/shard_map/ppermute | solution.py:35
  36.3 44.1 %collective-permute-start.1 = (f32[129,4,128]{0,2,1:T(8,128)S(1)}, f32[129,4,128]{0,2,1:T(8,128)}, u32[]{:S(2)}, u32[]{:S(2)}) collective-permute-start(f32[129,4,128]{0,2,1:T(8,128)S(1)} %get-tuple-element.42), channel_id=1, source_target_pairs={{4,0},{8,4},{12,8},{16,12},{20,16},{24,20},{28,24},{5,1},{9,5},{13... | collective-permute-start | bytes 792584 | tf_op jit(solution)/shard_map/ppermute | solution.py:36
  83.2 2.4 %copy-start = (f32[4,128,128]{2,1,0:T(8,128)}, f32[4,128,128]{2,1,0:T(8,128)S(1)}, u32[]{:S(2)}) copy-start(f32[4,128,128]{2,1,0:T(8,128)S(1)} %slice_bitcast_fusion.1.xb_ref) | copy-start | bytes 786436
  84.3 1.3 copy-start.1
  84.3 5.9 %copy-start.3 = (f32[1,256,128]{2,1,0:T(8,128)S(1)}, f32[1,256,128]{2,1,0:T(8,128)}, u32[]{:S(2)}) copy-start(f32[1,256,128]{2,1,0:T(8,128)} %param.19) | copy-start | bytes 393220
  84.3 8.9 %copy-start.2 = (f32[1,128,256]{2,1,0:T(8,128)S(1)}, f32[1,128,256]{2,1,0:T(8,128)}, u32[]{:S(2)}) copy-start(f32[1,128,256]{2,1,0:T(8,128)} %param.16) | copy-start | bytes 393220
  84.3 9.0 %copy-start.7 = (f32[1,256,256]{2,1,0:T(8,128)S(1)}, f32[1,256,256]{2,1,0:T(8,128)}, u32[]{:S(2)}) copy-start(f32[1,256,256]{2,1,0:T(8,128)} %param.18) | copy-start | bytes 786436
  84.4 11.8 %copy-start.6 = (f32[1,256,256]{2,1,0:T(8,128)S(1)}, f32[1,256,256]{2,1,0:T(8,128)}, u32[]{:S(2)}) copy-start(f32[1,256,256]{2,1,0:T(8,128)} %param.17) | copy-start | bytes 786436
  85.6 10.5 %collective-permute-start.2 = (f32[73,4,128]{2,1,0:T(4,128)S(1)}, f32[73,4,128]{2,1,0:T(4,128)S(1)}, u32[]{:S(2)}, u32[]{:S(2)}) collective-permute-start(f32[73,4,128]{2,1,0:T(4,128)S(1)} %get-tuple-element.77), channel_id=1, source_target_pairs={{1,0},{2,1},{3,2},{5,4},{6,5},{7,6},{9,8},{10,9},{11,10},{13,12},{... | collective-permute-start | bytes 448520 | tf_op jit(solution)/shard_map/ppermute | solution.py:57
  86.9 9.3 %collective-permute-start.3 = (f32[73,4,128]{2,1,0:T(4,128)S(1)}, f32[73,4,128]{2,1,0:T(4,128)S(1)}, u32[]{:S(2)}, u32[]{:S(2)}) collective-permute-start(f32[73,4,128]{2,1,0:T(4,128)S(1)} %get-tuple-element.78), channel_id=1, source_target_pairs={{0,1},{1,2},{2,3},{4,5},{5,6},{6,7},{8,9},{9,10},{10,11},{12,13},{... | collective-permute-start | bytes 448520 | tf_op jit(solution)/shard_map/ppermute | solution.py:56
  90.2 43.4 %collective-permute-start.7 = (f32[256,128]{1,0:T(8,128)S(1)}, f32[256,128]{1,0:T(8,128)}, u32[]{:S(2)}, u32[]{:S(2)}) collective-permute-start(f32[256,128]{1,0:T(8,128)S(1)} %bitcast.97), channel_id=1, source_target_pairs={{0,16},{4,20},{8,24},{12,28},{16,0},{20,4},{24,8},{28,12},{1,17},{... | collective-permute-start | bytes 393224 | tf_op jit(solution)/shard_map/ppermute | solution.py:247
  93.2 23.5 %collective-permute-start.4 = (f32[128,256]{1,0:T(8,128)S(1)}, f32[128,256]{1,0:T(8,128)S(1)}, u32[]{:S(2)}, u32[]{:S(2)}) collective-permute-start(f32[128,256]{1,0:T(8,128)S(1)} %bitcast.96), channel_id=1, source_target_pairs={{0,16},{4,20},{8,24},{12,28},{16,0},{20,4},{24,8},{28,12},{1,17},{... | collective-permute-start | bytes 393224 | tf_op jit(solution)/shard_map/ppermute | solution.py:247
  93.3 37.0 %collective-permute-start.6 = (f32[256,256]{1,0:T(8,128)S(1)}, f32[256,256]{1,0:T(8,128)}, u32[]{:S(2)}, u32[]{:S(2)}) collective-permute-start(f32[256,256]{1,0:T(8,128)S(1)} %bitcast.102), channel_id=1, source_target_pairs={{0,16},{4,20},{8,24},{12,28},{16,0},{20,4},{24,8},{28,12},{1,17},{... | collective-permute-start | bytes 786440 | tf_op jit(solution)/shard_map/ppermute | solution.py:247
  96.2 32.0 %collective-permute-start.5 = (f32[256,256]{1,0:T(8,128)S(1)}, f32[256,256]{1,0:T(8,128)}, u32[]{:S(2)}, u32[]{:S(2)}) collective-permute-start(f32[256,256]{1,0:T(8,128)S(1)} %bitcast.101), channel_id=1, source_target_pairs={{0,16},{4,20},{8,24},{12,28},{16,0},{20,4},{24,8},{28,12},{1,17},{... | collective-permute-start | bytes 786440 | tf_op jit(solution)/shard_map/ppermute | solution.py:247
  137.2 34.1 %all-to-all-start.1 = ((f32[16,256,128]{2,1,0:T(8,128)}), f32[16,256,128]{2,1,0:T(8,128)}, u32[]{:S(2)}, u32[]{:S(2)}) async-start(f32[16,256,128]{2,1,0:T(8,128)} %pad_maximum_fusion), calls=%async_computation.1 | async-start | bytes 4194304 | tf_op jit(solution)/shard_map/all_to_all | solution.py:292

commit v16 on v12

--- a/solution.py
+++ b/solution.py
@@ -76,7 +76,7 @@
     return jnp.dot(hidden, last_layer, precision=highest)
 
 
-def gather_kernel(slot_ref, act_ref, u_hbm, v_hbm, st_ref, o_ref, buf, sems):
+def gather_kernel(slot_ref, act_ref, u_hbm, v_hbm, st_hbm, o_ref, buf, st_ref, sems, st_sems):
     levels = u_hbm.shape[0]
     width_x, features, width_y = buf.shape
     chunk = 128
@@ -101,10 +101,15 @@
 
     lax.fori_loop(0, o_ref.shape[0] // chunk, clear, 0)
 
+    def write_back(x):
+        at = pl.ds(pl.multiple_of(x * width_y, width_y), width_y)
+        return pltpu.make_async_copy(st_ref.at[at, :], st_hbm.at[at, :], st_sems.at[x])
+
     def transpose_tile(x, carry):
         for copy in copies(x):
             copy.wait()
         st_ref[pl.ds(pl.multiple_of(x * width_y, width_y), width_y), :] = buf[x].T
+        write_back(x).start()
         return carry
 
     lax.fori_loop(0, width_x, transpose_tile, 0)
@@ -114,6 +119,12 @@
         return carry
 
     lax.fori_loop(0, act_ref.shape[0], place, 0, unroll=8)
+
+    def settle(x, carry):
+        write_back(x).wait()
+        return carry
+
+    lax.fori_loop(0, width_x, settle, 0)
 
 
 def diffuse_kernel(st_ref, xb_ref, xa_ref, yh_ref, c_ref, f_ref, e_ref, a_ref):
@@ -149,9 +160,19 @@
         sweep(src, dst, p, p == PASSES - 1)
 
 
-def finish_kernel(slot_ref, act_ref, r_ref, f_ref, uo_hbm, vo_hbm, d_ref, obuf, sems):
+def finish_kernel(slot_ref, act_ref, r_ref, f_hbm, uo_hbm, vo_hbm, d_ref, obuf, f_ref, sems, f_sems):
     levels = uo_hbm.shape[0]
     width_x, features, width_y = obuf.shape
+
+    def fetch(x):
+        at = pl.ds(pl.multiple_of(x * width_y, width_y), width_y)
+        return pltpu.make_async_copy(f_hbm.at[at, :], f_ref.at[at, :], f_sems.at[x])
+
+    def begin(x, carry):
+        fetch(x).start()
+        return carry
+
+    lax.fori_loop(0, width_x, begin, 0)
 
     def clear(x, carry):
         at = pl.ds(pl.multiple_of(x * width_y, width_y), width_y)
@@ -174,6 +195,7 @@
 
     def transpose_tile(x, carry):
         at = pl.ds(pl.multiple_of(x * width_y, width_y), width_y)
+        fetch(x).wait()
         obuf[x] = (f_ref[at, :] + d_ref[at, :]).T
         for copy in copies(x):
             copy.start()
@@ -254,10 +276,12 @@
             jax.ShapeDtypeStruct((slot_total, features), jnp.float32),
         ),
         in_specs=[smem, smem, hbm, hbm],
-        out_specs=(vmem, vmem),
+        out_specs=(hbm, vmem),
         scratch_shapes=[
             pltpu.VMEM((width_x, features, width_y), jnp.float32),
+            pltpu.VMEM((cells, features), jnp.float32),
             pltpu.SemaphoreType.DMA((2, width_x)),
+            pltpu.SemaphoreType.DMA((width_x,)),
         ],
     )(slot_index, active_columns, u_field, v_field)
     state_t = state_t.reshape(width_x, width_y, features)
@@ -315,12 +339,14 @@
             jax.ShapeDtypeStruct(u_field.shape, jnp.float32),
             jax.ShapeDtypeStruct(v_field.shape, jnp.float32),
         ),
-        in_specs=[smem, smem, vmem, vmem],
+        in_specs=[smem, smem, vmem, hbm],
         out_specs=(hbm, hbm),
         scratch_shapes=[
             pltpu.VMEM((cells, features), jnp.float32),
             pltpu.VMEM((width_x, features, width_y), jnp.float32),
+            pltpu.VMEM((cells, features), jnp.float32),
             pltpu.SemaphoreType.DMA((2, width_x)),
+            pltpu.SemaphoreType.DMA((width_x,)),
         ],
     )(slot_index, active_columns, returned_rows, diffused.reshape(cells, features))
     return (u_next, v_next)

time: 149 us -> 149 us (level)
  no operation moved by 1% of the time
where the time goes in v16:
time: 149 us; the launch traced here: 148 us
  Pallas kernels  46.1 us (31%)
  waiting for transfers between devices  38.3 us (26%)
  starting transfers between devices  27.1 us (18%)
  matrix products  14.2 us (10%)
  local copies, waits for them, and re-layouts  11.8 us (8%)
  other arithmetic  9.19 us (6%)
    all_to_all x1, waiting for transfers between devices, body(): lax.all_to_all(outgoing.reshape(group_size, pair_slots, features), ('tile...  26.6 us
    pallas_call x1, Pallas kernels, body(): pl.pallas_call(gather_kernel, out_shape=(jax.ShapeDtypeStruct((cells, fea...  15.6 us
    pallas_call x1, Pallas kernels, body(): pl.pallas_call(diffuse_kernel, out_shape=jax.ShapeDtypeStruct((width_x, w...  15.3 us
    pallas_call x1, Pallas kernels, body(): pl.pallas_call(finish_kernel, out_shape=(jax.ShapeDtypeStruct(u_field.sha...  15.2 us
    all_to_all x1, waiting for transfers between devices, body(): lax.all_to_all(answered, ('tile', 'inf'), split_axis=0, concat_axis=0, ti...  10.8 us
    all_to_all x1, starting transfers between devices, body(): lax.all_to_all(outgoing.reshape(group_size, pair_slots, features), ('tile...  6.04 us
    ppermute x4, starting transfers between devices, body(): lax.ppermute(w[0], 'tile', swap)  5.92 us
    ppermute x1, starting transfers between devices, stencil_start(): before = lax.ppermute(x_piece(width_x - depth), 'tile', up)  4.9 us
  transfers between devices with their start and end apart: 10, of which 3 were waited for; matrix products, arithmetic and copies ran while one was open for 19% of the time, Pallas kernels for 21%

profile of v16, /device:TPU:0, one launch (start us, length us, event | category | flops | bytes accessed | tf_op | source)
XLA Modules:
  0.0 148.2 jit_solution(140620017449897475)
XLA Ops:
  1.5 1.1 fusion.74
  2.7 1.1 fusion.75
  4.2 4.9 %collective-permute-start = (f32[129,4,128]{0,2,1:T(8,128)S(1)}, f32[129,4,128]{0,2,1:T(8,128)S(1)}, u32[]{:S(2)}, u32[]{:S(2)}) collective-permute-start(f32[129,4,128]{0,2,1:T(8,128)S(1)} %pad_maximum_fusion.1), channel_id=1, source_target_pairs={{0,4},{4,8},{8,12},{12,16},{16,20},{20,24},{24,28},{1,5},{5,9},{9,... | collective-permute-start | bytes 792584 | tf_op jit(solution)/shard_map/ppermute | solution.py:32
  9.7 1.3 collective-permute-start.1
  12.3 1.9 %while.13 = (s32[]{:T(128)}, f32[32]{0:T(128)S(1)}, f32[4,512]{1,0:T(4,128)S(1)}, bf16[4,512,32]{1,2,0:T(8,128)(2,1)S(1)}, s32[]{:T(128)}, /*index=5*/s32[]{:T(128)}) while((s32[]{:T(128)}, f32[32]{0:T(128)S(1)}, f32[4,512]{1,0:T(4,128)S(1)}, bf16[4,512,32]{1,2,0:T(8,128)(2,1)S(1)}, s32[]{:T(128)}, /*index=5*/s32[]{:T(128)}) %tuple.42), condition=%wide.region_3.4_spmd.clone, body=%wide.region_0.3_spmd.clone.sunk | while | flops 17399332 | bytes 106719 | solution.py:250
  14.9 15.6 %shard_map.104 = (f32[8192,128]{1,0:T(8,128)}, f32[4096,128]{1,0:T(8,128)}) custom-call(s32[2048]{0:T(1024)} %fusion.57.slot_ref, s32[2048]{0:T(1024)} %act_ref.3, f32[64,64,128]{2,1,0:T(8,128)} %u_hbm.1, f32[64,64,128]{2,1,0:T(8,128)} %v_hbm.1), custom_call_target="tpu_custom_call" | custom-call | tf_op jit(solution)/shard_map/pallas_call | solution.py:272
  30.5 0.9 collective-permute-done
  31.5 6.0 %all-to-all-start = ((f32[16,256,128]{2,1,0:T(8,128)}), f32[16,256,128]{2,1,0:T(8,128)S(1)}, u32[]{:S(2)}, u32[]{:S(2)}) async-start(f32[16,256,128]{2,1,0:T(8,128)} %bitcast.89), calls=%async_computation | async-start | bytes 4194304 | tf_op jit(solution)/shard_map/all_to_all | solution.py:291
  38.5 1.0 slice.70
  40.4 1.0 slice_bitcast_fusion
  41.5 1.3 fusion.50
  42.8 1.3 collective-permute-start.2
  44.1 3.2 %collective-permute-start.3 = (f32[73,4,128]{2,1,0:T(4,128)S(1)}, f32[73,4,128]{2,1,0:T(4,128)S(1)}, u32[]{:S(2)}, u32[]{:S(2)}) collective-permute-start(f32[73,4,128]{2,1,0:T(4,128)S(1)} %get-tuple-element.78), channel_id=1, source_target_pairs={{0,1},{1,2},{2,3},{4,5},{5,6},{6,7},{8,9},{9,10},{10,11},{12,13},{... | collective-permute-start | bytes 448520 | tf_op jit(solution)/shard_map/ppermute | solution.py:53
  47.4 2.7 %collective-permute-start.7 = (f32[256,128]{1,0:T(8,128)S(1)}, f32[256,128]{1,0:T(8,128)}, u32[]{:S(2)}, u32[]{:S(2)}) collective-permute-start(f32[256,128]{1,0:T(8,128)S(1)} %bitcast.97), channel_id=1, source_target_pairs={{0,16},{4,20},{8,24},{12,28},{16,0},{20,4},{24,8},{28,12},{1,17},{... | collective-permute-start | bytes 393224 | tf_op jit(solution)/shard_map/ppermute | solution.py:266
  50.4 2.6 %collective-permute-start.6 = (f32[256,256]{1,0:T(8,128)}, f32[256,256]{1,0:T(8,128)}, u32[]{:S(2)}, u32[]{:S(2)}) collective-permute-start(f32[256,256]{1,0:T(8,128)} %bitcast.16), channel_id=1, source_target_pairs={{0,16},{4,20},{8,24},{12,28},{16,0},{20,4},{24,8},{28,12},{1,17},{... | collective-permute-start | bytes 786440 | tf_op jit(solution)/shard_map/ppermute | solution.py:266
  54.1 26.6 %all-to-all-done = f32[16,256,128]{2,1,0:T(8,128)S(1)} async-done(((f32[16,256,128]{2,1,0:T(8,128)}), f32[16,256,128]{2,1,0:T(8,128)S(1)}, u32[]{:S(2)}, u32[]{:S(2)}) %all-to-all-start) | async-done | bytes 2097184 | tf_op jit(solution)/shard_map/all_to_all | solution.py:291
  81.1 0.9 multiply_reduce_fusion.1
  82.1 1.3 subtract_multiply_fusion
  83.4 1.0 fusion.65
  84.4 1.3 fusion.36
  85.6 2.3 %divide_multiply_fusion = f32[2048,256]{1,0:T(8,128)S(1)} fusion(f32[2048,256]{1,0:T(8,128)S(1)} %fusion.36, f32[1,256,256]{2,1,0:T(8,128)} %param.18), kind=kOutput, calls=%fused_computation.31 | convolution fusion | flops 809500672 | bytes 4456448 | tf_op jit(solution)/shard_map/dot_general | solution.py:75
  88.5 1.0 fusion.76
  89.5 2.2 %fusion.22 = f32[2048,256]{1,0:T(8,128)S(1)} fusion(f32[256,256]{1,0:T(8,128)} %collective-permute-done.5, f32[2048,256]{1,0:T(8,128)S(1)} %fusion.76), kind=kOutput, calls=%fused_computation.25 | convolution fusion | flops 807403520 | bytes 4456448 | tf_op jit(solution)/shard_map/dot_general | solution.py:74
  91.8 2.2 %fusion.16 = f32[2048,256]{1,0:T(8,128)S(1)} fusion(f32[256,256]{1,0:T(8,128)} %collective-permute-done.6, f32[2048,256]{1,0:T(8,128)S(1)} %fusion.22), kind=kOutput, calls=%fused_computation.19 | convolution fusion | flops 807403520 | bytes 4456448 | tf_op jit(solution)/shard_map/dot_general | solution.py:75
  94.0 1.0 fusion.51
  95.0 2.2 %fusion.10 = f32[2048,128]{1,0:T(8,128)S(1)} fusion(f32[256,128]{1,0:T(8,128)} %collective-permute-done.7, f32[2048,256]{1,0:T(8,128)S(1)} %fusion.16), kind=kOutput, calls=%fused_computation.13 | convolution fusion | flops 404750336 | bytes 3276800 | tf_op jit(solution)/shard_map/dot_general | solution.py:76
  97.2 1.5 pad_maximum_fusion
  98.6 4.4 %all-to-all-start.1 = ((f32[16,256,128]{2,1,0:T(8,128)}), f32[16,256,128]{2,1,0:T(8,128)}, u32[]{:S(2)}, u32[]{:S(2)}) async-start(f32[16,256,128]{2,1,0:T(8,128)} %pad_maximum_fusion), calls=%async_computation.1 | async-start | bytes 4194304 | tf_op jit(solution)/shard_map/all_to_all | solution.py:314
  103.3 3.4 %broadcast_in_dim.42.c_ref = f32[72,136,128]{2,1,0:T(8,128)} broadcast(f32[72,136]{1,0:T(8,128)S(1)} %copy.28), dimensions={0,1} | broadcast | bytes 5052672 | tf_op jit(solution)/shard_map/broadcast_in_dim | solution.py:61
  106.7 15.3 %shard_map.105 = f32[64,128,128]{2,1,0:T(8,128)} custom-call(f32[64,128,128]{2,1,0:T(8,128)} %bitcast.86, f32[4,128,128]{2,1,0:T(8,128)} %copy-done.1, f32[4,128,128]{2,1,0:T(8,128)} %copy-done, f32[72,8,128]{2,1,0:T(8,128)} %pad_maximum_fusion.3.yh_ref, f32[72,136,128]{2,1,0:T(8,128)} %broadcast_in_dim.42.c_ref), custom_call_target="tpu_custom_call" | custom-call | tf_op jit(solution)/shard_map/pallas_call | solution.py:325
  122.0 10.8 %all-to-all-done.1 = f32[16,256,128]{2,1,0:T(8,128)} async-done(((f32[16,256,128]{2,1,0:T(8,128)}), f32[16,256,128]{2,1,0:T(8,128)}, u32[]{:S(2)}, u32[]{:S(2)}) %all-to-all-start.1) | async-done | bytes 2097184 | tf_op jit(solution)/shard_map/all_to_all | solution.py:314
  132.8 15.2 %shard_map.106 = (f32[64,64,128]{2,1,0:T(8,128)}, f32[64,64,128]{2,1,0:T(8,128)}) custom-call(s32[2048]{0:T(1024)} %fusion.57.slot_ref, s32[2048]{0:T(1024)} %act_ref.3, f32[4096,128]{1,0:T(8,128)} %bitcast.24.r_ref, f32[8192,128]{1,0:T(8,128)} %bitcast.87), custom_call_target="tpu_custom_call" | custom-call | tf_op jit(solution)/shard_map/pallas_call | solution.py:336
  (76 shorter events, 10.3 us)
Async XLA Ops:
  3.8 7.8 %copy-start.5 = (s32[2048,1]{0,1:T(1,128)S(1)}, s32[2048,1]{0,1:T(1,128)}, u32[]{:S(2)}) copy-start(s32[2048,1]{0,1:T(1,128)} %param.15) | copy-start | bytes 24580
  4.2 27.3 %collective-permute-start = (f32[129,4,128]{0,2,1:T(8,128)S(1)}, f32[129,4,128]{0,2,1:T(8,128)S(1)}, u32[]{:S(2)}, u32[]{:S(2)}) collective-permute-start(f32[129,4,128]{0,2,1:T(8,128)S(1)} %pad_maximum_fusion.1), channel_id=1, source_target_pairs={{0,4},{4,8},{8,12},{12,16},{16,20},{20,24},{24,28},{1,5},{5,9},{9,... | collective-permute-start | bytes 792584 | tf_op jit(solution)/shard_map/ppermute | solution.py:32
  9.7 21.7 %collective-permute-start.1 = (f32[129,4,128]{0,2,1:T(8,128)S(1)}, f32[129,4,128]{0,2,1:T(8,128)}, u32[]{:S(2)}, u32[]{:S(2)}) collective-permute-start(f32[129,4,128]{0,2,1:T(8,128)S(1)} %pad_maximum_fusion.2), channel_id=1, source_target_pairs={{4,0},{8,4},{12,8},{16,12},{20,16},{24,20},{28,24},{5,1},{9,5},{13... | collective-permute-start | bytes 792584 | tf_op jit(solution)/shard_map/ppermute | solution.py:33
  31.5 6.0 %copy-start.4 = (f32[64,128]{1,0:T(8,128)S(1)}, f32[64,128]{1,0:T(8,128)}, u32[]{:S(2)}) copy-start(f32[64,128]{1,0:T(8,128)} %param.13) | copy-start | bytes 98308
  31.5 49.3 %all-to-all-start = ((f32[16,256,128]{2,1,0:T(8,128)}), f32[16,256,128]{2,1,0:T(8,128)S(1)}, u32[]{:S(2)}, u32[]{:S(2)}) async-start(f32[16,256,128]{2,1,0:T(8,128)} %bitcast.89), calls=%async_computation | async-start | bytes 4194304 | tf_op jit(solution)/shard_map/all_to_all | solution.py:291
  41.4 1.4 copy-start
  41.4 1.4 copy-start.1
  41.5 5.9 %copy-start.3 = (f32[1,256,128]{2,1,0:T(8,128)S(1)}, f32[1,256,128]{2,1,0:T(8,128)}, u32[]{:S(2)}) copy-start(f32[1,256,128]{2,1,0:T(8,128)} %param.19) | copy-start | bytes 393220
  41.5 8.6 %copy-start.2 = (f32[1,128,256]{2,1,0:T(8,128)S(1)}, f32[1,128,256]{2,1,0:T(8,128)}, u32[]{:S(2)}) copy-start(f32[1,128,256]{2,1,0:T(8,128)} %param.16) | copy-start | bytes 393220
  41.5 11.5 %copy-start.6 = (f32[1,256,256]{2,1,0:T(8,128)S(1)}, f32[1,256,256]{2,1,0:T(8,128)}, u32[]{:S(2)}) copy-start(f32[1,256,256]{2,1,0:T(8,128)} %param.17) | copy-start | bytes 786436
  42.8 10.1 %collective-permute-start.2 = (f32[73,4,128]{2,1,0:T(4,128)S(1)}, f32[73,4,128]{2,1,0:T(4,128)S(1)}, u32[]{:S(2)}, u32[]{:S(2)}) collective-permute-start(f32[73,4,128]{2,1,0:T(4,128)S(1)} %get-tuple-element.77), channel_id=1, source_target_pairs={{1,0},{2,1},{3,2},{5,4},{6,5},{7,6},{9,8},{10,9},{11,10},{13,12},{... | collective-permute-start | bytes 448520 | tf_op jit(solution)/shard_map/ppermute | solution.py:54
  44.1 9.2 %collective-permute-start.3 = (f32[73,4,128]{2,1,0:T(4,128)S(1)}, f32[73,4,128]{2,1,0:T(4,128)S(1)}, u32[]{:S(2)}, u32[]{:S(2)}) collective-permute-start(f32[73,4,128]{2,1,0:T(4,128)S(1)} %get-tuple-element.78), channel_id=1, source_target_pairs={{0,1},{1,2},{2,3},{4,5},{5,6},{6,7},{8,9},{9,10},{10,11},{12,13},{... | collective-permute-start | bytes 448520 | tf_op jit(solution)/shard_map/ppermute | solution.py:53
  47.4 47.6 %collective-permute-start.7 = (f32[256,128]{1,0:T(8,128)S(1)}, f32[256,128]{1,0:T(8,128)}, u32[]{:S(2)}, u32[]{:S(2)}) collective-permute-start(f32[256,128]{1,0:T(8,128)S(1)} %bitcast.97), channel_id=1, source_target_pairs={{0,16},{4,20},{8,24},{12,28},{16,0},{20,4},{24,8},{28,12},{1,17},{... | collective-permute-start | bytes 393224 | tf_op jit(solution)/shard_map/ppermute | solution.py:266
  50.0 38.5 %collective-permute-start.4 = (f32[128,256]{1,0:T(8,128)S(1)}, f32[128,256]{1,0:T(8,128)S(1)}, u32[]{:S(2)}, u32[]{:S(2)}) collective-permute-start(f32[128,256]{1,0:T(8,128)S(1)} %bitcast.96), channel_id=1, source_target_pairs={{0,16},{4,20},{8,24},{12,28},{16,0},{20,4},{24,8},{28,12},{1,17},{... | collective-permute-start | bytes 393224 | tf_op jit(solution)/shard_map/ppermute | solution.py:266
  50.4 41.4 %collective-permute-start.6 = (f32[256,256]{1,0:T(8,128)}, f32[256,256]{1,0:T(8,128)}, u32[]{:S(2)}, u32[]{:S(2)}) collective-permute-start(f32[256,256]{1,0:T(8,128)} %bitcast.16), channel_id=1, source_target_pairs={{0,16},{4,20},{8,24},{12,28},{16,0},{20,4},{24,8},{28,12},{1,17},{... | collective-permute-start | bytes 786440 | tf_op jit(solution)/shard_map/ppermute | solution.py:266
  53.0 36.6 %collective-permute-start.5 = (f32[256,256]{1,0:T(8,128)S(1)}, f32[256,256]{1,0:T(8,128)}, u32[]{:S(2)}, u32[]{:S(2)}) collective-permute-start(f32[256,256]{1,0:T(8,128)S(1)} %bitcast.101), channel_id=1, source_target_pairs={{0,16},{4,20},{8,24},{12,28},{16,0},{20,4},{24,8},{28,12},{1,17},{... | collective-permute-start | bytes 786440 | tf_op jit(solution)/shard_map/ppermute | solution.py:266
  98.6 34.1 %all-to-all-start.1 = ((f32[16,256,128]{2,1,0:T(8,128)}), f32[16,256,128]{2,1,0:T(8,128)}, u32[]{:S(2)}, u32[]{:S(2)}) async-start(f32[16,256,128]{2,1,0:T(8,128)} %pad_maximum_fusion), calls=%async_computation.1 | async-start | bytes 4194304 | tf_op jit(solution)/shard_map/all_to_all | solution.py:314

commit v17 on v12

--- a/solution.py
+++ b/solution.py
@@ -113,7 +113,7 @@
         o_ref[pl.ds(slot_ref[r], 1), :] = st_ref[pl.ds(act_ref[r], 1), :]
         return carry
 
-    lax.fori_loop(0, act_ref.shape[0], place, 0, unroll=8)
+    lax.fori_loop(0, act_ref.shape[0], place, 0, unroll=32)
 
 
 def diffuse_kernel(st_ref, xb_ref, xa_ref, yh_ref, c_ref, f_ref, e_ref, a_ref):
@@ -164,7 +164,7 @@
         d_ref[pl.ds(act_ref[r], 1), :] = r_ref[pl.ds(slot_ref[r], 1), :]
         return carry
 
-    lax.fori_loop(0, act_ref.shape[0], place, 0, unroll=8)
+    lax.fori_loop(0, act_ref.shape[0], place, 0, unroll=32)
 
     def copies(x):
         return (

time: 149 us -> 148 us (level)
  Pallas kernels: 46.5 us -> 44.9 us
where the time goes in v17:
time: 148 us; the launch traced here: 147 us
  Pallas kernels  44.9 us (30%)
  waiting for transfers between devices  38.8 us (26%)
  starting transfers between devices  27.1 us (18%)
  matrix products  14.2 us (10%)
  local copies, waits for them, and re-layouts  11.8 us (8%)
  other arithmetic  9.19 us (6%)
    all_to_all x1, waiting for transfers between devices, body(): lax.all_to_all(outgoing.reshape(group_size, pair_slots, features), ('tile...  26.6 us
    pallas_call x1, Pallas kernels, body(): pl.pallas_call(diffuse_kernel, out_shape=jax.ShapeDtypeStruct((width_x, w...  15.3 us
    pallas_call x1, Pallas kernels, body(): pl.pallas_call(gather_kernel, out_shape=(jax.ShapeDtypeStruct((cells, fea...  15.1 us
    pallas_call x1, Pallas kernels, body(): pl.pallas_call(finish_kernel, out_shape=(jax.ShapeDtypeStruct(u_field.sha...  14.5 us
    all_to_all x1, waiting for transfers between devices, body(): lax.all_to_all(answered, ('tile', 'inf'), split_axis=0, concat_axis=0, ti...  10.8 us
    all_to_all x1, starting transfers between devices, body(): lax.all_to_all(outgoing.reshape(group_size, pair_slots, features), ('tile...  6.04 us
    ppermute x4, starting transfers between devices, body(): lax.ppermute(w[0], 'tile', swap)  5.92 us
    ppermute x1, starting transfers between devices, stencil_start(): before = lax.ppermute(x_piece(width_x - depth), 'tile', up)  4.9 us
  transfers between devices with their start and end apart: 10, of which 3 were waited for; matrix products, arithmetic and copies ran while one was open for 19% of the time, Pallas kernels for 21%

profile of v17, /device:TPU:0, one launch (start us, length us, event | category | flops | bytes accessed | tf_op | source)
XLA Modules:
  0.0 147.4 jit_solution(16803912599751592703)
XLA Ops:
  1.5 1.1 fusion.74
  2.7 1.1 fusion.75
  4.2 4.9 %collective-permute-start = (f32[129,4,128]{0,2,1:T(8,128)S(1)}, f32[129,4,128]{0,2,1:T(8,128)S(1)}, u32[]{:S(2)}, u32[]{:S(2)}) collective-permute-start(f32[129,4,128]{0,2,1:T(8,128)S(1)} %pad_maximum_fusion.1), channel_id=1, source_target_pairs={{0,4},{4,8},{8,12},{12,16},{16,20},{20,24},{24,28},{1,5},{5,9},{9,... | collective-permute-start | bytes 792584 | tf_op jit(solution)/shard_map/ppermute | solution.py:32
  9.7 1.3 collective-permute-start.1
  12.3 1.9 %while.13 = (s32[]{:T(128)}, f32[32]{0:T(128)S(1)}, f32[4,512]{1,0:T(4,128)S(1)}, bf16[4,512,32]{1,2,0:T(8,128)(2,1)S(1)}, s32[]{:T(128)}, /*index=5*/s32[]{:T(128)}) while((s32[]{:T(128)}, f32[32]{0:T(128)S(1)}, f32[4,512]{1,0:T(4,128)S(1)}, bf16[4,512,32]{1,2,0:T(8,128)(2,1)S(1)}, s32[]{:T(128)}, /*index=5*/s32[]{:T(128)}) %tuple.42), condition=%wide.region_3.4_spmd.clone, body=%wide.region_0.3_spmd.clone.sunk | while | flops 17399332 | bytes 106719 | solution.py:228
  14.9 15.1 %shard_map.104 = (f32[8192,128]{1,0:T(8,128)}, f32[4096,128]{1,0:T(8,128)}) custom-call(s32[2048]{0:T(1024)} %fusion.57.slot_ref, s32[2048]{0:T(1024)} %act_ref.3, f32[64,64,128]{2,1,0:T(8,128)} %u_hbm.1, f32[64,64,128]{2,1,0:T(8,128)} %v_hbm.1), custom_call_target="tpu_custom_call" | custom-call | tf_op jit(solution)/shard_map/pallas_call | solution.py:250
  30.0 1.4 collective-permute-done
  31.5 6.0 %all-to-all-start = ((f32[16,256,128]{2,1,0:T(8,128)}), f32[16,256,128]{2,1,0:T(8,128)S(1)}, u32[]{:S(2)}, u32[]{:S(2)}) async-start(f32[16,256,128]{2,1,0:T(8,128)} %bitcast.89), calls=%async_computation | async-start | bytes 4194304 | tf_op jit(solution)/shard_map/all_to_all | solution.py:267
  38.5 1.0 slice.70
  40.4 1.0 slice_bitcast_fusion
  41.5 1.3 fusion.50
  42.8 1.3 collective-permute-start.2
  44.1 3.2 %collective-permute-start.3 = (f32[73,4,128]{2,1,0:T(4,128)S(1)}, f32[73,4,128]{2,1,0:T(4,128)S(1)}, u32[]{:S(2)}, u32[]{:S(2)}) collective-permute-start(f32[73,4,128]{2,1,0:T(4,128)S(1)} %get-tuple-element.78), channel_id=1, source_target_pairs={{0,1},{1,2},{2,3},{4,5},{5,6},{6,7},{8,9},{9,10},{10,11},{12,13},{... | collective-permute-start | bytes 448520 | tf_op jit(solution)/shard_map/ppermute | solution.py:53
  47.4 2.7 %collective-permute-start.7 = (f32[256,128]{1,0:T(8,128)S(1)}, f32[256,128]{1,0:T(8,128)}, u32[]{:S(2)}, u32[]{:S(2)}) collective-permute-start(f32[256,128]{1,0:T(8,128)S(1)} %bitcast.97), channel_id=1, source_target_pairs={{0,16},{4,20},{8,24},{12,28},{16,0},{20,4},{24,8},{28,12},{1,17},{... | collective-permute-start | bytes 393224 | tf_op jit(solution)/shard_map/ppermute | solution.py:244
  50.4 2.6 %collective-permute-start.6 = (f32[256,256]{1,0:T(8,128)}, f32[256,256]{1,0:T(8,128)}, u32[]{:S(2)}, u32[]{:S(2)}) collective-permute-start(f32[256,256]{1,0:T(8,128)} %bitcast.16), channel_id=1, source_target_pairs={{0,16},{4,20},{8,24},{12,28},{16,0},{20,4},{24,8},{28,12},{1,17},{... | collective-permute-start | bytes 786440 | tf_op jit(solution)/shard_map/ppermute | solution.py:244
  54.1 26.6 %all-to-all-done = f32[16,256,128]{2,1,0:T(8,128)S(1)} async-done(((f32[16,256,128]{2,1,0:T(8,128)}), f32[16,256,128]{2,1,0:T(8,128)S(1)}, u32[]{:S(2)}, u32[]{:S(2)}) %all-to-all-start) | async-done | bytes 2097184 | tf_op jit(solution)/shard_map/all_to_all | solution.py:267
  81.1 0.9 multiply_reduce_fusion.1
  82.1 1.3 subtract_multiply_fusion
  83.4 1.0 fusion.65
  84.4 1.3 fusion.36
  85.6 2.3 %divide_multiply_fusion = f32[2048,256]{1,0:T(8,128)S(1)} fusion(f32[2048,256]{1,0:T(8,128)S(1)} %fusion.36, f32[1,256,256]{2,1,0:T(8,128)} %param.18), kind=kOutput, calls=%fused_computation.31 | convolution fusion | flops 809500672 | bytes 4456448 | tf_op jit(solution)/shard_map/dot_general | solution.py:75
  88.5 1.0 fusion.76
  89.5 2.2 %fusion.22 = f32[2048,256]{1,0:T(8,128)S(1)} fusion(f32[256,256]{1,0:T(8,128)} %collective-permute-done.5, f32[2048,256]{1,0:T(8,128)S(1)} %fusion.76), kind=kOutput, calls=%fused_computation.25 | convolution fusion | flops 807403520 | bytes 4456448 | tf_op jit(solution)/shard_map/dot_general | solution.py:74
  91.8 2.2 %fusion.16 = f32[2048,256]{1,0:T(8,128)S(1)} fusion(f32[256,256]{1,0:T(8,128)} %collective-permute-done.6, f32[2048,256]{1,0:T(8,128)S(1)} %fusion.22), kind=kOutput, calls=%fused_computation.19 | convolution fusion | flops 807403520 | bytes 4456448 | tf_op jit(solution)/shard_map/dot_general | solution.py:75
  94.0 1.0 fusion.51
  95.0 2.2 %fusion.10 = f32[2048,128]{1,0:T(8,128)S(1)} fusion(f32[256,128]{1,0:T(8,128)} %collective-permute-done.7, f32[2048,256]{1,0:T(8,128)S(1)} %fusion.16), kind=kOutput, calls=%fused_computation.13 | convolution fusion | flops 404750336 | bytes 3276800 | tf_op jit(solution)/shard_map/dot_general | solution.py:76
  97.2 1.5 pad_maximum_fusion
  98.6 4.4 %all-to-all-start.1 = ((f32[16,256,128]{2,1,0:T(8,128)}), f32[16,256,128]{2,1,0:T(8,128)}, u32[]{:S(2)}, u32[]{:S(2)}) async-start(f32[16,256,128]{2,1,0:T(8,128)} %pad_maximum_fusion), calls=%async_computation.1 | async-start | bytes 4194304 | tf_op jit(solution)/shard_map/all_to_all | solution.py:290
  103.3 3.4 %broadcast_in_dim.42.c_ref = f32[72,136,128]{2,1,0:T(8,128)} broadcast(f32[72,136]{1,0:T(8,128)S(1)} %copy.28), dimensions={0,1} | broadcast | bytes 5052672 | tf_op jit(solution)/shard_map/broadcast_in_dim | solution.py:61
  106.7 15.3 %shard_map.105 = f32[64,128,128]{2,1,0:T(8,128)} custom-call(f32[64,128,128]{2,1,0:T(8,128)} %bitcast.86, f32[4,128,128]{2,1,0:T(8,128)} %copy-done.1, f32[4,128,128]{2,1,0:T(8,128)} %copy-done, f32[72,8,128]{2,1,0:T(8,128)} %pad_maximum_fusion.3.yh_ref, f32[72,136,128]{2,1,0:T(8,128)} %broadcast_in_dim.42.c_ref), custom_call_target="tpu_custom_call" | custom-call | tf_op jit(solution)/shard_map/pallas_call | solution.py:301
  122.0 10.8 %all-to-all-done.1 = f32[16,256,128]{2,1,0:T(8,128)} async-done(((f32[16,256,128]{2,1,0:T(8,128)}), f32[16,256,128]{2,1,0:T(8,128)}, u32[]{:S(2)}, u32[]{:S(2)}) %all-to-all-start.1) | async-done | bytes 2097184 | tf_op jit(solution)/shard_map/all_to_all | solution.py:290
  132.8 14.5 %shard_map.106 = (f32[64,64,128]{2,1,0:T(8,128)}, f32[64,64,128]{2,1,0:T(8,128)}) custom-call(s32[2048]{0:T(1024)} %fusion.57.slot_ref, s32[2048]{0:T(1024)} %act_ref.3, f32[4096,128]{1,0:T(8,128)} %bitcast.24.r_ref, f32[8192,128]{1,0:T(8,128)} %bitcast.87), custom_call_target="tpu_custom_call" | custom-call | tf_op jit(solution)/shard_map/pallas_call | solution.py:312
  (76 shorter events, 10.3 us)
Async XLA Ops:
  3.8 7.8 %copy-start.5 = (s32[2048,1]{0,1:T(1,128)S(1)}, s32[2048,1]{0,1:T(1,128)}, u32[]{:S(2)}) copy-start(s32[2048,1]{0,1:T(1,128)} %param.15) | copy-start | bytes 24580
  4.2 27.3 %collective-permute-start = (f32[129,4,128]{0,2,1:T(8,128)S(1)}, f32[129,4,128]{0,2,1:T(8,128)S(1)}, u32[]{:S(2)}, u32[]{:S(2)}) collective-permute-start(f32[129,4,128]{0,2,1:T(8,128)S(1)} %pad_maximum_fusion.1), channel_id=1, source_target_pairs={{0,4},{4,8},{8,12},{12,16},{16,20},{20,24},{24,28},{1,5},{5,9},{9,... | collective-permute-start | bytes 792584 | tf_op jit(solution)/shard_map/ppermute | solution.py:32
  9.7 21.7 %collective-permute-start.1 = (f32[129,4,128]{0,2,1:T(8,128)S(1)}, f32[129,4,128]{0,2,1:T(8,128)}, u32[]{:S(2)}, u32[]{:S(2)}) collective-permute-start(f32[129,4,128]{0,2,1:T(8,128)S(1)} %pad_maximum_fusion.2), channel_id=1, source_target_pairs={{4,0},{8,4},{12,8},{16,12},{20,16},{24,20},{28,24},{5,1},{9,5},{13... | collective-permute-start | bytes 792584 | tf_op jit(solution)/shard_map/ppermute | solution.py:33
  31.5 6.0 %copy-start.4 = (f32[64,128]{1,0:T(8,128)S(1)}, f32[64,128]{1,0:T(8,128)}, u32[]{:S(2)}) copy-start(f32[64,128]{1,0:T(8,128)} %param.13) | copy-start | bytes 98308
  31.5 49.3 %all-to-all-start = ((f32[16,256,128]{2,1,0:T(8,128)}), f32[16,256,128]{2,1,0:T(8,128)S(1)}, u32[]{:S(2)}, u32[]{:S(2)}) async-start(f32[16,256,128]{2,1,0:T(8,128)} %bitcast.89), calls=%async_computation | async-start | bytes 4194304 | tf_op jit(solution)/shard_map/all_to_all | solution.py:267
  41.4 1.4 copy-start
  41.4 1.4 copy-start.1
  41.5 5.9 %copy-start.3 = (f32[1,256,128]{2,1,0:T(8,128)S(1)}, f32[1,256,128]{2,1,0:T(8,128)}, u32[]{:S(2)}) copy-start(f32[1,256,128]{2,1,0:T(8,128)} %param.19) | copy-start | bytes 393220
  41.5 8.6 %copy-start.2 = (f32[1,128,256]{2,1,0:T(8,128)S(1)}, f32[1,128,256]{2,1,0:T(8,128)}, u32[]{:S(2)}) copy-start(f32[1,128,256]{2,1,0:T(8,128)} %param.16) | copy-start | bytes 393220
  41.5 11.5 %copy-start.6 = (f32[1,256,256]{2,1,0:T(8,128)S(1)}, f32[1,256,256]{2,1,0:T(8,128)}, u32[]{:S(2)}) copy-start(f32[1,256,256]{2,1,0:T(8,128)} %param.17) | copy-start | bytes 786436
  42.8 10.1 %collective-permute-start.2 = (f32[73,4,128]{2,1,0:T(4,128)S(1)}, f32[73,4,128]{2,1,0:T(4,128)S(1)}, u32[]{:S(2)}, u32[]{:S(2)}) collective-permute-start(f32[73,4,128]{2,1,0:T(4,128)S(1)} %get-tuple-element.77), channel_id=1, source_target_pairs={{1,0},{2,1},{3,2},{5,4},{6,5},{7,6},{9,8},{10,9},{11,10},{13,12},{... | collective-permute-start | bytes 448520 | tf_op jit(solution)/shard_map/ppermute | solution.py:54
  44.1 9.2 %collective-permute-start.3 = (f32[73,4,128]{2,1,0:T(4,128)S(1)}, f32[73,4,128]{2,1,0:T(4,128)S(1)}, u32[]{:S(2)}, u32[]{:S(2)}) collective-permute-start(f32[73,4,128]{2,1,0:T(4,128)S(1)} %get-tuple-element.78), channel_id=1, source_target_pairs={{0,1},{1,2},{2,3},{4,5},{5,6},{6,7},{8,9},{9,10},{10,11},{12,13},{... | collective-permute-start | bytes 448520 | tf_op jit(solution)/shard_map/ppermute | solution.py:53
  47.4 47.6 %collective-permute-start.7 = (f32[256,128]{1,0:T(8,128)S(1)}, f32[256,128]{1,0:T(8,128)}, u32[]{:S(2)}, u32[]{:S(2)}) collective-permute-start(f32[256,128]{1,0:T(8,128)S(1)} %bitcast.97), channel_id=1, source_target_pairs={{0,16},{4,20},{8,24},{12,28},{16,0},{20,4},{24,8},{28,12},{1,17},{... | collective-permute-start | bytes 393224 | tf_op jit(solution)/shard_map/ppermute | solution.py:244
  50.0 38.5 %collective-permute-start.4 = (f32[128,256]{1,0:T(8,128)S(1)}, f32[128,256]{1,0:T(8,128)S(1)}, u32[]{:S(2)}, u32[]{:S(2)}) collective-permute-start(f32[128,256]{1,0:T(8,128)S(1)} %bitcast.96), channel_id=1, source_target_pairs={{0,16},{4,20},{8,24},{12,28},{16,0},{20,4},{24,8},{28,12},{1,17},{... | collective-permute-start | bytes 393224 | tf_op jit(solution)/shard_map/ppermute | solution.py:244
  50.4 41.4 %collective-permute-start.6 = (f32[256,256]{1,0:T(8,128)}, f32[256,256]{1,0:T(8,128)}, u32[]{:S(2)}, u32[]{:S(2)}) collective-permute-start(f32[256,256]{1,0:T(8,128)} %bitcast.16), channel_id=1, source_target_pairs={{0,16},{4,20},{8,24},{12,28},{16,0},{20,4},{24,8},{28,12},{1,17},{... | collective-permute-start | bytes 786440 | tf_op jit(solution)/shard_map/ppermute | solution.py:244
  53.0 36.6 %collective-permute-start.5 = (f32[256,256]{1,0:T(8,128)S(1)}, f32[256,256]{1,0:T(8,128)}, u32[]{:S(2)}, u32[]{:S(2)}) collective-permute-start(f32[256,256]{1,0:T(8,128)S(1)} %bitcast.101), channel_id=1, source_target_pairs={{0,16},{4,20},{8,24},{12,28},{16,0},{20,4},{24,8},{28,12},{1,17},{... | collective-permute-start | bytes 786440 | tf_op jit(solution)/shard_map/ppermute | solution.py:244
  98.6 34.1 %all-to-all-start.1 = ((f32[16,256,128]{2,1,0:T(8,128)}), f32[16,256,128]{2,1,0:T(8,128)}, u32[]{:S(2)}, u32[]{:S(2)}) async-start(f32[16,256,128]{2,1,0:T(8,128)} %pad_maximum_fusion), calls=%async_computation.1 | async-start | bytes 4194304 | tf_op jit(solution)/shard_map/all_to_all | solution.py:290

commit v18 on v17

--- a/solution.py
+++ b/solution.py
@@ -107,13 +107,13 @@
         st_ref[pl.ds(pl.multiple_of(x * width_y, width_y), width_y), :] = buf[x].T
         return carry
 
-    lax.fori_loop(0, width_x, transpose_tile, 0)
+    lax.fori_loop(0, width_x, transpose_tile, 0, unroll=4)
 
     def place(r, carry):
         o_ref[pl.ds(slot_ref[r], 1), :] = st_ref[pl.ds(act_ref[r], 1), :]
         return carry
 
-    lax.fori_loop(0, act_ref.shape[0], place, 0, unroll=32)
+    lax.fori_loop(0, act_ref.shape[0], place, 0, unroll=64)
 
 
 def diffuse_kernel(st_ref, xb_ref, xa_ref, yh_ref, c_ref, f_ref, e_ref, a_ref):
@@ -164,7 +164,7 @@
         d_ref[pl.ds(act_ref[r], 1), :] = r_ref[pl.ds(slot_ref[r], 1), :]
         return carry
 
-    lax.fori_loop(0, act_ref.shape[0], place, 0, unroll=32)
+    lax.fori_loop(0, act_ref.shape[0], place, 0, unroll=64)
 
     def copies(x):
         return (
@@ -179,7 +179,7 @@
             copy.start()
         return carry
 
-    lax.fori_loop(0, width_x, transpose_tile, 0)
+    lax.fori_loop(0, width_x, transpose_tile, 0, unroll=4)
 
     def finish(x, carry):
         for copy in copies(x):

time: 148 us -> 144 us (0.973)
  Pallas kernels: 44.9 us -> 40.3 us
    pallas_call x1, Pallas kernels: 14.5 us -> 10.1 us  [body(): pl.pallas_call(finish_kernel, out_shape=(jax.ShapeDtypeStruct(u_field.sha...]
  transfers between devices with their start and end apart: 10 -> 10, of which waited for: 3 -> 3; matrix products, arithmetic and copies ran while one was open for 19% -> 20% of each run, Pallas kernels for 21% -> 21%
where the time goes in v18:
time: 144 us; the launch traced here: 143 us
  Pallas kernels  40.3 us (28%)
  waiting for transfers between devices  39 us (27%)
  starting transfers between devices  27.1 us (19%)
  matrix products  14.2 us (10%)
  local copies, waits for them, and re-layouts  11.8 us (8%)
  other arithmetic  9.19 us (6%)
    all_to_all x1, waiting for transfers between devices, body(): lax.all_to_all(outgoing.reshape(group_size, pair_slots, features), ('tile...  26.6 us
    pallas_call x1, Pallas kernels, body(): pl.pallas_call(diffuse_kernel, out_shape=jax.ShapeDtypeStruct((width_x, w...  15.3 us
    pallas_call x1, Pallas kernels, body(): pl.pallas_call(gather_kernel, out_shape=(jax.ShapeDtypeStruct((cells, fea...  15 us
    all_to_all x1, waiting for transfers between devices, body(): lax.all_to_all(answered, ('tile', 'inf'), split_axis=0, concat_axis=0, ti...  10.8 us
    pallas_call x1, Pallas kernels, body(): pl.pallas_call(finish_kernel, out_shape=(jax.ShapeDtypeStruct(u_field.sha...  10.1 us
    all_to_all x1, starting transfers between devices, body(): lax.all_to_all(outgoing.reshape(group_size, pair_slots, features), ('tile...  6.04 us
    ppermute x4, starting transfers between devices, body(): lax.ppermute(w[0], 'tile', swap)  5.92 us
    ppermute x1, starting transfers between devices, stencil_start(): before = lax.ppermute(x_piece(width_x - depth), 'tile', up)  4.9 us
  transfers between devices with their start and end apart: 10, of which 3 were waited for; matrix products, arithmetic and copies ran while one was open for 20% of the time, Pallas kernels for 21%

profile of v18, /device:TPU:0, one launch (start us, length us, event | category | flops | bytes accessed | tf_op | source)
XLA Modules:
  0.0 143.0 jit_solution(3596415869392921228)
XLA Ops:
  1.5 1.1 fusion.74
  2.7 1.1 fusion.75
  4.2 4.9 %collective-permute-start = (f32[129,4,128]{0,2,1:T(8,128)S(1)}, f32[129,4,128]{0,2,1:T(8,128)S(1)}, u32[]{:S(2)}, u32[]{:S(2)}) collective-permute-start(f32[129,4,128]{0,2,1:T(8,128)S(1)} %pad_maximum_fusion.1), channel_id=1, source_target_pairs={{0,4},{4,8},{8,12},{12,16},{16,20},{20,24},{24,28},{1,5},{5,9},{9,... | collective-permute-start | bytes 792584 | tf_op jit(solution)/shard_map/ppermute | solution.py:32
  9.7 1.3 collective-permute-start.1
  12.3 1.9 %while.13 = (s32[]{:T(128)}, f32[32]{0:T(128)S(1)}, f32[4,512]{1,0:T(4,128)S(1)}, bf16[4,512,32]{1,2,0:T(8,128)(2,1)S(1)}, s32[]{:T(128)}, /*index=5*/s32[]{:T(128)}) while((s32[]{:T(128)}, f32[32]{0:T(128)S(1)}, f32[4,512]{1,0:T(4,128)S(1)}, bf16[4,512,32]{1,2,0:T(8,128)(2,1)S(1)}, s32[]{:T(128)}, /*index=5*/s32[]{:T(128)}) %tuple.42), condition=%wide.region_3.4_spmd.clone, body=%wide.region_0.3_spmd.clone.sunk | while | flops 17399332 | bytes 106719 | solution.py:228
  14.9 15.0 %shard_map.104 = (f32[8192,128]{1,0:T(8,128)}, f32[4096,128]{1,0:T(8,128)}) custom-call(s32[2048]{0:T(1024)} %fusion.57.slot_ref, s32[2048]{0:T(1024)} %act_ref.3, f32[64,64,128]{2,1,0:T(8,128)} %u_hbm.1, f32[64,64,128]{2,1,0:T(8,128)} %v_hbm.1), custom_call_target="tpu_custom_call" | custom-call | tf_op jit(solution)/shard_map/pallas_call | solution.py:250
  29.9 1.6 %collective-permute-done = f32[129,4,128]{0,2,1:T(8,128)S(1)} collective-permute-done((f32[129,4,128]{0,2,1:T(8,128)S(1)}, f32[129,4,128]{0,2,1:T(8,128)S(1)}, u32[]{:S(2)}, u32[]{:S(2)}) %collective-permute-start) | collective-permute-done | bytes 264224 | tf_op jit(solution)/shard_map/ppermute | solution.py:32
  31.5 6.0 %all-to-all-start = ((f32[16,256,128]{2,1,0:T(8,128)}), f32[16,256,128]{2,1,0:T(8,128)S(1)}, u32[]{:S(2)}, u32[]{:S(2)}) async-start(f32[16,256,128]{2,1,0:T(8,128)} %bitcast.89), calls=%async_computation | async-start | bytes 4194304 | tf_op jit(solution)/shard_map/all_to_all | solution.py:267
  38.5 1.0 slice.70
  40.4 1.0 slice_bitcast_fusion
  41.5 1.3 fusion.50
  42.8 1.3 collective-permute-start.2
  44.1 3.2 %collective-permute-start.3 = (f32[73,4,128]{2,1,0:T(4,128)S(1)}, f32[73,4,128]{2,1,0:T(4,128)S(1)}, u32[]{:S(2)}, u32[]{:S(2)}) collective-permute-start(f32[73,4,128]{2,1,0:T(4,128)S(1)} %get-tuple-element.78), channel_id=1, source_target_pairs={{0,1},{1,2},{2,3},{4,5},{5,6},{6,7},{8,9},{9,10},{10,11},{12,13},{... | collective-permute-start | bytes 448520 | tf_op jit(solution)/shard_map/ppermute | solution.py:53
  47.4 2.7 %collective-permute-start.7 = (f32[256,128]{1,0:T(8,128)S(1)}, f32[256,128]{1,0:T(8,128)}, u32[]{:S(2)}, u32[]{:S(2)}) collective-permute-start(f32[256,128]{1,0:T(8,128)S(1)} %bitcast.97), channel_id=1, source_target_pairs={{0,16},{4,20},{8,24},{12,28},{16,0},{20,4},{24,8},{28,12},{1,17},{... | collective-permute-start | bytes 393224 | tf_op jit(solution)/shard_map/ppermute | solution.py:244
  50.4 2.6 %collective-permute-start.6 = (f32[256,256]{1,0:T(8,128)}, f32[256,256]{1,0:T(8,128)}, u32[]{:S(2)}, u32[]{:S(2)}) collective-permute-start(f32[256,256]{1,0:T(8,128)} %bitcast.16), channel_id=1, source_target_pairs={{0,16},{4,20},{8,24},{12,28},{16,0},{20,4},{24,8},{28,12},{1,17},{... | collective-permute-start | bytes 786440 | tf_op jit(solution)/shard_map/ppermute | solution.py:244
  54.1 26.6 %all-to-all-done = f32[16,256,128]{2,1,0:T(8,128)S(1)} async-done(((f32[16,256,128]{2,1,0:T(8,128)}), f32[16,256,128]{2,1,0:T(8,128)S(1)}, u32[]{:S(2)}, u32[]{:S(2)}) %all-to-all-start) | async-done | bytes 2097184 | tf_op jit(solution)/shard_map/all_to_all | solution.py:267
  81.1 0.9 multiply_reduce_fusion.1
  82.1 1.3 subtract_multiply_fusion
  83.4 1.0 fusion.65
  84.4 1.3 fusion.36
  85.6 2.3 %divide_multiply_fusion = f32[2048,256]{1,0:T(8,128)S(1)} fusion(f32[2048,256]{1,0:T(8,128)S(1)} %fusion.36, f32[1,256,256]{2,1,0:T(8,128)} %param.18), kind=kOutput, calls=%fused_computation.31 | convolution fusion | flops 809500672 | bytes 4456448 | tf_op jit(solution)/shard_map/dot_general | solution.py:75
  88.5 1.0 fusion.76
  89.5 2.2 %fusion.22 = f32[2048,256]{1,0:T(8,128)S(1)} fusion(f32[256,256]{1,0:T(8,128)} %collective-permute-done.5, f32[2048,256]{1,0:T(8,128)S(1)} %fusion.76), kind=kOutput, calls=%fused_computation.25 | convolution fusion | flops 807403520 | bytes 4456448 | tf_op jit(solution)/shard_map/dot_general | solution.py:74
  91.8 2.2 %fusion.16 = f32[2048,256]{1,0:T(8,128)S(1)} fusion(f32[256,256]{1,0:T(8,128)} %collective-permute-done.6, f32[2048,256]{1,0:T(8,128)S(1)} %fusion.22), kind=kOutput, calls=%fused_computation.19 | convolution fusion | flops 807403520 | bytes 4456448 | tf_op jit(solution)/shard_map/dot_general | solution.py:75
  94.0 1.0 fusion.51
  95.0 2.2 %fusion.10 = f32[2048,128]{1,0:T(8,128)S(1)} fusion(f32[256,128]{1,0:T(8,128)} %collective-permute-done.7, f32[2048,256]{1,0:T(8,128)S(1)} %fusion.16), kind=kOutput, calls=%fused_computation.13 | convolution fusion | flops 404750336 | bytes 3276800 | tf_op jit(solution)/shard_map/dot_general | solution.py:76
  97.2 1.5 %pad_maximum_fusion = f32[16,256,128]{2,1,0:T(8,128)} fusion(f32[16,128,128]{2,1,0:T(8,128)S(1)} %bitcast.91, f32[16,128,128]{2,1,0:T(8,128)S(1)} %fusion.51), kind=kLoop, calls=%fused_computation.12 | loop fusion | flops 524288 | bytes 4194304 | tf_op jit(solution)/shard_map/concatenate | solution.py:286
  98.6 4.4 %all-to-all-start.1 = ((f32[16,256,128]{2,1,0:T(8,128)}), f32[16,256,128]{2,1,0:T(8,128)}, u32[]{:S(2)}, u32[]{:S(2)}) async-start(f32[16,256,128]{2,1,0:T(8,128)} %pad_maximum_fusion), calls=%async_computation.1 | async-start | bytes 4194304 | tf_op jit(solution)/shard_map/all_to_all | solution.py:290
  103.3 3.4 %broadcast_in_dim.42.c_ref = f32[72,136,128]{2,1,0:T(8,128)} broadcast(f32[72,136]{1,0:T(8,128)S(1)} %copy.28), dimensions={0,1} | broadcast | bytes 5052672 | tf_op jit(solution)/shard_map/broadcast_in_dim | solution.py:61
  106.7 15.3 %shard_map.105 = f32[64,128,128]{2,1,0:T(8,128)} custom-call(f32[64,128,128]{2,1,0:T(8,128)} %bitcast.86, f32[4,128,128]{2,1,0:T(8,128)} %copy-done.1, f32[4,128,128]{2,1,0:T(8,128)} %copy-done, f32[72,8,128]{2,1,0:T(8,128)} %pad_maximum_fusion.3.yh_ref, f32[72,136,128]{2,1,0:T(8,128)} %broadcast_in_dim.42.c_ref), custom_call_target="tpu_custom_call" | custom-call | tf_op jit(solution)/shard_map/pallas_call | solution.py:301
  122.0 10.8 %all-to-all-done.1 = f32[16,256,128]{2,1,0:T(8,128)} async-done(((f32[16,256,128]{2,1,0:T(8,128)}), f32[16,256,128]{2,1,0:T(8,128)}, u32[]{:S(2)}, u32[]{:S(2)}) %all-to-all-start.1) | async-done | bytes 2097184 | tf_op jit(solution)/shard_map/all_to_all | solution.py:290
  132.8 10.1 %shard_map.106 = (f32[64,64,128]{2,1,0:T(8,128)}, f32[64,64,128]{2,1,0:T(8,128)}) custom-call(s32[2048]{0:T(1024)} %fusion.57.slot_ref, s32[2048]{0:T(1024)} %act_ref.3, f32[4096,128]{1,0:T(8,128)} %bitcast.24.r_ref, f32[8192,128]{1,0:T(8,128)} %bitcast.87), custom_call_target="tpu_custom_call" | custom-call | tf_op jit(solution)/shard_map/pallas_call | solution.py:312
  (76 shorter events, 10.3 us)
Async XLA Ops:
  3.8 7.8 %copy-start.5 = (s32[2048,1]{0,1:T(1,128)S(1)}, s32[2048,1]{0,1:T(1,128)}, u32[]{:S(2)}) copy-start(s32[2048,1]{0,1:T(1,128)} %param.15) | copy-start | bytes 24580
  4.2 27.3 %collective-permute-start = (f32[129,4,128]{0,2,1:T(8,128)S(1)}, f32[129,4,128]{0,2,1:T(8,128)S(1)}, u32[]{:S(2)}, u32[]{:S(2)}) collective-permute-start(f32[129,4,128]{0,2,1:T(8,128)S(1)} %pad_maximum_fusion.1), channel_id=1, source_target_pairs={{0,4},{4,8},{8,12},{12,16},{16,20},{20,24},{24,28},{1,5},{5,9},{9,... | collective-permute-start | bytes 792584 | tf_op jit(solution)/shard_map/ppermute | solution.py:32
  9.7 21.7 %collective-permute-start.1 = (f32[129,4,128]{0,2,1:T(8,128)S(1)}, f32[129,4,128]{0,2,1:T(8,128)}, u32[]{:S(2)}, u32[]{:S(2)}) collective-permute-start(f32[129,4,128]{0,2,1:T(8,128)S(1)} %pad_maximum_fusion.2), channel_id=1, source_target_pairs={{4,0},{8,4},{12,8},{16,12},{20,16},{24,20},{28,24},{5,1},{9,5},{13... | collective-permute-start | bytes 792584 | tf_op jit(solution)/shard_map/ppermute | solution.py:33
  31.5 6.0 %copy-start.4 = (f32[64,128]{1,0:T(8,128)S(1)}, f32[64,128]{1,0:T(8,128)}, u32[]{:S(2)}) copy-start(f32[64,128]{1,0:T(8,128)} %param.13) | copy-start | bytes 98308
  31.5 49.3 %all-to-all-start = ((f32[16,256,128]{2,1,0:T(8,128)}), f32[16,256,128]{2,1,0:T(8,128)S(1)}, u32[]{:S(2)}, u32[]{:S(2)}) async-start(f32[16,256,128]{2,1,0:T(8,128)} %bitcast.89), calls=%async_computation | async-start | bytes 4194304 | tf_op jit(solution)/shard_map/all_to_all | solution.py:267
  41.4 1.4 copy-start
  41.4 1.4 copy-start.1
  41.5 5.9 %copy-start.3 = (f32[1,256,128]{2,1,0:T(8,128)S(1)}, f32[1,256,128]{2,1,0:T(8,128)}, u32[]{:S(2)}) copy-start(f32[1,256,128]{2,1,0:T(8,128)} %param.19) | copy-start | bytes 393220
  41.5 8.6 %copy-start.2 = (f32[1,128,256]{2,1,0:T(8,128)S(1)}, f32[1,128,256]{2,1,0:T(8,128)}, u32[]{:S(2)}) copy-start(f32[1,128,256]{2,1,0:T(8,128)} %param.16) | copy-start | bytes 393220
  41.5 11.5 %copy-start.6 = (f32[1,256,256]{2,1,0:T(8,128)S(1)}, f32[1,256,256]{2,1,0:T(8,128)}, u32[]{:S(2)}) copy-start(f32[1,256,256]{2,1,0:T(8,128)} %param.17) | copy-start | bytes 786436
  42.8 10.1 %collective-permute-start.2 = (f32[73,4,128]{2,1,0:T(4,128)S(1)}, f32[73,4,128]{2,1,0:T(4,128)S(1)}, u32[]{:S(2)}, u32[]{:S(2)}) collective-permute-start(f32[73,4,128]{2,1,0:T(4,128)S(1)} %get-tuple-element.77), channel_id=1, source_target_pairs={{1,0},{2,1},{3,2},{5,4},{6,5},{7,6},{9,8},{10,9},{11,10},{13,12},{... | collective-permute-start | bytes 448520 | tf_op jit(solution)/shard_map/ppermute | solution.py:54
  44.1 9.2 %collective-permute-start.3 = (f32[73,4,128]{2,1,0:T(4,128)S(1)}, f32[73,4,128]{2,1,0:T(4,128)S(1)}, u32[]{:S(2)}, u32[]{:S(2)}) collective-permute-start(f32[73,4,128]{2,1,0:T(4,128)S(1)} %get-tuple-element.78), channel_id=1, source_target_pairs={{0,1},{1,2},{2,3},{4,5},{5,6},{6,7},{8,9},{9,10},{10,11},{12,13},{... | collective-permute-start | bytes 448520 | tf_op jit(solution)/shard_map/ppermute | solution.py:53
  47.4 47.6 %collective-permute-start.7 = (f32[256,128]{1,0:T(8,128)S(1)}, f32[256,128]{1,0:T(8,128)}, u32[]{:S(2)}, u32[]{:S(2)}) collective-permute-start(f32[256,128]{1,0:T(8,128)S(1)} %bitcast.97), channel_id=1, source_target_pairs={{0,16},{4,20},{8,24},{12,28},{16,0},{20,4},{24,8},{28,12},{1,17},{... | collective-permute-start | bytes 393224 | tf_op jit(solution)/shard_map/ppermute | solution.py:244
  50.0 38.5 %collective-permute-start.4 = (f32[128,256]{1,0:T(8,128)S(1)}, f32[128,256]{1,0:T(8,128)S(1)}, u32[]{:S(2)}, u32[]{:S(2)}) collective-permute-start(f32[128,256]{1,0:T(8,128)S(1)} %bitcast.96), channel_id=1, source_target_pairs={{0,16},{4,20},{8,24},{12,28},{16,0},{20,4},{24,8},{28,12},{1,17},{... | collective-permute-start | bytes 393224 | tf_op jit(solution)/shard_map/ppermute | solution.py:244
  50.4 41.4 %collective-permute-start.6 = (f32[256,256]{1,0:T(8,128)}, f32[256,256]{1,0:T(8,128)}, u32[]{:S(2)}, u32[]{:S(2)}) collective-permute-start(f32[256,256]{1,0:T(8,128)} %bitcast.16), channel_id=1, source_target_pairs={{0,16},{4,20},{8,24},{12,28},{16,0},{20,4},{24,8},{28,12},{1,17},{... | collective-permute-start | bytes 786440 | tf_op jit(solution)/shard_map/ppermute | solution.py:244
  53.0 36.6 %collective-permute-start.5 = (f32[256,256]{1,0:T(8,128)S(1)}, f32[256,256]{1,0:T(8,128)}, u32[]{:S(2)}, u32[]{:S(2)}) collective-permute-start(f32[256,256]{1,0:T(8,128)S(1)} %bitcast.101), channel_id=1, source_target_pairs={{0,16},{4,20},{8,24},{12,28},{16,0},{20,4},{24,8},{28,12},{1,17},{... | collective-permute-start | bytes 786440 | tf_op jit(solution)/shard_map/ppermute | solution.py:244
  98.6 34.1 %all-to-all-start.1 = ((f32[16,256,128]{2,1,0:T(8,128)}), f32[16,256,128]{2,1,0:T(8,128)}, u32[]{:S(2)}, u32[]{:S(2)}) async-start(f32[16,256,128]{2,1,0:T(8,128)} %pad_maximum_fusion), calls=%async_computation.1 | async-start | bytes 4194304 | tf_op jit(solution)/shard_map/all_to_all | solution.py:290

commit v19 on v18

--- a/solution.py
+++ b/solution.py
@@ -107,7 +107,7 @@
         st_ref[pl.ds(pl.multiple_of(x * width_y, width_y), width_y), :] = buf[x].T
         return carry
 
-    lax.fori_loop(0, width_x, transpose_tile, 0, unroll=4)
+    lax.fori_loop(0, width_x, transpose_tile, 0, unroll=8)
 
     def place(r, carry):
         o_ref[pl.ds(slot_ref[r], 1), :] = st_ref[pl.ds(act_ref[r], 1), :]
@@ -179,7 +179,7 @@
             copy.start()
         return carry
 
-    lax.fori_loop(0, width_x, transpose_tile, 0, unroll=4)
+    lax.fori_loop(0, width_x, transpose_tile, 0, unroll=8)
 
     def finish(x, carry):
         for copy in copies(x):

time: 144 us -> 143 us (level)
  no operation moved by 1% of the time
where the time goes in v19:
time: 143 us; the launch traced here: 142 us
  Pallas kernels  39.7 us (28%)
  waiting for transfers between devices  39 us (27%)
  starting transfers between devices  27.1 us (19%)
  matrix products  14.2 us (10%)
  local copies, waits for them, and re-layouts  11.8 us (8%)
  other arithmetic  9.19 us (6%)
    all_to_all x1, waiting for transfers between devices, body(): lax.all_to_all(outgoing.reshape(group_size, pair_slots, features), ('tile...  26.6 us
    pallas_call x1, Pallas kernels, body(): pl.pallas_call(diffuse_kernel, out_shape=jax.ShapeDtypeStruct((width_x, w...  15.3 us
    pallas_call x1, Pallas kernels, body(): pl.pallas_call(gather_kernel, out_shape=(jax.ShapeDtypeStruct((cells, fea...  15 us
    all_to_all x1, waiting for transfers between devices, body(): lax.all_to_all(answered, ('tile', 'inf'), split_axis=0, concat_axis=0, ti...  10.8 us
    pallas_call x1, Pallas kernels, body(): pl.pallas_call(finish_kernel, out_shape=(jax.ShapeDtypeStruct(u_field.sha...  9.51 us
    all_to_all x1, starting transfers between devices, body(): lax.all_to_all(outgoing.reshape(group_size, pair_slots, features), ('tile...  6.04 us
    ppermute x4, starting transfers between devices, body(): lax.ppermute(w[0], 'tile', swap)  5.92 us
    ppermute x1, starting transfers between devices, stencil_start(): before = lax.ppermute(x_piece(width_x - depth), 'tile', up)  4.9 us
  transfers between devices with their start and end apart: 10, of which 3 were waited for; matrix products, arithmetic and copies ran while one was open for 20% of the time, Pallas kernels for 21%

profile of v19, /device:TPU:0, one launch (start us, length us, event | category | flops | bytes accessed | tf_op | source)
XLA Modules:
  0.0 142.4 jit_solution(14531484192563686828)
XLA Ops:
  1.5 1.1 fusion.74
  2.7 1.1 fusion.75
  4.2 4.9 %collective-permute-start = (f32[129,4,128]{0,2,1:T(8,128)S(1)}, f32[129,4,128]{0,2,1:T(8,128)S(1)}, u32[]{:S(2)}, u32[]{:S(2)}) collective-permute-start(f32[129,4,128]{0,2,1:T(8,128)S(1)} %pad_maximum_fusion.1), channel_id=1, source_target_pairs={{0,4},{4,8},{8,12},{12,16},{16,20},{20,24},{24,28},{1,5},{5,9},{9,... | collective-permute-start | bytes 792584 | tf_op jit(solution)/shard_map/ppermute | solution.py:32
  9.7 1.3 collective-permute-start.1
  12.3 1.9 %while.13 = (s32[]{:T(128)}, f32[32]{0:T(128)S(1)}, f32[4,512]{1,0:T(4,128)S(1)}, bf16[4,512,32]{1,2,0:T(8,128)(2,1)S(1)}, s32[]{:T(128)}, /*index=5*/s32[]{:T(128)}) while((s32[]{:T(128)}, f32[32]{0:T(128)S(1)}, f32[4,512]{1,0:T(4,128)S(1)}, bf16[4,512,32]{1,2,0:T(8,128)(2,1)S(1)}, s32[]{:T(128)}, /*index=5*/s32[]{:T(128)}) %tuple.42), condition=%wide.region_3.4_spmd.clone, body=%wide.region_0.3_spmd.clone.sunk | while | flops 17399332 | bytes 106719 | solution.py:228
  14.9 15.0 %shard_map.104 = (f32[8192,128]{1,0:T(8,128)}, f32[4096,128]{1,0:T(8,128)}) custom-call(s32[2048]{0:T(1024)} %fusion.57.slot_ref, s32[2048]{0:T(1024)} %act_ref.3, f32[64,64,128]{2,1,0:T(8,128)} %u_hbm.1, f32[64,64,128]{2,1,0:T(8,128)} %v_hbm.1), custom_call_target="tpu_custom_call" | custom-call | tf_op jit(solution)/shard_map/pallas_call | solution.py:250
  29.9 1.6 %collective-permute-done = f32[129,4,128]{0,2,1:T(8,128)S(1)} collective-permute-done((f32[129,4,128]{0,2,1:T(8,128)S(1)}, f32[129,4,128]{0,2,1:T(8,128)S(1)}, u32[]{:S(2)}, u32[]{:S(2)}) %collective-permute-start) | collective-permute-done | bytes 264224 | tf_op jit(solution)/shard_map/ppermute | solution.py:32
  31.5 6.0 %all-to-all-start = ((f32[16,256,128]{2,1,0:T(8,128)}), f32[16,256,128]{2,1,0:T(8,128)S(1)}, u32[]{:S(2)}, u32[]{:S(2)}) async-start(f32[16,256,128]{2,1,0:T(8,128)} %bitcast.89), calls=%async_computation | async-start | bytes 4194304 | tf_op jit(solution)/shard_map/all_to_all | solution.py:267
  38.5 1.0 slice.70
  40.4 1.0 slice_bitcast_fusion
  41.5 1.3 fusion.50
  42.8 1.3 collective-permute-start.2
  44.1 3.2 %collective-permute-start.3 = (f32[73,4,128]{2,1,0:T(4,128)S(1)}, f32[73,4,128]{2,1,0:T(4,128)S(1)}, u32[]{:S(2)}, u32[]{:S(2)}) collective-permute-start(f32[73,4,128]{2,1,0:T(4,128)S(1)} %get-tuple-element.78), channel_id=1, source_target_pairs={{0,1},{1,2},{2,3},{4,5},{5,6},{6,7},{8,9},{9,10},{10,11},{12,13},{... | collective-permute-start | bytes 448520 | tf_op jit(solution)/shard_map/ppermute | solution.py:53
  47.4 2.7 %collective-permute-start.7 = (f32[256,128]{1,0:T(8,128)S(1)}, f32[256,128]{1,0:T(8,128)}, u32[]{:S(2)}, u32[]{:S(2)}) collective-permute-start(f32[256,128]{1,0:T(8,128)S(1)} %bitcast.97), channel_id=1, source_target_pairs={{0,16},{4,20},{8,24},{12,28},{16,0},{20,4},{24,8},{28,12},{1,17},{... | collective-permute-start | bytes 393224 | tf_op jit(solution)/shard_map/ppermute | solution.py:244
  50.4 2.6 %collective-permute-start.6 = (f32[256,256]{1,0:T(8,128)}, f32[256,256]{1,0:T(8,128)}, u32[]{:S(2)}, u32[]{:S(2)}) collective-permute-start(f32[256,256]{1,0:T(8,128)} %bitcast.16), channel_id=1, source_target_pairs={{0,16},{4,20},{8,24},{12,28},{16,0},{20,4},{24,8},{28,12},{1,17},{... | collective-permute-start | bytes 786440 | tf_op jit(solution)/shard_map/ppermute | solution.py:244
  54.1 26.6 %all-to-all-done = f32[16,256,128]{2,1,0:T(8,128)S(1)} async-done(((f32[16,256,128]{2,1,0:T(8,128)}), f32[16,256,128]{2,1,0:T(8,128)S(1)}, u32[]{:S(2)}, u32[]{:S(2)}) %all-to-all-start) | async-done | bytes 2097184 | tf_op jit(solution)/shard_map/all_to_all | solution.py:267
  81.1 0.9 multiply_reduce_fusion.1
  82.1 1.3 subtract_multiply_fusion
  83.4 1.0 fusion.65
  84.4 1.3 fusion.36
  85.6 2.3 %divide_multiply_fusion = f32[2048,256]{1,0:T(8,128)S(1)} fusion(f32[2048,256]{1,0:T(8,128)S(1)} %fusion.36, f32[1,256,256]{2,1,0:T(8,128)} %param.18), kind=kOutput, calls=%fused_computation.31 | convolution fusion | flops 809500672 | bytes 4456448 | tf_op jit(solution)/shard_map/dot_general | solution.py:75
  88.5 1.0 fusion.76
  89.5 2.2 %fusion.22 = f32[2048,256]{1,0:T(8,128)S(1)} fusion(f32[256,256]{1,0:T(8,128)} %collective-permute-done.5, f32[2048,256]{1,0:T(8,128)S(1)} %fusion.76), kind=kOutput, calls=%fused_computation.25 | convolution fusion | flops 807403520 | bytes 4456448 | tf_op jit(solution)/shard_map/dot_general | solution.py:74
  91.8 2.2 %fusion.16 = f32[2048,256]{1,0:T(8,128)S(1)} fusion(f32[256,256]{1,0:T(8,128)} %collective-permute-done.6, f32[2048,256]{1,0:T(8,128)S(1)} %fusion.22), kind=kOutput, calls=%fused_computation.19 | convolution fusion | flops 807403520 | bytes 4456448 | tf_op jit(solution)/shard_map/dot_general | solution.py:75
  94.0 1.0 fusion.51
  95.0 2.2 %fusion.10 = f32[2048,128]{1,0:T(8,128)S(1)} fusion(f32[256,128]{1,0:T(8,128)} %collective-permute-done.7, f32[2048,256]{1,0:T(8,128)S(1)} %fusion.16), kind=kOutput, calls=%fused_computation.13 | convolution fusion | flops 404750336 | bytes 3276800 | tf_op jit(solution)/shard_map/dot_general | solution.py:76
  97.2 1.5 %pad_maximum_fusion = f32[16,256,128]{2,1,0:T(8,128)} fusion(f32[16,128,128]{2,1,0:T(8,128)S(1)} %bitcast.91, f32[16,128,128]{2,1,0:T(8,128)S(1)} %fusion.51), kind=kLoop, calls=%fused_computation.12 | loop fusion | flops 524288 | bytes 4194304 | tf_op jit(solution)/shard_map/concatenate | solution.py:286
  98.6 4.4 %all-to-all-start.1 = ((f32[16,256,128]{2,1,0:T(8,128)}), f32[16,256,128]{2,1,0:T(8,128)}, u32[]{:S(2)}, u32[]{:S(2)}) async-start(f32[16,256,128]{2,1,0:T(8,128)} %pad_maximum_fusion), calls=%async_computation.1 | async-start | bytes 4194304 | tf_op jit(solution)/shard_map/all_to_all | solution.py:290
  103.3 3.4 %broadcast_in_dim.42.c_ref = f32[72,136,128]{2,1,0:T(8,128)} broadcast(f32[72,136]{1,0:T(8,128)S(1)} %copy.28), dimensions={0,1} | broadcast | bytes 5052672 | tf_op jit(solution)/shard_map/broadcast_in_dim | solution.py:61
  106.7 15.3 %shard_map.105 = f32[64,128,128]{2,1,0:T(8,128)} custom-call(f32[64,128,128]{2,1,0:T(8,128)} %bitcast.86, f32[4,128,128]{2,1,0:T(8,128)} %copy-done.1, f32[4,128,128]{2,1,0:T(8,128)} %copy-done, f32[72,8,128]{2,1,0:T(8,128)} %pad_maximum_fusion.3.yh_ref, f32[72,136,128]{2,1,0:T(8,128)} %broadcast_in_dim.42.c_ref), custom_call_target="tpu_custom_call" | custom-call | tf_op jit(solution)/shard_map/pallas_call | solution.py:301
  122.0 10.8 %all-to-all-done.1 = f32[16,256,128]{2,1,0:T(8,128)} async-done(((f32[16,256,128]{2,1,0:T(8,128)}), f32[16,256,128]{2,1,0:T(8,128)}, u32[]{:S(2)}, u32[]{:S(2)}) %all-to-all-start.1) | async-done | bytes 2097184 | tf_op jit(solution)/shard_map/all_to_all | solution.py:290
  132.8 9.5 %shard_map.106 = (f32[64,64,128]{2,1,0:T(8,128)}, f32[64,64,128]{2,1,0:T(8,128)}) custom-call(s32[2048]{0:T(1024)} %fusion.57.slot_ref, s32[2048]{0:T(1024)} %act_ref.3, f32[4096,128]{1,0:T(8,128)} %bitcast.24.r_ref, f32[8192,128]{1,0:T(8,128)} %bitcast.87), custom_call_target="tpu_custom_call" | custom-call | tf_op jit(solution)/shard_map/pallas_call | solution.py:312
  (76 shorter events, 10.3 us)
Async XLA Ops:
  3.8 7.8 %copy-start.5 = (s32[2048,1]{0,1:T(1,128)S(1)}, s32[2048,1]{0,1:T(1,128)}, u32[]{:S(2)}) copy-start(s32[2048,1]{0,1:T(1,128)} %param.15) | copy-start | bytes 24580
  4.2 27.3 %collective-permute-start = (f32[129,4,128]{0,2,1:T(8,128)S(1)}, f32[129,4,128]{0,2,1:T(8,128)S(1)}, u32[]{:S(2)}, u32[]{:S(2)}) collective-permute-start(f32[129,4,128]{0,2,1:T(8,128)S(1)} %pad_maximum_fusion.1), channel_id=1, source_target_pairs={{0,4},{4,8},{8,12},{12,16},{16,20},{20,24},{24,28},{1,5},{5,9},{9,... | collective-permute-start | bytes 792584 | tf_op jit(solution)/shard_map/ppermute | solution.py:32
  9.7 21.7 %collective-permute-start.1 = (f32[129,4,128]{0,2,1:T(8,128)S(1)}, f32[129,4,128]{0,2,1:T(8,128)}, u32[]{:S(2)}, u32[]{:S(2)}) collective-permute-start(f32[129,4,128]{0,2,1:T(8,128)S(1)} %pad_maximum_fusion.2), channel_id=1, source_target_pairs={{4,0},{8,4},{12,8},{16,12},{20,16},{24,20},{28,24},{5,1},{9,5},{13... | collective-permute-start | bytes 792584 | tf_op jit(solution)/shard_map/ppermute | solution.py:33
  31.5 6.0 %copy-start.4 = (f32[64,128]{1,0:T(8,128)S(1)}, f32[64,128]{1,0:T(8,128)}, u32[]{:S(2)}) copy-start(f32[64,128]{1,0:T(8,128)} %param.13) | copy-start | bytes 98308
  31.5 49.3 %all-to-all-start = ((f32[16,256,128]{2,1,0:T(8,128)}), f32[16,256,128]{2,1,0:T(8,128)S(1)}, u32[]{:S(2)}, u32[]{:S(2)}) async-start(f32[16,256,128]{2,1,0:T(8,128)} %bitcast.89), calls=%async_computation | async-start | bytes 4194304 | tf_op jit(solution)/shard_map/all_to_all | solution.py:267
  41.4 1.4 copy-start
  41.4 1.4 copy-start.1
  41.5 5.9 %copy-start.3 = (f32[1,256,128]{2,1,0:T(8,128)S(1)}, f32[1,256,128]{2,1,0:T(8,128)}, u32[]{:S(2)}) copy-start(f32[1,256,128]{2,1,0:T(8,128)} %param.19) | copy-start | bytes 393220
  41.5 8.6 %copy-start.2 = (f32[1,128,256]{2,1,0:T(8,128)S(1)}, f32[1,128,256]{2,1,0:T(8,128)}, u32[]{:S(2)}) copy-start(f32[1,128,256]{2,1,0:T(8,128)} %param.16) | copy-start | bytes 393220
  41.5 11.5 %copy-start.6 = (f32[1,256,256]{2,1,0:T(8,128)S(1)}, f32[1,256,256]{2,1,0:T(8,128)}, u32[]{:S(2)}) copy-start(f32[1,256,256]{2,1,0:T(8,128)} %param.17) | copy-start | bytes 786436
  42.8 10.1 %collective-permute-start.2 = (f32[73,4,128]{2,1,0:T(4,128)S(1)}, f32[73,4,128]{2,1,0:T(4,128)S(1)}, u32[]{:S(2)}, u32[]{:S(2)}) collective-permute-start(f32[73,4,128]{2,1,0:T(4,128)S(1)} %get-tuple-element.77), channel_id=1, source_target_pairs={{1,0},{2,1},{3,2},{5,4},{6,5},{7,6},{9,8},{10,9},{11,10},{13,12},{... | collective-permute-start | bytes 448520 | tf_op jit(solution)/shard_map/ppermute | solution.py:54
  44.1 9.2 %collective-permute-start.3 = (f32[73,4,128]{2,1,0:T(4,128)S(1)}, f32[73,4,128]{2,1,0:T(4,128)S(1)}, u32[]{:S(2)}, u32[]{:S(2)}) collective-permute-start(f32[73,4,128]{2,1,0:T(4,128)S(1)} %get-tuple-element.78), channel_id=1, source_target_pairs={{0,1},{1,2},{2,3},{4,5},{5,6},{6,7},{8,9},{9,10},{10,11},{12,13},{... | collective-permute-start | bytes 448520 | tf_op jit(solution)/shard_map/ppermute | solution.py:53
  47.4 47.6 %collective-permute-start.7 = (f32[256,128]{1,0:T(8,128)S(1)}, f32[256,128]{1,0:T(8,128)}, u32[]{:S(2)}, u32[]{:S(2)}) collective-permute-start(f32[256,128]{1,0:T(8,128)S(1)} %bitcast.97), channel_id=1, source_target_pairs={{0,16},{4,20},{8,24},{12,28},{16,0},{20,4},{24,8},{28,12},{1,17},{... | collective-permute-start | bytes 393224 | tf_op jit(solution)/shard_map/ppermute | solution.py:244
  50.0 38.5 %collective-permute-start.4 = (f32[128,256]{1,0:T(8,128)S(1)}, f32[128,256]{1,0:T(8,128)S(1)}, u32[]{:S(2)}, u32[]{:S(2)}) collective-permute-start(f32[128,256]{1,0:T(8,128)S(1)} %bitcast.96), channel_id=1, source_target_pairs={{0,16},{4,20},{8,24},{12,28},{16,0},{20,4},{24,8},{28,12},{1,17},{... | collective-permute-start | bytes 393224 | tf_op jit(solution)/shard_map/ppermute | solution.py:244
  50.4 41.4 %collective-permute-start.6 = (f32[256,256]{1,0:T(8,128)}, f32[256,256]{1,0:T(8,128)}, u32[]{:S(2)}, u32[]{:S(2)}) collective-permute-start(f32[256,256]{1,0:T(8,128)} %bitcast.16), channel_id=1, source_target_pairs={{0,16},{4,20},{8,24},{12,28},{16,0},{20,4},{24,8},{28,12},{1,17},{... | collective-permute-start | bytes 786440 | tf_op jit(solution)/shard_map/ppermute | solution.py:244
  53.0 36.6 %collective-permute-start.5 = (f32[256,256]{1,0:T(8,128)S(1)}, f32[256,256]{1,0:T(8,128)}, u32[]{:S(2)}, u32[]{:S(2)}) collective-permute-start(f32[256,256]{1,0:T(8,128)S(1)} %bitcast.101), channel_id=1, source_target_pairs={{0,16},{4,20},{8,24},{12,28},{16,0},{20,4},{24,8},{28,12},{1,17},{... | collective-permute-start | bytes 786440 | tf_op jit(solution)/shard_map/ppermute | solution.py:244
  98.6 34.1 %all-to-all-start.1 = ((f32[16,256,128]{2,1,0:T(8,128)}), f32[16,256,128]{2,1,0:T(8,128)}, u32[]{:S(2)}, u32[]{:S(2)}) async-start(f32[16,256,128]{2,1,0:T(8,128)} %pad_maximum_fusion), calls=%async_computation.1 | async-start | bytes 4194304 | tf_op jit(solution)/shard_map/all_to_all | solution.py:290

commit v20 on v19

--- a/solution.py
+++ b/solution.py
@@ -99,7 +99,7 @@
         o_ref[at, :] = jnp.zeros((chunk, features), jnp.float32)
         return carry
 
-    lax.fori_loop(0, o_ref.shape[0] // chunk, clear, 0)
+    lax.fori_loop(0, o_ref.shape[0] // chunk, clear, 0, unroll=8)
 
     def transpose_tile(x, carry):
         for copy in copies(x):
@@ -158,7 +158,7 @@
         d_ref[at, :] = jnp.zeros((width_y, features), jnp.float32)
         return carry
 
-    lax.fori_loop(0, width_x, clear, 0)
+    lax.fori_loop(0, width_x, clear, 0, unroll=8)
 
     def place(r, carry):
         d_ref[pl.ds(act_ref[r], 1), :] = r_ref[pl.ds(slot_ref[r], 1), :]

time: 143 us -> 143 us (level)
  no operation moved by 1% of the time
where the time goes in v20:
time: 143 us; the launch traced here: 142 us
  Pallas kernels  39.6 us (28%)
  waiting for transfers between devices  39 us (27%)
  starting transfers between devices  27.1 us (19%)
  matrix products  14.2 us (10%)
  local copies, waits for them, and re-layouts  11.8 us (8%)
  other arithmetic  9.19 us (6%)
    all_to_all x1, waiting for transfers between devices, body(): lax.all_to_all(outgoing.reshape(group_size, pair_slots, features), ('tile...  26.6 us
    pallas_call x1, Pallas kernels, body(): pl.pallas_call(diffuse_kernel, out_shape=jax.ShapeDtypeStruct((width_x, w...  15.3 us
    pallas_call x1, Pallas kernels, body(): pl.pallas_call(gather_kernel, out_shape=(jax.ShapeDtypeStruct((cells, fea...  14.9 us
    all_to_all x1, waiting for transfers between devices, body(): lax.all_to_all(answered, ('tile', 'inf'), split_axis=0, concat_axis=0, ti...  10.8 us
    pallas_call x1, Pallas kernels, body(): pl.pallas_call(finish_kernel, out_shape=(jax.ShapeDtypeStruct(u_field.sha...  9.42 us
    all_to_all x1, starting transfers between devices, body(): lax.all_to_all(outgoing.reshape(group_size, pair_slots, features), ('tile...  6.04 us
    ppermute x4, starting transfers between devices, body(): lax.ppermute(w[0], 'tile', swap)  5.92 us
    ppermute x1, starting transfers between devices, stencil_start(): before = lax.ppermute(x_piece(width_x - depth), 'tile', up)  4.9 us
  transfers between devices with their start and end apart: 10, of which 3 were waited for; matrix products, arithmetic and copies ran while one was open for 20% of the time, Pallas kernels for 21%

profile of v20, /device:TPU:0, one launch (start us, length us, event | category | flops | bytes accessed | tf_op | source)
XLA Modules:
  0.0 142.3 jit_solution(8408766156065853796)
XLA Ops:
  1.5 1.1 fusion.74
  2.7 1.1 fusion.75
  4.2 4.9 %collective-permute-start = (f32[129,4,128]{0,2,1:T(8,128)S(1)}, f32[129,4,128]{0,2,1:T(8,128)S(1)}, u32[]{:S(2)}, u32[]{:S(2)}) collective-permute-start(f32[129,4,128]{0,2,1:T(8,128)S(1)} %pad_maximum_fusion.1), channel_id=1, source_target_pairs={{0,4},{4,8},{8,12},{12,16},{16,20},{20,24},{24,28},{1,5},{5,9},{9,... | collective-permute-start | bytes 792584 | tf_op jit(solution)/shard_map/ppermute | solution.py:32
  9.7 1.3 collective-permute-start.1
  12.3 1.9 %while.13 = (s32[]{:T(128)}, f32[32]{0:T(128)S(1)}, f32[4,512]{1,0:T(4,128)S(1)}, bf16[4,512,32]{1,2,0:T(8,128)(2,1)S(1)}, s32[]{:T(128)}, /*index=5*/s32[]{:T(128)}) while((s32[]{:T(128)}, f32[32]{0:T(128)S(1)}, f32[4,512]{1,0:T(4,128)S(1)}, bf16[4,512,32]{1,2,0:T(8,128)(2,1)S(1)}, s32[]{:T(128)}, /*index=5*/s32[]{:T(128)}) %tuple.42), condition=%wide.region_3.4_spmd.clone, body=%wide.region_0.3_spmd.clone.sunk | while | flops 17399332 | bytes 106719 | solution.py:228
  14.9 14.9 %shard_map.104 = (f32[8192,128]{1,0:T(8,128)}, f32[4096,128]{1,0:T(8,128)}) custom-call(s32[2048]{0:T(1024)} %fusion.57.slot_ref, s32[2048]{0:T(1024)} %act_ref.3, f32[64,64,128]{2,1,0:T(8,128)} %u_hbm.1, f32[64,64,128]{2,1,0:T(8,128)} %v_hbm.1), custom_call_target="tpu_custom_call" | custom-call | tf_op jit(solution)/shard_map/pallas_call | solution.py:250
  29.8 1.6 %collective-permute-done = f32[129,4,128]{0,2,1:T(8,128)S(1)} collective-permute-done((f32[129,4,128]{0,2,1:T(8,128)S(1)}, f32[129,4,128]{0,2,1:T(8,128)S(1)}, u32[]{:S(2)}, u32[]{:S(2)}) %collective-permute-start) | collective-permute-done | bytes 264224 | tf_op jit(solution)/shard_map/ppermute | solution.py:32
  31.5 6.0 %all-to-all-start = ((f32[16,256,128]{2,1,0:T(8,128)}), f32[16,256,128]{2,1,0:T(8,128)S(1)}, u32[]{:S(2)}, u32[]{:S(2)}) async-start(f32[16,256,128]{2,1,0:T(8,128)} %bitcast.89), calls=%async_computation | async-start | bytes 4194304 | tf_op jit(solution)/shard_map/all_to_all | solution.py:267
  38.5 1.0 slice.70
  40.4 1.0 slice_bitcast_fusion
  41.5 1.3 fusion.50
  42.8 1.3 collective-permute-start.2
  44.1 3.2 %collective-permute-start.3 = (f32[73,4,128]{2,1,0:T(4,128)S(1)}, f32[73,4,128]{2,1,0:T(4,128)S(1)}, u32[]{:S(2)}, u32[]{:S(2)}) collective-permute-start(f32[73,4,128]{2,1,0:T(4,128)S(1)} %get-tuple-element.78), channel_id=1, source_target_pairs={{0,1},{1,2},{2,3},{4,5},{5,6},{6,7},{8,9},{9,10},{10,11},{12,13},{... | collective-permute-start | bytes 448520 | tf_op jit(solution)/shard_map/ppermute | solution.py:53
  47.4 2.7 %collective-permute-start.7 = (f32[256,128]{1,0:T(8,128)S(1)}, f32[256,128]{1,0:T(8,128)}, u32[]{:S(2)}, u32[]{:S(2)}) collective-permute-start(f32[256,128]{1,0:T(8,128)S(1)} %bitcast.97), channel_id=1, source_target_pairs={{0,16},{4,20},{8,24},{12,28},{16,0},{20,4},{24,8},{28,12},{1,17},{... | collective-permute-start | bytes 393224 | tf_op jit(solution)/shard_map/ppermute | solution.py:244
  50.4 2.6 %collective-permute-start.6 = (f32[256,256]{1,0:T(8,128)}, f32[256,256]{1,0:T(8,128)}, u32[]{:S(2)}, u32[]{:S(2)}) collective-permute-start(f32[256,256]{1,0:T(8,128)} %bitcast.16), channel_id=1, source_target_pairs={{0,16},{4,20},{8,24},{12,28},{16,0},{20,4},{24,8},{28,12},{1,17},{... | collective-permute-start | bytes 786440 | tf_op jit(solution)/shard_map/ppermute | solution.py:244
  54.1 26.6 %all-to-all-done = f32[16,256,128]{2,1,0:T(8,128)S(1)} async-done(((f32[16,256,128]{2,1,0:T(8,128)}), f32[16,256,128]{2,1,0:T(8,128)S(1)}, u32[]{:S(2)}, u32[]{:S(2)}) %all-to-all-start) | async-done | bytes 2097184 | tf_op jit(solution)/shard_map/all_to_all | solution.py:267
  81.1 0.9 multiply_reduce_fusion.1
  82.1 1.3 subtract_multiply_fusion
  83.4 1.0 fusion.65
  84.4 1.3 fusion.36
  85.6 2.3 %divide_multiply_fusion = f32[2048,256]{1,0:T(8,128)S(1)} fusion(f32[2048,256]{1,0:T(8,128)S(1)} %fusion.36, f32[1,256,256]{2,1,0:T(8,128)} %param.18), kind=kOutput, calls=%fused_computation.31 | convolution fusion | flops 809500672 | bytes 4456448 | tf_op jit(solution)/shard_map/dot_general | solution.py:75
  88.5 1.0 fusion.76
  89.5 2.2 %fusion.22 = f32[2048,256]{1,0:T(8,128)S(1)} fusion(f32[256,256]{1,0:T(8,128)} %collective-permute-done.5, f32[2048,256]{1,0:T(8,128)S(1)} %fusion.76), kind=kOutput, calls=%fused_computation.25 | convolution fusion | flops 807403520 | bytes 4456448 | tf_op jit(solution)/shard_map/dot_general | solution.py:74
  91.8 2.2 %fusion.16 = f32[2048,256]{1,0:T(8,128)S(1)} fusion(f32[256,256]{1,0:T(8,128)} %collective-permute-done.6, f32[2048,256]{1,0:T(8,128)S(1)} %fusion.22), kind=kOutput, calls=%fused_computation.19 | convolution fusion | flops 807403520 | bytes 4456448 | tf_op jit(solution)/shard_map/dot_general | solution.py:75
  94.0 1.0 fusion.51
  95.0 2.2 %fusion.10 = f32[2048,128]{1,0:T(8,128)S(1)} fusion(f32[256,128]{1,0:T(8,128)} %collective-permute-done.7, f32[2048,256]{1,0:T(8,128)S(1)} %fusion.16), kind=kOutput, calls=%fused_computation.13 | convolution fusion | flops 404750336 | bytes 3276800 | tf_op jit(solution)/shard_map/dot_general | solution.py:76
  97.2 1.5 %pad_maximum_fusion = f32[16,256,128]{2,1,0:T(8,128)} fusion(f32[16,128,128]{2,1,0:T(8,128)S(1)} %bitcast.91, f32[16,128,128]{2,1,0:T(8,128)S(1)} %fusion.51), kind=kLoop, calls=%fused_computation.12 | loop fusion | flops 524288 | bytes 4194304 | tf_op jit(solution)/shard_map/concatenate | solution.py:286
  98.6 4.4 %all-to-all-start.1 = ((f32[16,256,128]{2,1,0:T(8,128)}), f32[16,256,128]{2,1,0:T(8,128)}, u32[]{:S(2)}, u32[]{:S(2)}) async-start(f32[16,256,128]{2,1,0:T(8,128)} %pad_maximum_fusion), calls=%async_computation.1 | async-start | bytes 4194304 | tf_op jit(solution)/shard_map/all_to_all | solution.py:290
  103.3 3.4 %broadcast_in_dim.42.c_ref = f32[72,136,128]{2,1,0:T(8,128)} broadcast(f32[72,136]{1,0:T(8,128)S(1)} %copy.28), dimensions={0,1} | broadcast | bytes 5052672 | tf_op jit(solution)/shard_map/broadcast_in_dim | solution.py:61
  106.7 15.3 %shard_map.105 = f32[64,128,128]{2,1,0:T(8,128)} custom-call(f32[64,128,128]{2,1,0:T(8,128)} %bitcast.86, f32[4,128,128]{2,1,0:T(8,128)} %copy-done.1, f32[4,128,128]{2,1,0:T(8,128)} %copy-done, f32[72,8,128]{2,1,0:T(8,128)} %pad_maximum_fusion.3.yh_ref, f32[72,136,128]{2,1,0:T(8,128)} %broadcast_in_dim.42.c_ref), custom_call_target="tpu_custom_call" | custom-call | tf_op jit(solution)/shard_map/pallas_call | solution.py:301
  122.0 10.8 %all-to-all-done.1 = f32[16,256,128]{2,1,0:T(8,128)} async-done(((f32[16,256,128]{2,1,0:T(8,128)}), f32[16,256,128]{2,1,0:T(8,128)}, u32[]{:S(2)}, u32[]{:S(2)}) %all-to-all-start.1) | async-done | bytes 2097184 | tf_op jit(solution)/shard_map/all_to_all | solution.py:290
  132.8 9.4 %shard_map.106 = (f32[64,64,128]{2,1,0:T(8,128)}, f32[64,64,128]{2,1,0:T(8,128)}) custom-call(s32[2048]{0:T(1024)} %fusion.57.slot_ref, s32[2048]{0:T(1024)} %act_ref.3, f32[4096,128]{1,0:T(8,128)} %bitcast.24.r_ref, f32[8192,128]{1,0:T(8,128)} %bitcast.87), custom_call_target="tpu_custom_call" | custom-call | tf_op jit(solution)/shard_map/pallas_call | solution.py:312
  (76 shorter events, 10.3 us)
Async XLA Ops:
  3.8 7.8 %copy-start.5 = (s32[2048,1]{0,1:T(1,128)S(1)}, s32[2048,1]{0,1:T(1,128)}, u32[]{:S(2)}) copy-start(s32[2048,1]{0,1:T(1,128)} %param.15) | copy-start | bytes 24580
  4.2 27.3 %collective-permute-start = (f32[129,4,128]{0,2,1:T(8,128)S(1)}, f32[129,4,128]{0,2,1:T(8,128)S(1)}, u32[]{:S(2)}, u32[]{:S(2)}) collective-permute-start(f32[129,4,128]{0,2,1:T(8,128)S(1)} %pad_maximum_fusion.1), channel_id=1, source_target_pairs={{0,4},{4,8},{8,12},{12,16},{16,20},{20,24},{24,28},{1,5},{5,9},{9,... | collective-permute-start | bytes 792584 | tf_op jit(solution)/shard_map/ppermute | solution.py:32
  9.7 21.7 %collective-permute-start.1 = (f32[129,4,128]{0,2,1:T(8,128)S(1)}, f32[129,4,128]{0,2,1:T(8,128)}, u32[]{:S(2)}, u32[]{:S(2)}) collective-permute-start(f32[129,4,128]{0,2,1:T(8,128)S(1)} %pad_maximum_fusion.2), channel_id=1, source_target_pairs={{4,0},{8,4},{12,8},{16,12},{20,16},{24,20},{28,24},{5,1},{9,5},{13... | collective-permute-start | bytes 792584 | tf_op jit(solution)/shard_map/ppermute | solution.py:33
  31.5 6.0 %copy-start.4 = (f32[64,128]{1,0:T(8,128)S(1)}, f32[64,128]{1,0:T(8,128)}, u32[]{:S(2)}) copy-start(f32[64,128]{1,0:T(8,128)} %param.13) | copy-start | bytes 98308
  31.5 49.3 %all-to-all-start = ((f32[16,256,128]{2,1,0:T(8,128)}), f32[16,256,128]{2,1,0:T(8,128)S(1)}, u32[]{:S(2)}, u32[]{:S(2)}) async-start(f32[16,256,128]{2,1,0:T(8,128)} %bitcast.89), calls=%async_computation | async-start | bytes 4194304 | tf_op jit(solution)/shard_map/all_to_all | solution.py:267
  41.4 1.4 copy-start
  41.4 1.4 copy-start.1
  41.5 5.9 %copy-start.3 = (f32[1,256,128]{2,1,0:T(8,128)S(1)}, f32[1,256,128]{2,1,0:T(8,128)}, u32[]{:S(2)}) copy-start(f32[1,256,128]{2,1,0:T(8,128)} %param.19) | copy-start | bytes 393220
  41.5 8.6 %copy-start.2 = (f32[1,128,256]{2,1,0:T(8,128)S(1)}, f32[1,128,256]{2,1,0:T(8,128)}, u32[]{:S(2)}) copy-start(f32[1,128,256]{2,1,0:T(8,128)} %param.16) | copy-start | bytes 393220
  41.5 11.5 %copy-start.6 = (f32[1,256,256]{2,1,0:T(8,128)S(1)}, f32[1,256,256]{2,1,0:T(8,128)}, u32[]{:S(2)}) copy-start(f32[1,256,256]{2,1,0:T(8,128)} %param.17) | copy-start | bytes 786436
  42.8 10.1 %collective-permute-start.2 = (f32[73,4,128]{2,1,0:T(4,128)S(1)}, f32[73,4,128]{2,1,0:T(4,128)S(1)}, u32[]{:S(2)}, u32[]{:S(2)}) collective-permute-start(f32[73,4,128]{2,1,0:T(4,128)S(1)} %get-tuple-element.77), channel_id=1, source_target_pairs={{1,0},{2,1},{3,2},{5,4},{6,5},{7,6},{9,8},{10,9},{11,10},{13,12},{... | collective-permute-start | bytes 448520 | tf_op jit(solution)/shard_map/ppermute | solution.py:54
  44.1 9.2 %collective-permute-start.3 = (f32[73,4,128]{2,1,0:T(4,128)S(1)}, f32[73,4,128]{2,1,0:T(4,128)S(1)}, u32[]{:S(2)}, u32[]{:S(2)}) collective-permute-start(f32[73,4,128]{2,1,0:T(4,128)S(1)} %get-tuple-element.78), channel_id=1, source_target_pairs={{0,1},{1,2},{2,3},{4,5},{5,6},{6,7},{8,9},{9,10},{10,11},{12,13},{... | collective-permute-start | bytes 448520 | tf_op jit(solution)/shard_map/ppermute | solution.py:53
  47.4 47.6 %collective-permute-start.7 = (f32[256,128]{1,0:T(8,128)S(1)}, f32[256,128]{1,0:T(8,128)}, u32[]{:S(2)}, u32[]{:S(2)}) collective-permute-start(f32[256,128]{1,0:T(8,128)S(1)} %bitcast.97), channel_id=1, source_target_pairs={{0,16},{4,20},{8,24},{12,28},{16,0},{20,4},{24,8},{28,12},{1,17},{... | collective-permute-start | bytes 393224 | tf_op jit(solution)/shard_map/ppermute | solution.py:244
  50.0 38.5 %collective-permute-start.4 = (f32[128,256]{1,0:T(8,128)S(1)}, f32[128,256]{1,0:T(8,128)S(1)}, u32[]{:S(2)}, u32[]{:S(2)}) collective-permute-start(f32[128,256]{1,0:T(8,128)S(1)} %bitcast.96), channel_id=1, source_target_pairs={{0,16},{4,20},{8,24},{12,28},{16,0},{20,4},{24,8},{28,12},{1,17},{... | collective-permute-start | bytes 393224 | tf_op jit(solution)/shard_map/ppermute | solution.py:244
  50.4 41.4 %collective-permute-start.6 = (f32[256,256]{1,0:T(8,128)}, f32[256,256]{1,0:T(8,128)}, u32[]{:S(2)}, u32[]{:S(2)}) collective-permute-start(f32[256,256]{1,0:T(8,128)} %bitcast.16), channel_id=1, source_target_pairs={{0,16},{4,20},{8,24},{12,28},{16,0},{20,4},{24,8},{28,12},{1,17},{... | collective-permute-start | bytes 786440 | tf_op jit(solution)/shard_map/ppermute | solution.py:244
  53.0 36.6 %collective-permute-start.5 = (f32[256,256]{1,0:T(8,128)S(1)}, f32[256,256]{1,0:T(8,128)}, u32[]{:S(2)}, u32[]{:S(2)}) collective-permute-start(f32[256,256]{1,0:T(8,128)S(1)} %bitcast.101), channel_id=1, source_target_pairs={{0,16},{4,20},{8,24},{12,28},{16,0},{20,4},{24,8},{28,12},{1,17},{... | collective-permute-start | bytes 786440 | tf_op jit(solution)/shard_map/ppermute | solution.py:244
  98.6 34.1 %all-to-all-start.1 = ((f32[16,256,128]{2,1,0:T(8,128)}), f32[16,256,128]{2,1,0:T(8,128)}, u32[]{:S(2)}, u32[]{:S(2)}) async-start(f32[16,256,128]{2,1,0:T(8,128)} %pad_maximum_fusion), calls=%async_computation.1 | async-start | bytes 4194304 | tf_op jit(solution)/shard_map/all_to_all | solution.py:290
